TPU v7x, 256 devices: a whole 4x4x8 slice. The times are simulated.
256 devices in a mesh: dp: 4 (over z_lo), frame: 16 (over x, y), row: 4 (over z_hi, core).
Axes of the slice: x: 4, y: 4, z: 8 (z_hi: 2, z_lo: 4; z = z_hi * 4 + z_lo), core: 2. Of those that a mesh axis runs over, the one named last changes fastest.
Arguments:
- clip_input: bfloat16 [4, 64, 16, 240, 128], P('dp', 'frame', 'row'), may hold values from -6 to 6
- cotangent: bfloat16 [4, 64, 16, 240, 128], P('dp', 'frame', 'row'), may hold values from -6 to 6
- spatial_weight: bfloat16 [3, 3, 128, 128], replicated, may hold values from -0.1875 to 0.1875
- temporal_weight: bfloat16 [3, 128, 128], replicated, may hold values from -0.3125 to 0.3125
Outputs:
- block_output: bfloat16 [4, 64, 16, 240, 128], P('dp', 'frame', 'row')
- input_grad: bfloat16 [4, 64, 16, 240, 128], P('dp', 'frame', 'row')
- weight_grads: float32 [1536, 128], P(('dp', 'frame', 'row'))
All inputs are finite; a program needn't handle non-finite values.
Results may differ from a plain program's by a relative error of at most 0.0045.
Values may be sent and summed in bfloat16 or wider, within the bound.
No kernel may reach another device: no remote copies, remote signals or barrier semaphores. Data moves between devices by JAX's collectives and lax.ppermute only.
A program may use at most 64 MiB of HBM per device.

v0:
```python
import math

import jax
import jax.numpy as jnp
from jax import lax
from jax.sharding import PartitionSpec as P


def extended_2(shard, sides, width):
    for axis, dim in sides:
        peers, length = (lax.axis_size(axis), shard.shape[dim])
        up = [(i, (i + 1) % peers) for i in range(peers - 1)]
        down = [(j, i) for i, j in up]
        last = lax.slice_in_dim(shard, length - width, length, axis=dim)
        first = lax.slice_in_dim(shard, 0, width, axis=dim)
        before = lax.ppermute(last, axis, up)
        after = lax.ppermute(first, axis, down)
        shard = jnp.concatenate([before, shard, after], axis=dim)
    return shard


def spatial_taps(padded, weights, rows, cols):
    chans = padded.shape[-1]
    total = jnp.zeros((padded.shape[0] * rows * cols, weights.shape[-1]), jnp.float32)
    for i in range(3):
        for j in range(3):
            piece = padded[:, i : i + rows, j : j + cols, :].reshape(-1, chans)
            total = total + jnp.dot(piece, weights[i, j], preferred_element_type=jnp.float32)
    return total.reshape(padded.shape[0], rows, cols, -1)


def contract_rows(left, right):
    return lax.dot_general(
        left, right, (((0,), (0,)), ((), ())), preferred_element_type=jnp.float32
    )


def temporal_pass(earlier, act_now, grad_now, later, temporal_weight):
    frames = act_now.shape[0]
    chans = act_now.shape[-1]
    act_ext = jnp.concatenate([earlier, act_now], axis=0)
    grad_ext = jnp.concatenate([grad_now, later], axis=0)
    grad_flat = grad_now.reshape(-1, chans)
    mixed = jnp.zeros((grad_flat.shape[0], chans), jnp.float32)
    act_grad = jnp.zeros((grad_flat.shape[0], chans), jnp.float32)
    temporal_list = []
    for k in range(3):
        shifted = act_ext[2 - k : 2 - k + frames].reshape(-1, chans)
        mixed = mixed + jnp.dot(shifted, temporal_weight[k], preferred_element_type=jnp.float32)
        ahead = grad_ext[k : k + frames].reshape(-1, chans)
        act_grad = act_grad + jnp.dot(
            ahead, temporal_weight[k].T, preferred_element_type=jnp.float32
        )
        temporal_list.append(contract_rows(shifted, grad_flat))
    mixed = mixed.astype(jnp.bfloat16).reshape(act_now.shape)
    act_grad = act_grad.astype(jnp.bfloat16).reshape(act_now.shape)
    return (mixed, act_grad, jnp.concatenate(temporal_list, axis=0))


def on_device(clip_input, cotangent, spatial_weight, temporal_weight):
    frames = clip_input.shape[1]
    rows = clip_input.shape[2]
    cols = clip_input.shape[3]
    chans = clip_input.shape[4]
    cells = (
        lax.axis_size("dp") * frames * lax.axis_size("frame") * rows * lax.axis_size("row") * cols
    )
    scale = 1.0 / math.sqrt(cells)
    extended = extended_2(clip_input, (("row", 2),), 1)[0]
    xpad = jnp.pad(extended, ((0, 0), (0, 0), (1, 1), (0, 0)))
    pre = spatial_taps(xpad, spatial_weight, rows, cols)
    act = jax.nn.silu(pre).astype(jnp.bfloat16)
    grad_out = cotangent[0]
    act_band, grad_band = (
        lax.all_to_all(act[None], "frame", split_axis=3, concat_axis=1, tiled=True),
        lax.all_to_all(grad_out[None], "frame", split_axis=3, concat_axis=1, tiled=True),
    )
    act_band = act_band[0]
    grad_band = grad_band[0]
    edge_shape = (2,) + act_band.shape[1:]
    earlier = jnp.zeros(edge_shape, jnp.bfloat16)
    later = jnp.zeros(edge_shape, jnp.bfloat16)
    mixed_band, grad_act_band, temporal_terms = temporal_pass(
        earlier, act_band, grad_band, later, temporal_weight
    )
    mixed, act_grad = (
        lax.all_to_all(mixed_band[None], "frame", split_axis=1, concat_axis=3, tiled=True),
        lax.all_to_all(grad_act_band[None], "frame", split_axis=1, concat_axis=3, tiled=True),
    )
    mixed = mixed[0]
    act_grad = act_grad[0]
    block_output = (clip_input[0].astype(jnp.float32) + mixed.astype(jnp.float32)).astype(
        jnp.bfloat16
    )
    sigma = jax.nn.sigmoid(pre)
    pre_grad = (act_grad.astype(jnp.float32) * sigma * (1.0 + pre * (1.0 - sigma))).astype(
        jnp.bfloat16
    )
    pg_flat = pre_grad.reshape(-1, chans)
    spatial_list = []
    for i in range(3):
        for j in range(3):
            piece = xpad[:, i : i + rows, j : j + cols, :].reshape(-1, chans)
            spatial_list.append(contract_rows(piece, pg_flat))
    grad_ext = extended_2(pre_grad[None], (("row", 2),), 1)[0]
    gpad = jnp.pad(grad_ext, ((0, 0), (0, 0), (1, 1), (0, 0)))
    backward = jnp.zeros((frames * rows * cols, chans), jnp.float32)
    for i in range(3):
        for j in range(3):
            piece = gpad[:, 2 - i : 2 - i + rows, 2 - j : 2 - j + cols, :].reshape(-1, chans)
            backward = backward + jnp.dot(
                piece, spatial_weight[i, j].T, preferred_element_type=jnp.float32
            )
    input_grad = (grad_out.astype(jnp.float32).reshape(-1, chans) + backward).astype(jnp.bfloat16)
    input_grad = input_grad.reshape(clip_input.shape)
    partial_terms = jnp.concatenate(spatial_list + [temporal_terms], axis=0)
    summed = lax.psum_scatter(
        partial_terms, ("dp", "frame", "row"), scatter_dimension=0, tiled=True
    )
    return (block_output[None], input_grad, summed * scale)


def solution(mesh):
    placed = (P("dp", "frame", "row", None, None), P("dp", "frame", "row", None, None), P(), P())
    return jax.shard_map(
        on_device,
        mesh=mesh,
        in_specs=placed,
        out_specs=(
            P("dp", "frame", "row", None, None),
            P("dp", "frame", "row", None, None),
            P(("dp", "frame", "row"), None),
        ),
        check_vma=False,
    )
```

profile of v0, /device:TPU:1, one launch (start us, length us, event | category | flops | bytes accessed | tf_op | source)
XLA Modules:
  0.0 428.3 jit_solution(6160687649008563596)
XLA Ops:
  8.3 10.2 %collective-permute-start = (bf16[1,4,1,240,128]{4,3,2,1,0:T(8,128)(2,1)S(1)}, bf16[1,4,1,240,128]{4,3,2,1,0:T(8,128)(2,1)S(1)}, u32[]{:S(2)}, u32[]{:S(2)}) collective-permute-start(bf16[1,4,1,240,128]{4,3,2,1,0:T(8,128)(2,1)S(1)} %get-tuple-element.41), channel_id=1, source_target_pairs={{0,1},{1,2},{2,3},{4,5},{5,6},{6,7},{8,9},{9,10},{10,11},{12,13},{... | collective-permute-start | bytes 737288 | tf_op jit(solution)/shard_map/ppermute | solution.py:16
  18.5 2.1 collective-permute-start.1
  20.5 2.5 copy.129
  23.1 6.8 %all-to-all-start.2 = ((bf16[1,4,4,240,128]{4,2,1,0,3:T(4,128)(2,1)}), bf16[1,4,4,240,128]{4,2,1,0,3:T(4,128)(2,1)S(1)}, u32[]{:S(2)}, u32[]{:S(2)}) async-start(bf16[1,4,4,240,128]{4,2,1,0,3:T(4,128)(2,1)} %copy.129), calls=%async_computation.2 | async-start | bytes 1966080 | tf_op jit(solution)/shard_map/all_to_all | solution.py:76
  33.0 3.6 pad_slice_fusion.10
  38.6 1.7 convolution_add_fusion.15
  42.4 2.2 copy.133
  45.0 3.7 pad_slice_fusion
  50.6 1.8 copy.135
  60.3 6.0 %all-to-all-start.3 = ((bf16[1,64,4,15,128]{4,2,3,0,1:T(4,128)(2,1)}), bf16[1,64,4,15,128]{4,2,3,0,1:T(4,128)(2,1)}, u32[]{:S(2)}, u32[]{:S(2)}) async-start(bf16[1,64,4,15,128]{4,2,3,0,1:T(4,128)(2,1)} %copy.136), calls=%async_computation.3 | async-start | bytes 1966080 | tf_op jit(solution)/shard_map/all_to_all | solution.py:88
  66.3 2.1 convolution_add_fusion.14
  69.7 2.5 convolution_add_fusion.12
  72.1 5.6 %all-to-all-done.3 = bf16[1,64,4,15,128]{4,2,3,0,1:T(4,128)(2,1)} async-done(((bf16[1,64,4,15,128]{4,2,3,0,1:T(4,128)(2,1)}), bf16[1,64,4,15,128]{4,2,3,0,1:T(4,128)(2,1)}, u32[]{:S(2)}, u32[]{:S(2)}) %all-to-all-start.3) | async-done | bytes 983072 | tf_op jit(solution)/shard_map/all_to_all | solution.py:88
  77.8 1.5 copy.137
  81.6 2.0 fusion.17
  89.1 1.9 fusion.7
  92.3 4.3 %all-to-all-start = ((bf16[1,4,4,240,128]{4,2,1,0,3:T(4,128)(2,1)}), bf16[1,4,4,240,128]{4,2,1,0,3:T(4,128)(2,1)}, u32[]{:S(2)}, u32[]{:S(2)}) async-start(bf16[1,4,4,240,128]{4,2,1,0,3:T(4,128)(2,1)} %copy.120), calls=%async_computation | async-start | bytes 1966080 | tf_op jit(solution)/shard_map/all_to_all | solution.py:75
  97.7 8.7 %collective-permute-start.2 = (bf16[1,4,1,240,128]{4,3,2,1,0:T(8,128)(2,1)S(1)}, bf16[1,4,1,240,128]{4,3,2,1,0:T(8,128)(2,1)S(1)}, u32[]{:S(2)}, u32[]{:S(2)}) collective-permute-start(bf16[1,4,1,240,128]{4,3,2,1,0:T(8,128)(2,1)S(1)} %get-tuple-element.35), channel_id=1, source_target_pairs={{0,1},{1,2},{2,3},{4,5},{5,6},{6,7},{8,9},{9,10},{10,11},{12,13},{... | collective-permute-start | bytes 737288 | tf_op jit(solution)/shard_map/ppermute | solution.py:16
  106.4 1.9 collective-permute-start.3
  108.4 2.3 fusion.15
  111.8 7.8 %collective-permute-done.3 = bf16[1,4,1,240,128]{4,3,2,1,0:T(8,128)(2,1)S(1)} collective-permute-done((bf16[1,4,1,240,128]{4,3,2,1,0:T(8,128)(2,1)S(1)}, bf16[1,4,1,240,128]{4,3,2,1,0:T(8,128)(2,1)S(1)}, u32[]{:S(2)}, u32[]{:S(2)}) %collective-permute-start.3) | collective-permute-done | bytes 245792 | tf_op jit(solution)/shard_map/ppermute | solution.py:17
  119.8 4.1 pad_slice_fusion.4
  126.4 1.7 convolution_add_fusion.2
  132.1 2.5 fusion.8
  137.0 2.8 copy.126
  139.8 1.5 reshape.208
  141.3 2.2 reshape_squeeze.7
  143.5 1.6 fusion.28
  150.7 7.0 %all-to-all-start.1 = ((bf16[1,64,4,15,128]{4,2,3,0,1:T(4,128)(2,1)}), bf16[1,64,4,15,128]{4,2,3,0,1:T(4,128)(2,1)}, u32[]{:S(2)}, u32[]{:S(2)}) async-start(bf16[1,64,4,15,128]{4,2,3,0,1:T(4,128)(2,1)} %copy.127), calls=%async_computation.1 | async-start | bytes 1966080 | tf_op jit(solution)/shard_map/all_to_all | solution.py:87
  158.9 2.1 convolution_add_fusion.1
  161.0 2.1 fusion.3
  163.2 254.0 %all-reduce.7.cloned.1.call-done = f32[1536,128]{1,0:T(8,128)} async-done(((f32[1536,128]{1,0:T(8,128)}), f32[1536,128]{1,0:T(8,128)}) %all-reduce.7.cloned.1.call-update) | async-done | bytes 786448
  (102 shorter events, 50.9 us)
Async XLA Ops:
  8.3 21.6 %collective-permute-start = (bf16[1,4,1,240,128]{4,3,2,1,0:T(8,128)(2,1)S(1)}, bf16[1,4,1,240,128]{4,3,2,1,0:T(8,128)(2,1)S(1)}, u32[]{:S(2)}, u32[]{:S(2)}) collective-permute-start(bf16[1,4,1,240,128]{4,3,2,1,0:T(8,128)(2,1)S(1)} %get-tuple-element.41), channel_id=1, source_target_pairs={{0,1},{1,2},{2,3},{4,5},{5,6},{6,7},{8,9},{9,10},{10,11},{12,13},{... | collective-permute-start | bytes 737288 | tf_op jit(solution)/shard_map/ppermute | solution.py:16
  18.5 13.2 %copy-start.2 = (bf16[1,4,4,240,128]{4,3,2,1,0:T(8,128)(2,1)S(1)}, bf16[1,4,4,240,128]{4,3,2,1,0:T(8,128)(2,1)}, u32[]{:S(2)}) copy-start(bf16[1,4,4,240,128]{4,3,2,1,0:T(8,128)(2,1)} %param.4) | copy-start | bytes 2949124
  18.5 13.2 %collective-permute-start.1 = (bf16[1,4,1,240,128]{4,3,2,1,0:T(8,128)(2,1)S(1)}, bf16[1,4,1,240,128]{4,3,2,1,0:T(8,128)(2,1)}, u32[]{:S(2)}, u32[]{:S(2)}) collective-permute-start(bf16[1,4,1,240,128]{4,3,2,1,0:T(8,128)(2,1)S(1)} %get-tuple-element.42), channel_id=1, source_target_pairs={{1,0},{2,1},{3,2},{5,4},{6,5},{7,6},{9,8},{10,9},{11,10},{13,12},{... | collective-permute-start | bytes 737288 | tf_op jit(solution)/shard_map/ppermute | solution.py:17
  23.1 18.2 %all-to-all-start.2 = ((bf16[1,4,4,240,128]{4,2,1,0,3:T(4,128)(2,1)}), bf16[1,4,4,240,128]{4,2,1,0,3:T(4,128)(2,1)S(1)}, u32[]{:S(2)}, u32[]{:S(2)}) async-start(bf16[1,4,4,240,128]{4,2,1,0,3:T(4,128)(2,1)} %copy.129), calls=%async_computation.2 | async-start | bytes 1966080 | tf_op jit(solution)/shard_map/all_to_all | solution.py:76
  29.9 0.7 copy-start.19
  33.0 3.6 copy-start.15
  41.2 0.9 copy-start.12
  53.7 1.3 copy-start.11
  53.7 1.3 copy-start.17
  55.0 1.2 copy-start.14
  60.3 6.0 %copy-start.10 = (bf16[4,4,240,128]{3,2,1,0:T(8,128)(2,1)S(1)}, bf16[4,4,240,128]{3,2,1,0:T(8,128)(2,1)}, u32[]{:S(2)}) copy-start(bf16[4,4,240,128]{3,2,1,0:T(8,128)(2,1)} %get-tuple-element.30) | copy-start | bytes 2949124
  60.3 17.5 %all-to-all-start.3 = ((bf16[1,64,4,15,128]{4,2,3,0,1:T(4,128)(2,1)}), bf16[1,64,4,15,128]{4,2,3,0,1:T(4,128)(2,1)}, u32[]{:S(2)}, u32[]{:S(2)}) async-start(bf16[1,64,4,15,128]{4,2,3,0,1:T(4,128)(2,1)} %copy.136), calls=%async_computation.3 | async-start | bytes 1966080 | tf_op jit(solution)/shard_map/all_to_all | solution.py:88
  66.3 2.1 copy-start.9
  68.4 1.3 copy-start.8
  77.8 1.8 copy-start
  80.4 1.2 copy-start.3
  80.4 1.2 copy-start.20
  92.3 35.8 %all-to-all-start = ((bf16[1,4,4,240,128]{4,2,1,0,3:T(4,128)(2,1)}), bf16[1,4,4,240,128]{4,2,1,0,3:T(4,128)(2,1)}, u32[]{:S(2)}, u32[]{:S(2)}) async-start(bf16[1,4,4,240,128]{4,2,1,0,3:T(4,128)(2,1)} %copy.120), calls=%async_computation | async-start | bytes 1966080 | tf_op jit(solution)/shard_map/all_to_all | solution.py:75
  97.7 14.1 %collective-permute-start.2 = (bf16[1,4,1,240,128]{4,3,2,1,0:T(8,128)(2,1)S(1)}, bf16[1,4,1,240,128]{4,3,2,1,0:T(8,128)(2,1)S(1)}, u32[]{:S(2)}, u32[]{:S(2)}) collective-permute-start(bf16[1,4,1,240,128]{4,3,2,1,0:T(8,128)(2,1)S(1)} %get-tuple-element.35), channel_id=1, source_target_pairs={{0,1},{1,2},{2,3},{4,5},{5,6},{6,7},{8,9},{9,10},{10,11},{12,13},{... | collective-permute-start | bytes 737288 | tf_op jit(solution)/shard_map/ppermute | solution.py:16
  106.4 13.1 %collective-permute-start.3 = (bf16[1,4,1,240,128]{4,3,2,1,0:T(8,128)(2,1)S(1)}, bf16[1,4,1,240,128]{4,3,2,1,0:T(8,128)(2,1)S(1)}, u32[]{:S(2)}, u32[]{:S(2)}) collective-permute-start(bf16[1,4,1,240,128]{4,3,2,1,0:T(8,128)(2,1)S(1)} %get-tuple-element.36), channel_id=1, source_target_pairs={{1,0},{2,1},{3,2},{5,4},{6,5},{7,6},{9,8},{10,9},{11,10},{13,12},{... | collective-permute-start | bytes 737288 | tf_op jit(solution)/shard_map/ppermute | solution.py:17
  110.7 8.9 %copy-start.1 = (bf16[1,4,4,240,128]{4,3,2,1,0:T(8,128)(2,1)S(1)}, bf16[1,4,4,240,128]{4,3,2,1,0:T(8,128)(2,1)}, u32[]{:S(2)}) copy-start(bf16[1,4,4,240,128]{4,3,2,1,0:T(8,128)(2,1)} %get-tuple-element.15) | copy-start | bytes 2949124
  119.8 4.1 copy-start.16
  129.6 2.6 copy-start.13
  139.8 3.7 copy-start.18
  150.7 8.2 %copy-start.7 = (bf16[4,4,240,128]{3,2,1,0:T(8,128)(2,1)S(1)}, bf16[4,4,240,128]{3,2,1,0:T(8,128)(2,1)}, u32[]{:S(2)}) copy-start(bf16[4,4,240,128]{3,2,1,0:T(8,128)(2,1)} %get-tuple-element.22) | copy-start | bytes 2949124
  150.7 267.8 %all-to-all-start.1 = ((bf16[1,64,4,15,128]{4,2,3,0,1:T(4,128)(2,1)}), bf16[1,64,4,15,128]{4,2,3,0,1:T(4,128)(2,1)}, u32[]{:S(2)}, u32[]{:S(2)}) async-start(bf16[1,64,4,15,128]{4,2,3,0,1:T(4,128)(2,1)} %copy.127), calls=%async_computation.1 | async-start | bytes 1966080 | tf_op jit(solution)/shard_map/all_to_all | solution.py:87
  157.7 259.5 %all-reduce.7.cloned.1.call-start = ((), (), s32[]{:S(2)}) async-start(), calls=%async_computation.4 | async-start | bytes 1572864
  158.8 2.2 copy-start.5
  158.9 2.2 copy-start.6
  163.2 256.7 %copy-start.4 = (bf16[1,4,4,240,128]{4,3,2,1,0:T(8,128)(2,1)S(1)}, bf16[1,4,4,240,128]{4,3,2,1,0:T(8,128)(2,1)}, u32[]{:S(2)}) copy-start(bf16[1,4,4,240,128]{4,3,2,1,0:T(8,128)(2,1)} %param.4) | copy-start | bytes 2949124
Sparse Core Ops, SparseCore 0:
  163.9 253.2 all-reduce.6
where the time goes:
time: 430 us; the launch traced here: 428 us
  waiting for transfers between devices  270 us (63%)
  local copies, waits for them, and re-layouts  50.4 us (12%)
  starting transfers between devices  47 us (11%)
  matrix products  41 us (10%)
  between operations  14.5 us (3%)
  other arithmetic  5.85 us (1%)
    unnamed x2, waiting for transfers between devices  254 us
    ppermute x2, starting transfers between devices, extended_2(): before = lax.ppermute(last, axis, up)  18.9 us
    dot_general x12, matrix products, contract_rows(): lax.dot_general(left, right, (((0,), (0,)), ((), ())), preferred_element_...  16.6 us
    dot_general x9, matrix products, spatial_taps(): jnp.dot(piece, weights[i, j], preferred_element_type=jnp.float32)  9.48 us
    ppermute x2, waiting for transfers between devices, extended_2(): after = lax.ppermute(first, axis, down)  8.94 us
  transfers between devices with their start and end apart: 9, of which 5 were waited for; matrix products, arithmetic and copies ran while one was open for 9% of the time, Pallas kernels for 0%

commit v1 on v0

--- a/solution.py
+++ b/solution.py
@@ -57,6 +57,17 @@
     return (mixed, act_grad, jnp.concatenate(temporal_list, axis=0))
 
 
+def staged_scatter(terms):
+    n_dp, n_frame, n_row = (lax.axis_size(a) for a in ("dp", "frame", "row"))
+    rows = terms.shape[0] // (n_dp * n_frame * n_row)
+    blocks = terms.reshape(n_dp, n_frame, n_row, rows, terms.shape[-1])
+    blocks = jnp.transpose(blocks, (2, 0, 1, 3, 4))
+    blocks = lax.psum_scatter(blocks, "row", scatter_dimension=0, tiled=False)
+    blocks = jnp.transpose(blocks, (1, 0, 2, 3))
+    blocks = lax.psum_scatter(blocks, "frame", scatter_dimension=0, tiled=False)
+    return lax.psum_scatter(blocks, "dp", scatter_dimension=0, tiled=False)
+
+
 def on_device(clip_input, cotangent, spatial_weight, temporal_weight):
     frames = clip_input.shape[1]
     rows = clip_input.shape[2]
@@ -114,9 +125,7 @@
     input_grad = (grad_out.astype(jnp.float32).reshape(-1, chans) + backward).astype(jnp.bfloat16)
     input_grad = input_grad.reshape(clip_input.shape)
     partial_terms = jnp.concatenate(spatial_list + [temporal_terms], axis=0)
-    summed = lax.psum_scatter(
-        partial_terms, ("dp", "frame", "row"), scatter_dimension=0, tiled=True
-    )
+    summed = staged_scatter(partial_terms)
     return (block_output[None], input_grad, summed * scale)
 
 

time: 430 us -> 308 us (0.72)
  waiting for transfers between devices: 270 us -> 125 us
  blocking collectives: 0 us -> 15.4 us
  local copies, waits for them, and re-layouts: 50.4 us -> 59.1 us
  matrix products: 41 us -> 34.4 us
    unnamed x2 -> x3, waiting for transfers between devices: 254 us -> 88.8 us
    reduce_scatter x0 -> x1, waiting for transfers between devices: none -> 15.8 us  [staged_scatter(): blocks = lax.psum_scatter(blocks, 'row', scatter_dimension=0, tiled=False)]
    unnamed x0 -> x1, blocking collectives: none -> 15.4 us
    all_to_all x1, waiting for transfers between devices: 0.01 us -> 6.21 us  [on_device(): lax.all_to_all(mixed_band[None], 'frame', split_axis=1, concat_axis=3, ti...]
    dot_general x12, matrix products: 16.6 us -> 12.2 us  [contract_rows(): lax.dot_general(left, right, (((0,), (0,)), ((), ())), preferred_element_...]
    transpose x0 -> x2, local copies, waits for them, and re-layouts: none -> 4.34 us  [the longest x1 2.62 us: staged_scatter(): blocks = jnp.transpose(blocks, (2, 0, 1, 3, 4))]
    unnamed x44 -> x56, local copies, waits for them, and re-layouts: 6.29 us -> 9.17 us
  transfers between devices with their start and end apart: 9 -> 10, of which waited for: 5 -> 6; matrix products, arithmetic and copies ran while one was open for 9% -> 14% of each run, Pallas kernels for 0% -> 0%
where the time goes in v1:
time: 308 us; the launch traced here: 302 us
  waiting for transfers between devices  125 us (41%)
  local copies, waits for them, and re-layouts  59.1 us (19%)
  starting transfers between devices  48 us (16%)
  matrix products  34.4 us (11%)
  blocking collectives  15.4 us (5%)
  between operations  14.6 us (5%)
  other arithmetic  5.73 us (2%)
    unnamed x3, waiting for transfers between devices  88.8 us
    ppermute x2, starting transfers between devices, extended_2(): before = lax.ppermute(last, axis, up)  19.6 us
    reduce_scatter x1, waiting for transfers between devices, staged_scatter(): blocks = lax.psum_scatter(blocks, 'row', scatter_dimension=0, tiled=False)  15.8 us
    unnamed x1, blocking collectives  15.4 us
    dot_general x12, matrix products, contract_rows(): lax.dot_general(left, right, (((0,), (0,)), ((), ())), preferred_element_...  12.2 us
    dot_general x9, matrix products, spatial_taps(): jnp.dot(piece, weights[i, j], preferred_element_type=jnp.float32)  9.46 us
    unnamed x56, local copies, waits for them, and re-layouts  9.17 us
    dot_general x9, matrix products, on_device(): jnp.dot(piece, spatial_weight[i, j].T, preferred_element_type=jnp.float32)  8.5 us
  transfers between devices with their start and end apart: 10, of which 6 were waited for; matrix products, arithmetic and copies ran while one was open for 14% of the time, Pallas kernels for 0%

profile of v1, /device:TPU:1, one launch (start us, length us, event | category | flops | bytes accessed | tf_op | source)
XLA Modules:
  0.0 302.4 jit_solution(15115124727655329899)
XLA Ops:
  8.3 10.2 %collective-permute-start = (bf16[1,4,1,240,128]{4,3,2,1,0:T(8,128)(2,1)S(1)}, bf16[1,4,1,240,128]{4,3,2,1,0:T(8,128)(2,1)S(1)}, u32[]{:S(2)}, u32[]{:S(2)}) collective-permute-start(bf16[1,4,1,240,128]{4,3,2,1,0:T(8,128)(2,1)S(1)} %get-tuple-element.41), channel_id=1, source_target_pairs={{0,1},{1,2},{2,3},{4,5},{5,6},{6,7},{8,9},{9,10},{10,11},{12,13},{... | collective-permute-start | bytes 737288 | tf_op jit(solution)/shard_map/ppermute | solution.py:16
  18.5 2.1 collective-permute-start.1
  20.6 2.5 copy.133
  23.1 6.8 %all-to-all-start.2 = ((bf16[1,4,4,240,128]{4,2,1,0,3:T(4,128)(2,1)}), bf16[1,4,4,240,128]{4,2,1,0,3:T(4,128)(2,1)S(1)}, u32[]{:S(2)}, u32[]{:S(2)}) async-start(bf16[1,4,4,240,128]{4,2,1,0,3:T(4,128)(2,1)} %copy.133), calls=%async_computation.2 | async-start | bytes 1966080 | tf_op jit(solution)/shard_map/all_to_all | solution.py:87
  33.0 3.6 %pad_slice_fusion.10 = (bf16[4,4,240,128]{3,2,1,0:T(8,128)(2,1)}, bf16[4,4,240,128]{3,2,1,0:T(8,128)(2,1)S(1)}, bf16[4,4,240,128]{3,2,1,0:T(8,128)(2,1)S(1)}, bf...) fusion(bf16[4,6,240,128]{3,2,1,0:T(8,128)(2,1)S(1)} %maximum_bi, ...), kind=kLoop, calls=%fused_computation.73 | loop fusion | bytes 13271040 | tf_op jit(solution)/shard_map/slice | solution.py:27
  38.6 1.7 convolution_add_fusion.15
  42.5 2.2 copy.137
  45.0 3.6 %pad_slice_fusion = (bf16[64,4,15,128]{3,0,2,1:T(8,128)(2,1)}, bf16[64,4,15,128]{3,0,2,1:T(8,128)(2,1)S(1)}) fusion(bf16[64,4,15,128]{3,0,2,1:T(8,128)(2,1)} %bitcast.259), kind=kLoop, calls=%fused_computation.57 | loop fusion | bytes 2949120 | tf_op jit(solution)/shard_map/slice | solution.py:50
  50.6 1.8 copy.139
  60.3 6.0 %all-to-all-start.3 = ((bf16[1,64,4,15,128]{4,2,3,0,1:T(4,128)(2,1)}), bf16[1,64,4,15,128]{4,2,3,0,1:T(4,128)(2,1)}, u32[]{:S(2)}, u32[]{:S(2)}) async-start(bf16[1,64,4,15,128]{4,2,3,0,1:T(4,128)(2,1)} %copy.140), calls=%async_computation.3 | async-start | bytes 1966080 | tf_op jit(solution)/shard_map/all_to_all | solution.py:99
  66.3 2.1 convolution_add_fusion.14
  69.6 2.4 convolution_add_fusion.12
  72.0 5.7 %all-to-all-done.3 = bf16[1,64,4,15,128]{4,2,3,0,1:T(4,128)(2,1)} async-done(((bf16[1,64,4,15,128]{4,2,3,0,1:T(4,128)(2,1)}), bf16[1,64,4,15,128]{4,2,3,0,1:T(4,128)(2,1)}, u32[]{:S(2)}, u32[]{:S(2)}) %all-to-all-start.3) | async-done | bytes 983072 | tf_op jit(solution)/shard_map/all_to_all | solution.py:99
  86.2 1.9 fusion.7
  89.4 4.3 %all-to-all-start = ((bf16[1,4,4,240,128]{4,2,1,0,3:T(4,128)(2,1)}), bf16[1,4,4,240,128]{4,2,1,0,3:T(4,128)(2,1)}, u32[]{:S(2)}, u32[]{:S(2)}) async-start(bf16[1,4,4,240,128]{4,2,1,0,3:T(4,128)(2,1)} %copy.124), calls=%async_computation | async-start | bytes 1966080 | tf_op jit(solution)/shard_map/all_to_all | solution.py:86
  94.9 9.4 %collective-permute-start.2 = (bf16[1,4,1,240,128]{4,3,2,1,0:T(8,128)(2,1)S(1)}, bf16[1,4,1,240,128]{4,3,2,1,0:T(8,128)(2,1)S(1)}, u32[]{:S(2)}, u32[]{:S(2)}) collective-permute-start(bf16[1,4,1,240,128]{4,3,2,1,0:T(8,128)(2,1)S(1)} %get-tuple-element.35), channel_id=1, source_target_pairs={{0,1},{1,2},{2,3},{4,5},{5,6},{6,7},{8,9},{9,10},{10,11},{12,13},{... | collective-permute-start | bytes 737288 | tf_op jit(solution)/shard_map/ppermute | solution.py:16
  104.4 1.9 collective-permute-start.3
  106.3 2.3 fusion.15
  109.7 7.8 %collective-permute-done.3 = bf16[1,4,1,240,128]{4,3,2,1,0:T(8,128)(2,1)S(1)} collective-permute-done((bf16[1,4,1,240,128]{4,3,2,1,0:T(8,128)(2,1)S(1)}, bf16[1,4,1,240,128]{4,3,2,1,0:T(8,128)(2,1)S(1)}, u32[]{:S(2)}, u32[]{:S(2)}) %collective-permute-start.3) | collective-permute-done | bytes 245792 | tf_op jit(solution)/shard_map/ppermute | solution.py:17
  117.7 3.7 %pad_slice_fusion.4 = (bf16[4,4,240,128]{3,2,1,0:T(8,128)(2,1)}, bf16[4,4,240,128]{3,2,1,0:T(8,128)(2,1)S(1)}, bf16[4,4,240,128]{3,2,1,0:T(8,128)(2,1)S(1)}, bf1...) fusion(bf16[4,6,240,128]{3,2,1,0:T(8,128)(2,1)S(1)} %maximum_bi, ...), kind=kLoop, calls=%fused_computation.67 | loop fusion | bytes 13271040 | tf_op jit(solution)/shard_map/slice | solution.py:121
  123.4 1.7 convolution_add_fusion.3
  129.2 2.4 fusion.8
  134.1 2.9 copy.130
  140.6 2.3 reshape.229
  142.9 2.6 copy.144
  149.9 7.0 %all-to-all-start.1 = ((bf16[1,64,4,15,128]{4,2,3,0,1:T(4,128)(2,1)}), bf16[1,64,4,15,128]{4,2,3,0,1:T(4,128)(2,1)}, u32[]{:S(2)}, u32[]{:S(2)}) async-start(bf16[1,64,4,15,128]{4,2,3,0,1:T(4,128)(2,1)} %copy.131), calls=%async_computation.1 | async-start | bytes 1966080 | tf_op jit(solution)/shard_map/all_to_all | solution.py:98
  160.0 2.1 fusion.3
  162.1 6.2 %all-to-all-done.1 = bf16[1,64,4,15,128]{4,2,3,0,1:T(4,128)(2,1)} async-done(((bf16[1,64,4,15,128]{4,2,3,0,1:T(4,128)(2,1)}), bf16[1,64,4,15,128]{4,2,3,0,1:T(4,128)(2,1)}, u32[]{:S(2)}, u32[]{:S(2)}) %all-to-all-start.1) | async-done | bytes 983072 | tf_op jit(solution)/shard_map/all_to_all | solution.py:98
  169.7 15.8 %reduce-scatter.2.cloned.1.call-done = f32[1,4,16,6,128]{4,2,3,1,0:T(8,128)} async-done(((f32[4,4,16,6,128]{4,2,3,1,0:T(8,128)}), f32[1,4,16,6,128]{4,2,3,1,0:T(8,128)}) %reduce-scatter.2.cloned.1.call-update) | async-done | bytes 196624 | tf_op jit(solution)/shard_map/reduce_scatter | solution.py:65
  185.5 1.7 copy.145
  188.9 88.8 %all-reduce.8.cloned.1.call-done = f32[16,4,6,128]{3,1,2,0:T(4,128)} async-done(((f32[16,4,6,128]{3,1,2,0:T(4,128)}), f32[16,4,6,128]{3,1,2,0:T(4,128)}) %all-reduce.8.cloned.1.call-update) | async-done | bytes 196624
  279.0 15.4 %all-reduce.5 = f32[4,6,128]{2,1,0:T(8,128)S(1)} all-reduce(f32[4,6,128]{2,1,0:T(8,128)S(1)} %copy.146), channel_id=4, replica_groups=mesh['dp'=4,'frame'=16,'row'=4] {'dp'}, use_global_device_ids=true, to_apply=%region_2.3.clone | all-reduce | flops 3072 | bytes 24576
  (123 shorter events, 56.8 us)
Async XLA Ops:
  8.3 22.8 %collective-permute-start = (bf16[1,4,1,240,128]{4,3,2,1,0:T(8,128)(2,1)S(1)}, bf16[1,4,1,240,128]{4,3,2,1,0:T(8,128)(2,1)S(1)}, u32[]{:S(2)}, u32[]{:S(2)}) collective-permute-start(bf16[1,4,1,240,128]{4,3,2,1,0:T(8,128)(2,1)S(1)} %get-tuple-element.41), channel_id=1, source_target_pairs={{0,1},{1,2},{2,3},{4,5},{5,6},{6,7},{8,9},{9,10},{10,11},{12,13},{... | collective-permute-start | bytes 737288 | tf_op jit(solution)/shard_map/ppermute | solution.py:16
  18.5 11.4 %copy-start.25 = (u32[256]{0:T(256)S(1)}, u32[256]{0:T(256)}, u32[]{:S(2)}) copy-start(u32[256]{0:T(256)} %constant.22) | copy-start | bytes 3076
  18.5 12.0 %copy-start.24 = (u32[256]{0:T(256)S(1)}, u32[256]{0:T(256)}, u32[]{:S(2)}) copy-start(u32[256]{0:T(256)} %constant.26) | copy-start | bytes 3076
  18.5 13.3 %copy-start.3 = (bf16[1,4,4,240,128]{4,3,2,1,0:T(8,128)(2,1)S(1)}, bf16[1,4,4,240,128]{4,3,2,1,0:T(8,128)(2,1)}, u32[]{:S(2)}) copy-start(bf16[1,4,4,240,128]{4,3,2,1,0:T(8,128)(2,1)} %param.4) | copy-start | bytes 2949124
  18.5 13.2 %collective-permute-start.1 = (bf16[1,4,1,240,128]{4,3,2,1,0:T(8,128)(2,1)S(1)}, bf16[1,4,1,240,128]{4,3,2,1,0:T(8,128)(2,1)}, u32[]{:S(2)}, u32[]{:S(2)}) collective-permute-start(bf16[1,4,1,240,128]{4,3,2,1,0:T(8,128)(2,1)S(1)} %get-tuple-element.42), channel_id=1, source_target_pairs={{1,0},{2,1},{3,2},{5,4},{6,5},{7,6},{9,8},{10,9},{11,10},{13,12},{... | collective-permute-start | bytes 737288 | tf_op jit(solution)/shard_map/ppermute | solution.py:17
  23.1 18.2 %all-to-all-start.2 = ((bf16[1,4,4,240,128]{4,2,1,0,3:T(4,128)(2,1)}), bf16[1,4,4,240,128]{4,2,1,0,3:T(4,128)(2,1)S(1)}, u32[]{:S(2)}, u32[]{:S(2)}) async-start(bf16[1,4,4,240,128]{4,2,1,0,3:T(4,128)(2,1)} %copy.133), calls=%async_computation.2 | async-start | bytes 1966080 | tf_op jit(solution)/shard_map/all_to_all | solution.py:87
  33.0 3.6 %copy-start.17 = (bf16[3,3,128,128]{3,2,1,0:T(8,128)(2,1)S(1)}, bf16[3,3,128,128]{3,2,1,0:T(8,128)(2,1)}, u32[]{:S(2)}) copy-start(bf16[3,3,128,128]{3,2,1,0:T(8,128)(2,1)} %param.6) | copy-start | bytes 884740
  53.7 1.3 copy-start.13
  53.7 1.3 copy-start.20
  55.0 1.2 copy-start.16
  60.3 6.0 %copy-start.12 = (bf16[4,4,240,128]{3,2,1,0:T(8,128)(2,1)S(1)}, bf16[4,4,240,128]{3,2,1,0:T(8,128)(2,1)}, u32[]{:S(2)}) copy-start(bf16[4,4,240,128]{3,2,1,0:T(8,128)(2,1)} %get-tuple-element.30) | copy-start | bytes 2949124
  60.3 17.4 %all-to-all-start.3 = ((bf16[1,64,4,15,128]{4,2,3,0,1:T(4,128)(2,1)}), bf16[1,64,4,15,128]{4,2,3,0,1:T(4,128)(2,1)}, u32[]{:S(2)}, u32[]{:S(2)}) async-start(bf16[1,64,4,15,128]{4,2,3,0,1:T(4,128)(2,1)} %copy.140), calls=%async_computation.3 | async-start | bytes 1966080 | tf_op jit(solution)/shard_map/all_to_all | solution.py:99
  66.3 2.1 copy-start.11
  68.3 1.3 copy-start.10
  77.7 1.8 copy-start
  80.3 1.2 copy-start.23
  89.4 35.8 %all-to-all-start = ((bf16[1,4,4,240,128]{4,2,1,0,3:T(4,128)(2,1)}), bf16[1,4,4,240,128]{4,2,1,0,3:T(4,128)(2,1)}, u32[]{:S(2)}, u32[]{:S(2)}) async-start(bf16[1,4,4,240,128]{4,2,1,0,3:T(4,128)(2,1)} %copy.124), calls=%async_computation | async-start | bytes 1966080 | tf_op jit(solution)/shard_map/all_to_all | solution.py:86
  93.7 91.8 %reduce-scatter.2.cloned.1.call-start = ((), (), s32[]{:S(2)}) async-start(), calls=%async_computation.5 | async-start | bytes 983040 | tf_op jit(solution)/shard_map/reduce_scatter | solution.py:65
  94.9 14.8 %collective-permute-start.2 = (bf16[1,4,1,240,128]{4,3,2,1,0:T(8,128)(2,1)S(1)}, bf16[1,4,1,240,128]{4,3,2,1,0:T(8,128)(2,1)S(1)}, u32[]{:S(2)}, u32[]{:S(2)}) collective-permute-start(bf16[1,4,1,240,128]{4,3,2,1,0:T(8,128)(2,1)S(1)} %get-tuple-element.35), channel_id=1, source_target_pairs={{0,1},{1,2},{2,3},{4,5},{5,6},{6,7},{8,9},{9,10},{10,11},{12,13},{... | collective-permute-start | bytes 737288 | tf_op jit(solution)/shard_map/ppermute | solution.py:16
  104.4 13.1 %collective-permute-start.3 = (bf16[1,4,1,240,128]{4,3,2,1,0:T(8,128)(2,1)S(1)}, bf16[1,4,1,240,128]{4,3,2,1,0:T(8,128)(2,1)S(1)}, u32[]{:S(2)}, u32[]{:S(2)}) collective-permute-start(bf16[1,4,1,240,128]{4,3,2,1,0:T(8,128)(2,1)S(1)} %get-tuple-element.36), channel_id=1, source_target_pairs={{1,0},{2,1},{3,2},{5,4},{6,5},{7,6},{9,8},{10,9},{11,10},{13,12},{... | collective-permute-start | bytes 737288 | tf_op jit(solution)/shard_map/ppermute | solution.py:17
  108.6 8.9 %copy-start.2 = (bf16[1,4,4,240,128]{4,3,2,1,0:T(8,128)(2,1)S(1)}, bf16[1,4,4,240,128]{4,3,2,1,0:T(8,128)(2,1)}, u32[]{:S(2)}) copy-start(bf16[1,4,4,240,128]{4,3,2,1,0:T(8,128)(2,1)} %get-tuple-element.15) | copy-start | bytes 2949124
  117.7 3.7 %copy-start.18 = (bf16[3,3,128,128]{3,2,1,0:T(8,128)(2,1)S(1)}, bf16[3,3,128,128]{3,2,1,0:T(8,128)(2,1)}, u32[]{:S(2)}) copy-start(bf16[3,3,128,128]{3,2,1,0:T(8,128)(2,1)} %param.6) | copy-start | bytes 884740
  126.6 2.6 copy-start.15
  142.9 4.1 %copy-start.21 = (bf16[3,128,128]{2,1,0:T(8,128)(2,1)S(1)}, bf16[3,128,128]{2,1,0:T(8,128)(2,1)}, u32[]{:S(2)}) copy-start(bf16[3,128,128]{2,1,0:T(8,128)(2,1)} %param.7) | copy-start | bytes 294916
  148.5 8.6 %copy-start.1 = (f32[3840,128]{1,0:T(8,128)S(1)}, f32[3840,128]{1,0:T(8,128)}, u32[]{:S(2)}) copy-start(f32[3840,128]{1,0:T(8,128)} %convolution_add_fusion.3) | copy-start | bytes 5898244
  149.9 7.3 %copy-start.9 = (bf16[4,4,240,128]{3,2,1,0:T(8,128)(2,1)S(1)}, bf16[4,4,240,128]{3,2,1,0:T(8,128)(2,1)}, u32[]{:S(2)}) copy-start(bf16[4,4,240,128]{3,2,1,0:T(8,128)(2,1)} %get-tuple-element.21) | copy-start | bytes 2949124
  149.9 18.4 %all-to-all-start.1 = ((bf16[1,64,4,15,128]{4,2,3,0,1:T(4,128)(2,1)}), bf16[1,64,4,15,128]{4,2,3,0,1:T(4,128)(2,1)}, u32[]{:S(2)}, u32[]{:S(2)}) async-start(bf16[1,64,4,15,128]{4,2,3,0,1:T(4,128)(2,1)} %copy.131), calls=%async_computation.1 | async-start | bytes 1966080 | tf_op jit(solution)/shard_map/all_to_all | solution.py:98
  156.9 120.8 %all-reduce.8.cloned.1.call-start = ((), (), s32[]{:S(2)}) async-start(), calls=%async_computation.6 | async-start | bytes 393216
  157.2 1.3 copy-start.8
  158.5 1.3 copy-start.6
  158.5 1.5 copy-start.7
  162.1 25.1 %copy-start.5 = (bf16[1,4,4,240,128]{4,3,2,1,0:T(8,128)(2,1)S(1)}, bf16[1,4,4,240,128]{4,3,2,1,0:T(8,128)(2,1)}, u32[]{:S(2)}) copy-start(bf16[1,4,4,240,128]{4,3,2,1,0:T(8,128)(2,1)} %param.4) | copy-start | bytes 2949124
  (4 other events, 3.7 us)
Sparse Core Ops, SparseCore 0:
  145.7 39.7 reduce-scatter.1
  188.7 88.9 all-reduce.7

commit v2 on v1

v2 whole, which is shorter than its diff:
```python
import math

import jax
import jax.numpy as jnp
from jax import lax
from jax.sharding import PartitionSpec as P

CONV_DIMS = ("NHWC", "HWIO", "NHWC")
KERNEL_GRAD_DIMS = ("CHWN", "IHWO", "HWNC")


def row_halo(shard):
    peers = lax.axis_size("row")
    up = [(i, i + 1) for i in range(peers - 1)]
    down = [(i + 1, i) for i in range(peers - 1)]
    before = lax.ppermute(shard[:, -1:], "row", up)
    after = lax.ppermute(shard[:, :1], "row", down)
    return jnp.concatenate([before, shard, after], axis=1)


def frame_shift(piece, forward):
    peers = lax.axis_size("frame")
    if forward:
        pairs = [(i, i + 1) for i in range(peers - 1)]
    else:
        pairs = [(i + 1, i) for i in range(peers - 1)]
    return lax.ppermute(piece, "frame", pairs)


def a2a_sum(blocks, axis):
    got = lax.all_to_all(blocks, axis, split_axis=0, concat_axis=0, tiled=True)
    return jnp.sum(got, axis=0)


def staged_scatter(terms):
    n_dp, n_frame, n_row = (lax.axis_size(a) for a in ("dp", "frame", "row"))
    rows = terms.shape[0] // (n_dp * n_frame * n_row)
    chans = terms.shape[-1]
    blocks = terms.reshape(n_dp, n_frame, n_row, rows, chans)
    blocks = jnp.transpose(blocks, (2, 0, 1, 3, 4))
    blocks = a2a_sum(blocks, "row")
    blocks = jnp.transpose(blocks, (1, 0, 2, 3))
    blocks = a2a_sum(blocks, "frame")
    return a2a_sum(blocks, "dp")


def on_device(clip_input, cotangent, spatial_weight, temporal_weight):
    x = clip_input[0]
    g = cotangent[0]
    frames, rows, cols, chans = x.shape
    cells = (
        lax.axis_size("dp") * frames * lax.axis_size("frame") * rows * lax.axis_size("row") * cols
    )
    scale = 1.0 / math.sqrt(cells)
    f32 = jnp.float32

    x_ext = row_halo(x)
    g_next = frame_shift(g[:2], forward=False)
    pre = lax.conv_general_dilated(
        x_ext, spatial_weight, (1, 1), ((0, 0), (1, 1)),
        dimension_numbers=CONV_DIMS, preferred_element_type=f32,
    )
    act = jax.nn.silu(pre).astype(jnp.bfloat16)
    act_prev = frame_shift(act[frames - 2 :], forward=True)
    act_ext = jnp.concatenate([act_prev, act], axis=0)
    g_ext = jnp.concatenate([g, g_next], axis=0)
    g_flat = g.reshape(-1, chans)

    mixed = jnp.zeros((frames * rows * cols, chans), f32)
    act_grad = jnp.zeros((frames * rows * cols, chans), f32)
    temporal_list = []
    for k in range(3):
        shifted = act_ext[2 - k : 2 - k + frames].reshape(-1, chans)
        mixed = mixed + jnp.dot(shifted, temporal_weight[k], preferred_element_type=f32)
        ahead = g_ext[k : k + frames].reshape(-1, chans)
        act_grad = act_grad + jnp.dot(ahead, temporal_weight[k].T, preferred_element_type=f32)
        temporal_list.append(
            lax.dot_general(shifted, g_flat, (((0,), (0,)), ((), ())), preferred_element_type=f32)
        )
    mixed = mixed.astype(jnp.bfloat16).reshape(x.shape)
    act_grad = act_grad.astype(jnp.bfloat16).reshape(x.shape)
    block_output = (x.astype(f32) + mixed.astype(f32)).astype(jnp.bfloat16)

    sigma = jax.nn.sigmoid(pre)
    pre_grad = (act_grad.astype(f32) * sigma * (1.0 + pre * (1.0 - sigma))).astype(jnp.bfloat16)

    xpad = jnp.pad(x_ext, ((0, 0), (0, 0), (1, 1), (0, 0)))
    spatial_grad = lax.conv_general_dilated(
        xpad, pre_grad, (1, 1), ((0, 0), (0, 0)),
        dimension_numbers=KERNEL_GRAD_DIMS, preferred_element_type=f32,
    )
    pg_ext = row_halo(pre_grad)
    back_weight = jnp.transpose(jnp.flip(spatial_weight, (0, 1)), (0, 1, 3, 2))
    back = lax.conv_general_dilated(
        pg_ext, back_weight, (1, 1), ((0, 0), (1, 1)),
        dimension_numbers=CONV_DIMS, preferred_element_type=f32,
    )
    input_grad = (g.astype(f32) + back).astype(jnp.bfloat16)

    partial_terms = jnp.concatenate(
        [spatial_grad.reshape(-1, chans)] + temporal_list, axis=0
    )
    summed = staged_scatter(partial_terms)
    return (block_output[None], input_grad[None], summed * scale)


def solution(mesh):
    placed = (P("dp", "frame", "row", None, None), P("dp", "frame", "row", None, None), P(), P())
    return jax.shard_map(
        on_device,
        mesh=mesh,
        in_specs=placed,
        out_specs=(
            P("dp", "frame", "row", None, None),
            P("dp", "frame", "row", None, None),
            P(("dp", "frame", "row"), None),
        ),
        check_vma=False,
    )
```

time: 308 us -> 133 us (0.43); the launches traced: 302 us -> 131 us
  waiting for transfers between devices: 125 us -> 14.7 us
  local copies, waits for them, and re-layouts: 59.1 us -> 39.6 us
  blocking collectives: 15.4 us -> 0 us
  matrix products: 34.4 us -> 20.5 us
  between operations: 14.6 us -> 1.01 us
  other arithmetic: 5.73 us -> 13.4 us
  starting transfers between devices: 48 us -> 41.7 us
    unnamed x3 -> x0, waiting for transfers between devices: 88.8 us -> none
    dot_general x36 -> x9, matrix products: 34.4 us -> 8.94 us  [the longest x3 4.99 us: on_device(): jnp.dot(shifted, temporal_weight[k], preferred_element_type=f32)]
    slice x10 -> x6, local copies, waits for them, and re-layouts: 20.7 us -> 2.79 us  [the longest x2 1 us: row_halo(): before = lax.ppermute(shard[:, -1:], 'row', up)]
    reduce_scatter x1 -> x0, waiting for transfers between devices: 15.8 us -> none  [staged_scatter(): blocks = lax.psum_scatter(blocks, 'row', scatter_dimension=0, tiled=False)]
    unnamed x1 -> x0, blocking collectives: 15.4 us -> none
    conv_general_dilated x0 -> x3, matrix products: none -> 11.5 us  [the longest x1 4.55 us: on_device(): lax.conv_general_dilated(x_ext, spatial_weight, (1, 1), ((0, 0), (1, 1)),...]
    conv_general_dilated x0 -> x6, local copies, waits for them, and re-layouts: none -> 9.91 us  [the longest x4 9.61 us: on_device(): lax.conv_general_dilated(pg_ext, back_weight, (1, 1), ((0, 0), (1, 1)), d...]
    add x0 -> x2, local copies, waits for them, and re-layouts: none -> 6.76 us  [on_device(): 1.0 + pre * (1.0 - sigma)]
  transfers between devices with their start and end apart: 10 -> 9, of which waited for: 6 -> 3; matrix products, arithmetic and copies ran while one was open for 14% -> 49% of each run, Pallas kernels for 0% -> 0%
where the time goes in v2:
time: 133 us; the launch traced here: 131 us
  starting transfers between devices  41.7 us (31%)
  local copies, waits for them, and re-layouts  39.6 us (30%)
  matrix products  20.5 us (15%)
  waiting for transfers between devices  14.7 us (11%)
  other arithmetic  13.4 us (10%)
    all_to_all x3, starting transfers between devices, a2a_sum(): got = lax.all_to_all(blocks, axis, split_axis=0, concat_axis=0, tiled=True)  19.9 us
    ppermute x2, starting transfers between devices, row_halo(): before = lax.ppermute(shard[:, -1:], 'row', up)  12.4 us
    conv_general_dilated x4, local copies, waits for them, and re-layouts, on_device(): lax.conv_general_dilated(pg_ext, back_weight, (1, 1), ((0, 0), (1, 1)), d...  9.61 us
    ppermute x2, waiting for transfers between devices, row_halo(): after = lax.ppermute(shard[:, :1], 'row', down)  7.34 us
    all_to_all x3, waiting for transfers between devices, a2a_sum(): got = lax.all_to_all(blocks, axis, split_axis=0, concat_axis=0, tiled=True)  7.34 us
    add x2, local copies, waits for them, and re-layouts, on_device(): 1.0 + pre * (1.0 - sigma)  6.76 us
    unnamed x35, local copies, waits for them, and re-layouts  5.83 us
    div x2, local copies, waits for them, and re-layouts, on_device(): act = jax.nn.silu(pre).astype(jnp.bfloat16)  5.16 us
  transfers between devices with their start and end apart: 9, of which 3 were waited for; matrix products, arithmetic and copies ran while one was open for 49% of the time, Pallas kernels for 0%

profile of v2, /device:TPU:1, one launch (start us, length us, event | category | flops | bytes accessed | tf_op | source)
XLA Modules:
  0.0 130.9 jit_solution(13283752263366989625)
XLA Ops:
  0.7 2.1 %copy.110 = bf16[1,4,4,240,128]{4,1,3,2,0:T(4,128)(2,1)S(1)} copy(bf16[1,4,4,240,128]{4,3,2,1,0:T(8,128)(2,1)} %param.4) | data formatting | bytes 1966080 | tf_op args[0]
  2.9 10.2 %collective-permute-start = (bf16[4,1,240,128]{3,0,2,1:T(4,128)(2,1)S(1)}, bf16[4,1,240,128]{3,0,2,1:T(4,128)(2,1)S(1)}, u32[]{:S(2)}, u32[]{:S(2)}) collective-permute-start(bf16[4,1,240,128]{3,0,2,1:T(4,128)(2,1)S(1)} %get-tuple-element.15), channel_id=1, source_target_pairs={{0,1},{1,2},{2,3},{4,5},{5,6},{6,7},{8,9},{9,10},{10,11},{12,13},{... | collective-permute-start | bytes 737288 | tf_op jit(solution)/shard_map/ppermute | solution.py:16
  13.1 1.9 %collective-permute-start.1 = (bf16[4,1,240,128]{3,0,2,1:T(4,128)(2,1)S(1)}, bf16[4,1,240,128]{3,0,2,1:T(4,128)(2,1)S(1)}, u32[]{:S(2)}, u32[]{:S(2)}) collective-permute-start(bf16[4,1,240,128]{3,0,2,1:T(4,128)(2,1)S(1)} %get-tuple-element.16), channel_id=1, source_target_pairs={{1,0},{2,1},{3,2},{5,4},{6,5},{7,6},{9,8},{10,9},{11,10},{13,12},{... | collective-permute-start | bytes 737288 | tf_op jit(solution)/shard_map/ppermute | solution.py:17
  17.2 1.7 %fusion.34 = f32[3840,128]{1,0:T(8,128)} fusion(bf16[3840,128]{1,0:T(8,128)(2,1)S(1)} %bitcast.90, bf16[3,128,128]{2,1,0:T(8,128)(2,1)S(1)} %copy-done.11), kind=kOutput, calls=%fused_computation.56 | convolution fusion | flops 125829120 | bytes 2981888 | tf_op jit(solution)/shard_map/dot_general | solution.py:76
  18.9 7.3 %collective-permute-done.1 = bf16[4,1,240,128]{3,0,2,1:T(4,128)(2,1)S(1)} collective-permute-done((bf16[4,1,240,128]{3,0,2,1:T(4,128)(2,1)S(1)}, bf16[4,1,240,128]{3,0,2,1:T(4,128)(2,1)S(1)}, u32[]{:S(2)}, u32[]{:S(2)}) %collective-permute-start.1) | collective-permute-done | bytes 245792 | tf_op jit(solution)/shard_map/ppermute | solution.py:17
  29.4 4.5 %add_divide_fusion = (f32[4,32,31,128]{3,1,2,0:T(8,128)}, bf16[4,32,31,128]{3,1,2,0:T(8,128)(2,1)S(1)}, f32[4,32,31,128]{3,1,2,0:T(8,128)}) fusion(pred[32,31]{0,1:T(8,128)(4,1)S(1)} %copy-done.16, bf16[3,3,128,128]{3,2,1,0:T(8,128)(2,1)S(1)} %copy-done, bf16[6,4,7,2,128]{4,2,1,3,0:T(8,128)(2,1)S(1)} %slice.67, bf16[6,4,8,31,128]{4,2,1,3,0:T(8,128)(2,1)S(1)} %copy.77), kind=kOutput, calls=%fused_computation.12 | convolution fusion | flops 1179648000 | bytes 6984672 | tf_op jit(solution)/shard_map/conv_general_dilated | solution.py:59
  36.5 2.5 %copy.82 = f32[4,32,31,128]{3,2,1,0:T(8,128)} copy(f32[4,32,31,128]{3,1,2,0:T(8,128)S(1)} %copy-done.10) | data formatting | bytes 4063232 | tf_op jit(solution)/shard_map/jit(silu)/div | solution.py:63
  39.0 2.6 %reshape.64 = f32[4,4,248,128]{3,2,1,0:T(8,128)} reshape(f32[4,32,31,128]{3,2,1,0:T(8,128)} %copy.82) | data formatting | bytes 4063232 | tf_op jit(solution)/shard_map/jit(silu)/div | solution.py:63
  41.6 4.1 %copy.84 = f32[4,32,31,128]{3,2,1,0:T(8,128)} copy(f32[4,32,31,128]{3,1,2,0:T(8,128)} %get-tuple-element.8) | data formatting | bytes 4063232 | tf_op jit(solution)/shard_map/add | solution.py:85
  45.7 2.7 %reshape.66 = f32[4,4,248,128]{3,2,1,0:T(8,128)} reshape(f32[4,32,31,128]{3,2,1,0:T(8,128)} %copy.84) | data formatting | bytes 4063232 | tf_op jit(solution)/shard_map/add | solution.py:85
  48.4 3.2 %collective-permute-start.2 = (bf16[2,4,240,128]{3,2,0,1:T(8,128)(2,1)}, bf16[2,4,240,128]{3,2,0,1:T(8,128)(2,1)S(1)}, u32[]{:S(2)}, u32[]{:S(2)}) collective-permute-start(bf16[2,4,240,128]{3,2,0,1:T(8,128)(2,1)} %slice.69), channel_id=1, source_target_pairs={{0,4},{4,8},{8,12},{12,16},{16,20},{20,24},{24,28},{28,32},{32,36}... | collective-permute-start | bytes 1474568 | tf_op jit(solution)/shard_map/ppermute | solution.py:27
  52.1 1.7 %fusion.36 = f32[3840,128]{1,0:T(8,128)} fusion(bf16[3840,128]{1,0:T(8,128)(2,1)S(1)} %bitcast.98, bf16[3,128,128]{2,1,0:T(8,128)(2,1)S(1)} %copy-done.11), kind=kOutput, calls=%fused_computation.58 | convolution fusion | flops 125829120 | bytes 2981888 | tf_op jit(solution)/shard_map/dot_general | solution.py:74
  53.8 1.4 %pad_maximum_fusion.1 = (bf16[4,4,240,128]{3,2,1,0:T(8,128)(2,1)S(1)}, bf16[4,4,240,128]{3,2,1,0:T(8,128)(2,1)S(1)}) fusion(bf16[2,4,240,128]{3,2,1,0:T(8,128)(2,1)} %collective-permute-done.3, bf16[4,4,240,128]{3,2,1,0:T(8,128)(2,1)S(1)} %bitcast.92), kind=kLoop, calls=%fused_computation.43 | loop fusion | flops 983040 | bytes 3440640 | tf_op jit(solution)/shard_map/concatenate | solution.py:66
  59.0 2.2 %collective-permute-start.4 = (bf16[4,1,240,128]{3,2,0,1:T(8,128)(2,1)}, bf16[4,1,240,128]{3,2,0,1:T(8,128)(2,1)}, u32[]{:S(2)}, u32[]{:S(2)}) collective-permute-start(bf16[4,1,240,128]{3,2,0,1:T(8,128)(2,1)} %get-tuple-element.13), channel_id=1, source_target_pairs={{0,1},{1,2},{2,3},{4,5},{5,6},{6,7},{8,9},{9,10},{10,11},{12,13},{... | collective-permute-start | bytes 737288 | tf_op jit(solution)/shard_map/ppermute | solution.py:16
  61.2 3.0 %collective-permute-start.5 = (bf16[4,1,240,128]{3,2,0,1:T(8,128)(2,1)}, bf16[4,1,240,128]{3,2,0,1:T(8,128)(2,1)}, u32[]{:S(2)}, u32[]{:S(2)}) collective-permute-start(bf16[4,1,240,128]{3,2,0,1:T(8,128)(2,1)} %get-tuple-element.14), channel_id=1, source_target_pairs={{1,0},{2,1},{3,2},{5,4},{6,5},{7,6},{9,8},{10,9},{11,10},{13,12},{... | collective-permute-start | bytes 737288 | tf_op jit(solution)/shard_map/ppermute | solution.py:17
  64.2 4.3 %fusion.27 = f32[3,3,128,128]{3,2,1,0:T(8,128)S(1)} fusion(bf16[4,4,240,128]{3,2,0,1:T(8,128)(2,1)S(1)} %fusion.6, bf16[4,1,240,128]{3,0,2,1:T(4,128)(2,1)S(1)} %copy-done.15, bf16[4,4,240,128]{3,0,2,1:T(4,128)(2,1)S(1)} %bitcast.103, bf16[4,1,240,128]{3,0,2,1:T(4,128)(2,1)S(1)} %copy-done.13), kind=kOutput, calls=%fused_computation.46 | convolution fusion | flops 1133740032 | bytes 3047424 | tf_op jit(solution)/shard_map/conv_general_dilated | solution.py:88
  70.7 2.2 %reshape.50 = f32[4,16,4,6,128]{4,3,2,1,0:T(8,128)} reshape(f32[1536,128]{1,0:T(8,128)} %pad_maximum_fusion.3) | data formatting | bytes 1572864 | tf_op jit(solution)/shard_map/reshape | solution.py:39
  73.0 2.6 %copy.89 = f32[4,4,16,6,128]{4,2,3,1,0:T(8,128)} copy(f32[4,4,16,6,128]{4,3,0,2,1:T(8,128)} %bitcast.105) | data formatting | bytes 1572864 | tf_op jit(solution)/shard_map/transpose | solution.py:40
  75.6 6.5 %all-to-all-start = ((f32[4,4,16,6,128]{4,2,3,1,0:T(8,128)}), f32[4,4,16,6,128]{4,2,3,1,0:T(8,128)}, u32[]{:S(2)}, u32[]{:S(2)}) async-start(f32[4,4,16,6,128]{4,2,3,1,0:T(8,128)} %copy.89), calls=%async_computation | async-start | bytes 1572864 | tf_op jit(solution)/shard_map/all_to_all | solution.py:31
  82.0 1.5 %maximum_bitcast_fusion = bf16[6,4,240,128]{3,2,1,0:T(8,128)(2,1)S(1)} fusion(bf16[4,1,240,128]{3,2,0,1:T(8,128)(2,1)} %collective-permute-done.5, bf16[4,4,240,128]{3,2,0,1:T(8,128)(2,1)} %copy-done.7, bf16[4,1,240,128]{3,2,0,1:T(8,128)(2,1)} %collective-permute-done.4), kind=kLoop, calls=%fused_computation.39 | loop fusion | flops 1474560 | bytes 2949120 | tf_op jit(solution)/shard_map/concatenate | solution.py:18
  83.6 1.5 %pad.4 = bf16[6,4,248,128]{3,2,1,0:T(8,128)(2,1)} pad(bf16[6,4,240,128]{3,2,1,0:T(8,128)(2,1)S(1)} %maximum_bitcast_fusion, bf16[]{:T(256)} %constant.12), padding=0_0x0_0x1_7x0_0 | pad | bytes 2998274 | tf_op jit(solution)/shard_map/concatenate | solution.py:18
  85.1 3.4 %reshape.60 = bf16[6,4,8,31,128]{4,3,2,1,0:T(8,128)(2,1)} reshape(bf16[6,4,248,128]{3,2,1,0:T(8,128)(2,1)} %pad.4) | data formatting | bytes 3047424 | tf_op jit(solution)/shard_map/conv_general_dilated | solution.py:94
  89.5 2.1 %fusion.4 = bf16[6,4,8,33,128]{4,3,2,1,0:T(8,128)(2,1)S(1)} fusion(bf16[6,4,7,2,128]{4,3,2,1,0:T(2,128)(2,1)S(1)} %slice.78, bf16[6,4,8,31,128]{4,3,2,1,0:T(8,128)(2,1)} %reshape.60), kind=kLoop, calls=%fused_computation.13 | loop fusion | flops 4866048 | bytes 3231744 | tf_op jit(solution)/shard_map/conv_general_dilated | solution.py:94
  91.7 2.6 %fusion.21 = f32[4,32,31,128]{3,1,2,0:T(8,128)S(1)} fusion(bf16[3,3,128,128]{3,2,1,0:T(8,128)(2,1)S(1)} %copy-done, bf16[6,4,8,33,128]{4,3,2,1,0:T(8,128)(2,1)S(1)} %fusion.4, pred[32,31]{0,1:T(8,128)(4,1)S(1)} %copy-done.16), kind=kOutput, calls=%fused_computation.33 | convolution fusion | flops 1170718720 | bytes 3949536 | tf_op jit(solution)/shard_map/conv_general_dilated | solution.py:94
  94.3 2.5 %copy.86 = f32[4,32,31,128]{3,2,1,0:T(8,128)} copy(f32[4,32,31,128]{3,1,2,0:T(8,128)S(1)} %fusion.21) | data formatting | bytes 4063232 | tf_op jit(solution)/shard_map/conv_general_dilated | solution.py:94
  96.8 2.6 %reshape.68 = f32[4,4,248,128]{3,2,1,0:T(8,128)} reshape(f32[4,32,31,128]{3,2,1,0:T(8,128)} %copy.86) | data formatting | bytes 4063232 | tf_op jit(solution)/shard_map/conv_general_dilated | solution.py:94
  99.4 1.9 %convolution_add_fusion.3 = f32[3840,128]{1,0:T(8,128)S(1)} fusion(f32[3840,128]{1,0:T(8,128)} %fusion.36, bf16[3840,128]{1,0:T(8,128)(2,1)S(1)} %bitcast.96, bf16[3,128,128]{2,1,0:T(8,128)(2,1)S(1)} %copy-done.11), kind=kOutput, calls=%fused_computation.3 | convolution fusion | flops 126320640 | bytes 4947968 | tf_op jit(solution)/shard_map/dot_general | solution.py:74
  104.7 8.6 %all-to-all-start.1 = ((f32[16,4,6,128]{3,1,2,0:T(4,128)}), f32[16,4,6,128]{3,1,2,0:T(4,128)S(1)}, u32[]{:S(2)}, u32[]{:S(2)}) async-start(f32[16,4,6,128]{3,1,2,0:T(4,128)} %copy.90), calls=%async_computation.1 | async-start | bytes 393216 | tf_op jit(solution)/shard_map/all_to_all | solution.py:31
  113.4 2.8 %fusion.26 = bf16[1,4,4,240,128]{4,3,2,1,0:T(8,128)(2,1)} fusion(bf16[1,4,4,240,128]{4,3,2,1,0:T(8,128)(2,1)S(1)} %copy-done.1, f32[4,4,248,128]{3,2,1,0:T(8,128)} %reshape.68), kind=kLoop, calls=%fused_computation.42 | loop fusion | flops 1474560 | bytes 3932160 | tf_op jit(solution)/shard_map/broadcast_in_dim | solution.py:104
  116.2 4.1 %all-to-all-done.1 = f32[16,4,6,128]{3,1,2,0:T(4,128)S(1)} async-done(((f32[16,4,6,128]{3,1,2,0:T(4,128)}), f32[16,4,6,128]{3,1,2,0:T(4,128)S(1)}, u32[]{:S(2)}, u32[]{:S(2)}) %all-to-all-start.1) | async-done | bytes 196640 | tf_op jit(solution)/shard_map/all_to_all | solution.py:31
  121.0 4.8 %all-to-all-start.2 = ((f32[4,6,128]{2,1,0:T(8,128)}), f32[4,6,128]{2,1,0:T(8,128)S(1)}, u32[]{:S(2)}, u32[]{:S(2)}) async-start(f32[4,6,128]{2,1,0:T(8,128)} %copy.91), calls=%async_computation.2 | async-start | bytes 32768 | tf_op jit(solution)/shard_map/all_to_all | solution.py:31
  127.0 3.3 %all-to-all-done.2 = f32[4,6,128]{2,1,0:T(8,128)S(1)} async-done(((f32[4,6,128]{2,1,0:T(8,128)}), f32[4,6,128]{2,1,0:T(8,128)S(1)}, u32[]{:S(2)}, u32[]{:S(2)}) %all-to-all-start.2) | async-done | bytes 12320 | tf_op jit(solution)/shard_map/all_to_all | solution.py:31
  (72 shorter events, 21.1 us)
Async XLA Ops:
  0.6 28.4 %copy-start = (bf16[3,3,128,128]{3,2,1,0:T(8,128)(2,1)S(1)}, bf16[3,3,128,128]{3,2,1,0:T(8,128)(2,1)}, u32[]{:S(2)}) copy-start(bf16[3,3,128,128]{3,2,1,0:T(8,128)(2,1)} %param.6) | copy-start | bytes 884740
  0.6 14.4 %copy-start.1 = (bf16[1,4,4,240,128]{4,3,2,1,0:T(8,128)(2,1)S(1)}, bf16[1,4,4,240,128]{4,3,2,1,0:T(8,128)(2,1)}, u32[]{:S(2)}) copy-start(bf16[1,4,4,240,128]{4,3,2,1,0:T(8,128)(2,1)} %param.5) | copy-start | bytes 2949124
  0.7 16.5 %copy-start.11 = (bf16[3,128,128]{2,1,0:T(8,128)(2,1)S(1)}, bf16[3,128,128]{2,1,0:T(8,128)(2,1)}, u32[]{:S(2)}) copy-start(bf16[3,128,128]{2,1,0:T(8,128)(2,1)} %param.7) | copy-start | bytes 294916
  2.7 23.5 %copy-start.5 = (bf16[1,4,4,240,128]{4,1,3,2,0:T(4,128)(2,1)}, bf16[1,4,4,240,128]{4,1,3,2,0:T(4,128)(2,1)S(1)}, u32[]{:S(2)}) copy-start(bf16[1,4,4,240,128]{4,1,3,2,0:T(4,128)(2,1)S(1)} %copy.110) | copy-start | bytes 2949124
  2.9 16.0 %collective-permute-start = (bf16[4,1,240,128]{3,0,2,1:T(4,128)(2,1)S(1)}, bf16[4,1,240,128]{3,0,2,1:T(4,128)(2,1)S(1)}, u32[]{:S(2)}, u32[]{:S(2)}) collective-permute-start(bf16[4,1,240,128]{3,0,2,1:T(4,128)(2,1)S(1)} %get-tuple-element.15), channel_id=1, source_target_pairs={{0,1},{1,2},{2,3},{4,5},{5,6},{6,7},{8,9},{9,10},{10,11},{12,13},{... | collective-permute-start | bytes 737288 | tf_op jit(solution)/shard_map/ppermute | solution.py:16
  13.1 13.1 %collective-permute-start.1 = (bf16[4,1,240,128]{3,0,2,1:T(4,128)(2,1)S(1)}, bf16[4,1,240,128]{3,0,2,1:T(4,128)(2,1)S(1)}, u32[]{:S(2)}, u32[]{:S(2)}) collective-permute-start(bf16[4,1,240,128]{3,0,2,1:T(4,128)(2,1)S(1)} %get-tuple-element.16), channel_id=1, source_target_pairs={{1,0},{2,1},{3,2},{5,4},{6,5},{7,6},{9,8},{10,9},{11,10},{13,12},{... | collective-permute-start | bytes 737288 | tf_op jit(solution)/shard_map/ppermute | solution.py:17
  15.9 37.9 %collective-permute-start.3 = (bf16[2,4,240,128]{3,2,1,0:T(8,128)(2,1)}, bf16[2,4,240,128]{3,2,1,0:T(8,128)(2,1)}, u32[]{:S(2)}, u32[]{:S(2)}) collective-permute-start(bf16[2,4,240,128]{3,2,1,0:T(8,128)(2,1)} %slice_bitcast_fusion.3), channel_id=1, source_target_pairs={{4,0},{8,4},{12,8},{16,12},{20,16},{24,20},{28,24},{32,28},{36,32}... | collective-permute-start | bytes 1474568 | tf_op jit(solution)/shard_map/ppermute | solution.py:27
  18.9 7.3 %copy-start.12 = (bf16[4,1,240,128]{3,0,2,1:T(4,128)(2,1)}, bf16[4,1,240,128]{3,0,2,1:T(4,128)(2,1)S(1)}, u32[]{:S(2)}) copy-start(bf16[4,1,240,128]{3,0,2,1:T(4,128)(2,1)S(1)} %collective-permute-done) | copy-start | bytes 737284
  26.3 0.7 copy-start.14
  28.7 0.7 copy-start.16
  34.7 1.7 %copy-start.10 = (f32[4,32,31,128]{3,1,2,0:T(8,128)S(1)}, f32[4,32,31,128]{3,1,2,0:T(8,128)}, u32[]{:S(2)}) copy-start(f32[4,32,31,128]{3,1,2,0:T(8,128)} %get-tuple-element.6) | copy-start | bytes 6094852
  48.4 20.2 %collective-permute-start.2 = (bf16[2,4,240,128]{3,2,0,1:T(8,128)(2,1)}, bf16[2,4,240,128]{3,2,0,1:T(8,128)(2,1)S(1)}, u32[]{:S(2)}, u32[]{:S(2)}) collective-permute-start(bf16[2,4,240,128]{3,2,0,1:T(8,128)(2,1)} %slice.69), channel_id=1, source_target_pairs={{0,4},{4,8},{8,12},{12,16},{16,20},{20,24},{24,28},{28,32},{32,36}... | collective-permute-start | bytes 1474568 | tf_op jit(solution)/shard_map/ppermute | solution.py:27
  53.8 1.8 %copy-start.4 = (f32[3840,128]{1,0:T(8,128)S(1)}, f32[3840,128]{1,0:T(8,128)}, u32[]{:S(2)}) copy-start(f32[3840,128]{1,0:T(8,128)} %fusion.34) | copy-start | bytes 5898244
  55.6 1.6 %copy-start.3 = (f32[4,4,248,128]{3,2,1,0:T(8,128)S(1)}, f32[4,4,248,128]{3,2,1,0:T(8,128)}, u32[]{:S(2)}) copy-start(f32[4,4,248,128]{3,2,1,0:T(8,128)} %reshape.66) | copy-start | bytes 6094852
  56.0 1.9 %copy-start.2 = (f32[4,4,248,128]{3,2,1,0:T(8,128)S(1)}, f32[4,4,248,128]{3,2,1,0:T(8,128)}, u32[]{:S(2)}) copy-start(f32[4,4,248,128]{3,2,1,0:T(8,128)} %reshape.64) | copy-start | bytes 6094852
  57.9 6.3 %copy-start.6 = (bf16[1,4,4,240,128]{4,1,3,2,0:T(4,128)(2,1)S(1)}, bf16[1,4,4,240,128]{4,1,3,2,0:T(4,128)(2,1)}, u32[]{:S(2)}) copy-start(bf16[1,4,4,240,128]{4,1,3,2,0:T(4,128)(2,1)} %copy-done.5) | copy-start | bytes 2949124
  57.9 6.3 %copy-start.13 = (bf16[4,1,240,128]{3,0,2,1:T(4,128)(2,1)S(1)}, bf16[4,1,240,128]{3,0,2,1:T(4,128)(2,1)}, u32[]{:S(2)}) copy-start(bf16[4,1,240,128]{3,0,2,1:T(4,128)(2,1)} %copy-done.12) | copy-start | bytes 737284
  57.9 6.3 %copy-start.15 = (bf16[4,1,240,128]{3,0,2,1:T(4,128)(2,1)S(1)}, bf16[4,1,240,128]{3,0,2,1:T(4,128)(2,1)}, u32[]{:S(2)}) copy-start(bf16[4,1,240,128]{3,0,2,1:T(4,128)(2,1)} %copy-done.14) | copy-start | bytes 737284
  58.1 10.4 %copy-start.7 = (bf16[4,4,240,128]{3,2,0,1:T(8,128)(2,1)}, bf16[4,4,240,128]{3,2,0,1:T(8,128)(2,1)S(1)}, u32[]{:S(2)}) copy-start(bf16[4,4,240,128]{3,2,0,1:T(8,128)(2,1)S(1)} %fusion.6) | copy-start | bytes 2949124
  59.0 23.0 %collective-permute-start.4 = (bf16[4,1,240,128]{3,2,0,1:T(8,128)(2,1)}, bf16[4,1,240,128]{3,2,0,1:T(8,128)(2,1)}, u32[]{:S(2)}, u32[]{:S(2)}) collective-permute-start(bf16[4,1,240,128]{3,2,0,1:T(8,128)(2,1)} %get-tuple-element.13), channel_id=1, source_target_pairs={{0,1},{1,2},{2,3},{4,5},{5,6},{6,7},{8,9},{9,10},{10,11},{12,13},{... | collective-permute-start | bytes 737288 | tf_op jit(solution)/shard_map/ppermute | solution.py:16
  61.2 20.8 %collective-permute-start.5 = (bf16[4,1,240,128]{3,2,0,1:T(8,128)(2,1)}, bf16[4,1,240,128]{3,2,0,1:T(8,128)(2,1)}, u32[]{:S(2)}, u32[]{:S(2)}) collective-permute-start(bf16[4,1,240,128]{3,2,0,1:T(8,128)(2,1)} %get-tuple-element.14), channel_id=1, source_target_pairs={{1,0},{2,1},{3,2},{5,4},{6,5},{7,6},{9,8},{10,9},{11,10},{13,12},{... | collective-permute-start | bytes 737288 | tf_op jit(solution)/shard_map/ppermute | solution.py:17
  75.6 27.2 %all-to-all-start = ((f32[4,4,16,6,128]{4,2,3,1,0:T(8,128)}), f32[4,4,16,6,128]{4,2,3,1,0:T(8,128)}, u32[]{:S(2)}, u32[]{:S(2)}) async-start(f32[4,4,16,6,128]{4,2,3,1,0:T(8,128)} %copy.89), calls=%async_computation | async-start | bytes 1572864 | tf_op jit(solution)/shard_map/all_to_all | solution.py:31
  104.7 15.6 %all-to-all-start.1 = ((f32[16,4,6,128]{3,1,2,0:T(4,128)}), f32[16,4,6,128]{3,1,2,0:T(4,128)S(1)}, u32[]{:S(2)}, u32[]{:S(2)}) async-start(f32[16,4,6,128]{3,1,2,0:T(4,128)} %copy.90), calls=%async_computation.1 | async-start | bytes 393216 | tf_op jit(solution)/shard_map/all_to_all | solution.py:31
  113.4 12.4 %copy-start.8 = (bf16[1,4,4,240,128]{4,3,2,1,0:T(8,128)(2,1)S(1)}, bf16[1,4,4,240,128]{4,3,2,1,0:T(8,128)(2,1)}, u32[]{:S(2)}) copy-start(bf16[1,4,4,240,128]{4,3,2,1,0:T(8,128)(2,1)} %param.4) | copy-start | bytes 2949124
  113.4 12.4 %copy-start.9 = (bf16[3840,128]{1,0:T(8,128)(2,1)S(1)}, bf16[3840,128]{1,0:T(8,128)(2,1)}, u32[]{:S(2)}) copy-start(bf16[3840,128]{1,0:T(8,128)(2,1)} %fusion) | copy-start | bytes 2949124
  121.0 9.3 %all-to-all-start.2 = ((f32[4,6,128]{2,1,0:T(8,128)}), f32[4,6,128]{2,1,0:T(8,128)S(1)}, u32[]{:S(2)}, u32[]{:S(2)}) async-start(f32[4,6,128]{2,1,0:T(8,128)} %copy.91), calls=%async_computation.2 | async-start | bytes 32768 | tf_op jit(solution)/shard_map/all_to_all | solution.py:31

commit v3 on v2

--- a/solution.py
+++ b/solution.py
@@ -4,9 +4,6 @@
 import jax.numpy as jnp
 from jax import lax
 from jax.sharding import PartitionSpec as P
-
-CONV_DIMS = ("NHWC", "HWIO", "NHWC")
-KERNEL_GRAD_DIMS = ("CHWN", "IHWO", "HWNC")
 
 
 def row_halo(shard):
@@ -44,6 +41,14 @@
     return a2a_sum(blocks, "dp")
 
 
+def width_taps(a, reverse):
+    zero = jnp.zeros_like(a[:, :, :1])
+    left = jnp.concatenate([zero, a[:, :, :-1]], axis=2)
+    right = jnp.concatenate([a[:, :, 1:], zero], axis=2)
+    parts = [right, a, left] if reverse else [left, a, right]
+    return jnp.concatenate(parts, axis=-1)
+
+
 def on_device(clip_input, cotangent, spatial_weight, temporal_weight):
     x = clip_input[0]
     g = cotangent[0]
@@ -56,10 +61,13 @@
 
     x_ext = row_halo(x)
     g_next = frame_shift(g[:2], forward=False)
-    pre = lax.conv_general_dilated(
-        x_ext, spatial_weight, (1, 1), ((0, 0), (1, 1)),
-        dimension_numbers=CONV_DIMS, preferred_element_type=f32,
-    )
+    x3 = width_taps(x_ext, reverse=False)
+    fwd_weight = spatial_weight.reshape(3, 3 * chans, chans)
+    pre = jnp.zeros((frames * rows * cols, chans), f32)
+    for i in range(3):
+        piece = x3[:, i : i + rows].reshape(-1, 3 * chans)
+        pre = pre + jnp.dot(piece, fwd_weight[i], preferred_element_type=f32)
+    pre = pre.reshape(x.shape)
     act = jax.nn.silu(pre).astype(jnp.bfloat16)
     act_prev = frame_shift(act[frames - 2 :], forward=True)
     act_ext = jnp.concatenate([act_prev, act], axis=0)
@@ -83,23 +91,23 @@
 
     sigma = jax.nn.sigmoid(pre)
     pre_grad = (act_grad.astype(f32) * sigma * (1.0 + pre * (1.0 - sigma))).astype(jnp.bfloat16)
+    pg_flat = pre_grad.reshape(-1, chans)
 
-    xpad = jnp.pad(x_ext, ((0, 0), (0, 0), (1, 1), (0, 0)))
-    spatial_grad = lax.conv_general_dilated(
-        xpad, pre_grad, (1, 1), ((0, 0), (0, 0)),
-        dimension_numbers=KERNEL_GRAD_DIMS, preferred_element_type=f32,
-    )
-    pg_ext = row_halo(pre_grad)
-    back_weight = jnp.transpose(jnp.flip(spatial_weight, (0, 1)), (0, 1, 3, 2))
-    back = lax.conv_general_dilated(
-        pg_ext, back_weight, (1, 1), ((0, 0), (1, 1)),
-        dimension_numbers=CONV_DIMS, preferred_element_type=f32,
-    )
-    input_grad = (g.astype(f32) + back).astype(jnp.bfloat16)
+    spatial_list = []
+    for i in range(3):
+        piece = x3[:, i : i + rows].reshape(-1, 3 * chans)
+        spatial_list.append(
+            lax.dot_general(piece, pg_flat, (((0,), (0,)), ((), ())), preferred_element_type=f32)
+        )
+    pg3 = width_taps(row_halo(pre_grad), reverse=True)
+    back_weight = jnp.transpose(spatial_weight, (0, 1, 3, 2)).reshape(3, 3 * chans, chans)
+    back = g.astype(f32).reshape(-1, chans)
+    for i in range(3):
+        piece = pg3[:, 2 - i : 2 - i + rows].reshape(-1, 3 * chans)
+        back = back + jnp.dot(piece, back_weight[i], preferred_element_type=f32)
+    input_grad = back.astype(jnp.bfloat16).reshape(x.shape)
 
-    partial_terms = jnp.concatenate(
-        [spatial_grad.reshape(-1, chans)] + temporal_list, axis=0
-    )
+    partial_terms = jnp.concatenate(spatial_list + temporal_list, axis=0)
     summed = staged_scatter(partial_terms)
     return (block_output[None], input_grad[None], summed * scale)
 

time: 133 us -> 126 us (0.947)
  local copies, waits for them, and re-layouts: 39.6 us -> 20.6 us
  waiting for transfers between devices: 14.7 us -> 21.4 us
  other arithmetic: 13.4 us -> 7.34 us
  starting transfers between devices: 41.7 us -> 47.6 us
  matrix products: 20.5 us -> 26 us
    dot_general x0 -> x9, matrix products: none -> 13.6 us  [the longest x3 5.78 us: on_device(): back = back + jnp.dot(piece, back_weight[i], preferred_element_type=f32)]
    conv_general_dilated x3 -> x0, matrix products: 11.5 us -> none  [the longest x1 4.55 us: on_device(): lax.conv_general_dilated(x_ext, spatial_weight, (1, 1), ((0, 0), (1, 1)),...]
    conv_general_dilated x6 -> x0, local copies, waits for them, and re-layouts: 9.91 us -> none  [the longest x4 9.61 us: on_device(): lax.conv_general_dilated(pg_ext, back_weight, (1, 1), ((0, 0), (1, 1)), d...]
    all_to_all x3, waiting for transfers between devices: 7.34 us -> 15.5 us  [a2a_sum(): got = lax.all_to_all(blocks, axis, split_axis=0, concat_axis=0, tiled=True)]
    slice x2 -> x6, local copies, waits for them, and re-layouts: 0.13 us -> 7.92 us  [the longest x1 3.66 us: on_device(): piece = pg3[:, 2 - i:2 - i + rows].reshape(-1, 3 * chans)]
    add x2 -> x0, local copies, waits for them, and re-layouts: 6.76 us -> none  [on_device(): 1.0 + pre * (1.0 - sigma)]
    div x2 -> x0, local copies, waits for them, and re-layouts: 5.16 us -> none  [on_device(): act = jax.nn.silu(pre).astype(jnp.bfloat16)]
    all_to_all x3, starting transfers between devices: 19.9 us -> 24 us  [a2a_sum(): got = lax.all_to_all(blocks, axis, split_axis=0, concat_axis=0, tiled=True)]
  transfers between devices with their start and end apart: 9 -> 9, of which waited for: 3 -> 5; matrix products, arithmetic and copies ran while one was open for 49% -> 29% of each run, Pallas kernels for 0% -> 0%
where the time goes in v3:
time: 126 us; the launch traced here: 124 us
  starting transfers between devices  47.6 us (38%)
  matrix products  26 us (21%)
  waiting for transfers between devices  21.4 us (17%)
  local copies, waits for them, and re-layouts  20.6 us (16%)
  other arithmetic  7.34 us (6%)
    all_to_all x3, starting transfers between devices, a2a_sum(): got = lax.all_to_all(blocks, axis, split_axis=0, concat_axis=0, tiled=True)  24 us
    all_to_all x3, waiting for transfers between devices, a2a_sum(): got = lax.all_to_all(blocks, axis, split_axis=0, concat_axis=0, tiled=True)  15.5 us
    ppermute x2, starting transfers between devices, row_halo(): before = lax.ppermute(shard[:, -1:], 'row', up)  13.9 us
    ppermute x2, waiting for transfers between devices, row_halo(): after = lax.ppermute(shard[:, :1], 'row', down)  5.9 us
    dot_general x3, matrix products, on_device(): back = back + jnp.dot(piece, back_weight[i], preferred_element_type=f32)  5.78 us
    ppermute x2, starting transfers between devices, frame_shift(): return lax.ppermute(piece, 'frame', pairs)  5.75 us
    dot_general x3, matrix products, on_device(): jnp.dot(shifted, temporal_weight[k], preferred_element_type=f32)  5.53 us
    dot_general x3, matrix products, on_device(): lax.dot_general(piece, pg_flat, (((0,), (0,)), ((), ())), preferred_eleme...  4.95 us
  transfers between devices with their start and end apart: 9, of which 5 were waited for; matrix products, arithmetic and copies ran while one was open for 29% of the time, Pallas kernels for 0%

profile of v3, /device:TPU:1, one launch (start us, length us, event | category | flops | bytes accessed | tf_op | source)
XLA Modules:
  0.0 123.9 jit_solution(10630028376047548168)
XLA Ops:
  0.6 2.0 %fusion.38 = (bf16[4,1,240,128]{3,2,1,0:T(8,128)(2,1)}, bf16[4,1,240,128]{3,2,1,0:T(8,128)(2,1)}) fusion(bf16[4,4,240,128]{3,2,1,0:T(8,128)(2,1)} %bitcast.104), kind=kLoop, calls=%fused_computation.70 | loop fusion | bytes 983040 | tf_op jit(solution)/shard_map/slice | solution.py:13
  2.6 10.2 %collective-permute-start = (bf16[4,1,240,128]{3,2,1,0:T(8,128)(2,1)}, bf16[4,1,240,128]{3,2,1,0:T(8,128)(2,1)S(1)}, u32[]{:S(2)}, u32[]{:S(2)}) collective-permute-start(bf16[4,1,240,128]{3,2,1,0:T(8,128)(2,1)} %get-tuple-element.21), channel_id=1, source_target_pairs={{0,1},{1,2},{2,3},{4,5},{5,6},{6,7},{8,9},{9,10},{10,11},{12,13},{... | collective-permute-start | bytes 737288 | tf_op jit(solution)/shard_map/ppermute | solution.py:13
  12.8 2.1 %collective-permute-start.1 = (bf16[4,1,240,128]{3,2,1,0:T(8,128)(2,1)}, bf16[4,1,240,128]{3,2,1,0:T(8,128)(2,1)S(1)}, u32[]{:S(2)}, u32[]{:S(2)}) collective-permute-start(bf16[4,1,240,128]{3,2,1,0:T(8,128)(2,1)} %get-tuple-element.22), channel_id=1, source_target_pairs={{1,0},{2,1},{3,2},{5,4},{6,5},{7,6},{9,8},{10,9},{11,10},{13,12},{... | collective-permute-start | bytes 737288 | tf_op jit(solution)/shard_map/ppermute | solution.py:14
  14.9 1.8 %slice_bitcast_fusion = bf16[2,4,240,128]{3,2,1,0:T(8,128)(2,1)} fusion(bf16[1,4,4,240,128]{4,3,2,1,0:T(8,128)(2,1)} %param.5), kind=kLoop, calls=%fused_computation.49 | loop fusion | bytes 983040 | tf_op jit(solution)/shard_map/slice | solution.py:63
  16.7 1.3 %collective-permute-start.3 = (bf16[2,4,240,128]{3,2,1,0:T(8,128)(2,1)}, bf16[2,4,240,128]{3,2,1,0:T(8,128)(2,1)S(1)}, u32[]{:S(2)}, u32[]{:S(2)}) collective-permute-start(bf16[2,4,240,128]{3,2,1,0:T(8,128)(2,1)} %slice_bitcast_fusion), channel_id=1, source_target_pairs={{4,0},{8,4},{12,8},{16,12},{20,16},{24,20},{28,24},{32,28},{36,32}... | collective-permute-start | bytes 1474568 | tf_op jit(solution)/shard_map/ppermute | solution.py:24
  18.0 2.5 %fusion.23 = f32[3840,128]{1,0:T(8,128)} fusion(bf16[3840,128]{1,0:T(8,128)(2,1)S(1)} %bitcast.91, bf16[3,128,128]{2,1,0:T(8,128)(2,1)} %param.7), kind=kOutput, calls=%fused_computation.54 | convolution fusion | flops 125829120 | bytes 2981888 | tf_op jit(solution)/shard_map/dot_general | solution.py:84
  22.3 3.9 %collective-permute-done.1 = bf16[4,1,240,128]{3,2,1,0:T(8,128)(2,1)S(1)} collective-permute-done((bf16[4,1,240,128]{3,2,1,0:T(8,128)(2,1)}, bf16[4,1,240,128]{3,2,1,0:T(8,128)(2,1)S(1)}, u32[]{:S(2)}, u32[]{:S(2)}) %collective-permute-start.1) | collective-permute-done | bytes 245792 | tf_op jit(solution)/shard_map/ppermute | solution.py:14
  27.2 1.3 %fusion.8 = bf16[4,6,240,384]{3,2,1,0:T(8,128)(2,1)S(1)} fusion(bf16[4,6,239,128]{3,2,1,0:T(8,128)(2,1)S(1)} %get-tuple-element.18, bf16[4,6,239,128]{3,2,1,0:T(8,128)(2,1)S(1)} %get-tuple-element.17, bf16[4,1,240,128]{3,2,1,0:T(8,128)(2,1)S(1)} %collective-permute-done.1, bf16[4,4,240,128]{3,2,1,0:T(8,128)(2,1)S(1)} %bitcast.106, ...), kind=kLoop, calls=%fused_computation.19 | loop fusion | flops 30965760 | bytes 8835072 | tf_op jit(solution)/shard_map/concatenate | solution.py:49
  32.6 1.9 %fusion.25 = f32[3840,128]{1,0:T(8,128)} fusion(bf16[3,128,128]{2,1,0:T(8,128)(2,1)S(1)} %copy-done.15, f32[3840,128]{1,0:T(8,128)S(1)} %convolution_add_fusion.7), kind=kOutput, calls=%fused_computation.56 | convolution fusion | flops 128286720 | bytes 3964928 | tf_op jit(solution)/shard_map/dot_general | solution.py:82
  34.7 1.4 %copy-done.6 = f32[3840,128]{1,0:T(8,128)S(1)} copy-done((f32[3840,128]{1,0:T(8,128)S(1)}, f32[3840,128]{1,0:T(8,128)}, u32[]{:S(2)}) %copy-start.6) | copy-done | bytes 1966104
  37.9 1.7 %fusion.16 = f32[1536,128]{1,0:T(8,128)} fusion(bf16[4,6,240,384]{3,2,1,0:T(8,128)(2,1)S(1)} %fusion.8, bf16[4,4,240,128]{3,2,1,0:T(8,128)(2,1)S(1)} %get-tuple-element.9), kind=kOutput, calls=%fused_computation.41 | convolution fusion | flops 377487360 | bytes 5603328 | tf_op jit(solution)/shard_map/dot_general | solution.py:100
  39.6 3.7 %collective-permute-start.4 = (bf16[4,1,240,128]{3,2,1,0:T(8,128)(2,1)S(1)}, bf16[4,1,240,128]{3,2,1,0:T(8,128)(2,1)S(1)}, u32[]{:S(2)}, u32[]{:S(2)}) collective-permute-start(bf16[4,1,240,128]{3,2,1,0:T(8,128)(2,1)S(1)} %get-tuple-element.19), channel_id=1, source_target_pairs={{0,1},{1,2},{2,3},{4,5},{5,6},{6,7},{8,9},{9,10},{10,11},{12,13},{... | collective-permute-start | bytes 737288 | tf_op jit(solution)/shard_map/ppermute | solution.py:13
  43.3 1.9 %collective-permute-start.5 = (bf16[4,1,240,128]{3,2,1,0:T(8,128)(2,1)S(1)}, bf16[4,1,240,128]{3,2,1,0:T(8,128)(2,1)S(1)}, u32[]{:S(2)}, u32[]{:S(2)}) collective-permute-start(bf16[4,1,240,128]{3,2,1,0:T(8,128)(2,1)S(1)} %get-tuple-element.20), channel_id=1, source_target_pairs={{1,0},{2,1},{3,2},{5,4},{6,5},{7,6},{9,8},{10,9},{11,10},{13,12},{... | collective-permute-start | bytes 737288 | tf_op jit(solution)/shard_map/ppermute | solution.py:14
  45.2 4.5 %collective-permute-start.2 = (bf16[2,4,240,128]{3,2,1,0:T(8,128)(2,1)S(1)}, bf16[2,4,240,128]{3,2,1,0:T(8,128)(2,1)S(1)}, u32[]{:S(2)}, u32[]{:S(2)}) collective-permute-start(bf16[2,4,240,128]{3,2,1,0:T(8,128)(2,1)S(1)} %slice.139), channel_id=1, source_target_pairs={{0,4},{4,8},{8,12},{12,16},{16,20},{20,24},{24,28},{28,32},{32,36}... | collective-permute-start | bytes 1474568 | tf_op jit(solution)/shard_map/ppermute | solution.py:24
  49.7 1.7 %fusion.15 = f32[1536,128]{1,0:T(8,128)} fusion(f32[1536,128]{1,0:T(8,128)} %fusion.16, bf16[4,6,240,384]{3,2,1,0:T(8,128)(2,1)S(1)} %fusion.8, bf16[4,4,240,128]{3,2,1,0:T(8,128)(2,1)S(1)} %get-tuple-element.9), kind=kOutput, calls=%fused_computation.39 | convolution fusion | flops 377487360 | bytes 5603328 | tf_op jit(solution)/shard_map/dot_general | solution.py:100
  51.4 1.6 %fusion.14 = f32[1536,128]{1,0:T(8,128)} fusion(f32[1536,128]{1,0:T(8,128)} %fusion.15, bf16[4,6,240,384]{3,2,1,0:T(8,128)(2,1)S(1)} %fusion.8, bf16[4,4,240,128]{3,2,1,0:T(8,128)(2,1)S(1)} %get-tuple-element.9), kind=kOutput, calls=%fused_computation.37 | convolution fusion | flops 377487360 | bytes 5603328 | tf_op jit(solution)/shard_map/dot_general | solution.py:100
  53.0 1.4 %convolution_dynamic-update-slice_fusion.2 = f32[1536,128]{1,0:T(8,128)} fusion(f32[1536,128]{1,0:T(8,128)} %fusion.14, bf16[3840,128]{1,0:T(8,128)(2,1)S(1)} %bitcast.93, f32[3840,128]{1,0:T(8,128)S(1)} %convolution_add_fusion.7), kind=kOutput, calls=%fused_computation.44 | convolution fusion | flops 128286720 | bytes 3014656 | tf_op jit(solution)/shard_map/dot_general | solution.py:86
  54.4 2.0 %collective-permute-done.5 = bf16[4,1,240,128]{3,2,1,0:T(8,128)(2,1)S(1)} collective-permute-done((bf16[4,1,240,128]{3,2,1,0:T(8,128)(2,1)S(1)}, bf16[4,1,240,128]{3,2,1,0:T(8,128)(2,1)S(1)}, u32[]{:S(2)}, u32[]{:S(2)}) %collective-permute-start.5) | collective-permute-done | bytes 245792 | tf_op jit(solution)/shard_map/ppermute | solution.py:14
  57.4 1.3 %fusion.10 = bf16[4,6,240,384]{3,2,1,0:T(8,128)(2,1)S(1)} fusion(bf16[4,6,239,128]{3,2,1,0:T(8,128)(2,1)S(1)} %get-tuple-element.12, bf16[4,6,239,128]{3,2,1,0:T(8,128)(2,1)S(1)} %get-tuple-element.11, bf16[4,1,240,128]{3,2,1,0:T(8,128)(2,1)S(1)} %collective-permute-done.5, bf16[4,4,240,128]{3,2,1,0:T(8,128)(2,1)S(1)} %get-tuple-element.9, ...), kind=kLoop, calls=%fused_computation.21 | loop fusion | flops 30965760 | bytes 8835072 | tf_op jit(solution)/shard_map/concatenate | solution.py:49
  58.7 3.7 %fusion.33 = (bf16[4,4,240,384]{3,2,1,0:T(8,128)(2,1)}, bf16[4,4,240,384]{3,2,1,0:T(8,128)(2,1)}, bf16[4,4,240,384]{3,2,1,0:T(8,128)(2,1)}) fusion(bf16[4,6,240,384]{3,2,1,0:T(8,128)(2,1)S(1)} %fusion.10), kind=kLoop, calls=%fused_computation.65 | loop fusion | bytes 17694720 | tf_op jit(solution)/shard_map/slice | solution.py:106
  64.8 2.2 %reshape.91 = f32[4,16,4,6,128]{4,3,2,1,0:T(8,128)} reshape(f32[1536,128]{1,0:T(8,128)} %convolution_dynamic-update-slice_fusion) | data formatting | bytes 1572864 | tf_op jit(solution)/shard_map/reshape | solution.py:36
  67.0 2.6 %copy.14 = f32[4,4,16,6,128]{4,2,3,1,0:T(8,128)} copy(f32[4,4,16,6,128]{4,3,0,2,1:T(8,128)} %bitcast.111) | data formatting | bytes 1572864 | tf_op jit(solution)/shard_map/transpose | solution.py:37
  69.6 5.6 %all-to-all-start = ((f32[4,4,16,6,128]{4,2,3,1,0:T(8,128)}), f32[4,4,16,6,128]{4,2,3,1,0:T(8,128)}, u32[]{:S(2)}, u32[]{:S(2)}) async-start(f32[4,4,16,6,128]{4,2,3,1,0:T(8,128)} %copy.14), calls=%async_computation | async-start | bytes 1572864 | tf_op jit(solution)/shard_map/all_to_all | solution.py:28
  75.1 2.9 %convolution_add_fusion.2 = f32[3840,128]{1,0:T(8,128)S(1)} fusion(bf16[3840,384]{1,0:T(8,128)(2,1)} %bitcast.99, bf16[384,128]{1,0:T(8,128)(2,1)S(1)} %bitcast.121, bf16[3840,128]{1,0:T(8,128)(2,1)S(1)} %bitcast.96), kind=kOutput, calls=%fused_computation.8 | convolution fusion | flops 378470400 | bytes 5996544 | tf_op jit(solution)/shard_map/dot_general | solution.py:107
  80.0 1.9 %fusion.6 = bf16[3840,128]{1,0:T(8,128)(2,1)} fusion(f32[3840,128]{1,0:T(8,128)S(1)} %convolution_add_fusion.1, bf16[3840,384]{1,0:T(8,128)(2,1)S(1)} %bitcast.97, bf16[384,128]{1,0:T(8,128)(2,1)S(1)} %bitcast.119), kind=kOutput, calls=%fused_computation.17 | convolution fusion | flops 378470400 | bytes 5996544 | tf_op jit(solution)/shard_map/dot_general | solution.py:107
  81.9 1.7 %convolution_add_fusion.6 = f32[3840,128]{1,0:T(8,128)} fusion(f32[3840,128]{1,0:T(8,128)S(1)} %copy-done.7, bf16[3840,128]{1,0:T(8,128)(2,1)S(1)} %bitcast.108, bf16[3,128,128]{2,1,0:T(8,128)(2,1)S(1)} %copy-done.16), kind=kOutput, calls=%fused_computation.12 | convolution fusion | flops 126320640 | bytes 4947968 | tf_op jit(solution)/shard_map/dot_general | solution.py:82
  83.6 7.3 %all-to-all-done = f32[4,4,16,6,128]{4,2,3,1,0:T(8,128)} async-done(((f32[4,4,16,6,128]{4,2,3,1,0:T(8,128)}), f32[4,4,16,6,128]{4,2,3,1,0:T(8,128)}, u32[]{:S(2)}, u32[]{:S(2)}) %all-to-all-start) | async-done | bytes 786464 | tf_op jit(solution)/shard_map/all_to_all | solution.py:28
  92.9 8.7 %all-to-all-start.1 = ((f32[16,4,6,128]{3,1,2,0:T(4,128)}), f32[16,4,6,128]{3,1,2,0:T(4,128)S(1)}, u32[]{:S(2)}, u32[]{:S(2)}) async-start(f32[16,4,6,128]{3,1,2,0:T(4,128)} %copy.15), calls=%async_computation.1 | async-start | bytes 393216 | tf_op jit(solution)/shard_map/all_to_all | solution.py:28
  101.6 1.9 %fusion.4 = bf16[3840,128]{1,0:T(8,128)(2,1)S(1)} fusion(f32[3840,128]{1,0:T(8,128)} %convolution_add_fusion.6, bf16[3840,128]{1,0:T(8,128)(2,1)S(1)} %bitcast.110, bf16[3,128,128]{2,1,0:T(8,128)(2,1)S(1)} %copy-done.16), kind=kOutput, calls=%fused_computation.15 | convolution fusion | flops 126812160 | bytes 3964928 | tf_op jit(solution)/shard_map/dot_general | solution.py:82
  103.5 5.0 %all-to-all-done.1 = f32[16,4,6,128]{3,1,2,0:T(4,128)S(1)} async-done(((f32[16,4,6,128]{3,1,2,0:T(4,128)}), f32[16,4,6,128]{3,1,2,0:T(4,128)S(1)}, u32[]{:S(2)}, u32[]{:S(2)}) %all-to-all-start.1) | async-done | bytes 196640 | tf_op jit(solution)/shard_map/all_to_all | solution.py:28
  109.1 9.7 %all-to-all-start.2 = ((f32[4,6,128]{2,1,0:T(8,128)}), f32[4,6,128]{2,1,0:T(8,128)S(1)}, u32[]{:S(2)}, u32[]{:S(2)}) async-start(f32[4,6,128]{2,1,0:T(8,128)} %copy.16), calls=%async_computation.2 | async-start | bytes 32768 | tf_op jit(solution)/shard_map/all_to_all | solution.py:28
  120.1 3.3 %all-to-all-done.2 = f32[4,6,128]{2,1,0:T(8,128)S(1)} async-done(((f32[4,6,128]{2,1,0:T(8,128)}), f32[4,6,128]{2,1,0:T(8,128)S(1)}, u32[]{:S(2)}, u32[]{:S(2)}) %all-to-all-start.2) | async-done | bytes 12320 | tf_op jit(solution)/shard_map/all_to_all | solution.py:28
  (65 shorter events, 18.4 us)
Async XLA Ops:
  0.6 17.4 %copy-start = (bf16[1,4,4,240,128]{4,3,2,1,0:T(8,128)(2,1)S(1)}, bf16[1,4,4,240,128]{4,3,2,1,0:T(8,128)(2,1)}, u32[]{:S(2)}) copy-start(bf16[1,4,4,240,128]{4,3,2,1,0:T(8,128)(2,1)} %param.5) | copy-start | bytes 2949124
  2.6 19.7 %collective-permute-start = (bf16[4,1,240,128]{3,2,1,0:T(8,128)(2,1)}, bf16[4,1,240,128]{3,2,1,0:T(8,128)(2,1)S(1)}, u32[]{:S(2)}, u32[]{:S(2)}) collective-permute-start(bf16[4,1,240,128]{3,2,1,0:T(8,128)(2,1)} %get-tuple-element.21), channel_id=1, source_target_pairs={{0,1},{1,2},{2,3},{4,5},{5,6},{6,7},{8,9},{9,10},{10,11},{12,13},{... | collective-permute-start | bytes 737288 | tf_op jit(solution)/shard_map/ppermute | solution.py:13
  12.8 7.8 %copy-start.8 = (bf16[3,3,128,128]{3,2,1,0:T(8,128)(2,1)S(1)}, bf16[3,3,128,128]{3,2,1,0:T(8,128)(2,1)}, u32[]{:S(2)}) copy-start(bf16[3,3,128,128]{3,2,1,0:T(8,128)(2,1)} %param.6) | copy-start | bytes 884740
  12.8 13.3 %collective-permute-start.1 = (bf16[4,1,240,128]{3,2,1,0:T(8,128)(2,1)}, bf16[4,1,240,128]{3,2,1,0:T(8,128)(2,1)S(1)}, u32[]{:S(2)}, u32[]{:S(2)}) collective-permute-start(bf16[4,1,240,128]{3,2,1,0:T(8,128)(2,1)} %get-tuple-element.22), channel_id=1, source_target_pairs={{1,0},{2,1},{3,2},{5,4},{6,5},{7,6},{9,8},{10,9},{11,10},{13,12},{... | collective-permute-start | bytes 737288 | tf_op jit(solution)/shard_map/ppermute | solution.py:14
  16.7 17.8 %collective-permute-start.3 = (bf16[2,4,240,128]{3,2,1,0:T(8,128)(2,1)}, bf16[2,4,240,128]{3,2,1,0:T(8,128)(2,1)S(1)}, u32[]{:S(2)}, u32[]{:S(2)}) collective-permute-start(bf16[2,4,240,128]{3,2,1,0:T(8,128)(2,1)} %slice_bitcast_fusion), channel_id=1, source_target_pairs={{4,0},{8,4},{12,8},{16,12},{20,16},{24,20},{28,24},{32,28},{36,32}... | collective-permute-start | bytes 1474568 | tf_op jit(solution)/shard_map/ppermute | solution.py:24
  18.0 8.1 %copy-start.3 = (bf16[1,4,4,240,128]{4,3,2,1,0:T(8,128)(2,1)S(1)}, bf16[1,4,4,240,128]{4,3,2,1,0:T(8,128)(2,1)}, u32[]{:S(2)}) copy-start(bf16[1,4,4,240,128]{4,3,2,1,0:T(8,128)(2,1)} %param.4) | copy-start | bytes 2949124
  28.5 1.2 copy-start.14
  29.7 1.0 copy-start.13
  30.7 1.0 copy-start.12
  31.6 1.0 copy-start.15
  34.5 1.5 %copy-start.6 = (f32[3840,128]{1,0:T(8,128)S(1)}, f32[3840,128]{1,0:T(8,128)}, u32[]{:S(2)}) copy-start(f32[3840,128]{1,0:T(8,128)} %fusion.23) | copy-start | bytes 5898244
  39.6 14.8 %collective-permute-start.4 = (bf16[4,1,240,128]{3,2,1,0:T(8,128)(2,1)S(1)}, bf16[4,1,240,128]{3,2,1,0:T(8,128)(2,1)S(1)}, u32[]{:S(2)}, u32[]{:S(2)}) collective-permute-start(bf16[4,1,240,128]{3,2,1,0:T(8,128)(2,1)S(1)} %get-tuple-element.19), channel_id=1, source_target_pairs={{0,1},{1,2},{2,3},{4,5},{5,6},{6,7},{8,9},{9,10},{10,11},{12,13},{... | collective-permute-start | bytes 737288 | tf_op jit(solution)/shard_map/ppermute | solution.py:13
  43.3 13.1 %collective-permute-start.5 = (bf16[4,1,240,128]{3,2,1,0:T(8,128)(2,1)S(1)}, bf16[4,1,240,128]{3,2,1,0:T(8,128)(2,1)S(1)}, u32[]{:S(2)}, u32[]{:S(2)}) collective-permute-start(bf16[4,1,240,128]{3,2,1,0:T(8,128)(2,1)S(1)} %get-tuple-element.20), channel_id=1, source_target_pairs={{1,0},{2,1},{3,2},{5,4},{6,5},{7,6},{9,8},{10,9},{11,10},{13,12},{... | collective-permute-start | bytes 737288 | tf_op jit(solution)/shard_map/ppermute | solution.py:14
  45.2 17.1 %collective-permute-start.2 = (bf16[2,4,240,128]{3,2,1,0:T(8,128)(2,1)S(1)}, bf16[2,4,240,128]{3,2,1,0:T(8,128)(2,1)S(1)}, u32[]{:S(2)}, u32[]{:S(2)}) collective-permute-start(bf16[2,4,240,128]{3,2,1,0:T(8,128)(2,1)S(1)} %slice.139), channel_id=1, source_target_pairs={{0,4},{4,8},{8,12},{12,16},{16,20},{20,24},{24,28},{28,32},{32,36}... | collective-permute-start | bytes 1474568 | tf_op jit(solution)/shard_map/ppermute | solution.py:24
  62.5 1.1 copy-start.4
  66.9 8.2 %copy-start.11 = (bf16[1,3,128,128]{3,2,1,0:T(8,128)(2,1)S(1)}, bf16[1,3,128,128]{3,2,1,0:T(8,128)(2,1)}, u32[]{:S(2)}) copy-start(bf16[1,3,128,128]{3,2,1,0:T(8,128)(2,1)} %get-tuple-element.25) | copy-start | bytes 294916
  69.6 21.3 %all-to-all-start = ((f32[4,4,16,6,128]{4,2,3,1,0:T(8,128)}), f32[4,4,16,6,128]{4,2,3,1,0:T(8,128)}, u32[]{:S(2)}, u32[]{:S(2)}) async-start(f32[4,4,16,6,128]{4,2,3,1,0:T(8,128)} %copy.14), calls=%async_computation | async-start | bytes 1572864 | tf_op jit(solution)/shard_map/all_to_all | solution.py:28
  75.1 3.0 %copy-start.2 = (bf16[4,4,240,384]{3,2,1,0:T(8,128)(2,1)S(1)}, bf16[4,4,240,384]{3,2,1,0:T(8,128)(2,1)}, u32[]{:S(2)}) copy-start(bf16[4,4,240,384]{3,2,1,0:T(8,128)(2,1)} %get-tuple-element.4) | copy-start | bytes 8847364
  75.1 3.0 %copy-start.10 = (bf16[1,3,128,128]{3,2,1,0:T(8,128)(2,1)S(1)}, bf16[1,3,128,128]{3,2,1,0:T(8,128)(2,1)}, u32[]{:S(2)}) copy-start(bf16[1,3,128,128]{3,2,1,0:T(8,128)(2,1)} %get-tuple-element.24) | copy-start | bytes 294916
  78.1 1.8 %copy-start.1 = (bf16[4,4,240,384]{3,2,1,0:T(8,128)(2,1)S(1)}, bf16[4,4,240,384]{3,2,1,0:T(8,128)(2,1)}, u32[]{:S(2)}) copy-start(bf16[4,4,240,384]{3,2,1,0:T(8,128)(2,1)} %get-tuple-element.3) | copy-start | bytes 8847364
  78.1 1.8 %copy-start.9 = (bf16[1,3,128,128]{3,2,1,0:T(8,128)(2,1)S(1)}, bf16[1,3,128,128]{3,2,1,0:T(8,128)(2,1)}, u32[]{:S(2)}) copy-start(bf16[1,3,128,128]{3,2,1,0:T(8,128)(2,1)} %get-tuple-element.23) | copy-start | bytes 294916
  80.0 1.9 %copy-start.7 = (f32[3840,128]{1,0:T(8,128)S(1)}, f32[3840,128]{1,0:T(8,128)}, u32[]{:S(2)}) copy-start(f32[3840,128]{1,0:T(8,128)} %fusion.25) | copy-start | bytes 5898244
  80.0 1.9 %copy-start.16 = (bf16[3,128,128]{2,1,0:T(8,128)(2,1)S(1)}, bf16[3,128,128]{2,1,0:T(8,128)(2,1)}, u32[]{:S(2)}) copy-start(bf16[3,128,128]{2,1,0:T(8,128)(2,1)} %param.7) | copy-start | bytes 294916
  83.6 18.0 %copy-start.5 = (bf16[4,4,240,128]{3,2,1,0:T(8,128)(2,1)S(1)}, bf16[4,4,240,128]{3,2,1,0:T(8,128)(2,1)}, u32[]{:S(2)}) copy-start(bf16[4,4,240,128]{3,2,1,0:T(8,128)(2,1)} %copy-done.4) | copy-start | bytes 2949124
  92.9 15.6 %all-to-all-start.1 = ((f32[16,4,6,128]{3,1,2,0:T(4,128)}), f32[16,4,6,128]{3,1,2,0:T(4,128)S(1)}, u32[]{:S(2)}, u32[]{:S(2)}) async-start(f32[16,4,6,128]{3,1,2,0:T(4,128)} %copy.15), calls=%async_computation.1 | async-start | bytes 393216 | tf_op jit(solution)/shard_map/all_to_all | solution.py:28
  109.1 14.2 %all-to-all-start.2 = ((f32[4,6,128]{2,1,0:T(8,128)}), f32[4,6,128]{2,1,0:T(8,128)S(1)}, u32[]{:S(2)}, u32[]{:S(2)}) async-start(f32[4,6,128]{2,1,0:T(8,128)} %copy.16), calls=%async_computation.2 | async-start | bytes 32768 | tf_op jit(solution)/shard_map/all_to_all | solution.py:28

commit v4 on v3

--- a/solution.py
+++ b/solution.py
@@ -6,12 +6,12 @@
 from jax.sharding import PartitionSpec as P
 
 
-def row_halo(shard):
+def row_halo(shard, width):
     peers = lax.axis_size("row")
     up = [(i, i + 1) for i in range(peers - 1)]
     down = [(i + 1, i) for i in range(peers - 1)]
-    before = lax.ppermute(shard[:, -1:], "row", up)
-    after = lax.ppermute(shard[:, :1], "row", down)
+    before = lax.ppermute(shard[:, shard.shape[1] - width :], "row", up)
+    after = lax.ppermute(shard[:, :width], "row", down)
     return jnp.concatenate([before, shard, after], axis=1)
 
 
@@ -30,15 +30,11 @@
 
 
 def staged_scatter(terms):
-    n_dp, n_frame, n_row = (lax.axis_size(a) for a in ("dp", "frame", "row"))
-    rows = terms.shape[0] // (n_dp * n_frame * n_row)
-    chans = terms.shape[-1]
-    blocks = terms.reshape(n_dp, n_frame, n_row, rows, chans)
-    blocks = jnp.transpose(blocks, (2, 0, 1, 3, 4))
-    blocks = a2a_sum(blocks, "row")
-    blocks = jnp.transpose(blocks, (1, 0, 2, 3))
-    blocks = a2a_sum(blocks, "frame")
-    return a2a_sum(blocks, "dp")
+    axes = ("dp", "frame", "row")
+    n = 1
+    for a in axes:
+        n *= lax.axis_size(a)
+    return a2a_sum(terms.reshape(n, terms.shape[0] // n, terms.shape[-1]), axes)
 
 
 def width_taps(a, reverse):
@@ -59,47 +55,49 @@
     scale = 1.0 / math.sqrt(cells)
     f32 = jnp.float32
 
-    x_ext = row_halo(x)
-    g_next = frame_shift(g[:2], forward=False)
-    x3 = width_taps(x_ext, reverse=False)
+    x_f = jnp.concatenate([frame_shift(x[frames - 2 :], forward=True), x], axis=0)
+    x_e = row_halo(x_f, 2)
+    g_f = jnp.concatenate([g, frame_shift(g[:2], forward=False)], axis=0)
+    g_e = row_halo(g_f, 1)
+
+    x3 = width_taps(x_e, reverse=False)
     fwd_weight = spatial_weight.reshape(3, 3 * chans, chans)
-    pre = jnp.zeros((frames * rows * cols, chans), f32)
+    wide = (frames + 2, rows + 2, cols, chans)
+    pre = jnp.zeros((math.prod(wide[:-1]), chans), f32)
     for i in range(3):
-        piece = x3[:, i : i + rows].reshape(-1, 3 * chans)
+        piece = x3[:, i : i + rows + 2].reshape(-1, 3 * chans)
         pre = pre + jnp.dot(piece, fwd_weight[i], preferred_element_type=f32)
-    pre = pre.reshape(x.shape)
-    act = jax.nn.silu(pre).astype(jnp.bfloat16)
-    act_prev = frame_shift(act[frames - 2 :], forward=True)
-    act_ext = jnp.concatenate([act_prev, act], axis=0)
-    g_ext = jnp.concatenate([g, g_next], axis=0)
+    pre = pre.reshape(wide)
+    act = jax.nn.silu(pre[:, 1 : rows + 1]).astype(jnp.bfloat16)
     g_flat = g.reshape(-1, chans)
 
     mixed = jnp.zeros((frames * rows * cols, chans), f32)
-    act_grad = jnp.zeros((frames * rows * cols, chans), f32)
+    act_grad = jnp.zeros((frames * (rows + 2) * cols, chans), f32)
     temporal_list = []
     for k in range(3):
-        shifted = act_ext[2 - k : 2 - k + frames].reshape(-1, chans)
+        shifted = act[2 - k : 2 - k + frames].reshape(-1, chans)
         mixed = mixed + jnp.dot(shifted, temporal_weight[k], preferred_element_type=f32)
-        ahead = g_ext[k : k + frames].reshape(-1, chans)
+        ahead = g_e[k : k + frames].reshape(-1, chans)
         act_grad = act_grad + jnp.dot(ahead, temporal_weight[k].T, preferred_element_type=f32)
         temporal_list.append(
             lax.dot_general(shifted, g_flat, (((0,), (0,)), ((), ())), preferred_element_type=f32)
         )
     mixed = mixed.astype(jnp.bfloat16).reshape(x.shape)
-    act_grad = act_grad.astype(jnp.bfloat16).reshape(x.shape)
+    act_grad = act_grad.astype(jnp.bfloat16).reshape(frames, rows + 2, cols, chans)
     block_output = (x.astype(f32) + mixed.astype(f32)).astype(jnp.bfloat16)
 
-    sigma = jax.nn.sigmoid(pre)
-    pre_grad = (act_grad.astype(f32) * sigma * (1.0 + pre * (1.0 - sigma))).astype(jnp.bfloat16)
-    pg_flat = pre_grad.reshape(-1, chans)
+    pre_now = pre[2:]
+    sigma = jax.nn.sigmoid(pre_now)
+    pg_ext = (act_grad.astype(f32) * sigma * (1.0 + pre_now * (1.0 - sigma))).astype(jnp.bfloat16)
+    pg_flat = pg_ext[:, 1 : rows + 1].reshape(-1, chans)
 
     spatial_list = []
     for i in range(3):
-        piece = x3[:, i : i + rows].reshape(-1, 3 * chans)
+        piece = x3[2:, 1 + i : 1 + i + rows].reshape(-1, 3 * chans)
         spatial_list.append(
             lax.dot_general(piece, pg_flat, (((0,), (0,)), ((), ())), preferred_element_type=f32)
         )
-    pg3 = width_taps(row_halo(pre_grad), reverse=True)
+    pg3 = width_taps(pg_ext, reverse=True)
     back_weight = jnp.transpose(spatial_weight, (0, 1, 3, 2)).reshape(3, 3 * chans, chans)
     back = g.astype(f32).reshape(-1, chans)
     for i in range(3):

time: 126 us -> 144 us (1.14); the launches traced: 124 us -> 144 us
  waiting for transfers between devices: 21.4 us -> 38.7 us
  starting transfers between devices: 47.6 us -> 43.5 us
  other arithmetic: 7.34 us -> 10 us
  matrix products: 26 us -> 28.3 us
  local copies, waits for them, and re-layouts: 20.6 us -> 22.1 us
    ppermute x4, waiting for transfers between devices: 5.9 us -> 16.2 us  [the longest x2 16.2 us: row_halo(): after = lax.ppermute(shard[:, :width], 'row', down)]
    all_to_all x3 -> x1, starting transfers between devices: 24 us -> 13.9 us  [a2a_sum(): got = lax.all_to_all(blocks, axis, split_axis=0, concat_axis=0, tiled=True)]
    ppermute x4, starting transfers between devices: 17.9 us -> 23.6 us  [the longest x2 19.8 us: row_halo(): before = lax.ppermute(shard[:, shard.shape[1] - width:], 'row', up)]
    dot_general x3, matrix products: 2.82 us -> 8.54 us  [on_device(): pre = pre + jnp.dot(piece, fwd_weight[i], preferred_element_type=f32)]
    slice x5 -> x6, local copies, waits for them, and re-layouts: 5.05 us -> 9.49 us  [the longest x1 4.51 us: on_device(): piece = x3[:, i:i + rows + 2].reshape(-1, 3 * chans)]
    all_to_all x3 -> x1, waiting for transfers between devices: 15.5 us -> 19.5 us  [a2a_sum(): got = lax.all_to_all(blocks, axis, split_axis=0, concat_axis=0, tiled=True)]
    transpose x2 -> x0, local copies, waits for them, and re-layouts: 3.43 us -> none  [the longest x1 2.63 us: staged_scatter(): blocks = jnp.transpose(blocks, (2, 0, 1, 3, 4))]
    ppermute x2, waiting for transfers between devices: 0.01 us -> 3 us  [frame_shift(): return lax.ppermute(piece, 'frame', pairs)]
  transfers between devices with their start and end apart: 9 -> 7, of which waited for: 5 -> 4; matrix products, arithmetic and copies ran while one was open for 29% -> 13% of each run, Pallas kernels for 0% -> 0%
where the time goes in v4:
time: 144 us
  starting transfers between devices  43.5 us (30%)
  waiting for transfers between devices  38.7 us (27%)
  matrix products  28.3 us (20%)
  local copies, waits for them, and re-layouts  22.1 us (15%)
  other arithmetic  10 us (7%)
    ppermute x2, starting transfers between devices, row_halo(): before = lax.ppermute(shard[:, shard.shape[1] - width:], 'row', up)  19.8 us
    all_to_all x1, waiting for transfers between devices, a2a_sum(): got = lax.all_to_all(blocks, axis, split_axis=0, concat_axis=0, tiled=True)  19.5 us
    ppermute x2, waiting for transfers between devices, row_halo(): after = lax.ppermute(shard[:, :width], 'row', down)  16.2 us
    all_to_all x1, starting transfers between devices, a2a_sum(): got = lax.all_to_all(blocks, axis, split_axis=0, concat_axis=0, tiled=True)  13.9 us
    dot_general x3, matrix products, on_device(): pre = pre + jnp.dot(piece, fwd_weight[i], preferred_element_type=f32)  8.54 us
    ppermute x2, starting transfers between devices, frame_shift(): return lax.ppermute(piece, 'frame', pairs)  5.94 us
    dot_general x3, matrix products, on_device(): lax.dot_general(piece, pg_flat, (((0,), (0,)), ((), ())), preferred_eleme...  4.97 us
    dot_general x3, matrix products, on_device(): jnp.dot(shifted, temporal_weight[k], preferred_element_type=f32)  4.66 us
  transfers between devices with their start and end apart: 7, of which 4 were waited for; matrix products, arithmetic and copies ran while one was open for 13% of the time, Pallas kernels for 0%

profile of v4, /device:TPU:1, one launch (start us, length us, event | category | flops | bytes accessed | tf_op | source)
XLA Modules:
  0.0 143.7 jit_solution(12018406503157228037)
XLA Ops:
  0.7 2.0 %slice_bitcast_fusion = bf16[2,4,240,128]{3,2,1,0:T(8,128)(2,1)} fusion(bf16[1,4,4,240,128]{4,3,2,1,0:T(8,128)(2,1)} %param.5), kind=kLoop, calls=%fused_computation.48 | loop fusion | bytes 983040 | tf_op jit(solution)/shard_map/slice | solution.py:60
  2.6 1.3 collective-permute-start.3
  3.9 1.8 %slice_bitcast_fusion.1 = bf16[2,4,240,128]{3,2,1,0:T(8,128)(2,1)} fusion(bf16[1,4,4,240,128]{4,3,2,1,0:T(8,128)(2,1)} %param.4), kind=kLoop, calls=%fused_computation.49 | loop fusion | bytes 983040 | tf_op jit(solution)/shard_map/slice | solution.py:58
  5.8 4.7 %collective-permute-start = (bf16[2,4,240,128]{3,2,1,0:T(8,128)(2,1)}, bf16[2,4,240,128]{3,2,1,0:T(8,128)(2,1)S(1)}, u32[]{:S(2)}, u32[]{:S(2)}) collective-permute-start(bf16[2,4,240,128]{3,2,1,0:T(8,128)(2,1)} %slice_bitcast_fusion.1), channel_id=1, source_target_pairs={{0,4},{4,8},{8,12},{12,16},{16,20},{20,24},{24,28},{28,32},{32,36}... | collective-permute-start | bytes 1474568 | tf_op jit(solution)/shard_map/ppermute | solution.py:24
  12.6 3.0 %collective-permute-done.3 = bf16[2,4,240,128]{3,2,1,0:T(8,128)(2,1)S(1)} collective-permute-done((bf16[2,4,240,128]{3,2,1,0:T(8,128)(2,1)}, bf16[2,4,240,128]{3,2,1,0:T(8,128)(2,1)S(1)}, u32[]{:S(2)}, u32[]{:S(2)}) %collective-permute-start.3) | collective-permute-done | bytes 491552 | tf_op jit(solution)/shard_map/ppermute | solution.py:24
  15.7 12.3 %collective-permute-start.4 = (bf16[6,1,240,128]{3,2,1,0:T(8,128)(2,1)S(1)}, bf16[6,1,240,128]{3,2,1,0:T(8,128)(2,1)S(1)}, u32[]{:S(2)}, u32[]{:S(2)}) collective-permute-start(bf16[6,1,240,128]{3,2,1,0:T(8,128)(2,1)S(1)} %get-tuple-element.16), channel_id=1, source_target_pairs={{0,1},{1,2},{2,3},{4,5},{5,6},{6,7},{8,9},{9,10},{10,11},{12,13},{... | collective-permute-start | bytes 1105928 | tf_op jit(solution)/shard_map/ppermute | solution.py:13
  28.0 1.9 %collective-permute-start.5 = (bf16[6,1,240,128]{3,2,1,0:T(8,128)(2,1)S(1)}, bf16[6,1,240,128]{3,2,1,0:T(8,128)(2,1)S(1)}, u32[]{:S(2)}, u32[]{:S(2)}) collective-permute-start(bf16[6,1,240,128]{3,2,1,0:T(8,128)(2,1)S(1)} %get-tuple-element.17), channel_id=1, source_target_pairs={{1,0},{2,1},{3,2},{5,4},{6,5},{7,6},{9,8},{10,9},{11,10},{13,12},{... | collective-permute-start | bytes 1105928 | tf_op jit(solution)/shard_map/ppermute | solution.py:14
  30.8 7.5 %collective-permute-start.1 = (bf16[6,2,240,128]{3,2,1,0:T(8,128)(2,1)S(1)}, bf16[6,2,240,128]{3,2,1,0:T(8,128)(2,1)S(1)}, u32[]{:S(2)}, u32[]{:S(2)}) collective-permute-start(bf16[6,2,240,128]{3,2,1,0:T(8,128)(2,1)S(1)} %get-tuple-element.21), channel_id=1, source_target_pairs={{0,1},{1,2},{2,3},{4,5},{5,6},{6,7},{8,9},{9,10},{10,11},{12,13},{... | collective-permute-start | bytes 2211848 | tf_op jit(solution)/shard_map/ppermute | solution.py:13
  38.4 1.9 %collective-permute-start.2 = (bf16[6,2,240,128]{3,2,1,0:T(8,128)(2,1)S(1)}, bf16[6,2,240,128]{3,2,1,0:T(8,128)(2,1)S(1)}, u32[]{:S(2)}, u32[]{:S(2)}) collective-permute-start(bf16[6,2,240,128]{3,2,1,0:T(8,128)(2,1)S(1)} %get-tuple-element.22), channel_id=1, source_target_pairs={{1,0},{2,1},{3,2},{5,4},{6,5},{7,6},{9,8},{10,9},{11,10},{13,12},{... | collective-permute-start | bytes 2211848 | tf_op jit(solution)/shard_map/ppermute | solution.py:14
  40.3 6.0 %collective-permute-done.5 = bf16[6,1,240,128]{3,2,1,0:T(8,128)(2,1)S(1)} collective-permute-done((bf16[6,1,240,128]{3,2,1,0:T(8,128)(2,1)S(1)}, bf16[6,1,240,128]{3,2,1,0:T(8,128)(2,1)S(1)}, u32[]{:S(2)}, u32[]{:S(2)}) %collective-permute-start.5) | collective-permute-done | bytes 368672 | tf_op jit(solution)/shard_map/ppermute | solution.py:14
  48.6 1.7 %fusion.6 = bf16[5760,128]{1,0:T(8,128)(2,1)} fusion(f32[5760,128]{1,0:T(8,128)S(1)} %convolution_add_fusion.3, bf16[5760,128]{1,0:T(8,128)(2,1)S(1)} %bitcast.118, bf16[3,128,128]{2,1,0:T(8,128)(2,1)S(1)} %copy-done.8), kind=kOutput, calls=%fused_computation.14 | convolution fusion | flops 190218240 | bytes 5931008 | tf_op jit(solution)/shard_map/dot_general | solution.py:81
  50.3 10.2 %collective-permute-done.2 = bf16[6,2,240,128]{3,2,1,0:T(8,128)(2,1)S(1)} collective-permute-done((bf16[6,2,240,128]{3,2,1,0:T(8,128)(2,1)S(1)}, bf16[6,2,240,128]{3,2,1,0:T(8,128)(2,1)S(1)}, u32[]{:S(2)}, u32[]{:S(2)}) %collective-permute-start.2) | collective-permute-done | bytes 737312 | tf_op jit(solution)/shard_map/ppermute | solution.py:14
  61.0 1.7 %fusion.37 = (bf16[6,8,239,128]{3,2,1,0:T(8,128)(2,1)S(1)}, bf16[6,8,239,128]{3,2,1,0:T(8,128)(2,1)S(1)}) fusion(bf16[6,8,240,128]{3,2,1,0:T(8,128)(2,1)S(1)} %pad_maximum_fusion), kind=kLoop, calls=%fused_computation.69 | loop fusion | bytes 11747328 | tf_op jit(solution)/shard_map/slice | solution.py:42
  62.8 2.8 %fusion.2 = bf16[6,8,240,384]{3,2,1,0:T(8,128)(2,1)S(1)} fusion(bf16[6,8,239,128]{3,2,1,0:T(8,128)(2,1)S(1)} %get-tuple-element.10, bf16[6,8,239,128]{3,2,1,0:T(8,128)(2,1)S(1)} %get-tuple-element.9, bf16[6,2,240,128]{3,2,1,0:T(8,128)(2,1)S(1)} %collective-permute-done.2, bf16[4,4,240,128]{3,2,1,0:T(8,128)(2,1)S(1)} %bitcast.108, ...), kind=kLoop, calls=%fused_computation.6 | loop fusion | flops 70778880 | bytes 17670144 | tf_op jit(solution)/shard_map/concatenate | solution.py:45
  65.6 4.5 %fusion.35 = (bf16[6,6,240,384]{3,2,1,0:T(8,128)(2,1)S(1)}, bf16[6,6,240,384]{3,2,1,0:T(8,128)(2,1)S(1)}, bf16[6,6,240,384]{3,2,1,0:T(8,128)(2,1)}) fusion(bf16[6,8,240,384]{3,2,1,0:T(8,128)(2,1)S(1)} %fusion.2), kind=kLoop, calls=%fused_computation.67 | loop fusion | bytes 39813120 | tf_op jit(solution)/shard_map/slice | solution.py:68
  70.1 4.8 %fusion.43 = f32[8640,128]{1,0:T(8,128)S(1)} fusion(bf16[8640,384]{1,0:T(8,128)(2,1)} %bitcast.102, bf16[384,128]{1,0:T(8,128)(2,1)S(1)} %bitcast.128), kind=kOutput, calls=%fused_computation.75 | convolution fusion | flops 849346560 | bytes 11157504 | tf_op jit(solution)/shard_map/dot_general | solution.py:69
  74.9 1.9 %convolution_add_fusion.1 = f32[8640,128]{1,0:T(8,128)S(1)} fusion(f32[8640,128]{1,0:T(8,128)S(1)} %fusion.43, bf16[8640,384]{1,0:T(8,128)(2,1)S(1)} %bitcast.100, bf16[384,128]{1,0:T(8,128)(2,1)S(1)} %bitcast.127), kind=kOutput, calls=%fused_computation.5 | convolution fusion | flops 850452480 | bytes 15581184 | tf_op jit(solution)/shard_map/dot_general | solution.py:69
  76.8 1.9 %convolution_add_fusion = f32[8640,128]{1,0:T(8,128)S(1)} fusion(f32[8640,128]{1,0:T(8,128)S(1)} %convolution_add_fusion.1, bf16[8640,384]{1,0:T(8,128)(2,1)S(1)} %bitcast.99, bf16[384,128]{1,0:T(8,128)(2,1)S(1)} %bitcast.126), kind=kOutput, calls=%fused_computation.4 | convolution fusion | flops 850452480 | bytes 15581184 | tf_op jit(solution)/shard_map/dot_general | solution.py:69
  81.2 1.6 %fusion.16 = f32[1536,128]{1,0:T(8,128)} fusion(bf16[6,8,240,384]{3,2,1,0:T(8,128)(2,1)S(1)} %fusion.2, bf16[4,6,240,128]{3,2,1,0:T(8,128)(2,1)S(1)} %fusion.12), kind=kOutput, calls=%fused_computation.39 | convolution fusion | flops 377487360 | bytes 10027008 | tf_op jit(solution)/shard_map/dot_general | solution.py:98
  82.8 2.3 %fusion.39 = (bf16[4,6,239,128]{3,2,1,0:T(8,128)(2,1)}, bf16[4,6,239,128]{3,2,1,0:T(8,128)(2,1)}) fusion(bf16[4,6,240,128]{3,2,1,0:T(8,128)(2,1)S(1)} %fusion.12), kind=kLoop, calls=%fused_computation.71 | loop fusion | bytes 5873664 | tf_op jit(solution)/shard_map/slice | solution.py:43
  85.1 1.7 %fusion.15 = f32[1536,128]{1,0:T(8,128)} fusion(f32[1536,128]{1,0:T(8,128)} %fusion.16, bf16[6,8,240,384]{3,2,1,0:T(8,128)(2,1)S(1)} %fusion.2, bf16[4,6,240,128]{3,2,1,0:T(8,128)(2,1)S(1)} %fusion.12), kind=kOutput, calls=%fused_computation.37 | convolution fusion | flops 377487360 | bytes 10027008 | tf_op jit(solution)/shard_map/dot_general | solution.py:98
  86.8 1.7 %fusion.14 = f32[1536,128]{1,0:T(8,128)} fusion(f32[1536,128]{1,0:T(8,128)} %fusion.15, bf16[6,8,240,384]{3,2,1,0:T(8,128)(2,1)S(1)} %fusion.2, bf16[4,6,240,128]{3,2,1,0:T(8,128)(2,1)S(1)} %fusion.12), kind=kOutput, calls=%fused_computation.35 | convolution fusion | flops 377487360 | bytes 10027008 | tf_op jit(solution)/shard_map/dot_general | solution.py:98
  89.7 1.9 %fusion.27 = f32[3840,128]{1,0:T(8,128)} fusion(bf16[3840,128]{1,0:T(8,128)(2,1)S(1)} %bitcast.112, bf16[3,128,128]{2,1,0:T(8,128)(2,1)S(1)} %copy-done.8), kind=kOutput, calls=%fused_computation.58 | convolution fusion | flops 125829120 | bytes 2981888 | tf_op jit(solution)/shard_map/dot_general | solution.py:79
  92.7 1.3 convolution_dynamic-update-slice_fusion.1
  95.2 2.2 %reshape.100 = f32[256,6,128]{2,1,0:T(8,128)} reshape(f32[1536,128]{1,0:T(8,128)} %convolution_dynamic-update-slice_fusion) | data formatting | bytes 1572864 | tf_op jit(solution)/shard_map/reshape | solution.py:37
  97.4 13.9 %all-to-all-start = ((f32[256,6,128]{2,1,0:T(8,128)}), f32[256,6,128]{2,1,0:T(8,128)}, u32[]{:S(2)}, u32[]{:S(2)}) async-start(f32[256,6,128]{2,1,0:T(8,128)} %reshape.100), calls=%async_computation | async-start | bytes 2097152 | tf_op jit(solution)/shard_map/all_to_all | solution.py:28
  111.4 2.3 %convolution_add_fusion.8 = f32[3840,128]{1,0:T(8,128)S(1)} fusion(f32[3840,128]{1,0:T(8,128)} %fusion.27, bf16[3840,128]{1,0:T(8,128)(2,1)} %bitcast.111, bf16[3,128,128]{2,1,0:T(8,128)(2,1)S(1)} %copy-done.8), kind=kOutput, calls=%fused_computation.19 | convolution fusion | flops 126320640 | bytes 4947968 | tf_op jit(solution)/shard_map/dot_general | solution.py:79
  114.2 1.2 fusion.13
  116.9 1.2 fusion.36
  120.1 1.9 %fusion.8 = bf16[3840,128]{1,0:T(8,128)(2,1)} fusion(f32[3840,128]{1,0:T(8,128)S(1)} %convolution_add_fusion.5, bf16[3840,384]{1,0:T(8,128)(2,1)S(1)} %bitcast.103, bf16[384,128]{1,0:T(8,128)(2,1)S(1)} %bitcast.123), kind=kOutput, calls=%fused_computation.21 | convolution fusion | flops 378470400 | bytes 5996544 | tf_op jit(solution)/shard_map/dot_general | solution.py:105
  122.1 19.5 %all-to-all-done = f32[256,6,128]{2,1,0:T(8,128)} async-done(((f32[256,6,128]{2,1,0:T(8,128)}), f32[256,6,128]{2,1,0:T(8,128)}, u32[]{:S(2)}, u32[]{:S(2)}) %all-to-all-start) | async-done | bytes 786464 | tf_op jit(solution)/shard_map/all_to_all | solution.py:28
  141.6 1.5 %reduce_sum.9 = f32[6,128]{1,0:T(8,128)S(1)} reduce(f32[256,6,128]{2,1,0:T(8,128)} %all-to-all-done, f32[]{:T(128)} %constant.1.clone.1), dimensions={0}, to_apply=%region_0.1 | reduce | flops 195840 | bytes 789508 | tf_op jit(solution)/shard_map/reduce_sum | solution.py:29
  (48 shorter events, 16.4 us)
Async XLA Ops:
  0.6 15.0 %copy-start = (bf16[1,4,4,240,128]{4,3,2,1,0:T(8,128)(2,1)S(1)}, bf16[1,4,4,240,128]{4,3,2,1,0:T(8,128)(2,1)}, u32[]{:S(2)}) copy-start(bf16[1,4,4,240,128]{4,3,2,1,0:T(8,128)(2,1)} %param.5) | copy-start | bytes 2949124
  0.6 30.0 %copy-start.1 = (bf16[1,4,4,240,128]{4,3,2,1,0:T(8,128)(2,1)S(1)}, bf16[1,4,4,240,128]{4,3,2,1,0:T(8,128)(2,1)}, u32[]{:S(2)}) copy-start(bf16[1,4,4,240,128]{4,3,2,1,0:T(8,128)(2,1)} %param.4) | copy-start | bytes 2949124
  2.6 13.0 %collective-permute-start.3 = (bf16[2,4,240,128]{3,2,1,0:T(8,128)(2,1)}, bf16[2,4,240,128]{3,2,1,0:T(8,128)(2,1)S(1)}, u32[]{:S(2)}, u32[]{:S(2)}) collective-permute-start(bf16[2,4,240,128]{3,2,1,0:T(8,128)(2,1)} %slice_bitcast_fusion), channel_id=1, source_target_pairs={{4,0},{8,4},{12,8},{16,12},{20,16},{24,20},{28,24},{32,28},{36,32}... | collective-permute-start | bytes 1474568 | tf_op jit(solution)/shard_map/ppermute | solution.py:24
  5.8 24.9 %collective-permute-start = (bf16[2,4,240,128]{3,2,1,0:T(8,128)(2,1)}, bf16[2,4,240,128]{3,2,1,0:T(8,128)(2,1)S(1)}, u32[]{:S(2)}, u32[]{:S(2)}) collective-permute-start(bf16[2,4,240,128]{3,2,1,0:T(8,128)(2,1)} %slice_bitcast_fusion.1), channel_id=1, source_target_pairs={{0,4},{4,8},{8,12},{12,16},{16,20},{20,24},{24,28},{28,32},{32,36}... | collective-permute-start | bytes 1474568 | tf_op jit(solution)/shard_map/ppermute | solution.py:24
  15.7 24.6 %collective-permute-start.4 = (bf16[6,1,240,128]{3,2,1,0:T(8,128)(2,1)S(1)}, bf16[6,1,240,128]{3,2,1,0:T(8,128)(2,1)S(1)}, u32[]{:S(2)}, u32[]{:S(2)}) collective-permute-start(bf16[6,1,240,128]{3,2,1,0:T(8,128)(2,1)S(1)} %get-tuple-element.16), channel_id=1, source_target_pairs={{0,1},{1,2},{2,3},{4,5},{5,6},{6,7},{8,9},{9,10},{10,11},{12,13},{... | collective-permute-start | bytes 1105928 | tf_op jit(solution)/shard_map/ppermute | solution.py:13
  28.0 18.4 %collective-permute-start.5 = (bf16[6,1,240,128]{3,2,1,0:T(8,128)(2,1)S(1)}, bf16[6,1,240,128]{3,2,1,0:T(8,128)(2,1)S(1)}, u32[]{:S(2)}, u32[]{:S(2)}) collective-permute-start(bf16[6,1,240,128]{3,2,1,0:T(8,128)(2,1)S(1)} %get-tuple-element.17), channel_id=1, source_target_pairs={{1,0},{2,1},{3,2},{5,4},{6,5},{7,6},{9,8},{10,9},{11,10},{13,12},{... | collective-permute-start | bytes 1105928 | tf_op jit(solution)/shard_map/ppermute | solution.py:14
  30.8 19.5 %collective-permute-start.1 = (bf16[6,2,240,128]{3,2,1,0:T(8,128)(2,1)S(1)}, bf16[6,2,240,128]{3,2,1,0:T(8,128)(2,1)S(1)}, u32[]{:S(2)}, u32[]{:S(2)}) collective-permute-start(bf16[6,2,240,128]{3,2,1,0:T(8,128)(2,1)S(1)} %get-tuple-element.21), channel_id=1, source_target_pairs={{0,1},{1,2},{2,3},{4,5},{5,6},{6,7},{8,9},{9,10},{10,11},{12,13},{... | collective-permute-start | bytes 2211848 | tf_op jit(solution)/shard_map/ppermute | solution.py:13
  38.4 22.2 %collective-permute-start.2 = (bf16[6,2,240,128]{3,2,1,0:T(8,128)(2,1)S(1)}, bf16[6,2,240,128]{3,2,1,0:T(8,128)(2,1)S(1)}, u32[]{:S(2)}, u32[]{:S(2)}) collective-permute-start(bf16[6,2,240,128]{3,2,1,0:T(8,128)(2,1)S(1)} %get-tuple-element.22), channel_id=1, source_target_pairs={{1,0},{2,1},{3,2},{5,4},{6,5},{7,6},{9,8},{10,9},{11,10},{13,12},{... | collective-permute-start | bytes 2211848 | tf_op jit(solution)/shard_map/ppermute | solution.py:14
  46.6 0.9 copy-start.8
  78.7 1.4 copy-start.5
  89.7 4.4 %copy-start.2 = (bf16[4,4,240,128]{3,2,1,0:T(8,128)(2,1)}, bf16[4,4,240,128]{3,2,1,0:T(8,128)(2,1)S(1)}, u32[]{:S(2)}) copy-start(bf16[4,4,240,128]{3,2,1,0:T(8,128)(2,1)S(1)} %get-tuple-element.19) | copy-start | bytes 2949124
  89.7 4.4 %copy-start.3 = (bf16[4,4,240,128]{3,2,1,0:T(8,128)(2,1)}, bf16[4,4,240,128]{3,2,1,0:T(8,128)(2,1)S(1)}, u32[]{:S(2)}) copy-start(bf16[4,4,240,128]{3,2,1,0:T(8,128)(2,1)S(1)} %get-tuple-element.18) | copy-start | bytes 2949124
  97.4 44.2 %all-to-all-start = ((f32[256,6,128]{2,1,0:T(8,128)}), f32[256,6,128]{2,1,0:T(8,128)}, u32[]{:S(2)}, u32[]{:S(2)}) async-start(f32[256,6,128]{2,1,0:T(8,128)} %reshape.100), calls=%async_computation | async-start | bytes 2097152 | tf_op jit(solution)/shard_map/all_to_all | solution.py:28
  111.4 2.3 %copy-start.4 = (bf16[4,4,240,128]{3,2,1,0:T(8,128)(2,1)S(1)}, bf16[4,4,240,128]{3,2,1,0:T(8,128)(2,1)}, u32[]{:S(2)}) copy-start(bf16[4,4,240,128]{3,2,1,0:T(8,128)(2,1)} %copy-done.3) | copy-start | bytes 2949124
  113.7 1.6 %copy-start.6 = (bf16[4,6,239,128]{3,2,1,0:T(8,128)(2,1)S(1)}, bf16[4,6,239,128]{3,2,1,0:T(8,128)(2,1)}, u32[]{:S(2)}) copy-start(bf16[4,6,239,128]{3,2,1,0:T(8,128)(2,1)} %get-tuple-element.14) | copy-start | bytes 4405252
  113.7 2.2 %copy-start.7 = (bf16[4,6,239,128]{3,2,1,0:T(8,128)(2,1)S(1)}, bf16[4,6,239,128]{3,2,1,0:T(8,128)(2,1)}, u32[]{:S(2)}) copy-start(bf16[4,6,239,128]{3,2,1,0:T(8,128)(2,1)} %get-tuple-element.15) | copy-start | bytes 4405252
  116.9 1.3 copy-start.11
  118.2 1.0 copy-start.10
  119.2 1.0 copy-start.9

commit v5 on v4

--- a/solution.py
+++ b/solution.py
@@ -30,11 +30,15 @@
 
 
 def staged_scatter(terms):
-    axes = ("dp", "frame", "row")
-    n = 1
-    for a in axes:
-        n *= lax.axis_size(a)
-    return a2a_sum(terms.reshape(n, terms.shape[0] // n, terms.shape[-1]), axes)
+    n_dp, n_frame, n_row = (lax.axis_size(a) for a in ("dp", "frame", "row"))
+    rows = terms.shape[0] // (n_dp * n_frame * n_row)
+    chans = terms.shape[-1]
+    blocks = terms.reshape(n_dp, n_frame, n_row, rows, chans)
+    blocks = jnp.transpose(blocks, (2, 0, 1, 3, 4))
+    blocks = a2a_sum(blocks, "row")
+    blocks = jnp.transpose(blocks, (1, 0, 2, 3))
+    blocks = a2a_sum(blocks, "frame")
+    return a2a_sum(blocks, "dp")
 
 
 def width_taps(a, reverse):
@@ -43,6 +47,44 @@
     right = jnp.concatenate([a[:, :, 1:], zero], axis=2)
     parts = [right, a, left] if reverse else [left, a, right]
     return jnp.concatenate(parts, axis=-1)
+
+
+def grid_shift(piece, df, dr):
+    n_f, n_r = lax.axis_size("frame"), lax.axis_size("row")
+    pairs = [
+        (f * n_r + r, (f + df) * n_r + (r + dr))
+        for f in range(n_f)
+        for r in range(n_r)
+        if 0 <= f + df < n_f and 0 <= r + dr < n_r
+    ]
+    return lax.ppermute(piece, ("frame", "row"), pairs)
+
+
+def halos(x, g):
+    frames, rows = x.shape[:2]
+    down = grid_shift(jnp.concatenate([x[:, rows - 2 :], g[:, rows - 1 :]], axis=1), 0, 1)
+    up = grid_shift(jnp.concatenate([x[:, :2], g[:, :1]], axis=1), 0, -1)
+    x_mid = grid_shift(x[frames - 2 :], 1, 0)
+    x_above = grid_shift(x[frames - 2 :, rows - 2 :], 1, 1)
+    x_below = grid_shift(x[frames - 2 :, :2], 1, -1)
+    g_mid = grid_shift(g[:2], -1, 0)
+    g_above = grid_shift(g[:2, rows - 1 :], -1, 1)
+    g_below = grid_shift(g[:2, :1], -1, -1)
+    x_e = jnp.concatenate(
+        [
+            jnp.concatenate([x_above, x_mid, x_below], axis=1),
+            jnp.concatenate([down[:, :2], x, up[:, :2]], axis=1),
+        ],
+        axis=0,
+    )
+    g_e = jnp.concatenate(
+        [
+            jnp.concatenate([down[:, 2:], g, up[:, 2:]], axis=1),
+            jnp.concatenate([g_above, g_mid, g_below], axis=1),
+        ],
+        axis=0,
+    )
+    return x_e, g_e
 
 
 def on_device(clip_input, cotangent, spatial_weight, temporal_weight):
@@ -55,10 +97,7 @@
     scale = 1.0 / math.sqrt(cells)
     f32 = jnp.float32
 
-    x_f = jnp.concatenate([frame_shift(x[frames - 2 :], forward=True), x], axis=0)
-    x_e = row_halo(x_f, 2)
-    g_f = jnp.concatenate([g, frame_shift(g[:2], forward=False)], axis=0)
-    g_e = row_halo(g_f, 1)
+    x_e, g_e = halos(x, g)
 
     x3 = width_taps(x_e, reverse=False)
     fwd_weight = spatial_weight.reshape(3, 3 * chans, chans)

time: 144 us -> 160 us (1.11); the launches traced: 144 us -> 158 us
  waiting for transfers between devices: 38.7 us -> 18.1 us
  starting transfers between devices: 43.5 us -> 61 us
  local copies, waits for them, and re-layouts: 22.1 us -> 31.7 us
  other arithmetic: 10 us -> 17.9 us
    all_to_all x1 -> x3, starting transfers between devices: 13.9 us -> 31.2 us  [a2a_sum(): got = lax.all_to_all(blocks, axis, split_axis=0, concat_axis=0, tiled=True)]
    ppermute x6 -> x8, waiting for transfers between devices: 19.2 us -> 3.77 us  [grid_shift(): return lax.ppermute(piece, ('frame', 'row'), pairs)]
    slice x2 -> x10, local copies, waits for them, and re-layouts: 3.82 us -> 10 us  [the longest x1 1.33 us: halos(): x[:, rows - 2:]]
    all_to_all x1 -> x3, waiting for transfers between devices: 19.5 us -> 14.3 us  [a2a_sum(): got = lax.all_to_all(blocks, axis, split_axis=0, concat_axis=0, tiled=True)]
    concatenate x3 -> x5, other arithmetic: 0.94 us -> 5.07 us  [the longest x1 1.57 us: halos(): jnp.concatenate([jnp.concatenate([down[:, 2:], g, up[:, 2:]], axis=1), jn...]
    concatenate x2, other arithmetic: 3.82 us -> 7.9 us  [width_taps(): return jnp.concatenate(parts, axis=-1)]
    transpose x0 -> x2, local copies, waits for them, and re-layouts: none -> 3.37 us  [the longest x1 2.57 us: staged_scatter(): blocks = jnp.transpose(blocks, (2, 0, 1, 3, 4))]
    unnamed x25 -> x37, local copies, waits for them, and re-layouts: 3.29 us -> 2.2 us
  transfers between devices with their start and end apart: 7 -> 11, of which waited for: 4 -> 4; matrix products, arithmetic and copies ran while one was open for 13% -> 28% of each run, Pallas kernels for 0% -> 0%
where the time goes in v5:
time: 160 us; the launch traced here: 158 us
  starting transfers between devices  61 us (38%)
  local copies, waits for them, and re-layouts  31.7 us (20%)
  matrix products  27.8 us (17%)
  waiting for transfers between devices  18.1 us (11%)
  other arithmetic  17.9 us (11%)
    all_to_all x3, starting transfers between devices, a2a_sum(): got = lax.all_to_all(blocks, axis, split_axis=0, concat_axis=0, tiled=True)  31.2 us
    ppermute x8, starting transfers between devices, grid_shift(): return lax.ppermute(piece, ('frame', 'row'), pairs)  29.8 us
    all_to_all x3, waiting for transfers between devices, a2a_sum(): got = lax.all_to_all(blocks, axis, split_axis=0, concat_axis=0, tiled=True)  14.3 us
    dot_general x3, matrix products, on_device(): pre = pre + jnp.dot(piece, fwd_weight[i], preferred_element_type=f32)  8.58 us
    concatenate x2, other arithmetic, width_taps(): return jnp.concatenate(parts, axis=-1)  7.9 us
    dot_general x3, matrix products, on_device(): jnp.dot(shifted, temporal_weight[k], preferred_element_type=f32)  5.59 us
    dot_general x3, matrix products, on_device(): lax.dot_general(piece, pg_flat, (((0,), (0,)), ((), ())), preferred_eleme...  4.99 us
    slice x1, local copies, waits for them, and re-layouts, on_device(): piece = x3[:, i:i + rows + 2].reshape(-1, 3 * chans)  4.5 us
  transfers between devices with their start and end apart: 11, of which 4 were waited for; matrix products, arithmetic and copies ran while one was open for 28% of the time, Pallas kernels for 0%

profile of v5, /device:TPU:1, one launch (start us, length us, event | category | flops | bytes accessed | tf_op | source)
XLA Modules:
  0.0 157.6 jit_solution(18213446755100161271)
XLA Ops:
  0.6 1.3 fusion.42
  4.1 10.3 %collective-permute-start.3 = (bf16[4,3,240,128]{3,2,1,0:T(8,128)(2,1)}, bf16[4,3,240,128]{3,2,1,0:T(8,128)(2,1)}, u32[]{:S(2)}, u32[]{:S(2)}) collective-permute-start(bf16[4,3,240,128]{3,2,1,0:T(8,128)(2,1)} %pad_maximum_fusion.1), channel_id=1, source_target_pairs={{0,1},{1,2},{2,3},{4,5},{5,6},{6,7},{8,9},{9,10},{10,11},{12,13},{... | collective-permute-start | bytes 2211848 | tf_op jit(solution)/shard_map/ppermute | solution.py:60
  15.3 1.9 %collective-permute-start.4 = (bf16[4,3,240,128]{3,2,1,0:T(8,128)(2,1)}, bf16[4,3,240,128]{3,2,1,0:T(8,128)(2,1)}, u32[]{:S(2)}, u32[]{:S(2)}) collective-permute-start(bf16[4,3,240,128]{3,2,1,0:T(8,128)(2,1)} %pad_maximum_fusion.2), channel_id=1, source_target_pairs={{1,0},{2,1},{3,2},{5,4},{6,5},{7,6},{9,8},{10,9},{11,10},{13,12},{... | collective-permute-start | bytes 2211848 | tf_op jit(solution)/shard_map/ppermute | solution.py:60
  18.1 9.3 %collective-permute-start = (bf16[2,2,240,128]{3,2,1,0:T(8,128)(2,1)}, bf16[2,2,240,128]{3,2,1,0:T(8,128)(2,1)}, u32[]{:S(2)}, u32[]{:S(2)}) collective-permute-start(bf16[2,2,240,128]{3,2,1,0:T(8,128)(2,1)} %get-tuple-element.20), channel_id=1, source_target_pairs={{0,5},{1,6},{2,7},{4,9},{5,10},{6,11},{8,13},{9,14},{10,15},{12,17... | collective-permute-start | bytes 737288 | tf_op jit(solution)/shard_map/ppermute | solution.py:60
  27.4 2.0 %collective-permute-start.2 = (bf16[2,2,240,128]{3,2,1,0:T(8,128)(2,1)}, bf16[2,2,240,128]{3,2,1,0:T(8,128)(2,1)}, u32[]{:S(2)}, u32[]{:S(2)}) collective-permute-start(bf16[2,2,240,128]{3,2,1,0:T(8,128)(2,1)} %get-tuple-element.21), channel_id=1, source_target_pairs={{1,4},{2,5},{3,6},{5,8},{6,9},{7,10},{9,12},{10,13},{11,14},{13,16... | collective-permute-start | bytes 737288 | tf_op jit(solution)/shard_map/ppermute | solution.py:60
  30.1 2.5 %collective-permute-start.1 = (bf16[2,4,240,128]{3,2,1,0:T(8,128)(2,1)}, bf16[2,4,240,128]{3,2,1,0:T(8,128)(2,1)S(1)}, u32[]{:S(2)}, u32[]{:S(2)}) collective-permute-start(bf16[2,4,240,128]{3,2,1,0:T(8,128)(2,1)} %slice_bitcast_fusion.1), channel_id=1, source_target_pairs={{0,4},{1,5},{2,6},{3,7},{4,8},{5,9},{6,10},{7,11},{8,12},{9,13},{1... | collective-permute-start | bytes 1474568 | tf_op jit(solution)/shard_map/ppermute | solution.py:60
  38.2 3.8 %collective-permute-done.4 = bf16[4,3,240,128]{3,2,1,0:T(8,128)(2,1)} collective-permute-done((bf16[4,3,240,128]{3,2,1,0:T(8,128)(2,1)}, bf16[4,3,240,128]{3,2,1,0:T(8,128)(2,1)}, u32[]{:S(2)}, u32[]{:S(2)}) %collective-permute-start.4) | collective-permute-done | bytes 737312 | tf_op jit(solution)/shard_map/ppermute | solution.py:60
  45.7 1.5 maximum_maximum_fusion
  47.1 1.7 %fusion.36 = (bf16[6,8,239,128]{3,2,1,0:T(8,128)(2,1)S(1)}, bf16[6,8,239,128]{3,2,1,0:T(8,128)(2,1)S(1)}) fusion(bf16[6,8,240,128]{3,2,1,0:T(8,128)(2,1)S(1)} %maximum_maximum_fusion), kind=kLoop, calls=%fused_computation.66 | loop fusion | bytes 11747328 | tf_op jit(solution)/shard_map/slice | solution.py:46
  48.9 5.7 %fusion.2 = bf16[6,8,240,384]{3,2,1,0:T(8,128)(2,1)S(1)} fusion(bf16[6,8,239,128]{3,2,1,0:T(8,128)(2,1)S(1)} %get-tuple-element.10, bf16[6,8,239,128]{3,2,1,0:T(8,128)(2,1)S(1)} %get-tuple-element.9, bf16[4,2,240,128]{3,2,1,0:T(8,128)(2,1)S(1)} %slice.204, bf16[4,4,240,128]{3,2,1,0:T(8,128)(2,1)S(1)} %bitcast.113, bf16[4,2,240,128]{3,2,1,0:T(8,128)(2,1)S(1)} %slice.201, ...), kind=kLoop, calls=%fused_computation.6 | loop fusion | flops 88473600 | bytes 17670144 | tf_op jit(solution)/shard_map/concatenate | solution.py:49
  54.5 4.5 %fusion.34 = (bf16[6,6,240,384]{3,2,1,0:T(8,128)(2,1)S(1)}, bf16[6,6,240,384]{3,2,1,0:T(8,128)(2,1)S(1)}, bf16[6,6,240,384]{3,2,1,0:T(8,128)(2,1)}) fusion(bf16[6,8,240,384]{3,2,1,0:T(8,128)(2,1)S(1)} %fusion.2), kind=kLoop, calls=%fused_computation.64 | loop fusion | bytes 39813120 | tf_op jit(solution)/shard_map/slice | solution.py:107
  59.0 4.8 %fusion.46 = f32[8640,128]{1,0:T(8,128)S(1)} fusion(bf16[8640,384]{1,0:T(8,128)(2,1)} %bitcast.109, bf16[384,128]{1,0:T(8,128)(2,1)S(1)} %bitcast.137), kind=kOutput, calls=%fused_computation.76 | convolution fusion | flops 849346560 | bytes 11157504 | tf_op jit(solution)/shard_map/dot_general | solution.py:108
  63.8 1.9 %convolution_add_fusion.1 = f32[8640,128]{1,0:T(8,128)S(1)} fusion(f32[8640,128]{1,0:T(8,128)S(1)} %fusion.46, bf16[8640,384]{1,0:T(8,128)(2,1)S(1)} %bitcast.104, bf16[384,128]{1,0:T(8,128)(2,1)S(1)} %bitcast.136), kind=kOutput, calls=%fused_computation.5 | convolution fusion | flops 850452480 | bytes 15581184 | tf_op jit(solution)/shard_map/dot_general | solution.py:108
  65.7 1.9 %convolution_add_fusion = f32[8640,128]{1,0:T(8,128)S(1)} fusion(f32[8640,128]{1,0:T(8,128)S(1)} %convolution_add_fusion.1, bf16[8640,384]{1,0:T(8,128)(2,1)S(1)} %bitcast.103, bf16[384,128]{1,0:T(8,128)(2,1)S(1)} %bitcast.135), kind=kOutput, calls=%fused_computation.4 | convolution fusion | flops 850452480 | bytes 15581184 | tf_op jit(solution)/shard_map/dot_general | solution.py:108
  70.9 1.6 maximum_maximum_fusion.1
  77.4 1.7 %fusion.16 = f32[1536,128]{1,0:T(8,128)} fusion(bf16[6,8,240,384]{3,2,1,0:T(8,128)(2,1)S(1)} %fusion.2, bf16[4,6,240,128]{3,2,1,0:T(8,128)(2,1)S(1)} %fusion.12), kind=kOutput, calls=%fused_computation.38 | convolution fusion | flops 377487360 | bytes 10027008 | tf_op jit(solution)/shard_map/dot_general | solution.py:137
  79.1 2.3 %fusion.38 = (bf16[4,6,239,128]{3,2,1,0:T(8,128)(2,1)}, bf16[4,6,239,128]{3,2,1,0:T(8,128)(2,1)}) fusion(bf16[4,6,240,128]{3,2,1,0:T(8,128)(2,1)S(1)} %fusion.12), kind=kLoop, calls=%fused_computation.68 | loop fusion | bytes 5873664 | tf_op jit(solution)/shard_map/slice | solution.py:47
  81.4 1.7 %fusion.15 = f32[1536,128]{1,0:T(8,128)} fusion(f32[1536,128]{1,0:T(8,128)} %fusion.16, bf16[6,8,240,384]{3,2,1,0:T(8,128)(2,1)S(1)} %fusion.2, bf16[4,6,240,128]{3,2,1,0:T(8,128)(2,1)S(1)} %fusion.12), kind=kOutput, calls=%fused_computation.36 | convolution fusion | flops 377487360 | bytes 10027008 | tf_op jit(solution)/shard_map/dot_general | solution.py:137
  83.1 1.6 %fusion.14 = f32[1536,128]{1,0:T(8,128)} fusion(f32[1536,128]{1,0:T(8,128)} %fusion.15, bf16[6,8,240,384]{3,2,1,0:T(8,128)(2,1)S(1)} %fusion.2, bf16[4,6,240,128]{3,2,1,0:T(8,128)(2,1)S(1)} %fusion.12), kind=kOutput, calls=%fused_computation.34 | convolution fusion | flops 377487360 | bytes 10027008 | tf_op jit(solution)/shard_map/dot_general | solution.py:137
  86.0 1.9 %fusion.26 = f32[3840,128]{1,0:T(8,128)} fusion(bf16[3840,128]{1,0:T(8,128)(2,1)S(1)} %bitcast.119, bf16[3,128,128]{2,1,0:T(8,128)(2,1)S(1)} %copy-done.10), kind=kOutput, calls=%fused_computation.55 | convolution fusion | flops 125829120 | bytes 2981888 | tf_op jit(solution)/shard_map/dot_general | solution.py:118
  91.2 2.2 %reshape.100 = f32[4,16,4,6,128]{4,3,2,1,0:T(8,128)} reshape(f32[1536,128]{1,0:T(8,128)} %convolution_dynamic-update-slice_fusion) | data formatting | bytes 1572864 | tf_op jit(solution)/shard_map/reshape | solution.py:36
  93.4 2.6 %copy.14 = f32[4,4,16,6,128]{4,2,3,1,0:T(8,128)} copy(f32[4,4,16,6,128]{4,3,0,2,1:T(8,128)} %bitcast.127) | data formatting | bytes 1572864 | tf_op jit(solution)/shard_map/transpose | solution.py:37
  96.0 4.6 %all-to-all-start = ((f32[4,4,16,6,128]{4,2,3,1,0:T(8,128)}), f32[4,4,16,6,128]{4,2,3,1,0:T(8,128)}, u32[]{:S(2)}, u32[]{:S(2)}) async-start(f32[4,4,16,6,128]{4,2,3,1,0:T(8,128)} %copy.14), calls=%async_computation | async-start | bytes 1572864 | tf_op jit(solution)/shard_map/all_to_all | solution.py:28
  100.5 2.3 %fusion.9 = bf16[4,6,240,384]{3,2,1,0:T(8,128)(2,1)S(1)} fusion(bf16[4,6,239,128]{3,2,1,0:T(8,128)(2,1)} %get-tuple-element.14, bf16[4,6,239,128]{3,2,1,0:T(8,128)(2,1)} %get-tuple-element.13, bf16[4,6,240,128]{3,2,1,0:T(8,128)(2,1)S(1)} %fusion.12), kind=kLoop, calls=%fused_computation.22 | loop fusion | flops 22118400 | bytes 8835072 | tf_op jit(solution)/shard_map/concatenate | solution.py:49
  104.7 1.7 %convolution_add_fusion.8 = f32[3840,128]{1,0:T(8,128)} fusion(f32[3840,128]{1,0:T(8,128)S(1)} %copy-done.7, bf16[3840,128]{1,0:T(8,128)(2,1)S(1)} %bitcast.118, bf16[3,128,128]{2,1,0:T(8,128)(2,1)S(1)} %copy-done.10), kind=kOutput, calls=%fused_computation.19 | convolution fusion | flops 126320640 | bytes 4947968 | tf_op jit(solution)/shard_map/dot_general | solution.py:118
  108.3 1.9 %fusion.8 = bf16[3840,128]{1,0:T(8,128)(2,1)} fusion(f32[3840,128]{1,0:T(8,128)S(1)} %convolution_add_fusion.5, bf16[3840,384]{1,0:T(8,128)(2,1)S(1)} %bitcast.114, bf16[384,128]{1,0:T(8,128)(2,1)S(1)} %bitcast.132), kind=kOutput, calls=%fused_computation.21 | convolution fusion | flops 378470400 | bytes 5996544 | tf_op jit(solution)/shard_map/dot_general | solution.py:144
  110.2 6.1 %all-to-all-done = f32[4,4,16,6,128]{4,2,3,1,0:T(8,128)} async-done(((f32[4,4,16,6,128]{4,2,3,1,0:T(8,128)}), f32[4,4,16,6,128]{4,2,3,1,0:T(8,128)}, u32[]{:S(2)}, u32[]{:S(2)}) %all-to-all-start) | async-done | bytes 786464 | tf_op jit(solution)/shard_map/all_to_all | solution.py:28
  118.3 16.8 %all-to-all-start.1 = ((f32[16,4,6,128]{3,1,2,0:T(4,128)}), f32[16,4,6,128]{3,1,2,0:T(4,128)S(1)}, u32[]{:S(2)}, u32[]{:S(2)}) async-start(f32[16,4,6,128]{3,1,2,0:T(4,128)} %copy.15), calls=%async_computation.1 | async-start | bytes 393216 | tf_op jit(solution)/shard_map/all_to_all | solution.py:28
  135.2 1.9 %fusion.7 = bf16[3840,128]{1,0:T(8,128)(2,1)S(1)} fusion(f32[3840,128]{1,0:T(8,128)} %convolution_add_fusion.8, bf16[3840,128]{1,0:T(8,128)(2,1)S(1)} %bitcast.122, bf16[3,128,128]{2,1,0:T(8,128)(2,1)S(1)} %copy-done.10), kind=kOutput, calls=%fused_computation.20 | convolution fusion | flops 126812160 | bytes 3964928 | tf_op jit(solution)/shard_map/dot_general | solution.py:118
  137.1 5.0 %all-to-all-done.1 = f32[16,4,6,128]{3,1,2,0:T(4,128)S(1)} async-done(((f32[16,4,6,128]{3,1,2,0:T(4,128)}), f32[16,4,6,128]{3,1,2,0:T(4,128)S(1)}, u32[]{:S(2)}, u32[]{:S(2)}) %all-to-all-start.1) | async-done | bytes 196640 | tf_op jit(solution)/shard_map/all_to_all | solution.py:28
  142.7 9.8 %all-to-all-start.2 = ((f32[4,6,128]{2,1,0:T(8,128)}), f32[4,6,128]{2,1,0:T(8,128)S(1)}, u32[]{:S(2)}, u32[]{:S(2)}) async-start(f32[4,6,128]{2,1,0:T(8,128)} %copy.16), calls=%async_computation.2 | async-start | bytes 32768 | tf_op jit(solution)/shard_map/all_to_all | solution.py:28
  153.7 3.3 %all-to-all-done.2 = f32[4,6,128]{2,1,0:T(8,128)S(1)} async-done(((f32[4,6,128]{2,1,0:T(8,128)}), f32[4,6,128]{2,1,0:T(8,128)S(1)}, u32[]{:S(2)}, u32[]{:S(2)}) %all-to-all-start.2) | async-done | bytes 12320 | tf_op jit(solution)/shard_map/all_to_all | solution.py:28
  (84 shorter events, 34.7 us)
Async XLA Ops:
  0.6 16.6 %copy-start.2 = (bf16[1,4,4,240,128]{4,3,2,1,0:T(8,128)(2,1)S(1)}, bf16[1,4,4,240,128]{4,3,2,1,0:T(8,128)(2,1)}, u32[]{:S(2)}) copy-start(bf16[1,4,4,240,128]{4,3,2,1,0:T(8,128)(2,1)} %param.4) | copy-start | bytes 2949124
  2.0 30.6 %copy-start.8 = (bf16[3,3,128,128]{3,2,1,0:T(8,128)(2,1)S(1)}, bf16[3,3,128,128]{3,2,1,0:T(8,128)(2,1)}, u32[]{:S(2)}) copy-start(bf16[3,3,128,128]{3,2,1,0:T(8,128)(2,1)} %param.6) | copy-start | bytes 884740
  3.1 30.2 %copy-start = (bf16[1,4,4,240,128]{4,3,2,1,0:T(8,128)(2,1)S(1)}, bf16[1,4,4,240,128]{4,3,2,1,0:T(8,128)(2,1)}, u32[]{:S(2)}) copy-start(bf16[1,4,4,240,128]{4,3,2,1,0:T(8,128)(2,1)} %param.5) | copy-start | bytes 2949124
  4.1 30.0 %copy-start.9 = (bf16[3,3,128,128]{3,2,1,0:T(8,128)(2,1)S(1)}, bf16[3,3,128,128]{3,2,1,0:T(8,128)(2,1)}, u32[]{:S(2)}) copy-start(bf16[3,3,128,128]{3,2,1,0:T(8,128)(2,1)} %param.6) | copy-start | bytes 884740
  4.1 31.8 %collective-permute-start.3 = (bf16[4,3,240,128]{3,2,1,0:T(8,128)(2,1)}, bf16[4,3,240,128]{3,2,1,0:T(8,128)(2,1)}, u32[]{:S(2)}, u32[]{:S(2)}) collective-permute-start(bf16[4,3,240,128]{3,2,1,0:T(8,128)(2,1)} %pad_maximum_fusion.1), channel_id=1, source_target_pairs={{0,1},{1,2},{2,3},{4,5},{5,6},{6,7},{8,9},{9,10},{10,11},{12,13},{... | collective-permute-start | bytes 2211848 | tf_op jit(solution)/shard_map/ppermute | solution.py:60
  15.3 26.6 %collective-permute-start.4 = (bf16[4,3,240,128]{3,2,1,0:T(8,128)(2,1)}, bf16[4,3,240,128]{3,2,1,0:T(8,128)(2,1)}, u32[]{:S(2)}, u32[]{:S(2)}) collective-permute-start(bf16[4,3,240,128]{3,2,1,0:T(8,128)(2,1)} %pad_maximum_fusion.2), channel_id=1, source_target_pairs={{1,0},{2,1},{3,2},{5,4},{6,5},{7,6},{9,8},{10,9},{11,10},{13,12},{... | collective-permute-start | bytes 2211848 | tf_op jit(solution)/shard_map/ppermute | solution.py:60
  18.1 26.3 %collective-permute-start = (bf16[2,2,240,128]{3,2,1,0:T(8,128)(2,1)}, bf16[2,2,240,128]{3,2,1,0:T(8,128)(2,1)}, u32[]{:S(2)}, u32[]{:S(2)}) collective-permute-start(bf16[2,2,240,128]{3,2,1,0:T(8,128)(2,1)} %get-tuple-element.20), channel_id=1, source_target_pairs={{0,5},{1,6},{2,7},{4,9},{5,10},{6,11},{8,13},{9,14},{10,15},{12,17... | collective-permute-start | bytes 737288 | tf_op jit(solution)/shard_map/ppermute | solution.py:60
  27.4 18.3 %collective-permute-start.2 = (bf16[2,2,240,128]{3,2,1,0:T(8,128)(2,1)}, bf16[2,2,240,128]{3,2,1,0:T(8,128)(2,1)}, u32[]{:S(2)}, u32[]{:S(2)}) collective-permute-start(bf16[2,2,240,128]{3,2,1,0:T(8,128)(2,1)} %get-tuple-element.21), channel_id=1, source_target_pairs={{1,4},{2,5},{3,6},{5,8},{6,9},{7,10},{9,12},{10,13},{11,14},{13,16... | collective-permute-start | bytes 737288 | tf_op jit(solution)/shard_map/ppermute | solution.py:60
  30.1 15.5 %collective-permute-start.1 = (bf16[2,4,240,128]{3,2,1,0:T(8,128)(2,1)}, bf16[2,4,240,128]{3,2,1,0:T(8,128)(2,1)S(1)}, u32[]{:S(2)}, u32[]{:S(2)}) collective-permute-start(bf16[2,4,240,128]{3,2,1,0:T(8,128)(2,1)} %slice_bitcast_fusion.1), channel_id=1, source_target_pairs={{0,4},{1,5},{2,6},{3,7},{4,8},{5,9},{6,10},{7,11},{8,12},{9,13},{1... | collective-permute-start | bytes 1474568 | tf_op jit(solution)/shard_map/ppermute | solution.py:60
  35.9 35.0 %collective-permute-start.5 = (bf16[2,1,240,128]{3,2,1,0:T(8,128)(2,1)}, bf16[2,1,240,128]{3,2,1,0:T(8,128)(2,1)}, u32[]{:S(2)}, u32[]{:S(2)}) collective-permute-start(bf16[2,1,240,128]{3,2,1,0:T(8,128)(2,1)} %get-tuple-element.18), channel_id=1, source_target_pairs={{4,1},{5,2},{6,3},{8,5},{9,6},{10,7},{12,9},{13,10},{14,11},{16,13... | collective-permute-start | bytes 368648 | tf_op jit(solution)/shard_map/ppermute | solution.py:60
  42.0 28.9 %collective-permute-start.7 = (bf16[2,1,240,128]{3,2,1,0:T(8,128)(2,1)}, bf16[2,1,240,128]{3,2,1,0:T(8,128)(2,1)}, u32[]{:S(2)}, u32[]{:S(2)}) collective-permute-start(bf16[2,1,240,128]{3,2,1,0:T(8,128)(2,1)} %get-tuple-element.19), channel_id=1, source_target_pairs={{5,0},{6,1},{7,2},{9,4},{10,5},{11,6},{13,8},{14,9},{15,10},{17,12... | collective-permute-start | bytes 368648 | tf_op jit(solution)/shard_map/ppermute | solution.py:60
  44.3 26.5 %collective-permute-start.6 = (bf16[2,4,240,128]{3,2,1,0:T(8,128)(2,1)}, bf16[2,4,240,128]{3,2,1,0:T(8,128)(2,1)}, u32[]{:S(2)}, u32[]{:S(2)}) collective-permute-start(bf16[2,4,240,128]{3,2,1,0:T(8,128)(2,1)} %slice_bitcast_fusion), channel_id=1, source_target_pairs={{4,0},{5,1},{6,2},{7,3},{8,4},{9,5},{10,6},{11,7},{12,8},{13,9},{1... | collective-permute-start | bytes 1474568 | tf_op jit(solution)/shard_map/ppermute | solution.py:60
  54.5 4.5 %copy-start.15 = (bf16[1,3,128,128]{3,2,1,0:T(8,128)(2,1)S(1)}, bf16[1,3,128,128]{3,2,1,0:T(8,128)(2,1)}, u32[]{:S(2)}) copy-start(bf16[1,3,128,128]{3,2,1,0:T(8,128)(2,1)} %get-tuple-element.31) | copy-start | bytes 294916
  59.0 4.8 %copy-start.14 = (bf16[1,3,128,128]{3,2,1,0:T(8,128)(2,1)S(1)}, bf16[1,3,128,128]{3,2,1,0:T(8,128)(2,1)}, u32[]{:S(2)}) copy-start(bf16[1,3,128,128]{3,2,1,0:T(8,128)(2,1)} %get-tuple-element.30) | copy-start | bytes 294916
  67.6 2.0 %copy-start.1 = (f32[8640,128]{1,0:T(8,128)}, f32[8640,128]{1,0:T(8,128)S(1)}, u32[]{:S(2)}) copy-start(f32[8640,128]{1,0:T(8,128)S(1)} %convolution_add_fusion) | copy-start | bytes 13271044
  72.4 0.9 copy-start.10
  74.4 1.8 %slice-start.2 = ((f32[8640,128]{1,0:T(8,128)}), f32[5760,128]{1,0:T(8,128)S(1)}, s32[]{:S(2)}) async-start(f32[8640,128]{1,0:T(8,128)} %copy-done.1), calls=%async_computation.5 | async-start | bytes 5898240 | tf_op jit(solution)/shard_map/slice | solution.py:128
  79.1 5.6 %slice-start = ((s8[4423680]{0:T(1024)(128)(4,1)}), s8[4194304]{0:T(1024)(128)(4,1)S(1)}, s32[]{:S(2)}) async-start(s8[4423680]{0:T(1024)(128)(4,1)} %bitcast.105), calls=%async_computation.3 | async-start | bytes 8388608
  81.4 3.3 %slice-start.1 = ((s8[4423680]{0:T(1024)(128)(4,1)}), s8[229376]{0:T(1024)(128)(4,1)S(1)}, s32[]{:S(2)}) async-start(s8[4423680]{0:T(1024)(128)(4,1)} %bitcast.105), calls=%async_computation.4 | async-start | bytes 458752
  85.9 4.1 %copy-start.3 = (bf16[4,4,240,128]{3,2,1,0:T(8,128)(2,1)}, bf16[4,4,240,128]{3,2,1,0:T(8,128)(2,1)S(1)}, u32[]{:S(2)}) copy-start(bf16[4,4,240,128]{3,2,1,0:T(8,128)(2,1)S(1)} %get-tuple-element.16) | copy-start | bytes 2949124
  86.0 4.1 %copy-start.5 = (bf16[4,4,240,128]{3,2,1,0:T(8,128)(2,1)}, bf16[4,4,240,128]{3,2,1,0:T(8,128)(2,1)S(1)}, u32[]{:S(2)}) copy-start(bf16[4,4,240,128]{3,2,1,0:T(8,128)(2,1)S(1)} %get-tuple-element.15) | copy-start | bytes 2949124
  96.0 20.3 %all-to-all-start = ((f32[4,4,16,6,128]{4,2,3,1,0:T(8,128)}), f32[4,4,16,6,128]{4,2,3,1,0:T(8,128)}, u32[]{:S(2)}, u32[]{:S(2)}) async-start(f32[4,4,16,6,128]{4,2,3,1,0:T(8,128)} %copy.14), calls=%async_computation | async-start | bytes 1572864 | tf_op jit(solution)/shard_map/all_to_all | solution.py:28
  102.8 1.3 copy-start.4
  102.8 1.8 %copy-start.7 = (f32[3840,128]{1,0:T(8,128)S(1)}, f32[3840,128]{1,0:T(8,128)}, u32[]{:S(2)}) copy-start(f32[3840,128]{1,0:T(8,128)} %fusion.26) | copy-start | bytes 5898244
  104.7 1.7 %copy-start.13 = (bf16[1,3,128,128]{3,2,1,0:T(8,128)(2,1)S(1)}, bf16[1,3,128,128]{3,2,1,0:T(8,128)(2,1)}, u32[]{:S(2)}) copy-start(bf16[1,3,128,128]{3,2,1,0:T(8,128)(2,1)} %get-tuple-element.28) | copy-start | bytes 294916
  106.4 1.0 copy-start.12
  107.3 1.0 copy-start.11
  108.3 26.8 %copy-start.6 = (bf16[4,4,240,128]{3,2,1,0:T(8,128)(2,1)S(1)}, bf16[4,4,240,128]{3,2,1,0:T(8,128)(2,1)}, u32[]{:S(2)}) copy-start(bf16[4,4,240,128]{3,2,1,0:T(8,128)(2,1)} %copy-done.5) | copy-start | bytes 2949124
  118.3 23.8 %all-to-all-start.1 = ((f32[16,4,6,128]{3,1,2,0:T(4,128)}), f32[16,4,6,128]{3,1,2,0:T(4,128)S(1)}, u32[]{:S(2)}, u32[]{:S(2)}) async-start(f32[16,4,6,128]{3,1,2,0:T(4,128)} %copy.15), calls=%async_computation.1 | async-start | bytes 393216 | tf_op jit(solution)/shard_map/all_to_all | solution.py:28
  142.7 14.2 %all-to-all-start.2 = ((f32[4,6,128]{2,1,0:T(8,128)}), f32[4,6,128]{2,1,0:T(8,128)S(1)}, u32[]{:S(2)}, u32[]{:S(2)}) async-start(f32[4,6,128]{2,1,0:T(8,128)} %copy.16), calls=%async_computation.2 | async-start | bytes 32768 | tf_op jit(solution)/shard_map/all_to_all | solution.py:28

commit v6 on v3

v6 whole, which is shorter than its diff:
```python
import math

import jax
import jax.numpy as jnp
from jax import lax
from jax.sharding import PartitionSpec as P


def row_halo(shard):
    peers = lax.axis_size("row")
    up = [(i, i + 1) for i in range(peers - 1)]
    down = [(i + 1, i) for i in range(peers - 1)]
    before = lax.ppermute(shard[-1:], "row", up)
    after = lax.ppermute(shard[:1], "row", down)
    return jnp.concatenate([before, shard, after], axis=0)


def frame_shift(piece, forward):
    peers = lax.axis_size("frame")
    if forward:
        pairs = [(i, i + 1) for i in range(peers - 1)]
    else:
        pairs = [(i + 1, i) for i in range(peers - 1)]
    return lax.ppermute(piece, "frame", pairs)


def a2a_sum(blocks, axis):
    got = lax.all_to_all(blocks, axis, split_axis=0, concat_axis=0, tiled=True)
    return jnp.sum(got, axis=0)


def staged_scatter(terms):
    n_dp, n_frame, n_row = (lax.axis_size(a) for a in ("dp", "frame", "row"))
    rows = terms.shape[0] // (n_dp * n_frame * n_row)
    chans = terms.shape[-1]
    blocks = terms.reshape(n_dp, n_frame, n_row, rows, chans)
    blocks = jnp.transpose(blocks, (2, 0, 1, 3, 4))
    blocks = a2a_sum(blocks, "row")
    blocks = jnp.transpose(blocks, (1, 0, 2, 3))
    blocks = a2a_sum(blocks, "frame")
    return a2a_sum(blocks, "dp")


def width_taps(a, reverse):
    zero = jnp.zeros_like(a[:, :, :1])
    left = jnp.concatenate([zero, a[:, :, :-1]], axis=2)
    right = jnp.concatenate([a[:, :, 1:], zero], axis=2)
    parts = [right, a, left] if reverse else [left, a, right]
    return jnp.concatenate(parts, axis=-1)


def frame_taps(ext, frames, later):
    if later:
        parts = [ext[:, k : k + frames] for k in range(3)]
    else:
        parts = [ext[:, 2 - k : 2 - k + frames] for k in range(3)]
    return jnp.concatenate(parts, axis=-1)


def on_device(clip_input, cotangent, spatial_weight, temporal_weight):
    x = jnp.transpose(clip_input[0], (1, 0, 2, 3))
    g = jnp.transpose(cotangent[0], (1, 0, 2, 3))
    rows, frames, cols, chans = x.shape
    cells = (
        lax.axis_size("dp") * frames * lax.axis_size("frame") * rows * lax.axis_size("row") * cols
    )
    scale = 1.0 / math.sqrt(cells)
    f32 = jnp.float32
    bf16 = jnp.bfloat16

    x_ext = row_halo(x)
    g_next = frame_shift(g[:, :2], forward=False)
    x3 = width_taps(x_ext, reverse=False)
    fwd_weight = spatial_weight.reshape(3, 3 * chans, chans)
    pre = jnp.zeros((rows * frames * cols, chans), f32)
    for i in range(3):
        piece = x3[i : i + rows].reshape(-1, 3 * chans)
        pre = pre + jnp.dot(piece, fwd_weight[i], preferred_element_type=f32)
    pre = pre.reshape(x.shape)
    act = jax.nn.silu(pre).astype(bf16)
    act_prev = frame_shift(act[:, frames - 2 :], forward=True)
    act3 = frame_taps(jnp.concatenate([act_prev, act], axis=1), frames, later=False)
    g3 = frame_taps(jnp.concatenate([g, g_next], axis=1), frames, later=True)
    act3_flat = act3.reshape(-1, 3 * chans)
    g_flat = g.reshape(-1, chans)

    mixed = jnp.dot(act3_flat, temporal_weight.reshape(3 * chans, chans), preferred_element_type=f32)
    back_temporal = jnp.transpose(temporal_weight, (0, 2, 1)).reshape(3 * chans, chans)
    act_grad = jnp.dot(g3.reshape(-1, 3 * chans), back_temporal, preferred_element_type=f32)
    temporal_grad = lax.dot_general(
        act3_flat, g_flat, (((0,), (0,)), ((), ())), preferred_element_type=f32
    )
    mixed = mixed.astype(bf16).reshape(x.shape)
    act_grad = act_grad.astype(bf16).reshape(x.shape)
    block_output = (x.astype(f32) + mixed.astype(f32)).astype(bf16)

    sigma = jax.nn.sigmoid(pre)
    pre_grad = (act_grad.astype(f32) * sigma * (1.0 + pre * (1.0 - sigma))).astype(bf16)
    pg_flat = pre_grad.reshape(-1, chans)

    spatial_list = []
    for i in range(3):
        piece = x3[i : i + rows].reshape(-1, 3 * chans)
        spatial_list.append(
            lax.dot_general(piece, pg_flat, (((0,), (0,)), ((), ())), preferred_element_type=f32)
        )
    pg3 = width_taps(row_halo(pre_grad), reverse=True)
    back_weight = jnp.transpose(spatial_weight, (0, 1, 3, 2)).reshape(3, 3 * chans, chans)
    back = g.astype(f32).reshape(-1, chans)
    for i in range(3):
        piece = pg3[2 - i : 2 - i + rows].reshape(-1, 3 * chans)
        back = back + jnp.dot(piece, back_weight[i], preferred_element_type=f32)
    input_grad = back.astype(bf16).reshape(x.shape)

    partial_terms = jnp.concatenate(spatial_list + [temporal_grad], axis=0)
    summed = staged_scatter(partial_terms)
    block_output = jnp.transpose(block_output, (1, 0, 2, 3))
    input_grad = jnp.transpose(input_grad, (1, 0, 2, 3))
    return (block_output[None], input_grad[None], summed * scale)


def solution(mesh):
    placed = (P("dp", "frame", "row", None, None), P("dp", "frame", "row", None, None), P(), P())
    return jax.shard_map(
        on_device,
        mesh=mesh,
        in_specs=placed,
        out_specs=(
            P("dp", "frame", "row", None, None),
            P("dp", "frame", "row", None, None),
            P(("dp", "frame", "row"), None),
        ),
        check_vma=False,
    )
```

time: 126 us -> 118 us (0.937)
  matrix products: 26 us -> 12.4 us
  waiting for transfers between devices: 21.4 us -> 28.1 us
  other arithmetic: 7.34 us -> 9.92 us
  starting transfers between devices: 47.6 us -> 45.8 us
  local copies, waits for them, and re-layouts: 20.6 us -> 19.2 us
    ppermute x4, waiting for transfers between devices: 5.9 us -> 16.9 us  [the longest x2 16.9 us: row_halo(): after = lax.ppermute(shard[:1], 'row', down)]
    dot_general x9 -> x3, matrix products: 12.5 us -> 3.77 us  [the longest x1 1.87 us: on_device(): jnp.dot(act3_flat, temporal_weight.reshape(3 * chans, chans), preferred_e...]
    all_to_all x3, waiting for transfers between devices: 15.5 us -> 11.2 us  [a2a_sum(): got = lax.all_to_all(blocks, axis, split_axis=0, concat_axis=0, tiled=True)]
    dot_general x3, matrix products: 5.78 us -> 2.82 us  [on_device(): back = back + jnp.dot(piece, back_weight[i], preferred_element_type=f32)]
    unnamed x35 -> x29, local copies, waits for them, and re-layouts: 2.53 us -> 5.34 us
    reshape x1, local copies, waits for them, and re-layouts: 2.19 us -> 0.1 us  [staged_scatter(): blocks = terms.reshape(n_dp, n_frame, n_row, rows, chans)]
    dot_general x3, matrix products: 4.95 us -> 2.94 us  [on_device(): lax.dot_general(piece, pg_flat, (((0,), (0,)), ((), ())), preferred_eleme...]
    slice x6, local copies, waits for them, and re-layouts: 8.71 us -> 6.85 us  [the longest x1 4.1 us: on_device(): piece = pg3[2 - i:2 - i + rows].reshape(-1, 3 * chans)]
  transfers between devices with their start and end apart: 9 -> 9, of which waited for: 5 -> 5; matrix products, arithmetic and copies ran while one was open for 29% -> 23% of each run, Pallas kernels for 0% -> 0%
where the time goes in v6:
time: 118 us; the launch traced here: 116 us
  starting transfers between devices  45.8 us (39%)
  waiting for transfers between devices  28.1 us (24%)
  local copies, waits for them, and re-layouts  19.2 us (16%)
  matrix products  12.4 us (11%)
  other arithmetic  9.92 us (8%)
    all_to_all x3, starting transfers between devices, a2a_sum(): got = lax.all_to_all(blocks, axis, split_axis=0, concat_axis=0, tiled=True)  24.7 us
    ppermute x2, waiting for transfers between devices, row_halo(): after = lax.ppermute(shard[:1], 'row', down)  16.9 us
    ppermute x2, starting transfers between devices, row_halo(): before = lax.ppermute(shard[-1:], 'row', up)  12.6 us
    all_to_all x3, waiting for transfers between devices, a2a_sum(): got = lax.all_to_all(blocks, axis, split_axis=0, concat_axis=0, tiled=True)  11.2 us
    unnamed x29, local copies, waits for them, and re-layouts  5.34 us
    ppermute x2, starting transfers between devices, frame_shift(): return lax.ppermute(piece, 'frame', pairs)  4.48 us
    slice x1, local copies, waits for them, and re-layouts, on_device(): piece = pg3[2 - i:2 - i + rows].reshape(-1, 3 * chans)  4.1 us
    ppermute x2, starting transfers between devices, row_halo(): after = lax.ppermute(shard[:1], 'row', down)  4.02 us
  transfers between devices with their start and end apart: 9, of which 5 were waited for; matrix products, arithmetic and copies ran while one was open for 23% of the time, Pallas kernels for 0%

profile of v6, /device:TPU:1, one launch (start us, length us, event | category | flops | bytes accessed | tf_op | source)
XLA Modules:
  0.0 116.5 jit_solution(646196561418965832)
XLA Ops:
  0.7 1.4 %copy.57 = bf16[1,4,4,240,128]{4,3,1,2,0:T(8,128)(2,1)S(1)} copy(bf16[1,4,4,240,128]{4,3,2,1,0:T(8,128)(2,1)} %param.4) | data formatting | bytes 1966080 | tf_op args[0]
  2.8 10.2 %collective-permute-start = (bf16[1,4,240,128]{3,2,1,0:T(8,128)(2,1)}, bf16[1,4,240,128]{3,2,1,0:T(8,128)(2,1)S(1)}, u32[]{:S(2)}, u32[]{:S(2)}) collective-permute-start(bf16[1,4,240,128]{3,2,1,0:T(8,128)(2,1)} %get-tuple-element.34), channel_id=1, source_target_pairs={{0,1},{1,2},{2,3},{4,5},{5,6},{6,7},{8,9},{9,10},{10,11},{12,13},{... | collective-permute-start | bytes 737288 | tf_op jit(solution)/shard_map/ppermute | solution.py:13
  13.0 1.9 %collective-permute-start.1 = (bf16[1,4,240,128]{3,2,1,0:T(8,128)(2,1)}, bf16[1,4,240,128]{3,2,1,0:T(8,128)(2,1)S(1)}, u32[]{:S(2)}, u32[]{:S(2)}) collective-permute-start(bf16[1,4,240,128]{3,2,1,0:T(8,128)(2,1)} %get-tuple-element.35), channel_id=1, source_target_pairs={{1,0},{2,1},{3,2},{5,4},{6,5},{7,6},{9,8},{10,9},{11,10},{13,12},{... | collective-permute-start | bytes 737288 | tf_op jit(solution)/shard_map/ppermute | solution.py:14
  15.9 1.3 %collective-permute-start.3 = (bf16[4,2,240,128]{3,2,1,0:T(8,128)(2,1)}, bf16[4,2,240,128]{3,2,1,0:T(8,128)(2,1)S(1)}, u32[]{:S(2)}, u32[]{:S(2)}) collective-permute-start(bf16[4,2,240,128]{3,2,1,0:T(8,128)(2,1)} %slice.123), channel_id=1, source_target_pairs={{4,0},{8,4},{12,8},{16,12},{20,16},{24,20},{28,24},{32,28},{36,32}... | collective-permute-start | bytes 1474568 | tf_op jit(solution)/shard_map/ppermute | solution.py:24
  18.1 1.0 copy.35
  19.9 6.5 %collective-permute-done.1 = bf16[1,4,240,128]{3,2,1,0:T(8,128)(2,1)S(1)} collective-permute-done((bf16[1,4,240,128]{3,2,1,0:T(8,128)(2,1)}, bf16[1,4,240,128]{3,2,1,0:T(8,128)(2,1)S(1)}, u32[]{:S(2)}, u32[]{:S(2)}) %collective-permute-start.1) | collective-permute-done | bytes 245792 | tf_op jit(solution)/shard_map/ppermute | solution.py:14
  27.4 1.4 %fusion.6 = bf16[6,4,240,384]{3,2,1,0:T(8,128)(2,1)S(1)} fusion(bf16[6,4,239,128]{3,2,1,0:T(8,128)(2,1)S(1)} %get-tuple-element.29, bf16[6,4,239,128]{3,2,1,0:T(8,128)(2,1)S(1)} %get-tuple-element.28, bf16[1,4,240,128]{3,2,1,0:T(8,128)(2,1)S(1)} %collective-permute-done.1, bf16[4,4,240,128]{3,2,1,0:T(8,128)(2,1)S(1)} %bitcast.106, ...), kind=kLoop, calls=%fused_computation.15 | loop fusion | flops 30965760 | bytes 8835072 | tf_op jit(solution)/shard_map/concatenate | solution.py:49
  28.8 1.1 fusion.20
  31.8 1.0 convolution_add_fusion.3
  35.2 1.0 convolution_bitcast_fusion
  36.2 1.0 convolution_bitcast_fusion.1
  37.2 3.2 %collective-permute-start.2 = (bf16[4,2,240,128]{3,2,1,0:T(8,128)(2,1)S(1)}, bf16[4,2,240,128]{3,2,1,0:T(8,128)(2,1)S(1)}, u32[]{:S(2)}, u32[]{:S(2)}) collective-permute-start(bf16[4,2,240,128]{3,2,1,0:T(8,128)(2,1)S(1)} %slice.120), channel_id=1, source_target_pairs={{0,4},{4,8},{8,12},{12,16},{16,20},{20,24},{24,28},{28,32},{32,36}... | collective-permute-start | bytes 1474568 | tf_op jit(solution)/shard_map/ppermute | solution.py:24
  40.4 2.5 %collective-permute-start.4 = (bf16[1,4,240,128]{3,2,1,0:T(8,128)(2,1)S(1)}, bf16[1,4,240,128]{3,2,1,0:T(8,128)(2,1)S(1)}, u32[]{:S(2)}, u32[]{:S(2)}) collective-permute-start(bf16[1,4,240,128]{3,2,1,0:T(8,128)(2,1)S(1)} %get-tuple-element.32), channel_id=1, source_target_pairs={{0,1},{1,2},{2,3},{4,5},{5,6},{6,7},{8,9},{9,10},{10,11},{12,13},{... | collective-permute-start | bytes 737288 | tf_op jit(solution)/shard_map/ppermute | solution.py:13
  42.9 2.1 %collective-permute-start.5 = (bf16[1,4,240,128]{3,2,1,0:T(8,128)(2,1)S(1)}, bf16[1,4,240,128]{3,2,1,0:T(8,128)(2,1)S(1)}, u32[]{:S(2)}, u32[]{:S(2)}) collective-permute-start(bf16[1,4,240,128]{3,2,1,0:T(8,128)(2,1)S(1)} %get-tuple-element.33), channel_id=1, source_target_pairs={{1,0},{2,1},{3,2},{5,4},{6,5},{7,6},{9,8},{10,9},{11,10},{13,12},{... | collective-permute-start | bytes 737288 | tf_op jit(solution)/shard_map/ppermute | solution.py:14
  45.0 1.0 convolution_bitcast_fusion.2
  46.0 10.4 %collective-permute-done.5 = bf16[1,4,240,128]{3,2,1,0:T(8,128)(2,1)S(1)} collective-permute-done((bf16[1,4,240,128]{3,2,1,0:T(8,128)(2,1)S(1)}, bf16[1,4,240,128]{3,2,1,0:T(8,128)(2,1)S(1)}, u32[]{:S(2)}, u32[]{:S(2)}) %collective-permute-start.5) | collective-permute-done | bytes 245792 | tf_op jit(solution)/shard_map/ppermute | solution.py:14
  57.4 2.5 %fusion.8 = bf16[6,4,240,384]{3,2,1,0:T(8,128)(2,1)} fusion(bf16[6,4,239,128]{3,2,1,0:T(8,128)(2,1)S(1)} %get-tuple-element.27, bf16[6,4,239,128]{3,2,1,0:T(8,128)(2,1)S(1)} %get-tuple-element.26, bf16[1,4,240,128]{3,2,1,0:T(8,128)(2,1)S(1)} %collective-permute-done.5, bf16[4,4,240,128]{3,2,1,0:T(8,128)(2,1)S(1)} %get-tuple-element.24, ...), kind=kLoop, calls=%fused_computation.17 | loop fusion | flops 30965760 | bytes 8835072 | tf_op jit(solution)/shard_map/concatenate | solution.py:49
  60.5 1.6 %copy-done = bf16[4,4,240,384]{3,2,1,0:T(8,128)(2,1)} copy-done((bf16[4,4,240,384]{3,2,1,0:T(8,128)(2,1)}, bf16[4,4,240,384]{3,2,1,0:T(8,128)(2,1)S(1)}, u32[]{:S(2)}) %copy-start) | copy-done | bytes 2949144
  62.1 1.0 convolution_bitcast_fusion.3
  63.3 1.3 %copy.38 = f32[4,4,16,6,128]{4,2,3,1,0:T(8,128)} copy(f32[4,4,16,6,128]{4,3,0,2,1:T(8,128)S(1)} %bitcast.110) | data formatting | bytes 1572864 | tf_op jit(solution)/shard_map/transpose | solution.py:37
  64.6 4.2 %all-to-all-start = ((f32[4,4,16,6,128]{4,2,3,1,0:T(8,128)}), f32[4,4,16,6,128]{4,2,3,1,0:T(8,128)}, u32[]{:S(2)}, u32[]{:S(2)}) async-start(f32[4,4,16,6,128]{4,2,3,1,0:T(8,128)} %copy.38), calls=%async_computation | async-start | bytes 1572864 | tf_op jit(solution)/shard_map/all_to_all | solution.py:28
  68.8 4.1 %fusion.19 = (bf16[4,4,240,384]{3,2,1,0:T(8,128)(2,1)S(1)}, bf16[4,4,240,384]{3,2,1,0:T(8,128)(2,1)S(1)}, bf16[4,4,240,384]{3,2,1,0:T(8,128)(2,1)S(1)}) fusion(bf16[6,4,240,384]{3,2,1,0:T(8,128)(2,1)} %fusion.8), kind=kLoop, calls=%fused_computation.49 | loop fusion | bytes 17694720 | tf_op jit(solution)/shard_map/slice | solution.py:111
  75.8 1.0 copy.56
  76.9 4.4 %all-to-all-done = f32[4,4,16,6,128]{4,2,3,1,0:T(8,128)} async-done(((f32[4,4,16,6,128]{4,2,3,1,0:T(8,128)}), f32[4,4,16,6,128]{4,2,3,1,0:T(8,128)}, u32[]{:S(2)}, u32[]{:S(2)}) %all-to-all-start) | async-done | bytes 786464 | tf_op jit(solution)/shard_map/all_to_all | solution.py:28
  81.2 1.2 %reduce_sum.27 = f32[4,16,6,128]{3,1,2,0:T(8,128)S(1)} reduce(f32[4,4,16,6,128]{4,2,3,1,0:T(8,128)} %all-to-all-done, f32[]{:T(128)} %constant.2.clone.1), dimensions={0}, to_apply=%region_0.1 | reduce | flops 147456 | bytes 983044 | tf_op jit(solution)/shard_map/reduce_sum | solution.py:29
  83.3 8.3 %all-to-all-start.1 = ((f32[16,4,6,128]{3,1,2,0:T(4,128)}), f32[16,4,6,128]{3,1,2,0:T(4,128)S(1)}, u32[]{:S(2)}, u32[]{:S(2)}) async-start(f32[16,4,6,128]{3,1,2,0:T(4,128)} %copy.39), calls=%async_computation.1 | async-start | bytes 393216 | tf_op jit(solution)/shard_map/all_to_all | solution.py:28
  91.5 1.9 %convolution_convert_fusion.1 = bf16[3840,128]{1,0:T(8,128)(2,1)} fusion(bf16[3840,384]{1,0:T(8,128)(2,1)S(1)} %bitcast.96, bf16[384,128]{1,0:T(8,128)(2,1)S(1)} %bitcast.119), kind=kOutput, calls=%fused_computation.13 | convolution fusion | flops 377978880 | bytes 4030464 | tf_op jit(solution)/shard_map/dot_general | solution.py:87
  93.4 5.1 %all-to-all-done.1 = f32[16,4,6,128]{3,1,2,0:T(4,128)S(1)} async-done(((f32[16,4,6,128]{3,1,2,0:T(4,128)}), f32[16,4,6,128]{3,1,2,0:T(4,128)S(1)}, u32[]{:S(2)}, u32[]{:S(2)}) %all-to-all-start.1) | async-done | bytes 196640 | tf_op jit(solution)/shard_map/all_to_all | solution.py:28
  99.2 12.2 %all-to-all-start.2 = ((f32[4,6,128]{2,1,0:T(8,128)}), f32[4,6,128]{2,1,0:T(8,128)S(1)}, u32[]{:S(2)}, u32[]{:S(2)}) async-start(f32[4,6,128]{2,1,0:T(8,128)} %copy.40), calls=%async_computation.2 | async-start | bytes 32768 | tf_op jit(solution)/shard_map/all_to_all | solution.py:28
  111.4 1.8 %fusion.16 = bf16[1,4,4,240,128]{4,3,1,2,0:T(8,128)(2,1)S(1)} fusion(bf16[4,4,240,128]{3,2,1,0:T(8,128)(2,1)} %bitcast.109, bf16[1,4,4,240,128]{4,3,2,1,0:T(8,128)(2,1)} %param.4), kind=kLoop, calls=%fused_computation.41 | loop fusion | flops 1966080 | bytes 2949120 | tf_op jit(solution)/shard_map/broadcast_in_dim | solution.py:119
  113.2 1.0 copy.41
  114.2 1.7 %all-to-all-done.2 = f32[4,6,128]{2,1,0:T(8,128)S(1)} async-done(((f32[4,6,128]{2,1,0:T(8,128)}), f32[4,6,128]{2,1,0:T(8,128)S(1)}, u32[]{:S(2)}, u32[]{:S(2)}) %all-to-all-start.2) | async-done | bytes 12320 | tf_op jit(solution)/shard_map/all_to_all | solution.py:28
  (57 shorter events, 15.4 us)
Async XLA Ops:
  0.6 14.3 %copy-start.3 = (bf16[1,4,4,240,128]{4,3,2,1,0:T(8,128)(2,1)S(1)}, bf16[1,4,4,240,128]{4,3,2,1,0:T(8,128)(2,1)}, u32[]{:S(2)}) copy-start(bf16[1,4,4,240,128]{4,3,2,1,0:T(8,128)(2,1)} %param.5) | copy-start | bytes 2949124
  0.6 16.5 %copy-start.2 = (bf16[3,3,128,128]{3,2,1,0:T(8,128)(2,1)S(1)}, bf16[3,3,128,128]{3,2,1,0:T(8,128)(2,1)}, u32[]{:S(2)}) copy-start(bf16[3,3,128,128]{3,2,1,0:T(8,128)(2,1)} %param.6) | copy-start | bytes 884740
  2.8 17.1 %collective-permute-start = (bf16[1,4,240,128]{3,2,1,0:T(8,128)(2,1)}, bf16[1,4,240,128]{3,2,1,0:T(8,128)(2,1)S(1)}, u32[]{:S(2)}, u32[]{:S(2)}) collective-permute-start(bf16[1,4,240,128]{3,2,1,0:T(8,128)(2,1)} %get-tuple-element.34), channel_id=1, source_target_pairs={{0,1},{1,2},{2,3},{4,5},{5,6},{6,7},{8,9},{9,10},{10,11},{12,13},{... | collective-permute-start | bytes 737288 | tf_op jit(solution)/shard_map/ppermute | solution.py:13
  13.0 13.3 %collective-permute-start.1 = (bf16[1,4,240,128]{3,2,1,0:T(8,128)(2,1)}, bf16[1,4,240,128]{3,2,1,0:T(8,128)(2,1)S(1)}, u32[]{:S(2)}, u32[]{:S(2)}) collective-permute-start(bf16[1,4,240,128]{3,2,1,0:T(8,128)(2,1)} %get-tuple-element.35), channel_id=1, source_target_pairs={{1,0},{2,1},{3,2},{5,4},{6,5},{7,6},{9,8},{10,9},{11,10},{13,12},{... | collective-permute-start | bytes 737288 | tf_op jit(solution)/shard_map/ppermute | solution.py:14
  15.9 16.9 %collective-permute-start.3 = (bf16[4,2,240,128]{3,2,1,0:T(8,128)(2,1)}, bf16[4,2,240,128]{3,2,1,0:T(8,128)(2,1)S(1)}, u32[]{:S(2)}, u32[]{:S(2)}) collective-permute-start(bf16[4,2,240,128]{3,2,1,0:T(8,128)(2,1)} %slice.123), channel_id=1, source_target_pairs={{4,0},{8,4},{12,8},{16,12},{20,16},{24,20},{28,24},{32,28},{36,32}... | collective-permute-start | bytes 1474568 | tf_op jit(solution)/shard_map/ppermute | solution.py:24
  28.8 1.1 copy-start.11
  29.8 1.0 copy-start.9
  30.8 1.0 copy-start.8
  37.2 22.7 %collective-permute-start.2 = (bf16[4,2,240,128]{3,2,1,0:T(8,128)(2,1)S(1)}, bf16[4,2,240,128]{3,2,1,0:T(8,128)(2,1)S(1)}, u32[]{:S(2)}, u32[]{:S(2)}) collective-permute-start(bf16[4,2,240,128]{3,2,1,0:T(8,128)(2,1)S(1)} %slice.120), channel_id=1, source_target_pairs={{0,4},{4,8},{8,12},{12,16},{16,20},{20,24},{24,28},{28,32},{32,36}... | collective-permute-start | bytes 1474568 | tf_op jit(solution)/shard_map/ppermute | solution.py:24
  40.4 5.6 %collective-permute-start.4 = (bf16[1,4,240,128]{3,2,1,0:T(8,128)(2,1)S(1)}, bf16[1,4,240,128]{3,2,1,0:T(8,128)(2,1)S(1)}, u32[]{:S(2)}, u32[]{:S(2)}) collective-permute-start(bf16[1,4,240,128]{3,2,1,0:T(8,128)(2,1)S(1)} %get-tuple-element.32), channel_id=1, source_target_pairs={{0,1},{1,2},{2,3},{4,5},{5,6},{6,7},{8,9},{9,10},{10,11},{12,13},{... | collective-permute-start | bytes 737288 | tf_op jit(solution)/shard_map/ppermute | solution.py:13
  42.9 13.5 %collective-permute-start.5 = (bf16[1,4,240,128]{3,2,1,0:T(8,128)(2,1)S(1)}, bf16[1,4,240,128]{3,2,1,0:T(8,128)(2,1)S(1)}, u32[]{:S(2)}, u32[]{:S(2)}) collective-permute-start(bf16[1,4,240,128]{3,2,1,0:T(8,128)(2,1)S(1)} %get-tuple-element.33), channel_id=1, source_target_pairs={{1,0},{2,1},{3,2},{5,4},{6,5},{7,6},{9,8},{10,9},{11,10},{13,12},{... | collective-permute-start | bytes 737288 | tf_op jit(solution)/shard_map/ppermute | solution.py:14
  60.0 2.1 %copy-start.4 = (bf16[1,4,4,240,128]{4,3,2,1,0:T(8,128)(2,1)S(1)}, bf16[1,4,4,240,128]{4,3,2,1,0:T(8,128)(2,1)}, u32[]{:S(2)}) copy-start(bf16[1,4,4,240,128]{4,3,2,1,0:T(8,128)(2,1)} %param.5) | copy-start | bytes 2949124
  60.5 1.6 %copy-start = (bf16[4,4,240,384]{3,2,1,0:T(8,128)(2,1)}, bf16[4,4,240,384]{3,2,1,0:T(8,128)(2,1)S(1)}, u32[]{:S(2)}) copy-start(bf16[4,4,240,384]{3,2,1,0:T(8,128)(2,1)S(1)} %fusion.10) | copy-start | bytes 8847364
  64.6 16.6 %all-to-all-start = ((f32[4,4,16,6,128]{4,2,3,1,0:T(8,128)}), f32[4,4,16,6,128]{4,2,3,1,0:T(8,128)}, u32[]{:S(2)}, u32[]{:S(2)}) async-start(f32[4,4,16,6,128]{4,2,3,1,0:T(8,128)} %copy.38), calls=%async_computation | async-start | bytes 1572864 | tf_op jit(solution)/shard_map/all_to_all | solution.py:28
  68.8 4.1 %copy-start.7 = (bf16[1,3,128,128]{3,2,1,0:T(8,128)(2,1)S(1)}, bf16[1,3,128,128]{3,2,1,0:T(8,128)(2,1)}, u32[]{:S(2)}) copy-start(bf16[1,3,128,128]{3,2,1,0:T(8,128)(2,1)} %get-tuple-element.38) | copy-start | bytes 294916
  72.9 1.0 copy-start.6
  73.9 0.9 copy-start.5
  75.8 15.7 %copy-start.1 = (bf16[4,4,240,384]{3,2,1,0:T(8,128)(2,1)S(1)}, bf16[4,4,240,384]{3,2,1,0:T(8,128)(2,1)}, u32[]{:S(2)}) copy-start(bf16[4,4,240,384]{3,2,1,0:T(8,128)(2,1)} %copy-done) | copy-start | bytes 8847364
  75.8 15.7 %copy-start.10 = (bf16[3,128,128]{2,1,0:T(8,128)(2,1)S(1)}, bf16[3,128,128]{2,1,0:T(8,128)(2,1)}, u32[]{:S(2)}) copy-start(bf16[3,128,128]{2,1,0:T(8,128)(2,1)} %param.7) | copy-start | bytes 294916
  83.3 15.3 %all-to-all-start.1 = ((f32[16,4,6,128]{3,1,2,0:T(4,128)}), f32[16,4,6,128]{3,1,2,0:T(4,128)S(1)}, u32[]{:S(2)}, u32[]{:S(2)}) async-start(f32[16,4,6,128]{3,1,2,0:T(4,128)} %copy.39), calls=%async_computation.1 | async-start | bytes 393216 | tf_op jit(solution)/shard_map/all_to_all | solution.py:28
  99.2 16.7 %all-to-all-start.2 = ((f32[4,6,128]{2,1,0:T(8,128)}), f32[4,6,128]{2,1,0:T(8,128)S(1)}, u32[]{:S(2)}, u32[]{:S(2)}) async-start(f32[4,6,128]{2,1,0:T(8,128)} %copy.40), calls=%async_computation.2 | async-start | bytes 32768 | tf_op jit(solution)/shard_map/all_to_all | solution.py:28

commit v7 on v6

--- a/solution.py
+++ b/solution.py
@@ -33,12 +33,10 @@
     n_dp, n_frame, n_row = (lax.axis_size(a) for a in ("dp", "frame", "row"))
     rows = terms.shape[0] // (n_dp * n_frame * n_row)
     chans = terms.shape[-1]
-    blocks = terms.reshape(n_dp, n_frame, n_row, rows, chans)
-    blocks = jnp.transpose(blocks, (2, 0, 1, 3, 4))
+    blocks = terms.reshape(n_dp * n_frame, n_row, rows, chans)
+    blocks = jnp.transpose(blocks, (1, 0, 2, 3))
     blocks = a2a_sum(blocks, "row")
-    blocks = jnp.transpose(blocks, (1, 0, 2, 3))
-    blocks = a2a_sum(blocks, "frame")
-    return a2a_sum(blocks, "dp")
+    return a2a_sum(blocks, ("dp", "frame"))
 
 
 def width_taps(a, reverse):

time: 118 us -> 116 us (0.983)
  waiting for transfers between devices: 28.1 us -> 30.3 us
  other arithmetic: 9.92 us -> 8.42 us
    all_to_all x3 -> x2, waiting for transfers between devices: 11.2 us -> 13.3 us  [a2a_sum(): got = lax.all_to_all(blocks, axis, split_axis=0, concat_axis=0, tiled=True)]
    broadcast_in_dim x1, other arithmetic: 1.75 us -> 0.26 us  [on_device(): return (block_output[None], input_grad[None], summed * scale)]
    transpose x1 -> x0, local copies, waits for them, and re-layouts: 1.34 us -> none  [staged_scatter(): blocks = jnp.transpose(blocks, (2, 0, 1, 3, 4))]
    all_to_all x3 -> x2, starting transfers between devices: 24.7 us -> 23.8 us  [a2a_sum(): got = lax.all_to_all(blocks, axis, split_axis=0, concat_axis=0, tiled=True)]
    unnamed x29 -> x31, local copies, waits for them, and re-layouts: 5.34 us -> 5.6 us
  transfers between devices with their start and end apart: 9 -> 8, of which waited for: 5 -> 4; matrix products, arithmetic and copies ran while one was open for 23% -> 21% of each run, Pallas kernels for 0% -> 0%
where the time goes in v7:
time: 116 us; the launch traced here: 115 us
  starting transfers between devices  45 us (39%)
  waiting for transfers between devices  30.3 us (26%)
  local copies, waits for them, and re-layouts  18.8 us (16%)
  matrix products  11.4 us (10%)
  other arithmetic  8.42 us (7%)
    all_to_all x2, starting transfers between devices, a2a_sum(): got = lax.all_to_all(blocks, axis, split_axis=0, concat_axis=0, tiled=True)  23.8 us
    ppermute x2, waiting for transfers between devices, row_halo(): after = lax.ppermute(shard[:1], 'row', down)  17 us
    all_to_all x2, waiting for transfers between devices, a2a_sum(): got = lax.all_to_all(blocks, axis, split_axis=0, concat_axis=0, tiled=True)  13.3 us
    ppermute x2, starting transfers between devices, row_halo(): before = lax.ppermute(shard[-1:], 'row', up)  12.6 us
    unnamed x31, local copies, waits for them, and re-layouts  5.6 us
    ppermute x2, starting transfers between devices, frame_shift(): return lax.ppermute(piece, 'frame', pairs)  4.52 us
    slice x1, local copies, waits for them, and re-layouts, on_device(): piece = pg3[2 - i:2 - i + rows].reshape(-1, 3 * chans)  4.1 us
    ppermute x2, starting transfers between devices, row_halo(): after = lax.ppermute(shard[:1], 'row', down)  4.05 us
  transfers between devices with their start and end apart: 8, of which 4 were waited for; matrix products, arithmetic and copies ran while one was open for 21% of the time, Pallas kernels for 0%

profile of v7, /device:TPU:1, one launch (start us, length us, event | category | flops | bytes accessed | tf_op | source)
XLA Modules:
  0.0 115.0 jit_solution(8463044333454554306)
XLA Ops:
  0.7 1.4 %copy.55 = bf16[1,4,4,240,128]{4,3,1,2,0:T(8,128)(2,1)S(1)} copy(bf16[1,4,4,240,128]{4,3,2,1,0:T(8,128)(2,1)} %param.4) | data formatting | bytes 1966080 | tf_op args[0]
  2.8 10.2 %collective-permute-start = (bf16[1,4,240,128]{3,2,1,0:T(8,128)(2,1)}, bf16[1,4,240,128]{3,2,1,0:T(8,128)(2,1)S(1)}, u32[]{:S(2)}, u32[]{:S(2)}) collective-permute-start(bf16[1,4,240,128]{3,2,1,0:T(8,128)(2,1)} %get-tuple-element.34), channel_id=1, source_target_pairs={{0,1},{1,2},{2,3},{4,5},{5,6},{6,7},{8,9},{9,10},{10,11},{12,13},{... | collective-permute-start | bytes 737288 | tf_op jit(solution)/shard_map/ppermute | solution.py:13
  13.0 1.9 %collective-permute-start.1 = (bf16[1,4,240,128]{3,2,1,0:T(8,128)(2,1)}, bf16[1,4,240,128]{3,2,1,0:T(8,128)(2,1)S(1)}, u32[]{:S(2)}, u32[]{:S(2)}) collective-permute-start(bf16[1,4,240,128]{3,2,1,0:T(8,128)(2,1)} %get-tuple-element.35), channel_id=1, source_target_pairs={{1,0},{2,1},{3,2},{5,4},{6,5},{7,6},{9,8},{10,9},{11,10},{13,12},{... | collective-permute-start | bytes 737288 | tf_op jit(solution)/shard_map/ppermute | solution.py:14
  15.9 1.3 %collective-permute-start.3 = (bf16[4,2,240,128]{3,2,1,0:T(8,128)(2,1)}, bf16[4,2,240,128]{3,2,1,0:T(8,128)(2,1)S(1)}, u32[]{:S(2)}, u32[]{:S(2)}) collective-permute-start(bf16[4,2,240,128]{3,2,1,0:T(8,128)(2,1)} %slice.123), channel_id=1, source_target_pairs={{4,0},{8,4},{12,8},{16,12},{20,16},{24,20},{28,24},{32,28},{36,32}... | collective-permute-start | bytes 1474568 | tf_op jit(solution)/shard_map/ppermute | solution.py:24
  18.1 1.0 copy.34
  19.9 6.5 %collective-permute-done.1 = bf16[1,4,240,128]{3,2,1,0:T(8,128)(2,1)S(1)} collective-permute-done((bf16[1,4,240,128]{3,2,1,0:T(8,128)(2,1)}, bf16[1,4,240,128]{3,2,1,0:T(8,128)(2,1)S(1)}, u32[]{:S(2)}, u32[]{:S(2)}) %collective-permute-start.1) | collective-permute-done | bytes 245792 | tf_op jit(solution)/shard_map/ppermute | solution.py:14
  27.4 1.4 %fusion.6 = bf16[6,4,240,384]{3,2,1,0:T(8,128)(2,1)S(1)} fusion(bf16[6,4,239,128]{3,2,1,0:T(8,128)(2,1)S(1)} %get-tuple-element.29, bf16[6,4,239,128]{3,2,1,0:T(8,128)(2,1)S(1)} %get-tuple-element.28, bf16[1,4,240,128]{3,2,1,0:T(8,128)(2,1)S(1)} %collective-permute-done.1, bf16[4,4,240,128]{3,2,1,0:T(8,128)(2,1)S(1)} %bitcast.105, ...), kind=kLoop, calls=%fused_computation.15 | loop fusion | flops 30965760 | bytes 8835072 | tf_op jit(solution)/shard_map/concatenate | solution.py:47
  28.8 1.1 fusion.20
  29.8 0.9 fusion.28
  31.8 1.0 convolution_add_fusion.3
  33.3 0.9 convolution_convert_fusion
  35.2 1.0 convolution_bitcast_fusion
  36.2 1.0 convolution_bitcast_fusion.1
  37.2 3.2 %collective-permute-start.2 = (bf16[4,2,240,128]{3,2,1,0:T(8,128)(2,1)S(1)}, bf16[4,2,240,128]{3,2,1,0:T(8,128)(2,1)S(1)}, u32[]{:S(2)}, u32[]{:S(2)}) collective-permute-start(bf16[4,2,240,128]{3,2,1,0:T(8,128)(2,1)S(1)} %slice.120), channel_id=1, source_target_pairs={{0,4},{4,8},{8,12},{12,16},{16,20},{20,24},{24,28},{28,32},{32,36}... | collective-permute-start | bytes 1474568 | tf_op jit(solution)/shard_map/ppermute | solution.py:24
  40.5 2.4 %collective-permute-start.4 = (bf16[1,4,240,128]{3,2,1,0:T(8,128)(2,1)S(1)}, bf16[1,4,240,128]{3,2,1,0:T(8,128)(2,1)S(1)}, u32[]{:S(2)}, u32[]{:S(2)}) collective-permute-start(bf16[1,4,240,128]{3,2,1,0:T(8,128)(2,1)S(1)} %get-tuple-element.32), channel_id=1, source_target_pairs={{0,1},{1,2},{2,3},{4,5},{5,6},{6,7},{8,9},{9,10},{10,11},{12,13},{... | collective-permute-start | bytes 737288 | tf_op jit(solution)/shard_map/ppermute | solution.py:13
  42.9 2.1 %collective-permute-start.5 = (bf16[1,4,240,128]{3,2,1,0:T(8,128)(2,1)S(1)}, bf16[1,4,240,128]{3,2,1,0:T(8,128)(2,1)S(1)}, u32[]{:S(2)}, u32[]{:S(2)}) collective-permute-start(bf16[1,4,240,128]{3,2,1,0:T(8,128)(2,1)S(1)} %get-tuple-element.33), channel_id=1, source_target_pairs={{1,0},{2,1},{3,2},{5,4},{6,5},{7,6},{9,8},{10,9},{11,10},{13,12},{... | collective-permute-start | bytes 737288 | tf_op jit(solution)/shard_map/ppermute | solution.py:14
  45.0 1.0 convolution_bitcast_fusion.2
  46.0 10.5 %collective-permute-done.5 = bf16[1,4,240,128]{3,2,1,0:T(8,128)(2,1)S(1)} collective-permute-done((bf16[1,4,240,128]{3,2,1,0:T(8,128)(2,1)S(1)}, bf16[1,4,240,128]{3,2,1,0:T(8,128)(2,1)S(1)}, u32[]{:S(2)}, u32[]{:S(2)}) %collective-permute-start.5) | collective-permute-done | bytes 245792 | tf_op jit(solution)/shard_map/ppermute | solution.py:14
  57.4 2.5 %fusion.8 = bf16[6,4,240,384]{3,2,1,0:T(8,128)(2,1)} fusion(bf16[6,4,239,128]{3,2,1,0:T(8,128)(2,1)S(1)} %get-tuple-element.27, bf16[6,4,239,128]{3,2,1,0:T(8,128)(2,1)S(1)} %get-tuple-element.26, bf16[1,4,240,128]{3,2,1,0:T(8,128)(2,1)S(1)} %collective-permute-done.5, bf16[4,4,240,128]{3,2,1,0:T(8,128)(2,1)S(1)} %get-tuple-element.24, ...), kind=kLoop, calls=%fused_computation.17 | loop fusion | flops 30965760 | bytes 8835072 | tf_op jit(solution)/shard_map/concatenate | solution.py:47
  60.5 1.6 %copy-done = bf16[4,4,240,384]{3,2,1,0:T(8,128)(2,1)} copy-done((bf16[4,4,240,384]{3,2,1,0:T(8,128)(2,1)}, bf16[4,4,240,384]{3,2,1,0:T(8,128)(2,1)S(1)}, u32[]{:S(2)}) %copy-start) | copy-done | bytes 2949144
  62.1 1.0 convolution_bitcast_fusion.3
  63.3 1.3 %copy.37 = f32[4,64,6,128]{3,1,2,0:T(8,128)} copy(f32[4,64,6,128]{3,2,0,1:T(8,128)S(1)} %bitcast.109) | data formatting | bytes 1572864 | tf_op jit(solution)/shard_map/transpose | solution.py:37
  64.6 4.2 %all-to-all-start = ((f32[4,64,6,128]{3,1,2,0:T(8,128)}), f32[4,64,6,128]{3,1,2,0:T(8,128)}, u32[]{:S(2)}, u32[]{:S(2)}) async-start(f32[4,64,6,128]{3,1,2,0:T(8,128)} %copy.37), calls=%async_computation | async-start | bytes 1572864 | tf_op jit(solution)/shard_map/all_to_all | solution.py:28
  68.8 4.1 %fusion.19 = (bf16[4,4,240,384]{3,2,1,0:T(8,128)(2,1)S(1)}, bf16[4,4,240,384]{3,2,1,0:T(8,128)(2,1)S(1)}, bf16[4,4,240,384]{3,2,1,0:T(8,128)(2,1)S(1)}) fusion(bf16[6,4,240,384]{3,2,1,0:T(8,128)(2,1)} %fusion.8), kind=kLoop, calls=%fused_computation.49 | loop fusion | bytes 17694720 | tf_op jit(solution)/shard_map/slice | solution.py:109
  73.0 0.9 convolution_add_fusion.2
  74.9 1.0 fusion.4
  75.9 1.0 copy.54
  76.9 4.4 %all-to-all-done = f32[4,64,6,128]{3,1,2,0:T(8,128)} async-done(((f32[4,64,6,128]{3,1,2,0:T(8,128)}), f32[4,64,6,128]{3,1,2,0:T(8,128)}, u32[]{:S(2)}, u32[]{:S(2)}) %all-to-all-start) | async-done | bytes 786464 | tf_op jit(solution)/shard_map/all_to_all | solution.py:28
  81.3 1.2 %reduce_sum.18 = f32[64,6,128]{2,0,1:T(8,128)S(1)} reduce(f32[4,64,6,128]{3,1,2,0:T(8,128)} %all-to-all-done, f32[]{:T(128)} %constant.2.clone.1), dimensions={0}, to_apply=%region_0.1 | reduce | flops 147456 | bytes 983044 | tf_op jit(solution)/shard_map/reduce_sum | solution.py:29
  83.3 19.6 %all-to-all-start.1 = ((f32[64,6,128]{2,1,0:T(8,128)}), f32[64,6,128]{2,1,0:T(8,128)S(1)}, u32[]{:S(2)}, u32[]{:S(2)}) async-start(f32[64,6,128]{2,1,0:T(8,128)} %copy.38), calls=%async_computation.1 | async-start | bytes 524288 | tf_op jit(solution)/shard_map/all_to_all | solution.py:28
  104.4 1.0 copy.39
  105.4 8.9 %all-to-all-done.1 = f32[64,6,128]{2,1,0:T(8,128)S(1)} async-done(((f32[64,6,128]{2,1,0:T(8,128)}), f32[64,6,128]{2,1,0:T(8,128)S(1)}, u32[]{:S(2)}, u32[]{:S(2)}) %all-to-all-start.1) | async-done | bytes 196640 | tf_op jit(solution)/shard_map/all_to_all | solution.py:28
  (55 shorter events, 12.4 us)
Async XLA Ops:
  0.6 14.3 %copy-start.4 = (bf16[1,4,4,240,128]{4,3,2,1,0:T(8,128)(2,1)S(1)}, bf16[1,4,4,240,128]{4,3,2,1,0:T(8,128)(2,1)}, u32[]{:S(2)}) copy-start(bf16[1,4,4,240,128]{4,3,2,1,0:T(8,128)(2,1)} %param.5) | copy-start | bytes 2949124
  0.6 16.5 %copy-start.3 = (bf16[3,3,128,128]{3,2,1,0:T(8,128)(2,1)S(1)}, bf16[3,3,128,128]{3,2,1,0:T(8,128)(2,1)}, u32[]{:S(2)}) copy-start(bf16[3,3,128,128]{3,2,1,0:T(8,128)(2,1)} %param.6) | copy-start | bytes 884740
  2.8 17.0 %collective-permute-start = (bf16[1,4,240,128]{3,2,1,0:T(8,128)(2,1)}, bf16[1,4,240,128]{3,2,1,0:T(8,128)(2,1)S(1)}, u32[]{:S(2)}, u32[]{:S(2)}) collective-permute-start(bf16[1,4,240,128]{3,2,1,0:T(8,128)(2,1)} %get-tuple-element.34), channel_id=1, source_target_pairs={{0,1},{1,2},{2,3},{4,5},{5,6},{6,7},{8,9},{9,10},{10,11},{12,13},{... | collective-permute-start | bytes 737288 | tf_op jit(solution)/shard_map/ppermute | solution.py:13
  13.0 13.3 %collective-permute-start.1 = (bf16[1,4,240,128]{3,2,1,0:T(8,128)(2,1)}, bf16[1,4,240,128]{3,2,1,0:T(8,128)(2,1)S(1)}, u32[]{:S(2)}, u32[]{:S(2)}) collective-permute-start(bf16[1,4,240,128]{3,2,1,0:T(8,128)(2,1)} %get-tuple-element.35), channel_id=1, source_target_pairs={{1,0},{2,1},{3,2},{5,4},{6,5},{7,6},{9,8},{10,9},{11,10},{13,12},{... | collective-permute-start | bytes 737288 | tf_op jit(solution)/shard_map/ppermute | solution.py:14
  15.9 16.9 %collective-permute-start.3 = (bf16[4,2,240,128]{3,2,1,0:T(8,128)(2,1)}, bf16[4,2,240,128]{3,2,1,0:T(8,128)(2,1)S(1)}, u32[]{:S(2)}, u32[]{:S(2)}) collective-permute-start(bf16[4,2,240,128]{3,2,1,0:T(8,128)(2,1)} %slice.123), channel_id=1, source_target_pairs={{4,0},{8,4},{12,8},{16,12},{20,16},{24,20},{28,24},{32,28},{36,32}... | collective-permute-start | bytes 1474568 | tf_op jit(solution)/shard_map/ppermute | solution.py:24
  28.8 1.1 copy-start.12
  29.8 1.0 copy-start.10
  30.8 1.0 copy-start.9
  37.2 22.7 %collective-permute-start.2 = (bf16[4,2,240,128]{3,2,1,0:T(8,128)(2,1)S(1)}, bf16[4,2,240,128]{3,2,1,0:T(8,128)(2,1)S(1)}, u32[]{:S(2)}, u32[]{:S(2)}) collective-permute-start(bf16[4,2,240,128]{3,2,1,0:T(8,128)(2,1)S(1)} %slice.120), channel_id=1, source_target_pairs={{0,4},{4,8},{8,12},{12,16},{16,20},{20,24},{24,28},{28,32},{32,36}... | collective-permute-start | bytes 1474568 | tf_op jit(solution)/shard_map/ppermute | solution.py:24
  40.5 5.5 %collective-permute-start.4 = (bf16[1,4,240,128]{3,2,1,0:T(8,128)(2,1)S(1)}, bf16[1,4,240,128]{3,2,1,0:T(8,128)(2,1)S(1)}, u32[]{:S(2)}, u32[]{:S(2)}) collective-permute-start(bf16[1,4,240,128]{3,2,1,0:T(8,128)(2,1)S(1)} %get-tuple-element.32), channel_id=1, source_target_pairs={{0,1},{1,2},{2,3},{4,5},{5,6},{6,7},{8,9},{9,10},{10,11},{12,13},{... | collective-permute-start | bytes 737288 | tf_op jit(solution)/shard_map/ppermute | solution.py:13
  42.9 13.6 %collective-permute-start.5 = (bf16[1,4,240,128]{3,2,1,0:T(8,128)(2,1)S(1)}, bf16[1,4,240,128]{3,2,1,0:T(8,128)(2,1)S(1)}, u32[]{:S(2)}, u32[]{:S(2)}) collective-permute-start(bf16[1,4,240,128]{3,2,1,0:T(8,128)(2,1)S(1)} %get-tuple-element.33), channel_id=1, source_target_pairs={{1,0},{2,1},{3,2},{5,4},{6,5},{7,6},{9,8},{10,9},{11,10},{13,12},{... | collective-permute-start | bytes 737288 | tf_op jit(solution)/shard_map/ppermute | solution.py:14
  60.1 2.1 %copy-start.5 = (bf16[1,4,4,240,128]{4,3,2,1,0:T(8,128)(2,1)S(1)}, bf16[1,4,4,240,128]{4,3,2,1,0:T(8,128)(2,1)}, u32[]{:S(2)}) copy-start(bf16[1,4,4,240,128]{4,3,2,1,0:T(8,128)(2,1)} %param.5) | copy-start | bytes 2949124
  60.5 1.6 %copy-start = (bf16[4,4,240,384]{3,2,1,0:T(8,128)(2,1)}, bf16[4,4,240,384]{3,2,1,0:T(8,128)(2,1)S(1)}, u32[]{:S(2)}) copy-start(bf16[4,4,240,384]{3,2,1,0:T(8,128)(2,1)S(1)} %fusion.10) | copy-start | bytes 8847364
  64.6 16.6 %all-to-all-start = ((f32[4,64,6,128]{3,1,2,0:T(8,128)}), f32[4,64,6,128]{3,1,2,0:T(8,128)}, u32[]{:S(2)}, u32[]{:S(2)}) async-start(f32[4,64,6,128]{3,1,2,0:T(8,128)} %copy.37), calls=%async_computation | async-start | bytes 1572864 | tf_op jit(solution)/shard_map/all_to_all | solution.py:28
  68.8 4.1 %copy-start.8 = (bf16[1,3,128,128]{3,2,1,0:T(8,128)(2,1)S(1)}, bf16[1,3,128,128]{3,2,1,0:T(8,128)(2,1)}, u32[]{:S(2)}) copy-start(bf16[1,3,128,128]{3,2,1,0:T(8,128)(2,1)} %get-tuple-element.38) | copy-start | bytes 294916
  72.9 1.0 copy-start.7
  73.9 1.0 copy-start.6
  75.8 27.1 %copy-start.1 = (bf16[4,4,240,384]{3,2,1,0:T(8,128)(2,1)S(1)}, bf16[4,4,240,384]{3,2,1,0:T(8,128)(2,1)}, u32[]{:S(2)}) copy-start(bf16[4,4,240,384]{3,2,1,0:T(8,128)(2,1)} %copy-done) | copy-start | bytes 8847364
  75.9 27.1 %copy-start.11 = (bf16[3,128,128]{2,1,0:T(8,128)(2,1)S(1)}, bf16[3,128,128]{2,1,0:T(8,128)(2,1)}, u32[]{:S(2)}) copy-start(bf16[3,128,128]{2,1,0:T(8,128)(2,1)} %param.7) | copy-start | bytes 294916
  83.3 31.1 %all-to-all-start.1 = ((f32[64,6,128]{2,1,0:T(8,128)}), f32[64,6,128]{2,1,0:T(8,128)S(1)}, u32[]{:S(2)}, u32[]{:S(2)}) async-start(f32[64,6,128]{2,1,0:T(8,128)} %copy.38), calls=%async_computation.1 | async-start | bytes 524288 | tf_op jit(solution)/shard_map/all_to_all | solution.py:28
  102.9 1.2 %copy-start.2 = (bf16[1,4,4,240,128]{4,3,2,1,0:T(8,128)(2,1)S(1)}, bf16[1,4,4,240,128]{4,3,2,1,0:T(8,128)(2,1)}, u32[]{:S(2)}) copy-start(bf16[1,4,4,240,128]{4,3,2,1,0:T(8,128)(2,1)} %param.4) | copy-start | bytes 2949124

commit v8 on v7

--- a/solution.py
+++ b/solution.py
@@ -29,13 +29,28 @@
     return jnp.sum(got, axis=0)
 
 
+def halving_sum(blocks, axis):
+    n = blocks.shape[0]
+    me = lax.axis_index(axis)
+    bit = 1
+    while bit < n:
+        mine = (me // bit) % 2
+        halves = blocks.reshape((-1, 2) + blocks.shape[1:])
+        keep = lax.dynamic_index_in_dim(halves, mine, axis=1, keepdims=False)
+        send = lax.dynamic_index_in_dim(halves, 1 - mine, axis=1, keepdims=False)
+        got = lax.ppermute(send, axis, [(i, i ^ bit) for i in range(n)])
+        blocks = keep + got
+        bit *= 2
+    return blocks[0]
+
+
 def staged_scatter(terms):
     n_dp, n_frame, n_row = (lax.axis_size(a) for a in ("dp", "frame", "row"))
     rows = terms.shape[0] // (n_dp * n_frame * n_row)
     chans = terms.shape[-1]
     blocks = terms.reshape(n_dp * n_frame, n_row, rows, chans)
     blocks = jnp.transpose(blocks, (1, 0, 2, 3))
-    blocks = a2a_sum(blocks, "row")
+    blocks = halving_sum(blocks, "row")
     return a2a_sum(blocks, ("dp", "frame"))
 
 

time: 116 us -> 113 us (0.974)
  starting transfers between devices: 45 us -> 38.2 us
  waiting for transfers between devices: 30.3 us -> 35.3 us
  matrix products: 11.4 us -> 13.5 us
  other arithmetic: 8.42 us -> 6.89 us
  local copies, waits for them, and re-layouts: 18.8 us -> 17.6 us
    ppermute x0 -> x2, waiting for transfers between devices: none -> 9.46 us  [halving_sum(): got = lax.ppermute(send, axis, [(i, i ^ bit) for i in range(n)])]
    all_to_all x2 -> x1, starting transfers between devices: 23.8 us -> 16.9 us  [a2a_sum(): got = lax.all_to_all(blocks, axis, split_axis=0, concat_axis=0, tiled=True)]
    all_to_all x2 -> x1, waiting for transfers between devices: 13.3 us -> 8.88 us  [a2a_sum(): got = lax.all_to_all(blocks, axis, split_axis=0, concat_axis=0, tiled=True)]
    dot_general x3, matrix products: 2.83 us -> 4.86 us  [on_device(): back = back + jnp.dot(piece, back_weight[i], preferred_element_type=f32)]
    transpose x1 -> x0, local copies, waits for them, and re-layouts: 1.34 us -> none  [staged_scatter(): blocks = jnp.transpose(blocks, (1, 0, 2, 3))]
    reduce_sum x2 -> x1, other arithmetic: 1.27 us -> 0.07 us  [a2a_sum(): return jnp.sum(got, axis=0)]
    concatenate x2, other arithmetic: 3.89 us -> 2.72 us  [width_taps(): return jnp.concatenate(parts, axis=-1)]
    unnamed x31 -> x33, local copies, waits for them, and re-layouts: 5.6 us -> 5.58 us
  transfers between devices with their start and end apart: 8 -> 9, of which waited for: 4 -> 4; matrix products, arithmetic and copies ran while one was open for 21% -> 21% of each run, Pallas kernels for 0% -> 0%
where the time goes in v8:
time: 113 us
  starting transfers between devices  38.2 us (34%)
  waiting for transfers between devices  35.3 us (31%)
  local copies, waits for them, and re-layouts  17.6 us (16%)
  matrix products  13.5 us (12%)
  other arithmetic  6.89 us (6%)
  between operations  1.19 us (1%)
    ppermute x2, waiting for transfers between devices, row_halo(): after = lax.ppermute(shard[:1], 'row', down)  16.9 us
    all_to_all x1, starting transfers between devices, a2a_sum(): got = lax.all_to_all(blocks, axis, split_axis=0, concat_axis=0, tiled=True)  16.9 us
    ppermute x2, starting transfers between devices, row_halo(): before = lax.ppermute(shard[-1:], 'row', up)  12.6 us
    ppermute x2, waiting for transfers between devices, halving_sum(): got = lax.ppermute(send, axis, [(i, i ^ bit) for i in range(n)])  9.46 us
    all_to_all x1, waiting for transfers between devices, a2a_sum(): got = lax.all_to_all(blocks, axis, split_axis=0, concat_axis=0, tiled=True)  8.88 us
    unnamed x33, local copies, waits for them, and re-layouts  5.58 us
    dot_general x3, matrix products, on_device(): back = back + jnp.dot(piece, back_weight[i], preferred_element_type=f32)  4.86 us
    ppermute x2, starting transfers between devices, frame_shift(): return lax.ppermute(piece, 'frame', pairs)  4.49 us
  transfers between devices with their start and end apart: 9, of which 4 were waited for; matrix products, arithmetic and copies ran while one was open for 21% of the time, Pallas kernels for 0%

profile of v8, /device:TPU:1, one launch (start us, length us, event | category | flops | bytes accessed | tf_op | source)
XLA Modules:
  0.0 112.7 jit_solution(16489394974816861853)
XLA Ops:
  0.7 1.4 %copy.33 = bf16[1,4,4,240,128]{4,3,1,2,0:T(8,128)(2,1)S(1)} copy(bf16[1,4,4,240,128]{4,3,2,1,0:T(8,128)(2,1)} %param.4) | data formatting | bytes 1966080 | tf_op args[0]
  2.8 10.2 %collective-permute-start = (bf16[1,4,240,128]{3,2,1,0:T(8,128)(2,1)}, bf16[1,4,240,128]{3,2,1,0:T(8,128)(2,1)S(1)}, u32[]{:S(2)}, u32[]{:S(2)}) collective-permute-start(bf16[1,4,240,128]{3,2,1,0:T(8,128)(2,1)} %get-tuple-element.25), channel_id=1, source_target_pairs={{0,1},{1,2},{2,3},{4,5},{5,6},{6,7},{8,9},{9,10},{10,11},{12,13},{... | collective-permute-start | bytes 737288 | tf_op jit(solution)/shard_map/ppermute | solution.py:13
  13.0 1.9 %collective-permute-start.1 = (bf16[1,4,240,128]{3,2,1,0:T(8,128)(2,1)}, bf16[1,4,240,128]{3,2,1,0:T(8,128)(2,1)S(1)}, u32[]{:S(2)}, u32[]{:S(2)}) collective-permute-start(bf16[1,4,240,128]{3,2,1,0:T(8,128)(2,1)} %get-tuple-element.26), channel_id=1, source_target_pairs={{1,0},{2,1},{3,2},{5,4},{6,5},{7,6},{9,8},{10,9},{11,10},{13,12},{... | collective-permute-start | bytes 737288 | tf_op jit(solution)/shard_map/ppermute | solution.py:14
  15.8 1.3 %collective-permute-start.3 = (bf16[4,2,240,128]{3,2,1,0:T(8,128)(2,1)}, bf16[4,2,240,128]{3,2,1,0:T(8,128)(2,1)S(1)}, u32[]{:S(2)}, u32[]{:S(2)}) collective-permute-start(bf16[4,2,240,128]{3,2,1,0:T(8,128)(2,1)} %slice.123), channel_id=1, source_target_pairs={{4,0},{8,4},{12,8},{16,12},{20,16},{24,20},{28,24},{32,28},{36,32}... | collective-permute-start | bytes 1474568 | tf_op jit(solution)/shard_map/ppermute | solution.py:24
  18.1 1.0 copy.14
  19.8 6.5 %collective-permute-done.1 = bf16[1,4,240,128]{3,2,1,0:T(8,128)(2,1)S(1)} collective-permute-done((bf16[1,4,240,128]{3,2,1,0:T(8,128)(2,1)}, bf16[1,4,240,128]{3,2,1,0:T(8,128)(2,1)S(1)}, u32[]{:S(2)}, u32[]{:S(2)}) %collective-permute-start.1) | collective-permute-done | bytes 245792 | tf_op jit(solution)/shard_map/ppermute | solution.py:14
  27.4 1.4 %fusion.6 = bf16[6,4,240,384]{3,2,1,0:T(8,128)(2,1)S(1)} fusion(bf16[6,4,239,128]{3,2,1,0:T(8,128)(2,1)S(1)} %get-tuple-element.20, bf16[6,4,239,128]{3,2,1,0:T(8,128)(2,1)S(1)} %get-tuple-element.19, bf16[1,4,240,128]{3,2,1,0:T(8,128)(2,1)S(1)} %collective-permute-done.1, bf16[4,4,240,128]{3,2,1,0:T(8,128)(2,1)S(1)} %bitcast.113, ...), kind=kLoop, calls=%fused_computation.15 | loop fusion | flops 30965760 | bytes 8835072 | tf_op jit(solution)/shard_map/concatenate | solution.py:62
  28.8 1.1 fusion.20
  30.8 0.9 convolution_add_fusion.4
  31.8 1.0 convolution_add_fusion.3
  33.3 0.9 convolution_convert_fusion
  35.2 1.0 convolution_bitcast_fusion
  36.2 1.0 convolution_bitcast_fusion.1
  37.2 3.2 %collective-permute-start.2 = (bf16[4,2,240,128]{3,2,1,0:T(8,128)(2,1)S(1)}, bf16[4,2,240,128]{3,2,1,0:T(8,128)(2,1)S(1)}, u32[]{:S(2)}, u32[]{:S(2)}) collective-permute-start(bf16[4,2,240,128]{3,2,1,0:T(8,128)(2,1)S(1)} %slice.120), channel_id=1, source_target_pairs={{0,4},{4,8},{8,12},{12,16},{16,20},{20,24},{24,28},{28,32},{32,36}... | collective-permute-start | bytes 1474568 | tf_op jit(solution)/shard_map/ppermute | solution.py:24
  40.4 2.4 %collective-permute-start.4 = (bf16[1,4,240,128]{3,2,1,0:T(8,128)(2,1)S(1)}, bf16[1,4,240,128]{3,2,1,0:T(8,128)(2,1)S(1)}, u32[]{:S(2)}, u32[]{:S(2)}) collective-permute-start(bf16[1,4,240,128]{3,2,1,0:T(8,128)(2,1)S(1)} %get-tuple-element.23), channel_id=1, source_target_pairs={{0,1},{1,2},{2,3},{4,5},{5,6},{6,7},{8,9},{9,10},{10,11},{12,13},{... | collective-permute-start | bytes 737288 | tf_op jit(solution)/shard_map/ppermute | solution.py:13
  42.9 2.1 %collective-permute-start.5 = (bf16[1,4,240,128]{3,2,1,0:T(8,128)(2,1)S(1)}, bf16[1,4,240,128]{3,2,1,0:T(8,128)(2,1)S(1)}, u32[]{:S(2)}, u32[]{:S(2)}) collective-permute-start(bf16[1,4,240,128]{3,2,1,0:T(8,128)(2,1)S(1)} %get-tuple-element.24), channel_id=1, source_target_pairs={{1,0},{2,1},{3,2},{5,4},{6,5},{7,6},{9,8},{10,9},{11,10},{13,12},{... | collective-permute-start | bytes 737288 | tf_op jit(solution)/shard_map/ppermute | solution.py:14
  45.0 1.0 convolution_bitcast_fusion.2
  46.0 10.4 %collective-permute-done.5 = bf16[1,4,240,128]{3,2,1,0:T(8,128)(2,1)S(1)} collective-permute-done((bf16[1,4,240,128]{3,2,1,0:T(8,128)(2,1)S(1)}, bf16[1,4,240,128]{3,2,1,0:T(8,128)(2,1)S(1)}, u32[]{:S(2)}, u32[]{:S(2)}) %collective-permute-start.5) | collective-permute-done | bytes 245792 | tf_op jit(solution)/shard_map/ppermute | solution.py:14
  57.4 1.4 %fusion.8 = bf16[6,4,240,384]{3,2,1,0:T(8,128)(2,1)S(1)} fusion(bf16[6,4,239,128]{3,2,1,0:T(8,128)(2,1)S(1)} %get-tuple-element.18, bf16[6,4,239,128]{3,2,1,0:T(8,128)(2,1)S(1)} %get-tuple-element.17, bf16[1,4,240,128]{3,2,1,0:T(8,128)(2,1)S(1)} %collective-permute-done.5, bf16[4,4,240,128]{3,2,1,0:T(8,128)(2,1)S(1)} %get-tuple-element.15, ...), kind=kLoop, calls=%fused_computation.17 | loop fusion | flops 30965760 | bytes 8835072 | tf_op jit(solution)/shard_map/concatenate | solution.py:62
  58.7 3.1 %fusion.19 = (bf16[4,4,240,384]{3,2,1,0:T(8,128)(2,1)}, bf16[4,4,240,384]{3,2,1,0:T(8,128)(2,1)}, bf16[4,4,240,384]{3,2,1,0:T(8,128)(2,1)S(1)}) fusion(bf16[6,4,240,384]{3,2,1,0:T(8,128)(2,1)S(1)} %fusion.8), kind=kLoop, calls=%fused_computation.53 | loop fusion | bytes 17694720 | tf_op jit(solution)/shard_map/slice | solution.py:124
  61.8 1.0 convolution_add_fusion.2
  63.3 1.6 %copy-done.1 = bf16[4,4,240,384]{3,2,1,0:T(8,128)(2,1)} copy-done((bf16[4,4,240,384]{3,2,1,0:T(8,128)(2,1)}, bf16[4,4,240,384]{3,2,1,0:T(8,128)(2,1)S(1)}, u32[]{:S(2)}) %copy-start.1) | copy-done | bytes 2949144
  64.9 1.0 convolution_bitcast_fusion.3
  66.0 1.1 reshape.98
  67.1 1.1 dynamic-slice_bitcast_fusion
  68.3 3.0 %convolution_add_fusion.1 = f32[3840,128]{1,0:T(8,128)S(1)} fusion(f32[3840,128]{1,0:T(8,128)S(1)} %convolution_add_fusion.2, bf16[3840,384]{1,0:T(8,128)(2,1)} %bitcast.105, bf16[384,128]{1,0:T(8,128)(2,1)S(1)} %bitcast.124), kind=kOutput, calls=%fused_computation.7 | convolution fusion | flops 377978880 | bytes 6979584 | tf_op jit(solution)/shard_map/dot_general | solution.py:125
  71.5 0.9 fusion.4
  72.5 1.0 copy.32
  73.5 9.5 %collective-permute-done.7 = f32[1,64,6,128]{3,2,0,1:T(8,128)S(1)} collective-permute-done((f32[1,64,6,128]{3,2,0,1:T(8,128)S(1)}, f32[1,64,6,128]{3,2,0,1:T(8,128)S(1)}, u32[]{:S(2)}, u32[]{:S(2)}) %collective-permute-start.7) | collective-permute-done | bytes 196640 | tf_op jit(solution)/shard_map/ppermute | solution.py:41
  83.7 16.9 %all-to-all-start = ((f32[64,6,128]{2,1,0:T(8,128)}), f32[64,6,128]{2,1,0:T(8,128)S(1)}, u32[]{:S(2)}, u32[]{:S(2)}) async-start(f32[64,6,128]{2,1,0:T(8,128)} %add_bitcast_fusion), calls=%async_computation | async-start | bytes 524288 | tf_op jit(solution)/shard_map/all_to_all | solution.py:28
  102.1 1.0 copy.17
  103.1 8.9 %all-to-all-done = f32[64,6,128]{2,1,0:T(8,128)S(1)} async-done(((f32[64,6,128]{2,1,0:T(8,128)}), f32[64,6,128]{2,1,0:T(8,128)S(1)}, u32[]{:S(2)}, u32[]{:S(2)}) %all-to-all-start) | async-done | bytes 196640 | tf_op jit(solution)/shard_map/all_to_all | solution.py:28
  (60 shorter events, 11.6 us)
Async XLA Ops:
  0.6 14.3 %copy-start.6 = (bf16[1,4,4,240,128]{4,3,2,1,0:T(8,128)(2,1)S(1)}, bf16[1,4,4,240,128]{4,3,2,1,0:T(8,128)(2,1)}, u32[]{:S(2)}) copy-start(bf16[1,4,4,240,128]{4,3,2,1,0:T(8,128)(2,1)} %param.5) | copy-start | bytes 2949124
  0.6 16.5 %copy-start.5 = (bf16[3,3,128,128]{3,2,1,0:T(8,128)(2,1)S(1)}, bf16[3,3,128,128]{3,2,1,0:T(8,128)(2,1)}, u32[]{:S(2)}) copy-start(bf16[3,3,128,128]{3,2,1,0:T(8,128)(2,1)} %param.6) | copy-start | bytes 884740
  2.8 17.0 %collective-permute-start = (bf16[1,4,240,128]{3,2,1,0:T(8,128)(2,1)}, bf16[1,4,240,128]{3,2,1,0:T(8,128)(2,1)S(1)}, u32[]{:S(2)}, u32[]{:S(2)}) collective-permute-start(bf16[1,4,240,128]{3,2,1,0:T(8,128)(2,1)} %get-tuple-element.25), channel_id=1, source_target_pairs={{0,1},{1,2},{2,3},{4,5},{5,6},{6,7},{8,9},{9,10},{10,11},{12,13},{... | collective-permute-start | bytes 737288 | tf_op jit(solution)/shard_map/ppermute | solution.py:13
  13.0 13.3 %collective-permute-start.1 = (bf16[1,4,240,128]{3,2,1,0:T(8,128)(2,1)}, bf16[1,4,240,128]{3,2,1,0:T(8,128)(2,1)S(1)}, u32[]{:S(2)}, u32[]{:S(2)}) collective-permute-start(bf16[1,4,240,128]{3,2,1,0:T(8,128)(2,1)} %get-tuple-element.26), channel_id=1, source_target_pairs={{1,0},{2,1},{3,2},{5,4},{6,5},{7,6},{9,8},{10,9},{11,10},{13,12},{... | collective-permute-start | bytes 737288 | tf_op jit(solution)/shard_map/ppermute | solution.py:14
  15.8 16.9 %collective-permute-start.3 = (bf16[4,2,240,128]{3,2,1,0:T(8,128)(2,1)}, bf16[4,2,240,128]{3,2,1,0:T(8,128)(2,1)S(1)}, u32[]{:S(2)}, u32[]{:S(2)}) collective-permute-start(bf16[4,2,240,128]{3,2,1,0:T(8,128)(2,1)} %slice.123), channel_id=1, source_target_pairs={{4,0},{8,4},{12,8},{16,12},{20,16},{24,20},{28,24},{32,28},{36,32}... | collective-permute-start | bytes 1474568 | tf_op jit(solution)/shard_map/ppermute | solution.py:24
  28.7 1.1 copy-start.13
  29.8 1.0 copy-start.10
  30.8 1.0 copy-start.9
  37.2 25.6 %collective-permute-start.2 = (bf16[4,2,240,128]{3,2,1,0:T(8,128)(2,1)S(1)}, bf16[4,2,240,128]{3,2,1,0:T(8,128)(2,1)S(1)}, u32[]{:S(2)}, u32[]{:S(2)}) collective-permute-start(bf16[4,2,240,128]{3,2,1,0:T(8,128)(2,1)S(1)} %slice.120), channel_id=1, source_target_pairs={{0,4},{4,8},{8,12},{12,16},{16,20},{20,24},{24,28},{28,32},{32,36}... | collective-permute-start | bytes 1474568 | tf_op jit(solution)/shard_map/ppermute | solution.py:24
  40.4 5.5 %collective-permute-start.4 = (bf16[1,4,240,128]{3,2,1,0:T(8,128)(2,1)S(1)}, bf16[1,4,240,128]{3,2,1,0:T(8,128)(2,1)S(1)}, u32[]{:S(2)}, u32[]{:S(2)}) collective-permute-start(bf16[1,4,240,128]{3,2,1,0:T(8,128)(2,1)S(1)} %get-tuple-element.23), channel_id=1, source_target_pairs={{0,1},{1,2},{2,3},{4,5},{5,6},{6,7},{8,9},{9,10},{10,11},{12,13},{... | collective-permute-start | bytes 737288 | tf_op jit(solution)/shard_map/ppermute | solution.py:13
  42.9 13.6 %collective-permute-start.5 = (bf16[1,4,240,128]{3,2,1,0:T(8,128)(2,1)S(1)}, bf16[1,4,240,128]{3,2,1,0:T(8,128)(2,1)S(1)}, u32[]{:S(2)}, u32[]{:S(2)}) collective-permute-start(bf16[1,4,240,128]{3,2,1,0:T(8,128)(2,1)S(1)} %get-tuple-element.24), channel_id=1, source_target_pairs={{1,0},{2,1},{3,2},{5,4},{6,5},{7,6},{9,8},{10,9},{11,10},{13,12},{... | collective-permute-start | bytes 737288 | tf_op jit(solution)/shard_map/ppermute | solution.py:14
  62.9 2.0 %copy-start.7 = (bf16[1,4,4,240,128]{4,3,2,1,0:T(8,128)(2,1)S(1)}, bf16[1,4,4,240,128]{4,3,2,1,0:T(8,128)(2,1)}, u32[]{:S(2)}) copy-start(bf16[1,4,4,240,128]{4,3,2,1,0:T(8,128)(2,1)} %param.5) | copy-start | bytes 2949124
  63.3 1.6 %copy-start.1 = (bf16[4,4,240,384]{3,2,1,0:T(8,128)(2,1)}, bf16[4,4,240,384]{3,2,1,0:T(8,128)(2,1)S(1)}, u32[]{:S(2)}) copy-start(bf16[4,4,240,384]{3,2,1,0:T(8,128)(2,1)S(1)} %fusion.10) | copy-start | bytes 8847364
  65.9 2.3 %copy-start.11 = (bf16[1,3,128,128]{3,2,1,0:T(8,128)(2,1)S(1)}, bf16[1,3,128,128]{3,2,1,0:T(8,128)(2,1)}, u32[]{:S(2)}) copy-start(bf16[1,3,128,128]{3,2,1,0:T(8,128)(2,1)} %get-tuple-element.28) | copy-start | bytes 294916
  68.1 3.1 %collective-permute-start.6 = (f32[2,64,6,128]{3,2,0,1:T(8,128)S(1)}, f32[2,64,6,128]{3,2,0,1:T(8,128)S(1)}, u32[]{:S(2)}, u32[]{:S(2)}) collective-permute-start(f32[2,64,6,128]{3,2,0,1:T(8,128)S(1)} %dynamic-slice_bitcast_fusion), channel_id=1, source_target_pairs={{0,1},{1,0},{2,3},{3,2},{4,5},{5,4},{6,7},{7,6},{8,9},{9,8},{10,11... | collective-permute-start | bytes 1179656 | tf_op jit(solution)/shard_map/ppermute | solution.py:41
  68.2 3.0 %copy-start.3 = (f32[64,4,6,128]{3,2,1,0:T(8,128)S(1)}, f32[64,4,6,128]{3,2,1,0:T(8,128)}, u32[]{:S(2)}) copy-start(f32[64,4,6,128]{3,2,1,0:T(8,128)} %reshape.98) | copy-start | bytes 2359300
  68.3 3.2 %copy-start = (bf16[4,4,240,384]{3,2,1,0:T(8,128)(2,1)S(1)}, bf16[4,4,240,384]{3,2,1,0:T(8,128)(2,1)}, u32[]{:S(2)}) copy-start(bf16[4,4,240,384]{3,2,1,0:T(8,128)(2,1)} %get-tuple-element.9) | copy-start | bytes 8847364
  68.3 3.2 %copy-start.8 = (bf16[1,3,128,128]{3,2,1,0:T(8,128)(2,1)S(1)}, bf16[1,3,128,128]{3,2,1,0:T(8,128)(2,1)}, u32[]{:S(2)}) copy-start(bf16[1,3,128,128]{3,2,1,0:T(8,128)(2,1)} %get-tuple-element.27) | copy-start | bytes 294916
  71.4 11.6 %collective-permute-start.7 = (f32[1,64,6,128]{3,2,0,1:T(8,128)S(1)}, f32[1,64,6,128]{3,2,0,1:T(8,128)S(1)}, u32[]{:S(2)}, u32[]{:S(2)}) collective-permute-start(f32[1,64,6,128]{3,2,0,1:T(8,128)S(1)} %constant_dynamic-slice_fusion), channel_id=1, source_target_pairs={{0,2},{1,3},{2,0},{3,1},{4,6},{5,7},{6,4},{7,5},{8,10},{9,11},{10,... | collective-permute-start | bytes 589832 | tf_op jit(solution)/shard_map/ppermute | solution.py:41
  72.5 28.2 %copy-start.2 = (bf16[4,4,240,384]{3,2,1,0:T(8,128)(2,1)S(1)}, bf16[4,4,240,384]{3,2,1,0:T(8,128)(2,1)}, u32[]{:S(2)}) copy-start(bf16[4,4,240,384]{3,2,1,0:T(8,128)(2,1)} %copy-done.1) | copy-start | bytes 8847364
  72.5 28.2 %copy-start.12 = (bf16[3,128,128]{2,1,0:T(8,128)(2,1)S(1)}, bf16[3,128,128]{2,1,0:T(8,128)(2,1)}, u32[]{:S(2)}) copy-start(bf16[3,128,128]{2,1,0:T(8,128)(2,1)} %param.7) | copy-start | bytes 294916
  83.7 28.3 %all-to-all-start = ((f32[64,6,128]{2,1,0:T(8,128)}), f32[64,6,128]{2,1,0:T(8,128)S(1)}, u32[]{:S(2)}, u32[]{:S(2)}) async-start(f32[64,6,128]{2,1,0:T(8,128)} %add_bitcast_fusion), calls=%async_computation | async-start | bytes 524288 | tf_op jit(solution)/shard_map/all_to_all | solution.py:28
  100.6 1.2 %copy-start.4 = (bf16[1,4,4,240,128]{4,3,2,1,0:T(8,128)(2,1)S(1)}, bf16[1,4,4,240,128]{4,3,2,1,0:T(8,128)(2,1)}, u32[]{:S(2)}) copy-start(bf16[1,4,4,240,128]{4,3,2,1,0:T(8,128)(2,1)} %param.4) | copy-start | bytes 2949124

commit v9 on v8

--- a/solution.py
+++ b/solution.py
@@ -4,15 +4,6 @@
 import jax.numpy as jnp
 from jax import lax
 from jax.sharding import PartitionSpec as P
-
-
-def row_halo(shard):
-    peers = lax.axis_size("row")
-    up = [(i, i + 1) for i in range(peers - 1)]
-    down = [(i + 1, i) for i in range(peers - 1)]
-    before = lax.ppermute(shard[-1:], "row", up)
-    after = lax.ppermute(shard[:1], "row", down)
-    return jnp.concatenate([before, shard, after], axis=0)
 
 
 def frame_shift(piece, forward):
@@ -81,19 +72,30 @@
     f32 = jnp.float32
     bf16 = jnp.bfloat16
 
-    x_ext = row_halo(x)
-    g_next = frame_shift(g[:, :2], forward=False)
-    x3 = width_taps(x_ext, reverse=False)
+    peers = lax.axis_size("row")
+    above = lax.ppermute(
+        jnp.concatenate([x[rows - 2 :], g[rows - 1 :]], axis=0), "row",
+        [(i, i + 1) for i in range(peers - 1)],
+    )
+    below = lax.ppermute(
+        jnp.concatenate([x[:2], g[:1]], axis=0), "row", [(i + 1, i) for i in range(peers - 1)]
+    )
+    x_e = jnp.concatenate([above[:2], x, below[:2]], axis=0)
+    g_e = jnp.concatenate([above[2:], g, below[2:]], axis=0)
+    g_next = frame_shift(g_e[:, :2], forward=False)
+
+    x3 = width_taps(x_e, reverse=False)
     fwd_weight = spatial_weight.reshape(3, 3 * chans, chans)
-    pre = jnp.zeros((rows * frames * cols, chans), f32)
+    wide = (rows + 2, frames, cols, chans)
+    pre = jnp.zeros((math.prod(wide[:-1]), chans), f32)
     for i in range(3):
-        piece = x3[i : i + rows].reshape(-1, 3 * chans)
+        piece = x3[i : i + rows + 2].reshape(-1, 3 * chans)
         pre = pre + jnp.dot(piece, fwd_weight[i], preferred_element_type=f32)
-    pre = pre.reshape(x.shape)
-    act = jax.nn.silu(pre).astype(bf16)
+    pre = pre.reshape(wide)
+    act = jax.nn.silu(pre[1 : rows + 1]).astype(bf16)
     act_prev = frame_shift(act[:, frames - 2 :], forward=True)
     act3 = frame_taps(jnp.concatenate([act_prev, act], axis=1), frames, later=False)
-    g3 = frame_taps(jnp.concatenate([g, g_next], axis=1), frames, later=True)
+    g3 = frame_taps(jnp.concatenate([g_e, g_next], axis=1), frames, later=True)
     act3_flat = act3.reshape(-1, 3 * chans)
     g_flat = g.reshape(-1, chans)
 
@@ -104,20 +106,20 @@
         act3_flat, g_flat, (((0,), (0,)), ((), ())), preferred_element_type=f32
     )
     mixed = mixed.astype(bf16).reshape(x.shape)
-    act_grad = act_grad.astype(bf16).reshape(x.shape)
+    act_grad = act_grad.astype(bf16).reshape(wide)
     block_output = (x.astype(f32) + mixed.astype(f32)).astype(bf16)
 
     sigma = jax.nn.sigmoid(pre)
-    pre_grad = (act_grad.astype(f32) * sigma * (1.0 + pre * (1.0 - sigma))).astype(bf16)
-    pg_flat = pre_grad.reshape(-1, chans)
+    pg_ext = (act_grad.astype(f32) * sigma * (1.0 + pre * (1.0 - sigma))).astype(bf16)
+    pg_flat = pg_ext[1 : rows + 1].reshape(-1, chans)
 
     spatial_list = []
     for i in range(3):
-        piece = x3[i : i + rows].reshape(-1, 3 * chans)
+        piece = x3[1 + i : 1 + i + rows].reshape(-1, 3 * chans)
         spatial_list.append(
             lax.dot_general(piece, pg_flat, (((0,), (0,)), ((), ())), preferred_element_type=f32)
         )
-    pg3 = width_taps(row_halo(pre_grad), reverse=True)
+    pg3 = width_taps(pg_ext, reverse=True)
     back_weight = jnp.transpose(spatial_weight, (0, 1, 3, 2)).reshape(3, 3 * chans, chans)
     back = g.astype(f32).reshape(-1, chans)
     for i in range(3):

time: 113 us -> 130 us (1.15)
  waiting for transfers between devices: 35.3 us -> 49.5 us
  starting transfers between devices: 38.2 us -> 28.7 us
  local copies, waits for them, and re-layouts: 17.6 us -> 24.9 us
  other arithmetic: 6.89 us -> 9.88 us
  matrix products: 13.5 us -> 15.2 us
    all_to_all x1, starting transfers between devices: 16.9 us -> 10.2 us  [a2a_sum(): got = lax.all_to_all(blocks, axis, split_axis=0, concat_axis=0, tiled=True)]
    ppermute x2, waiting for transfers between devices: 0.01 us -> 6.49 us  [frame_shift(): return lax.ppermute(piece, 'frame', pairs)]
    ppermute x2, waiting for transfers between devices: 9.46 us -> 15.2 us  [halving_sum(): got = lax.ppermute(send, axis, [(i, i ^ bit) for i in range(n)])]
    ppermute x4 -> x2, waiting for transfers between devices: 17 us -> 21.7 us  [the longest x1 14.4 us: on_device(): lax.ppermute(jnp.concatenate([x[:2], g[:1]], axis=0), 'row', [(i + 1, i)...]
    ppermute x4 -> x2, starting transfers between devices: 16.6 us -> 12.1 us  [the longest x1 10.2 us: on_device(): lax.ppermute(jnp.concatenate([x[rows - 2:], g[rows - 1:]], axis=0), 'row'...]
    unnamed x33 -> x35, local copies, waits for them, and re-layouts: 5.58 us -> 9.37 us
    all_to_all x1, waiting for transfers between devices: 8.88 us -> 6.11 us  [a2a_sum(): got = lax.all_to_all(blocks, axis, split_axis=0, concat_axis=0, tiled=True)]
    slice x4 -> x9, local copies, waits for them, and re-layouts: 2.7 us -> 4.24 us  [the longest x2 1.92 us: on_device(): g_e = jnp.concatenate([above[2:], g, below[2:]], axis=0)]
  transfers between devices with their start and end apart: 9 -> 7, of which waited for: 4 -> 5; matrix products, arithmetic and copies ran while one was open for 21% -> 17% of each run, Pallas kernels for 0% -> 0%
where the time goes in v9:
time: 130 us; the launch traced here: 129 us
  waiting for transfers between devices  49.5 us (38%)
  starting transfers between devices  28.7 us (22%)
  local copies, waits for them, and re-layouts  24.9 us (19%)
  matrix products  15.2 us (12%)
  other arithmetic  9.88 us (8%)
    ppermute x2, waiting for transfers between devices, halving_sum(): got = lax.ppermute(send, axis, [(i, i ^ bit) for i in range(n)])  15.2 us
    ppermute x1, waiting for transfers between devices, on_device(): lax.ppermute(jnp.concatenate([x[:2], g[:1]], axis=0), 'row', [(i + 1, i)...  14.4 us
    all_to_all x1, starting transfers between devices, a2a_sum(): got = lax.all_to_all(blocks, axis, split_axis=0, concat_axis=0, tiled=True)  10.2 us
    ppermute x1, starting transfers between devices, on_device(): lax.ppermute(jnp.concatenate([x[rows - 2:], g[rows - 1:]], axis=0), 'row'...  10.2 us
    unnamed x35, local copies, waits for them, and re-layouts  9.37 us
    ppermute x1, waiting for transfers between devices, on_device(): lax.ppermute(jnp.concatenate([x[rows - 2:], g[rows - 1:]], axis=0), 'row'...  7.33 us
    ppermute x2, waiting for transfers between devices, frame_shift(): return lax.ppermute(piece, 'frame', pairs)  6.49 us
    all_to_all x1, waiting for transfers between devices, a2a_sum(): got = lax.all_to_all(blocks, axis, split_axis=0, concat_axis=0, tiled=True)  6.11 us
  transfers between devices with their start and end apart: 7, of which 5 were waited for; matrix products, arithmetic and copies ran while one was open for 17% of the time, Pallas kernels for 0%

profile of v9, /device:TPU:1, one launch (start us, length us, event | category | flops | bytes accessed | tf_op | source)
XLA Modules:
  0.0 129.3 jit_solution(886257194763426301)
XLA Ops:
  0.6 1.4 %copy.33 = bf16[1,4,4,240,128]{4,3,1,2,0:T(8,128)(2,1)S(1)} copy(bf16[1,4,4,240,128]{4,3,2,1,0:T(8,128)(2,1)} %param.5) | data formatting | bytes 1966080 | tf_op args[1]
  2.4 10.2 %collective-permute-start = (bf16[3,4,240,128]{3,2,1,0:T(8,128)(2,1)S(1)}, bf16[3,4,240,128]{3,2,1,0:T(8,128)(2,1)S(1)}, u32[]{:S(2)}, u32[]{:S(2)}) collective-permute-start(bf16[3,4,240,128]{3,2,1,0:T(8,128)(2,1)S(1)} %pad_maximum_fusion.7), channel_id=1, source_target_pairs={{0,1},{1,2},{2,3},{4,5},{5,6},{6,7},{8,9},{9,10},{10,11},{12,13},{... | collective-permute-start | bytes 2211848 | tf_op jit(solution)/shard_map/ppermute | solution.py:76
  12.6 1.9 %collective-permute-start.1 = (bf16[3,4,240,128]{3,2,1,0:T(8,128)(2,1)S(1)}, bf16[3,4,240,128]{3,2,1,0:T(8,128)(2,1)S(1)}, u32[]{:S(2)}, u32[]{:S(2)}) collective-permute-start(bf16[3,4,240,128]{3,2,1,0:T(8,128)(2,1)S(1)} %pad_maximum_fusion.8), channel_id=1, source_target_pairs={{1,0},{2,1},{3,2},{5,4},{6,5},{7,6},{9,8},{10,9},{11,10},{13,12},{... | collective-permute-start | bytes 2211848 | tf_op jit(solution)/shard_map/ppermute | solution.py:80
  14.6 7.3 %collective-permute-done = bf16[3,4,240,128]{3,2,1,0:T(8,128)(2,1)S(1)} collective-permute-done((bf16[3,4,240,128]{3,2,1,0:T(8,128)(2,1)S(1)}, bf16[3,4,240,128]{3,2,1,0:T(8,128)(2,1)S(1)}, u32[]{:S(2)}, u32[]{:S(2)}) %collective-permute-start) | collective-permute-done | bytes 737312 | tf_op jit(solution)/shard_map/ppermute | solution.py:76
  22.0 14.4 %collective-permute-done.1 = bf16[3,4,240,128]{3,2,1,0:T(8,128)(2,1)S(1)} collective-permute-done((bf16[3,4,240,128]{3,2,1,0:T(8,128)(2,1)S(1)}, bf16[3,4,240,128]{3,2,1,0:T(8,128)(2,1)S(1)}, u32[]{:S(2)}, u32[]{:S(2)}) %collective-permute-start.1) | collective-permute-done | bytes 737312 | tf_op jit(solution)/shard_map/ppermute | solution.py:80
  37.5 1.1 fusion.23
  38.6 1.2 fusion.4
  39.9 1.6 %fusion.20 = (bf16[6,4,240,384]{3,2,1,0:T(8,128)(2,1)S(1)}, bf16[6,4,240,384]{3,2,1,0:T(8,128)(2,1)S(1)}, bf16[6,4,240,384]{3,2,1,0:T(8,128)(2,1)S(1)}) fusion(bf16[8,4,240,384]{3,2,1,0:T(8,128)(2,1)S(1)} %fusion.4), kind=kLoop, calls=%fused_computation.57 | loop fusion | bytes 26542080 | tf_op jit(solution)/shard_map/slice | solution.py:92
  42.4 1.3 %fusion.30 = f32[5760,128]{1,0:T(8,128)S(1)} fusion(bf16[5760,384]{1,0:T(8,128)(2,1)S(1)} %bitcast.108, bf16[384,128]{1,0:T(8,128)(2,1)S(1)} %bitcast.128), kind=kOutput, calls=%fused_computation.67 | convolution fusion | flops 566231040 | bytes 7471104 | tf_op jit(solution)/shard_map/dot_general | solution.py:93
  43.7 1.4 %convolution_add_fusion.1 = f32[5760,128]{1,0:T(8,128)S(1)} fusion(f32[5760,128]{1,0:T(8,128)S(1)} %fusion.30, bf16[5760,384]{1,0:T(8,128)(2,1)S(1)} %bitcast.105, bf16[384,128]{1,0:T(8,128)(2,1)S(1)} %bitcast.127), kind=kOutput, calls=%fused_computation.9 | convolution fusion | flops 566968320 | bytes 10420224 | tf_op jit(solution)/shard_map/dot_general | solution.py:93
  45.1 1.4 %convolution_add_fusion = f32[5760,128]{1,0:T(8,128)S(1)} fusion(f32[5760,128]{1,0:T(8,128)S(1)} %convolution_add_fusion.1, bf16[5760,384]{1,0:T(8,128)(2,1)S(1)} %bitcast.104, bf16[384,128]{1,0:T(8,128)(2,1)S(1)} %bitcast.126), kind=kOutput, calls=%fused_computation.8 | convolution fusion | flops 566968320 | bytes 10420224 | tf_op jit(solution)/shard_map/dot_general | solution.py:93
  49.0 3.2 %collective-permute-start.2 = (bf16[4,2,240,128]{3,2,1,0:T(8,128)(2,1)}, bf16[4,2,240,128]{3,2,1,0:T(8,128)(2,1)S(1)}, u32[]{:S(2)}, u32[]{:S(2)}) collective-permute-start(bf16[4,2,240,128]{3,2,1,0:T(8,128)(2,1)} %slice.162), channel_id=1, source_target_pairs={{0,4},{4,8},{8,12},{12,16},{16,20},{20,24},{24,28},{28,32},{32,36}... | collective-permute-start | bytes 1474568 | tf_op jit(solution)/shard_map/ppermute | solution.py:15
  52.2 1.9 %copy.14 = bf16[3,3,128,128]{2,3,1,0:T(8,128)(2,1)} copy(bf16[3,3,128,128]{3,2,1,0:T(8,128)(2,1)} %param.6) | data formatting | bytes 589824 | tf_op args[2]
  54.1 1.0 copy.13
  55.1 1.7 %fusion.28 = (bf16[1,3,128,128]{3,2,1,0:T(8,128)(2,1)}, bf16[1,3,128,128]{3,2,1,0:T(8,128)(2,1)}, bf16[1,3,128,128]{3,2,1,0:T(8,128)(2,1)}) fusion(bf16[3,3,128,128]{3,2,1,0:T(8,128)(2,1)} %bitcast.121), kind=kLoop, calls=%fused_computation.65 | loop fusion | bytes 589824 | tf_op jit(solution)/shard_map/slice | solution.py:127
  58.9 1.5 %collective-permute-start.3 = (bf16[6,2,240,128]{3,2,1,0:T(8,128)(2,1)S(1)}, bf16[6,2,240,128]{3,2,1,0:T(8,128)(2,1)S(1)}, u32[]{:S(2)}, u32[]{:S(2)}) collective-permute-start(bf16[6,2,240,128]{3,2,1,0:T(8,128)(2,1)S(1)} %pad_maximum_fusion.5), channel_id=1, source_target_pairs={{4,0},{8,4},{12,8},{16,12},{20,16},{24,20},{28,24},{32,28},{36,32}... | collective-permute-start | bytes 2211848 | tf_op jit(solution)/shard_map/ppermute | solution.py:15
  62.6 1.0 copy.16
  64.6 6.5 %collective-permute-done.3 = bf16[6,2,240,128]{3,2,1,0:T(8,128)(2,1)S(1)} collective-permute-done((bf16[6,2,240,128]{3,2,1,0:T(8,128)(2,1)S(1)}, bf16[6,2,240,128]{3,2,1,0:T(8,128)(2,1)S(1)}, u32[]{:S(2)}, u32[]{:S(2)}) %collective-permute-start.3) | collective-permute-done | bytes 737312 | tf_op jit(solution)/shard_map/ppermute | solution.py:15
  72.5 1.3 %convolution_convert_fusion = bf16[5760,128]{1,0:T(8,128)(2,1)S(1)} fusion(bf16[5760,384]{1,0:T(8,128)(2,1)S(1)} %bitcast.107, bf16[384,128]{1,0:T(8,128)(2,1)S(1)} %bitcast.129), kind=kOutput, calls=%fused_computation.10 | convolution fusion | flops 566968320 | bytes 5996544 | tf_op jit(solution)/shard_map/dot_general | solution.py:104
  74.7 1.1 fusion.11
  75.9 1.0 convolution_bitcast_fusion
  76.9 1.0 convolution_bitcast_fusion.1
  78.9 2.3 %fusion.24 = (bf16[6,4,239,128]{3,2,1,0:T(8,128)(2,1)}, bf16[6,4,239,128]{3,2,1,0:T(8,128)(2,1)}) fusion(bf16[6,4,240,128]{3,2,1,0:T(8,128)(2,1)S(1)} %fusion.11), kind=kLoop, calls=%fused_computation.61 | loop fusion | bytes 5873664 | tf_op jit(solution)/shard_map/slice | solution.py:51
  82.1 1.2 reshape.99
  83.5 2.3 %fusion.7 = bf16[6,4,240,384]{3,2,1,0:T(8,128)(2,1)S(1)} fusion(bf16[6,4,239,128]{3,2,1,0:T(8,128)(2,1)} %get-tuple-element.20, bf16[6,4,239,128]{3,2,1,0:T(8,128)(2,1)} %get-tuple-element.19, bf16[6,4,240,128]{3,2,1,0:T(8,128)(2,1)S(1)} %fusion.11), kind=kLoop, calls=%fused_computation.18 | loop fusion | flops 22118400 | bytes 8835072 | tf_op jit(solution)/shard_map/concatenate | solution.py:53
  85.8 3.0 %fusion.21 = (bf16[4,4,240,384]{3,2,1,0:T(8,128)(2,1)}, bf16[4,4,240,384]{3,2,1,0:T(8,128)(2,1)}, bf16[4,4,240,384]{3,2,1,0:T(8,128)(2,1)S(1)}) fusion(bf16[6,4,240,384]{3,2,1,0:T(8,128)(2,1)S(1)} %fusion.7), kind=kLoop, calls=%fused_computation.58 | loop fusion | bytes 17694720 | tf_op jit(solution)/shard_map/slice | solution.py:126
  88.9 1.6 %collective-permute-start.5 = (f32[1,64,6,128]{3,2,0,1:T(8,128)S(1)}, f32[1,64,6,128]{3,2,0,1:T(8,128)S(1)}, u32[]{:S(2)}, u32[]{:S(2)}) collective-permute-start(f32[1,64,6,128]{3,2,0,1:T(8,128)S(1)} %constant_dynamic-slice_fusion), channel_id=1, source_target_pairs={{0,2},{1,3},{2,0},{3,1},{4,6},{5,7},{6,4},{7,5},{8,10},{9,11},{10,... | collective-permute-start | bytes 589832 | tf_op jit(solution)/shard_map/ppermute | solution.py:32
  91.4 15.2 %collective-permute-done.5 = f32[1,64,6,128]{3,2,0,1:T(8,128)S(1)} collective-permute-done((f32[1,64,6,128]{3,2,0,1:T(8,128)S(1)}, f32[1,64,6,128]{3,2,0,1:T(8,128)S(1)}, u32[]{:S(2)}, u32[]{:S(2)}) %collective-permute-start.5) | collective-permute-done | bytes 196640 | tf_op jit(solution)/shard_map/ppermute | solution.py:32
  107.3 10.2 %all-to-all-start = ((f32[64,6,128]{2,1,0:T(8,128)}), f32[64,6,128]{2,1,0:T(8,128)S(1)}, u32[]{:S(2)}, u32[]{:S(2)}) async-start(f32[64,6,128]{2,1,0:T(8,128)} %add_bitcast_fusion), calls=%async_computation | async-start | bytes 524288 | tf_op jit(solution)/shard_map/all_to_all | solution.py:19
  117.6 3.0 %convolution_add_fusion.3 = f32[3840,128]{1,0:T(8,128)S(1)} fusion(f32[3840,128]{1,0:T(8,128)S(1)} %convolution_add_fusion.4, bf16[3840,384]{1,0:T(8,128)(2,1)} %bitcast.110, bf16[384,128]{1,0:T(8,128)(2,1)S(1)} %bitcast.124), kind=kOutput, calls=%fused_computation.14 | convolution fusion | flops 377978880 | bytes 6979584 | tf_op jit(solution)/shard_map/dot_general | solution.py:127
  121.6 1.0 copy.31
  122.6 6.1 %all-to-all-done = f32[64,6,128]{2,1,0:T(8,128)S(1)} async-done(((f32[64,6,128]{2,1,0:T(8,128)}), f32[64,6,128]{2,1,0:T(8,128)S(1)}, u32[]{:S(2)}, u32[]{:S(2)}) %all-to-all-start) | async-done | bytes 196640 | tf_op jit(solution)/shard_map/all_to_all | solution.py:19
  (67 shorter events, 17.9 us)
Async XLA Ops:
  0.6 1.5 %copy-start.4 = (bf16[1,4,4,240,128]{4,3,2,1,0:T(8,128)(2,1)S(1)}, bf16[1,4,4,240,128]{4,3,2,1,0:T(8,128)(2,1)}, u32[]{:S(2)}) copy-start(bf16[1,4,4,240,128]{4,3,2,1,0:T(8,128)(2,1)} %param.4) | copy-start | bytes 2949124
  2.2 12.4 %copy-start.5 = (bf16[3,3,128,128]{3,2,1,0:T(8,128)(2,1)S(1)}, bf16[3,3,128,128]{3,2,1,0:T(8,128)(2,1)}, u32[]{:S(2)}) copy-start(bf16[3,3,128,128]{3,2,1,0:T(8,128)(2,1)} %param.6) | copy-start | bytes 884740
  2.4 19.6 %collective-permute-start = (bf16[3,4,240,128]{3,2,1,0:T(8,128)(2,1)S(1)}, bf16[3,4,240,128]{3,2,1,0:T(8,128)(2,1)S(1)}, u32[]{:S(2)}, u32[]{:S(2)}) collective-permute-start(bf16[3,4,240,128]{3,2,1,0:T(8,128)(2,1)S(1)} %pad_maximum_fusion.7), channel_id=1, source_target_pairs={{0,1},{1,2},{2,3},{4,5},{5,6},{6,7},{8,9},{9,10},{10,11},{12,13},{... | collective-permute-start | bytes 2211848 | tf_op jit(solution)/shard_map/ppermute | solution.py:76
  12.6 23.7 %collective-permute-start.1 = (bf16[3,4,240,128]{3,2,1,0:T(8,128)(2,1)S(1)}, bf16[3,4,240,128]{3,2,1,0:T(8,128)(2,1)S(1)}, u32[]{:S(2)}, u32[]{:S(2)}) collective-permute-start(bf16[3,4,240,128]{3,2,1,0:T(8,128)(2,1)S(1)} %pad_maximum_fusion.8), channel_id=1, source_target_pairs={{1,0},{2,1},{3,2},{5,4},{6,5},{7,6},{9,8},{10,9},{11,10},{13,12},{... | collective-permute-start | bytes 2211848 | tf_op jit(solution)/shard_map/ppermute | solution.py:80
  21.9 14.4 %copy-start.7 = (bf16[3,4,240,128]{3,2,1,0:T(8,128)(2,1)}, bf16[3,4,240,128]{3,2,1,0:T(8,128)(2,1)S(1)}, u32[]{:S(2)}) copy-start(bf16[3,4,240,128]{3,2,1,0:T(8,128)(2,1)S(1)} %collective-permute-done) | copy-start | bytes 2211844
  36.3 0.9 copy-start.8
  39.9 2.5 %copy-start = (bf16[8,4,240,384]{3,2,1,0:T(8,128)(2,1)}, bf16[8,4,240,384]{3,2,1,0:T(8,128)(2,1)S(1)}, u32[]{:S(2)}) copy-start(bf16[8,4,240,384]{3,2,1,0:T(8,128)(2,1)S(1)} %fusion.4) | copy-start | bytes 17694724
  46.5 1.6 %copy-start.1 = (f32[5760,128]{1,0:T(8,128)}, f32[5760,128]{1,0:T(8,128)S(1)}, u32[]{:S(2)}) copy-start(f32[5760,128]{1,0:T(8,128)S(1)} %convolution_add_fusion) | copy-start | bytes 8847364
  49.0 11.4 %collective-permute-start.2 = (bf16[4,2,240,128]{3,2,1,0:T(8,128)(2,1)}, bf16[4,2,240,128]{3,2,1,0:T(8,128)(2,1)S(1)}, u32[]{:S(2)}, u32[]{:S(2)}) collective-permute-start(bf16[4,2,240,128]{3,2,1,0:T(8,128)(2,1)} %slice.162), channel_id=1, source_target_pairs={{0,4},{4,8},{8,12},{12,16},{16,20},{20,24},{24,28},{28,32},{32,36}... | collective-permute-start | bytes 1474568 | tf_op jit(solution)/shard_map/ppermute | solution.py:15
  58.9 12.2 %collective-permute-start.3 = (bf16[6,2,240,128]{3,2,1,0:T(8,128)(2,1)S(1)}, bf16[6,2,240,128]{3,2,1,0:T(8,128)(2,1)S(1)}, u32[]{:S(2)}, u32[]{:S(2)}) collective-permute-start(bf16[6,2,240,128]{3,2,1,0:T(8,128)(2,1)S(1)} %pad_maximum_fusion.5), channel_id=1, source_target_pairs={{4,0},{8,4},{12,8},{16,12},{20,16},{24,20},{28,24},{32,28},{36,32}... | collective-permute-start | bytes 2211848 | tf_op jit(solution)/shard_map/ppermute | solution.py:15
  60.4 0.9 copy-start.12
  62.3 1.3 %copy-start.6 = (bf16[1,4,4,240,128]{4,3,2,1,0:T(8,128)(2,1)S(1)}, bf16[1,4,4,240,128]{4,3,2,1,0:T(8,128)(2,1)}, u32[]{:S(2)}) copy-start(bf16[1,4,4,240,128]{4,3,2,1,0:T(8,128)(2,1)} %param.5) | copy-start | bytes 2949124
  71.8 4.1 %slice-start = ((s8[5898240]{0:T(1024)(128)(4,1)}), s8[4194304]{0:T(1024)(128)(4,1)S(1)}, s32[]{:S(2)}) async-start(s8[5898240]{0:T(1024)(128)(4,1)} %bitcast.96), calls=%async_computation.1 | async-start | bytes 8388608
  72.5 2.2 %copy-start.2 = (f32[5760,128]{1,0:T(8,128)S(1)}, f32[5760,128]{1,0:T(8,128)}, u32[]{:S(2)}) copy-start(f32[5760,128]{1,0:T(8,128)} %copy-done.1) | copy-start | bytes 8847364
  72.5 3.3 %slice-start.1 = ((s8[5898240]{0:T(1024)(128)(4,1)}), s8[1703936]{0:T(1024)(128)(4,1)S(1)}, s32[]{:S(2)}) async-start(s8[5898240]{0:T(1024)(128)(4,1)} %bitcast.96), calls=%async_computation.2 | async-start | bytes 3407872
  83.4 5.4 %collective-permute-start.4 = (f32[2,64,6,128]{3,2,0,1:T(8,128)S(1)}, f32[2,64,6,128]{3,2,0,1:T(8,128)S(1)}, u32[]{:S(2)}, u32[]{:S(2)}) collective-permute-start(f32[2,64,6,128]{3,2,0,1:T(8,128)S(1)} %dynamic-slice_bitcast_fusion), channel_id=1, source_target_pairs={{0,1},{1,0},{2,3},{3,2},{4,5},{5,4},{6,7},{7,6},{8,9},{9,8},{10,11... | collective-permute-start | bytes 1179656 | tf_op jit(solution)/shard_map/ppermute | solution.py:32
  85.8 4.7 %copy-start.11 = (bf16[1,3,128,128]{3,2,1,0:T(8,128)(2,1)S(1)}, bf16[1,3,128,128]{3,2,1,0:T(8,128)(2,1)}, u32[]{:S(2)}) copy-start(bf16[1,3,128,128]{3,2,1,0:T(8,128)(2,1)} %get-tuple-element.29) | copy-start | bytes 294916
  88.9 17.7 %collective-permute-start.5 = (f32[1,64,6,128]{3,2,0,1:T(8,128)S(1)}, f32[1,64,6,128]{3,2,0,1:T(8,128)S(1)}, u32[]{:S(2)}, u32[]{:S(2)}) collective-permute-start(f32[1,64,6,128]{3,2,0,1:T(8,128)S(1)} %constant_dynamic-slice_fusion), channel_id=1, source_target_pairs={{0,2},{1,3},{2,0},{3,1},{4,6},{5,7},{6,4},{7,5},{8,10},{9,11},{10,... | collective-permute-start | bytes 589832 | tf_op jit(solution)/shard_map/ppermute | solution.py:32
  90.5 27.1 %copy-start.10 = (bf16[1,3,128,128]{3,2,1,0:T(8,128)(2,1)S(1)}, bf16[1,3,128,128]{3,2,1,0:T(8,128)(2,1)}, u32[]{:S(2)}) copy-start(bf16[1,3,128,128]{3,2,1,0:T(8,128)(2,1)} %get-tuple-element.28) | copy-start | bytes 294916
  107.3 21.3 %all-to-all-start = ((f32[64,6,128]{2,1,0:T(8,128)}), f32[64,6,128]{2,1,0:T(8,128)S(1)}, u32[]{:S(2)}, u32[]{:S(2)}) async-start(f32[64,6,128]{2,1,0:T(8,128)} %add_bitcast_fusion), calls=%async_computation | async-start | bytes 524288 | tf_op jit(solution)/shard_map/all_to_all | solution.py:19
  117.6 3.0 %copy-start.3 = (bf16[4,4,240,384]{3,2,1,0:T(8,128)(2,1)S(1)}, bf16[4,4,240,384]{3,2,1,0:T(8,128)(2,1)}, u32[]{:S(2)}) copy-start(bf16[4,4,240,384]{3,2,1,0:T(8,128)(2,1)} %get-tuple-element.12) | copy-start | bytes 8847364
  117.6 3.0 %copy-start.9 = (bf16[1,3,128,128]{3,2,1,0:T(8,128)(2,1)S(1)}, bf16[1,3,128,128]{3,2,1,0:T(8,128)(2,1)}, u32[]{:S(2)}) copy-start(bf16[1,3,128,128]{3,2,1,0:T(8,128)(2,1)} %get-tuple-element.27) | copy-start | bytes 294916

commit v10 on v9

--- a/solution.py
+++ b/solution.py
@@ -13,6 +13,17 @@
     else:
         pairs = [(i + 1, i) for i in range(peers - 1)]
     return lax.ppermute(piece, "frame", pairs)
+
+
+def grid_shift(piece, df, dr):
+    n_f, n_r = lax.axis_size("frame"), lax.axis_size("row")
+    pairs = [
+        (f * n_r + r, (f + df) * n_r + (r + dr))
+        for f in range(n_f)
+        for r in range(n_r)
+        if 0 <= f + df < n_f and 0 <= r + dr < n_r
+    ]
+    return lax.ppermute(piece, ("frame", "row"), pairs)
 
 
 def a2a_sum(blocks, axis):
@@ -80,9 +91,16 @@
     below = lax.ppermute(
         jnp.concatenate([x[:2], g[:1]], axis=0), "row", [(i + 1, i) for i in range(peers - 1)]
     )
+    g_next = jnp.concatenate(
+        [
+            grid_shift(g[rows - 1 :, :2], -1, 1),
+            grid_shift(g[:, :2], -1, 0),
+            grid_shift(g[:1, :2], -1, -1),
+        ],
+        axis=0,
+    )
     x_e = jnp.concatenate([above[:2], x, below[:2]], axis=0)
     g_e = jnp.concatenate([above[2:], g, below[2:]], axis=0)
-    g_next = frame_shift(g_e[:, :2], forward=False)
 
     x3 = width_taps(x_e, reverse=False)
     fwd_weight = spatial_weight.reshape(3, 3 * chans, chans)

time: 130 us -> 117 us (0.900)
  waiting for transfers between devices: 49.5 us -> 37.8 us
  local copies, waits for them, and re-layouts: 24.9 us -> 20.8 us
  starting transfers between devices: 28.7 us -> 30.6 us
    ppermute x1, waiting for transfers between devices: 7.33 us -> 0.01 us  [on_device(): lax.ppermute(jnp.concatenate([x[rows - 2:], g[rows - 1:]], axis=0), 'row'...]
    ppermute x2 -> x1, waiting for transfers between devices: 6.49 us -> 0.01 us  [frame_shift(): return lax.ppermute(piece, 'frame', pairs)]
    ppermute x0 -> x3, starting transfers between devices: none -> 3.85 us  [grid_shift(): return lax.ppermute(piece, ('frame', 'row'), pairs)]
    unnamed x35 -> x33, local copies, waits for them, and re-layouts: 9.37 us -> 6 us
    all_to_all x1, waiting for transfers between devices: 6.11 us -> 8.47 us  [a2a_sum(): got = lax.all_to_all(blocks, axis, split_axis=0, concat_axis=0, tiled=True)]
    slice x1, local copies, waits for them, and re-layouts: 1.7 us -> 0.02 us  [on_device(): back = back + jnp.dot(piece, back_weight[i], preferred_element_type=f32)]
    slice x1, local copies, waits for them, and re-layouts: 2.3 us -> 0.77 us  [width_taps(): right = jnp.concatenate([a[:, :, 1:], zero], axis=2)]
    slice x0 -> x2, local copies, waits for them, and re-layouts: none -> 1.52 us  [the longest x1 0.81 us: on_device(): g[:, :2]]
  transfers between devices with their start and end apart: 7 -> 9, of which waited for: 5 -> 3; matrix products, arithmetic and copies ran while one was open for 17% -> 21% of each run, Pallas kernels for 0% -> 0%
where the time goes in v10:
time: 117 us
  waiting for transfers between devices  37.8 us (32%)
  starting transfers between devices  30.6 us (26%)
  local copies, waits for them, and re-layouts  20.8 us (18%)
  matrix products  15.2 us (13%)
  other arithmetic  10.9 us (9%)
  between operations  1.25 us (1%)
    ppermute x1, waiting for transfers between devices, on_device(): lax.ppermute(jnp.concatenate([x[:2], g[:1]], axis=0), 'row', [(i + 1, i)...  14.8 us
    ppermute x2, waiting for transfers between devices, halving_sum(): got = lax.ppermute(send, axis, [(i, i ^ bit) for i in range(n)])  14.5 us
    ppermute x1, starting transfers between devices, on_device(): lax.ppermute(jnp.concatenate([x[rows - 2:], g[rows - 1:]], axis=0), 'row'...  10.2 us
    all_to_all x1, starting transfers between devices, a2a_sum(): got = lax.all_to_all(blocks, axis, split_axis=0, concat_axis=0, tiled=True)  9.03 us
    all_to_all x1, waiting for transfers between devices, a2a_sum(): got = lax.all_to_all(blocks, axis, split_axis=0, concat_axis=0, tiled=True)  8.47 us
    unnamed x33, local copies, waits for them, and re-layouts  6 us
    dot_general x3, matrix products, on_device(): back = back + jnp.dot(piece, back_weight[i], preferred_element_type=f32)  4.87 us
    ppermute x1, starting transfers between devices, frame_shift(): return lax.ppermute(piece, 'frame', pairs)  4.55 us
  transfers between devices with their start and end apart: 9, of which 3 were waited for; matrix products, arithmetic and copies ran while one was open for 21% of the time, Pallas kernels for 0%

profile of v10, /device:TPU:1, one launch (start us, length us, event | category | flops | bytes accessed | tf_op | source)
XLA Modules:
  0.0 116.5 jit_solution(7526105078703307637)
XLA Ops:
  0.6 1.4 %copy.33 = bf16[1,4,4,240,128]{4,3,1,2,0:T(8,128)(2,1)S(1)} copy(bf16[1,4,4,240,128]{4,3,2,1,0:T(8,128)(2,1)} %param.5) | data formatting | bytes 1966080 | tf_op args[1]
  3.2 10.2 %collective-permute-start = (bf16[3,4,240,128]{3,2,1,0:T(8,128)(2,1)}, bf16[3,4,240,128]{3,2,1,0:T(8,128)(2,1)S(1)}, u32[]{:S(2)}, u32[]{:S(2)}) collective-permute-start(bf16[3,4,240,128]{3,2,1,0:T(8,128)(2,1)} %pad_maximum_fusion.4), channel_id=1, source_target_pairs={{0,1},{1,2},{2,3},{4,5},{5,6},{6,7},{8,9},{9,10},{10,11},{12,13},{... | collective-permute-start | bytes 2211848 | tf_op jit(solution)/shard_map/ppermute | solution.py:87
  14.3 1.9 %collective-permute-start.1 = (bf16[3,4,240,128]{3,2,1,0:T(8,128)(2,1)}, bf16[3,4,240,128]{3,2,1,0:T(8,128)(2,1)}, u32[]{:S(2)}, u32[]{:S(2)}) collective-permute-start(bf16[3,4,240,128]{3,2,1,0:T(8,128)(2,1)} %pad_maximum_fusion.5), channel_id=1, source_target_pairs={{1,0},{2,1},{3,2},{5,4},{6,5},{7,6},{9,8},{10,9},{11,10},{13,12},{... | collective-permute-start | bytes 2211848 | tf_op jit(solution)/shard_map/ppermute | solution.py:91
  17.0 1.3 %collective-permute-start.3 = (bf16[1,2,240,128]{3,2,1,0:T(8,128)(2,1)}, bf16[1,2,240,128]{3,2,1,0:T(8,128)(2,1)}, u32[]{:S(2)}, u32[]{:S(2)}) collective-permute-start(bf16[1,2,240,128]{3,2,1,0:T(8,128)(2,1)} %get-tuple-element.23), channel_id=1, source_target_pairs={{4,1},{5,2},{6,3},{8,5},{9,6},{10,7},{12,9},{13,10},{14,11},{16,13... | collective-permute-start | bytes 368648 | tf_op jit(solution)/shard_map/ppermute | solution.py:26
  18.3 1.3 %collective-permute-start.5 = (bf16[1,2,240,128]{3,2,1,0:T(8,128)(2,1)}, bf16[1,2,240,128]{3,2,1,0:T(8,128)(2,1)}, u32[]{:S(2)}, u32[]{:S(2)}) collective-permute-start(bf16[1,2,240,128]{3,2,1,0:T(8,128)(2,1)} %get-tuple-element.24), channel_id=1, source_target_pairs={{5,0},{6,1},{7,2},{9,4},{10,5},{11,6},{13,8},{14,9},{15,10},{17,12... | collective-permute-start | bytes 368648 | tf_op jit(solution)/shard_map/ppermute | solution.py:26
  20.4 1.3 %collective-permute-start.4 = (bf16[4,2,240,128]{3,2,1,0:T(8,128)(2,1)}, bf16[4,2,240,128]{3,2,1,0:T(8,128)(2,1)}, u32[]{:S(2)}, u32[]{:S(2)}) collective-permute-start(bf16[4,2,240,128]{3,2,1,0:T(8,128)(2,1)} %slice.176), channel_id=1, source_target_pairs={{4,0},{5,1},{6,2},{7,3},{8,4},{9,5},{10,6},{11,7},{12,8},{13,9},{1... | collective-permute-start | bytes 1474568 | tf_op jit(solution)/shard_map/ppermute | solution.py:26
  23.5 14.8 %collective-permute-done.1 = bf16[3,4,240,128]{3,2,1,0:T(8,128)(2,1)} collective-permute-done((bf16[3,4,240,128]{3,2,1,0:T(8,128)(2,1)}, bf16[3,4,240,128]{3,2,1,0:T(8,128)(2,1)}, u32[]{:S(2)}, u32[]{:S(2)}) %collective-permute-start.1) | collective-permute-done | bytes 737312 | tf_op jit(solution)/shard_map/ppermute | solution.py:91
  38.4 1.1 slice.163
  39.7 1.1 fusion.23
  40.8 1.5 %fusion.4 = bf16[8,4,240,384]{3,2,1,0:T(8,128)(2,1)S(1)} fusion(bf16[8,4,239,128]{3,2,1,0:T(8,128)(2,1)S(1)} %get-tuple-element.18, bf16[8,4,239,128]{3,2,1,0:T(8,128)(2,1)S(1)} %get-tuple-element.17, bf16[2,4,240,128]{3,2,1,0:T(8,128)(2,1)S(1)} %slice.163, bf16[4,4,240,128]{3,2,1,0:T(8,128)(2,1)S(1)} %bitcast.113, bf16[2,4,240,128]{3,2,1,0:T(8,128)(2,1)S(1)} %slice.160), kind=kLoop, calls=%fused_computation.11 | loop fusion | flops 41287680 | bytes 11780096 | tf_op jit(solution)/shard_map/concatenate | solution.py:64
  42.3 1.6 %fusion.20 = (bf16[6,4,240,384]{3,2,1,0:T(8,128)(2,1)S(1)}, bf16[6,4,240,384]{3,2,1,0:T(8,128)(2,1)S(1)}, bf16[6,4,240,384]{3,2,1,0:T(8,128)(2,1)S(1)}) fusion(bf16[8,4,240,384]{3,2,1,0:T(8,128)(2,1)S(1)} %fusion.4), kind=kLoop, calls=%fused_computation.55 | loop fusion | bytes 26542080 | tf_op jit(solution)/shard_map/slice | solution.py:110
  44.9 1.4 %maximum_maximum_fusion = bf16[6,6,240,128]{3,2,1,0:T(8,128)(2,1)S(1)} fusion(bf16[1,2,240,128]{3,2,1,0:T(8,128)(2,1)} %collective-permute-done.5, bf16[4,2,240,128]{3,2,1,0:T(8,128)(2,1)} %collective-permute-done.4, bf16[1,2,240,128]{3,2,1,0:T(8,128)(2,1)} %collective-permute-done.3, bf16[1,4,240,128]{3,2,1,0:T(8,128)(2,1)S(1)} %slice.174, ...), kind=kLoop, calls=%fused_computation.26 | loop fusion | flops 5529600 | bytes 4423680 | tf_op jit(solution)/shard_map/concatenate | solution.py:116
  47.2 1.3 %fusion.31 = f32[5760,128]{1,0:T(8,128)S(1)} fusion(bf16[5760,384]{1,0:T(8,128)(2,1)S(1)} %bitcast.107, bf16[384,128]{1,0:T(8,128)(2,1)S(1)} %bitcast.127), kind=kOutput, calls=%fused_computation.66 | convolution fusion | flops 566231040 | bytes 7471104 | tf_op jit(solution)/shard_map/dot_general | solution.py:111
  49.4 1.3 %convolution_convert_fusion = bf16[5760,128]{1,0:T(8,128)(2,1)S(1)} fusion(bf16[5760,384]{1,0:T(8,128)(2,1)S(1)} %bitcast.106, bf16[384,128]{1,0:T(8,128)(2,1)S(1)} %bitcast.128), kind=kOutput, calls=%fused_computation.10 | convolution fusion | flops 566968320 | bytes 5996544 | tf_op jit(solution)/shard_map/dot_general | solution.py:122
  50.7 1.4 %convolution_add_fusion.1 = f32[5760,128]{1,0:T(8,128)S(1)} fusion(f32[5760,128]{1,0:T(8,128)S(1)} %fusion.31, bf16[5760,384]{1,0:T(8,128)(2,1)S(1)} %bitcast.104, bf16[384,128]{1,0:T(8,128)(2,1)S(1)} %bitcast.126), kind=kOutput, calls=%fused_computation.9 | convolution fusion | flops 566968320 | bytes 10420224 | tf_op jit(solution)/shard_map/dot_general | solution.py:111
  52.1 1.5 %convolution_add_fusion = f32[5760,128]{1,0:T(8,128)S(1)} fusion(f32[5760,128]{1,0:T(8,128)S(1)} %convolution_add_fusion.1, bf16[5760,384]{1,0:T(8,128)(2,1)S(1)} %bitcast.103, bf16[384,128]{1,0:T(8,128)(2,1)S(1)} %bitcast.125), kind=kOutput, calls=%fused_computation.8 | convolution fusion | flops 566968320 | bytes 10420224 | tf_op jit(solution)/shard_map/dot_general | solution.py:111
  53.6 1.2 %fusion.11 = bf16[6,4,240,128]{3,2,1,0:T(8,128)(2,1)S(1)} fusion(bf16[6,4,240,128]{3,2,1,0:T(8,128)(2,1)S(1)} %bitcast.115, f32[6,4,240,128]{3,2,1,0:T(8,128)S(1)} %bitcast.102), kind=kLoop, calls=%fused_computation.25 | loop fusion | flops 7372800 | bytes 5898240 | tf_op jit(solution)/shard_map/convert_element_type | solution.py:131
  55.8 1.0 convolution_bitcast_fusion.1
  58.3 4.5 %collective-permute-start.2 = (bf16[4,2,240,128]{3,2,1,0:T(8,128)(2,1)S(1)}, bf16[4,2,240,128]{3,2,1,0:T(8,128)(2,1)S(1)}, u32[]{:S(2)}, u32[]{:S(2)}) collective-permute-start(bf16[4,2,240,128]{3,2,1,0:T(8,128)(2,1)S(1)} %slice.170), channel_id=1, source_target_pairs={{0,4},{4,8},{8,12},{12,16},{16,20},{20,24},{24,28},{28,32},{32,36}... | collective-permute-start | bytes 1474568 | tf_op jit(solution)/shard_map/ppermute | solution.py:15
  62.8 1.2 %fusion.7 = bf16[6,4,240,384]{3,2,1,0:T(8,128)(2,1)S(1)} fusion(bf16[6,4,239,128]{3,2,1,0:T(8,128)(2,1)S(1)} %get-tuple-element.20, bf16[6,4,239,128]{3,2,1,0:T(8,128)(2,1)S(1)} %get-tuple-element.19, bf16[6,4,240,128]{3,2,1,0:T(8,128)(2,1)S(1)} %fusion.11), kind=kLoop, calls=%fused_computation.18 | loop fusion | flops 22118400 | bytes 8835072 | tf_op jit(solution)/shard_map/concatenate | solution.py:64
  64.0 3.0 %fusion.21 = (bf16[4,4,240,384]{3,2,1,0:T(8,128)(2,1)}, bf16[4,4,240,384]{3,2,1,0:T(8,128)(2,1)}, bf16[4,4,240,384]{3,2,1,0:T(8,128)(2,1)S(1)}) fusion(bf16[6,4,240,384]{3,2,1,0:T(8,128)(2,1)S(1)} %fusion.7), kind=kLoop, calls=%fused_computation.56 | loop fusion | bytes 17694720 | tf_op jit(solution)/shard_map/slice | solution.py:144
  68.0 1.0 convolution_bitcast_fusion.2
  69.6 1.6 %copy-done.1 = bf16[4,4,240,384]{3,2,1,0:T(8,128)(2,1)} copy-done((bf16[4,4,240,384]{3,2,1,0:T(8,128)(2,1)}, bf16[4,4,240,384]{3,2,1,0:T(8,128)(2,1)S(1)}, u32[]{:S(2)}) %copy-start.1) | copy-done | bytes 2949144
  72.2 1.1 reshape.99
  73.3 1.1 dynamic-slice_bitcast_fusion
  74.5 2.9 %convolution_add_fusion.3 = f32[3840,128]{1,0:T(8,128)S(1)} fusion(f32[3840,128]{1,0:T(8,128)S(1)} %convolution_add_fusion.4, bf16[3840,384]{1,0:T(8,128)(2,1)} %bitcast.109, bf16[384,128]{1,0:T(8,128)(2,1)S(1)} %bitcast.123), kind=kOutput, calls=%fused_computation.14 | convolution fusion | flops 377978880 | bytes 6979584 | tf_op jit(solution)/shard_map/dot_general | solution.py:145
  77.6 1.0 collective-permute-start.7
  79.6 1.0 copy.31
  80.6 14.5 %collective-permute-done.7 = f32[1,64,6,128]{3,2,0,1:T(8,128)S(1)} collective-permute-done((f32[1,64,6,128]{3,2,0,1:T(8,128)S(1)}, f32[1,64,6,128]{3,2,0,1:T(8,128)S(1)}, u32[]{:S(2)}, u32[]{:S(2)}) %collective-permute-start.7) | collective-permute-done | bytes 196640 | tf_op jit(solution)/shard_map/ppermute | solution.py:43
  95.8 9.0 %all-to-all-start = ((f32[64,6,128]{2,1,0:T(8,128)}), f32[64,6,128]{2,1,0:T(8,128)S(1)}, u32[]{:S(2)}, u32[]{:S(2)}) async-start(f32[64,6,128]{2,1,0:T(8,128)} %add_bitcast_fusion), calls=%async_computation | async-start | bytes 524288 | tf_op jit(solution)/shard_map/all_to_all | solution.py:30
  106.4 1.0 copy.16
  107.4 8.5 %all-to-all-done = f32[64,6,128]{2,1,0:T(8,128)S(1)} async-done(((f32[64,6,128]{2,1,0:T(8,128)}), f32[64,6,128]{2,1,0:T(8,128)S(1)}, u32[]{:S(2)}, u32[]{:S(2)}) %all-to-all-start) | async-done | bytes 196640 | tf_op jit(solution)/shard_map/all_to_all | solution.py:30
  (69 shorter events, 17.4 us)
Async XLA Ops:
  0.6 1.5 %copy-start.4 = (bf16[1,4,4,240,128]{4,3,2,1,0:T(8,128)(2,1)S(1)}, bf16[1,4,4,240,128]{4,3,2,1,0:T(8,128)(2,1)}, u32[]{:S(2)}) copy-start(bf16[1,4,4,240,128]{4,3,2,1,0:T(8,128)(2,1)} %param.4) | copy-start | bytes 2949124
  2.2 19.5 %copy-start.12 = (bf16[3,128,128]{2,1,0:T(8,128)(2,1)S(1)}, bf16[3,128,128]{2,1,0:T(8,128)(2,1)}, u32[]{:S(2)}) copy-start(bf16[3,128,128]{2,1,0:T(8,128)(2,1)} %param.7) | copy-start | bytes 294916
  2.2 20.3 %copy-start.6 = (bf16[3,3,128,128]{3,2,1,0:T(8,128)(2,1)S(1)}, bf16[3,3,128,128]{3,2,1,0:T(8,128)(2,1)}, u32[]{:S(2)}) copy-start(bf16[3,3,128,128]{3,2,1,0:T(8,128)(2,1)} %param.6) | copy-start | bytes 884740
  3.2 20.3 %collective-permute-start = (bf16[3,4,240,128]{3,2,1,0:T(8,128)(2,1)}, bf16[3,4,240,128]{3,2,1,0:T(8,128)(2,1)S(1)}, u32[]{:S(2)}, u32[]{:S(2)}) collective-permute-start(bf16[3,4,240,128]{3,2,1,0:T(8,128)(2,1)} %pad_maximum_fusion.4), channel_id=1, source_target_pairs={{0,1},{1,2},{2,3},{4,5},{5,6},{6,7},{8,9},{9,10},{10,11},{12,13},{... | collective-permute-start | bytes 2211848 | tf_op jit(solution)/shard_map/ppermute | solution.py:87
  14.3 24.0 %collective-permute-start.1 = (bf16[3,4,240,128]{3,2,1,0:T(8,128)(2,1)}, bf16[3,4,240,128]{3,2,1,0:T(8,128)(2,1)}, u32[]{:S(2)}, u32[]{:S(2)}) collective-permute-start(bf16[3,4,240,128]{3,2,1,0:T(8,128)(2,1)} %pad_maximum_fusion.5), channel_id=1, source_target_pairs={{1,0},{2,1},{3,2},{5,4},{6,5},{7,6},{9,8},{10,9},{11,10},{13,12},{... | collective-permute-start | bytes 2211848 | tf_op jit(solution)/shard_map/ppermute | solution.py:91
  17.0 27.9 %collective-permute-start.3 = (bf16[1,2,240,128]{3,2,1,0:T(8,128)(2,1)}, bf16[1,2,240,128]{3,2,1,0:T(8,128)(2,1)}, u32[]{:S(2)}, u32[]{:S(2)}) collective-permute-start(bf16[1,2,240,128]{3,2,1,0:T(8,128)(2,1)} %get-tuple-element.23), channel_id=1, source_target_pairs={{4,1},{5,2},{6,3},{8,5},{9,6},{10,7},{12,9},{13,10},{14,11},{16,13... | collective-permute-start | bytes 368648 | tf_op jit(solution)/shard_map/ppermute | solution.py:26
  18.3 26.6 %collective-permute-start.5 = (bf16[1,2,240,128]{3,2,1,0:T(8,128)(2,1)}, bf16[1,2,240,128]{3,2,1,0:T(8,128)(2,1)}, u32[]{:S(2)}, u32[]{:S(2)}) collective-permute-start(bf16[1,2,240,128]{3,2,1,0:T(8,128)(2,1)} %get-tuple-element.24), channel_id=1, source_target_pairs={{5,0},{6,1},{7,2},{9,4},{10,5},{11,6},{13,8},{14,9},{15,10},{17,12... | collective-permute-start | bytes 368648 | tf_op jit(solution)/shard_map/ppermute | solution.py:26
  20.4 24.5 %collective-permute-start.4 = (bf16[4,2,240,128]{3,2,1,0:T(8,128)(2,1)}, bf16[4,2,240,128]{3,2,1,0:T(8,128)(2,1)}, u32[]{:S(2)}, u32[]{:S(2)}) collective-permute-start(bf16[4,2,240,128]{3,2,1,0:T(8,128)(2,1)} %slice.176), channel_id=1, source_target_pairs={{4,0},{5,1},{6,2},{7,3},{8,4},{9,5},{10,6},{11,7},{12,8},{13,9},{1... | collective-permute-start | bytes 1474568 | tf_op jit(solution)/shard_map/ppermute | solution.py:26
  46.3 0.9 copy-start.10
  48.5 0.9 copy-start.11
  49.4 1.3 %copy-start.9 = (bf16[1,3,128,128]{3,2,1,0:T(8,128)(2,1)S(1)}, bf16[1,3,128,128]{3,2,1,0:T(8,128)(2,1)}, u32[]{:S(2)}) copy-start(bf16[1,3,128,128]{3,2,1,0:T(8,128)(2,1)} %get-tuple-element.33) | copy-start | bytes 294916
  50.7 1.4 %copy-start.8 = (bf16[1,3,128,128]{3,2,1,0:T(8,128)(2,1)S(1)}, bf16[1,3,128,128]{3,2,1,0:T(8,128)(2,1)}, u32[]{:S(2)}) copy-start(bf16[1,3,128,128]{3,2,1,0:T(8,128)(2,1)} %get-tuple-element.32) | copy-start | bytes 294916
  58.3 10.8 %collective-permute-start.2 = (bf16[4,2,240,128]{3,2,1,0:T(8,128)(2,1)S(1)}, bf16[4,2,240,128]{3,2,1,0:T(8,128)(2,1)S(1)}, u32[]{:S(2)}, u32[]{:S(2)}) collective-permute-start(bf16[4,2,240,128]{3,2,1,0:T(8,128)(2,1)S(1)} %slice.170), channel_id=1, source_target_pairs={{0,4},{4,8},{8,12},{12,16},{16,20},{20,24},{24,28},{28,32},{32,36}... | collective-permute-start | bytes 1474568 | tf_op jit(solution)/shard_map/ppermute | solution.py:15
  69.1 2.0 %copy-start.7 = (bf16[1,4,4,240,128]{4,3,2,1,0:T(8,128)(2,1)S(1)}, bf16[1,4,4,240,128]{4,3,2,1,0:T(8,128)(2,1)}, u32[]{:S(2)}) copy-start(bf16[1,4,4,240,128]{4,3,2,1,0:T(8,128)(2,1)} %param.5) | copy-start | bytes 2949124
  69.6 1.6 %copy-start.1 = (bf16[4,4,240,384]{3,2,1,0:T(8,128)(2,1)}, bf16[4,4,240,384]{3,2,1,0:T(8,128)(2,1)S(1)}, u32[]{:S(2)}) copy-start(bf16[4,4,240,384]{3,2,1,0:T(8,128)(2,1)S(1)} %fusion.9) | copy-start | bytes 8847364
  74.4 3.1 %collective-permute-start.6 = (f32[2,64,6,128]{3,2,0,1:T(8,128)S(1)}, f32[2,64,6,128]{3,2,0,1:T(8,128)S(1)}, u32[]{:S(2)}, u32[]{:S(2)}) collective-permute-start(f32[2,64,6,128]{3,2,0,1:T(8,128)S(1)} %dynamic-slice_bitcast_fusion), channel_id=1, source_target_pairs={{0,1},{1,0},{2,3},{3,2},{4,5},{5,4},{6,7},{7,6},{8,9},{9,8},{10,11... | collective-permute-start | bytes 1179656 | tf_op jit(solution)/shard_map/ppermute | solution.py:43
  74.5 3.0 %copy-start.3 = (f32[64,4,6,128]{3,2,1,0:T(8,128)S(1)}, f32[64,4,6,128]{3,2,1,0:T(8,128)}, u32[]{:S(2)}) copy-start(f32[64,4,6,128]{3,2,1,0:T(8,128)} %reshape.99) | copy-start | bytes 2359300
  74.5 4.1 %copy-start = (bf16[4,4,240,384]{3,2,1,0:T(8,128)(2,1)S(1)}, bf16[4,4,240,384]{3,2,1,0:T(8,128)(2,1)}, u32[]{:S(2)}) copy-start(bf16[4,4,240,384]{3,2,1,0:T(8,128)(2,1)} %get-tuple-element.12) | copy-start | bytes 8847364
  77.6 17.5 %collective-permute-start.7 = (f32[1,64,6,128]{3,2,0,1:T(8,128)S(1)}, f32[1,64,6,128]{3,2,0,1:T(8,128)S(1)}, u32[]{:S(2)}, u32[]{:S(2)}) collective-permute-start(f32[1,64,6,128]{3,2,0,1:T(8,128)S(1)} %constant_dynamic-slice_fusion), channel_id=1, source_target_pairs={{0,2},{1,3},{2,0},{3,1},{4,6},{5,7},{6,4},{7,5},{8,10},{9,11},{10,... | collective-permute-start | bytes 589832 | tf_op jit(solution)/shard_map/ppermute | solution.py:43
  79.6 25.3 %copy-start.2 = (bf16[4,4,240,384]{3,2,1,0:T(8,128)(2,1)S(1)}, bf16[4,4,240,384]{3,2,1,0:T(8,128)(2,1)}, u32[]{:S(2)}) copy-start(bf16[4,4,240,384]{3,2,1,0:T(8,128)(2,1)} %copy-done.1) | copy-start | bytes 8847364
  79.6 25.3 %copy-start.13 = (bf16[3,128,128]{2,1,0:T(8,128)(2,1)S(1)}, bf16[3,128,128]{2,1,0:T(8,128)(2,1)}, u32[]{:S(2)}) copy-start(bf16[3,128,128]{2,1,0:T(8,128)(2,1)} %param.7) | copy-start | bytes 294916
  95.8 20.0 %all-to-all-start = ((f32[64,6,128]{2,1,0:T(8,128)}), f32[64,6,128]{2,1,0:T(8,128)S(1)}, u32[]{:S(2)}, u32[]{:S(2)}) async-start(f32[64,6,128]{2,1,0:T(8,128)} %add_bitcast_fusion), calls=%async_computation | async-start | bytes 524288 | tf_op jit(solution)/shard_map/all_to_all | solution.py:30
  104.9 1.2 %copy-start.5 = (bf16[1,4,4,240,128]{4,3,2,1,0:T(8,128)(2,1)S(1)}, bf16[1,4,4,240,128]{4,3,2,1,0:T(8,128)(2,1)}, u32[]{:S(2)}) copy-start(bf16[1,4,4,240,128]{4,3,2,1,0:T(8,128)(2,1)} %param.4) | copy-start | bytes 2949124

commit v11 on v8

--- a/solution.py
+++ b/solution.py
@@ -48,10 +48,9 @@
     n_dp, n_frame, n_row = (lax.axis_size(a) for a in ("dp", "frame", "row"))
     rows = terms.shape[0] // (n_dp * n_frame * n_row)
     chans = terms.shape[-1]
-    blocks = terms.reshape(n_dp * n_frame, n_row, rows, chans)
-    blocks = jnp.transpose(blocks, (1, 0, 2, 3))
-    blocks = halving_sum(blocks, "row")
-    return a2a_sum(blocks, ("dp", "frame"))
+    blocks = terms.reshape(n_dp * n_frame, n_row * rows, chans)
+    blocks = a2a_sum(blocks, ("dp", "frame"))
+    return halving_sum(blocks.reshape(n_row, rows, chans), "row")
 
 
 def width_taps(a, reverse):

time: 113 us -> 99.4 us (0.88)
  waiting for transfers between devices: 35.3 us -> 28.8 us
  starting transfers between devices: 38.2 us -> 33 us
  other arithmetic: 6.89 us -> 9.25 us
  local copies, waits for them, and re-layouts: 17.6 us -> 15.3 us
  matrix products: 13.5 us -> 11.4 us
    all_to_all x1, starting transfers between devices: 16.9 us -> 11.1 us  [a2a_sum(): got = lax.all_to_all(blocks, axis, split_axis=0, concat_axis=0, tiled=True)]
    ppermute x2, waiting for transfers between devices: 9.46 us -> 4.61 us  [halving_sum(): got = lax.ppermute(send, axis, [(i, i ^ bit) for i in range(n)])]
    dot_general x3, matrix products: 4.86 us -> 2.83 us  [on_device(): back = back + jnp.dot(piece, back_weight[i], preferred_element_type=f32)]
    all_to_all x1, waiting for transfers between devices: 8.88 us -> 7.19 us  [a2a_sum(): got = lax.all_to_all(blocks, axis, split_axis=0, concat_axis=0, tiled=True)]
    concatenate x2, other arithmetic: 2.72 us -> 3.89 us  [width_taps(): return jnp.concatenate(parts, axis=-1)]
    reduce_sum x1, other arithmetic: 0.07 us -> 1.22 us  [a2a_sum(): return jnp.sum(got, axis=0)]
    unnamed x33 -> x27, local copies, waits for them, and re-layouts: 5.58 us -> 4.47 us
  transfers between devices with their start and end apart: 9 -> 9, of which waited for: 4 -> 5; matrix products, arithmetic and copies ran while one was open for 21% -> 25% of each run, Pallas kernels for 0% -> 0%
where the time goes in v11:
time: 99.4 us; the launch traced here: 98.9 us
  starting transfers between devices  33 us (33%)
  waiting for transfers between devices  28.8 us (29%)
  local copies, waits for them, and re-layouts  15.3 us (15%)
  matrix products  11.4 us (11%)
  other arithmetic  9.25 us (9%)
  between operations  1.11 us (1%)
    ppermute x2, waiting for transfers between devices, row_halo(): after = lax.ppermute(shard[:1], 'row', down)  17 us
    ppermute x2, starting transfers between devices, row_halo(): before = lax.ppermute(shard[-1:], 'row', up)  12.5 us
    all_to_all x1, starting transfers between devices, a2a_sum(): got = lax.all_to_all(blocks, axis, split_axis=0, concat_axis=0, tiled=True)  11.1 us
    all_to_all x1, waiting for transfers between devices, a2a_sum(): got = lax.all_to_all(blocks, axis, split_axis=0, concat_axis=0, tiled=True)  7.19 us
    ppermute x2, waiting for transfers between devices, halving_sum(): got = lax.ppermute(send, axis, [(i, i ^ bit) for i in range(n)])  4.61 us
    ppermute x2, starting transfers between devices, frame_shift(): return lax.ppermute(piece, 'frame', pairs)  4.52 us
    unnamed x27, local copies, waits for them, and re-layouts  4.47 us
    ppermute x2, starting transfers between devices, row_halo(): after = lax.ppermute(shard[:1], 'row', down)  4.11 us
  transfers between devices with their start and end apart: 9, of which 5 were waited for; matrix products, arithmetic and copies ran while one was open for 25% of the time, Pallas kernels for 0%

profile of v11, /device:TPU:1, one launch (start us, length us, event | category | flops | bytes accessed | tf_op | source)
XLA Modules:
  0.0 98.9 jit_solution(16717699350737891849)
XLA Ops:
  0.7 1.4 %copy.33 = bf16[1,4,4,240,128]{4,3,1,2,0:T(8,128)(2,1)S(1)} copy(bf16[1,4,4,240,128]{4,3,2,1,0:T(8,128)(2,1)} %param.4) | data formatting | bytes 1966080 | tf_op args[0]
  2.8 10.2 %collective-permute-start = (bf16[1,4,240,128]{3,2,1,0:T(8,128)(2,1)}, bf16[1,4,240,128]{3,2,1,0:T(8,128)(2,1)S(1)}, u32[]{:S(2)}, u32[]{:S(2)}) collective-permute-start(bf16[1,4,240,128]{3,2,1,0:T(8,128)(2,1)} %get-tuple-element.25), channel_id=1, source_target_pairs={{0,1},{1,2},{2,3},{4,5},{5,6},{6,7},{8,9},{9,10},{10,11},{12,13},{... | collective-permute-start | bytes 737288 | tf_op jit(solution)/shard_map/ppermute | solution.py:13
  13.0 1.9 %collective-permute-start.1 = (bf16[1,4,240,128]{3,2,1,0:T(8,128)(2,1)}, bf16[1,4,240,128]{3,2,1,0:T(8,128)(2,1)S(1)}, u32[]{:S(2)}, u32[]{:S(2)}) collective-permute-start(bf16[1,4,240,128]{3,2,1,0:T(8,128)(2,1)} %get-tuple-element.26), channel_id=1, source_target_pairs={{1,0},{2,1},{3,2},{5,4},{6,5},{7,6},{9,8},{10,9},{11,10},{13,12},{... | collective-permute-start | bytes 737288 | tf_op jit(solution)/shard_map/ppermute | solution.py:14
  15.9 1.3 %collective-permute-start.3 = (bf16[4,2,240,128]{3,2,1,0:T(8,128)(2,1)}, bf16[4,2,240,128]{3,2,1,0:T(8,128)(2,1)S(1)}, u32[]{:S(2)}, u32[]{:S(2)}) collective-permute-start(bf16[4,2,240,128]{3,2,1,0:T(8,128)(2,1)} %slice.123), channel_id=1, source_target_pairs={{4,0},{8,4},{12,8},{16,12},{20,16},{24,20},{28,24},{32,28},{36,32}... | collective-permute-start | bytes 1474568 | tf_op jit(solution)/shard_map/ppermute | solution.py:24
  18.1 1.0 %copy.14 = bf16[3,128,128]{1,2,0:T(8,128)(2,1)S(1)} copy(bf16[3,128,128]{2,1,0:T(8,128)(2,1)} %param.7) | data formatting | bytes 196608 | tf_op args[3]
  19.8 6.6 %collective-permute-done.1 = bf16[1,4,240,128]{3,2,1,0:T(8,128)(2,1)S(1)} collective-permute-done((bf16[1,4,240,128]{3,2,1,0:T(8,128)(2,1)}, bf16[1,4,240,128]{3,2,1,0:T(8,128)(2,1)S(1)}, u32[]{:S(2)}, u32[]{:S(2)}) %collective-permute-start.1) | collective-permute-done | bytes 245792 | tf_op jit(solution)/shard_map/ppermute | solution.py:14
  27.4 1.4 %fusion.6 = bf16[6,4,240,384]{3,2,1,0:T(8,128)(2,1)S(1)} fusion(bf16[6,4,239,128]{3,2,1,0:T(8,128)(2,1)S(1)} %get-tuple-element.20, bf16[6,4,239,128]{3,2,1,0:T(8,128)(2,1)S(1)} %get-tuple-element.19, bf16[1,4,240,128]{3,2,1,0:T(8,128)(2,1)S(1)} %collective-permute-done.1, bf16[4,4,240,128]{3,2,1,0:T(8,128)(2,1)S(1)} %bitcast.111, ...), kind=kLoop, calls=%fused_computation.15 | loop fusion | flops 30965760 | bytes 8835072 | tf_op jit(solution)/shard_map/concatenate | solution.py:61
  28.8 1.1 %fusion.20 = (bf16[4,4,240,384]{3,2,1,0:T(8,128)(2,1)S(1)}, bf16[4,4,240,384]{3,2,1,0:T(8,128)(2,1)S(1)}, bf16[4,4,240,384]{3,2,1,0:T(8,128)(2,1)S(1)}) fusion(bf16[6,4,240,384]{3,2,1,0:T(8,128)(2,1)S(1)} %fusion.6), kind=kLoop, calls=%fused_computation.53 | loop fusion | bytes 17694720 | tf_op jit(solution)/shard_map/slice | solution.py:89
  29.8 0.9 fusion.28
  30.8 0.9 convolution_add_fusion.4
  31.8 1.0 convolution_add_fusion.3
  33.3 0.9 convolution_convert_fusion
  35.2 1.0 convolution_bitcast_fusion
  36.2 1.0 convolution_bitcast_fusion.1
  37.2 3.2 %collective-permute-start.2 = (bf16[4,2,240,128]{3,2,1,0:T(8,128)(2,1)S(1)}, bf16[4,2,240,128]{3,2,1,0:T(8,128)(2,1)S(1)}, u32[]{:S(2)}, u32[]{:S(2)}) collective-permute-start(bf16[4,2,240,128]{3,2,1,0:T(8,128)(2,1)S(1)} %slice.120), channel_id=1, source_target_pairs={{0,4},{4,8},{8,12},{12,16},{16,20},{20,24},{24,28},{28,32},{32,36}... | collective-permute-start | bytes 1474568 | tf_op jit(solution)/shard_map/ppermute | solution.py:24
  40.5 2.3 %collective-permute-start.4 = (bf16[1,4,240,128]{3,2,1,0:T(8,128)(2,1)S(1)}, bf16[1,4,240,128]{3,2,1,0:T(8,128)(2,1)S(1)}, u32[]{:S(2)}, u32[]{:S(2)}) collective-permute-start(bf16[1,4,240,128]{3,2,1,0:T(8,128)(2,1)S(1)} %get-tuple-element.23), channel_id=1, source_target_pairs={{0,1},{1,2},{2,3},{4,5},{5,6},{6,7},{8,9},{9,10},{10,11},{12,13},{... | collective-permute-start | bytes 737288 | tf_op jit(solution)/shard_map/ppermute | solution.py:13
  42.8 2.2 %collective-permute-start.5 = (bf16[1,4,240,128]{3,2,1,0:T(8,128)(2,1)S(1)}, bf16[1,4,240,128]{3,2,1,0:T(8,128)(2,1)S(1)}, u32[]{:S(2)}, u32[]{:S(2)}) collective-permute-start(bf16[1,4,240,128]{3,2,1,0:T(8,128)(2,1)S(1)} %get-tuple-element.24), channel_id=1, source_target_pairs={{1,0},{2,1},{3,2},{5,4},{6,5},{7,6},{9,8},{10,9},{11,10},{13,12},{... | collective-permute-start | bytes 737288 | tf_op jit(solution)/shard_map/ppermute | solution.py:14
  45.0 1.0 convolution_bitcast_fusion.2
  46.0 10.5 %collective-permute-done.5 = bf16[1,4,240,128]{3,2,1,0:T(8,128)(2,1)S(1)} collective-permute-done((bf16[1,4,240,128]{3,2,1,0:T(8,128)(2,1)S(1)}, bf16[1,4,240,128]{3,2,1,0:T(8,128)(2,1)S(1)}, u32[]{:S(2)}, u32[]{:S(2)}) %collective-permute-start.5) | collective-permute-done | bytes 245792 | tf_op jit(solution)/shard_map/ppermute | solution.py:14
  57.4 2.5 %fusion.8 = bf16[6,4,240,384]{3,2,1,0:T(8,128)(2,1)} fusion(bf16[6,4,239,128]{3,2,1,0:T(8,128)(2,1)S(1)} %get-tuple-element.18, bf16[6,4,239,128]{3,2,1,0:T(8,128)(2,1)S(1)} %get-tuple-element.17, bf16[1,4,240,128]{3,2,1,0:T(8,128)(2,1)S(1)} %collective-permute-done.5, bf16[4,4,240,128]{3,2,1,0:T(8,128)(2,1)S(1)} %get-tuple-element.15, ...), kind=kLoop, calls=%fused_computation.17 | loop fusion | flops 30965760 | bytes 8835072 | tf_op jit(solution)/shard_map/concatenate | solution.py:61
  61.3 1.0 convolution_bitcast_fusion.3
  62.2 0.9 pad_maximum_fusion.4
  63.2 11.1 %all-to-all-start = ((f32[64,24,128]{2,1,0:T(8,128)}), f32[64,24,128]{2,1,0:T(8,128)}, u32[]{:S(2)}, u32[]{:S(2)}) async-start(f32[64,24,128]{2,1,0:T(8,128)} %bitcast.41), calls=%async_computation | async-start | bytes 1572864 | tf_op jit(solution)/shard_map/all_to_all | solution.py:28
  74.3 4.1 %fusion.19 = (bf16[4,4,240,384]{3,2,1,0:T(8,128)(2,1)S(1)}, bf16[4,4,240,384]{3,2,1,0:T(8,128)(2,1)S(1)}, bf16[4,4,240,384]{3,2,1,0:T(8,128)(2,1)S(1)}) fusion(bf16[6,4,240,384]{3,2,1,0:T(8,128)(2,1)} %fusion.8), kind=kLoop, calls=%fused_computation.52 | loop fusion | bytes 17694720 | tf_op jit(solution)/shard_map/slice | solution.py:123
  78.4 0.9 convolution_add_fusion.2
  79.3 0.9 convolution_add_fusion.1
  80.3 0.9 fusion.4
  81.3 1.0 %copy.32 = bf16[4,4,240,128]{3,2,0,1:T(8,128)(2,1)} copy(bf16[4,4,240,128]{3,2,1,0:T(8,128)(2,1)S(1)} %bitcast.112) | data formatting | bytes 1966080 | tf_op jit(solution)/shard_map/reshape | solution.py:125
  82.3 7.2 %all-to-all-done = f32[64,24,128]{2,1,0:T(8,128)} async-done(((f32[64,24,128]{2,1,0:T(8,128)}), f32[64,24,128]{2,1,0:T(8,128)}, u32[]{:S(2)}, u32[]{:S(2)}) %all-to-all-start) | async-done | bytes 786464 | tf_op jit(solution)/shard_map/all_to_all | solution.py:28
  89.5 1.2 %reduce_sum.9 = f32[24,128]{1,0:T(8,128)S(1)} reduce(f32[64,24,128]{2,1,0:T(8,128)} %all-to-all-done, f32[]{:T(128)} %constant.58.clone.1), dimensions={0}, to_apply=%region_0.1 | reduce | flops 193536 | bytes 798724 | tf_op jit(solution)/shard_map/reduce_sum | solution.py:29
  92.9 1.0 %copy.17 = bf16[1,4,4,240,128]{4,3,2,1,0:T(8,128)(2,1)} copy(bf16[1,4,4,240,128]{4,3,1,2,0:T(8,128)(2,1)S(1)} %fusion.16) | data formatting | bytes 1966080
  93.9 4.4 %collective-permute-done.7 = f32[1,6,128]{2,1,0:T(8,128)S(1)} collective-permute-done((f32[1,6,128]{2,1,0:T(8,128)S(1)}, f32[1,6,128]{2,1,0:T(8,128)S(1)}, u32[]{:S(2)}, u32[]{:S(2)}) %collective-permute-start.7) | collective-permute-done | bytes 3104 | tf_op jit(solution)/shard_map/ppermute | solution.py:41
  (53 shorter events, 10.9 us)
Async XLA Ops:
  0.6 14.3 %copy-start.4 = (bf16[1,4,4,240,128]{4,3,2,1,0:T(8,128)(2,1)S(1)}, bf16[1,4,4,240,128]{4,3,2,1,0:T(8,128)(2,1)}, u32[]{:S(2)}) copy-start(bf16[1,4,4,240,128]{4,3,2,1,0:T(8,128)(2,1)} %param.5) | copy-start | bytes 2949124
  0.6 16.5 %copy-start.3 = (bf16[3,3,128,128]{3,2,1,0:T(8,128)(2,1)S(1)}, bf16[3,3,128,128]{3,2,1,0:T(8,128)(2,1)}, u32[]{:S(2)}) copy-start(bf16[3,3,128,128]{3,2,1,0:T(8,128)(2,1)} %param.6) | copy-start | bytes 884740
  2.8 17.0 %collective-permute-start = (bf16[1,4,240,128]{3,2,1,0:T(8,128)(2,1)}, bf16[1,4,240,128]{3,2,1,0:T(8,128)(2,1)S(1)}, u32[]{:S(2)}, u32[]{:S(2)}) collective-permute-start(bf16[1,4,240,128]{3,2,1,0:T(8,128)(2,1)} %get-tuple-element.25), channel_id=1, source_target_pairs={{0,1},{1,2},{2,3},{4,5},{5,6},{6,7},{8,9},{9,10},{10,11},{12,13},{... | collective-permute-start | bytes 737288 | tf_op jit(solution)/shard_map/ppermute | solution.py:13
  13.0 13.3 %collective-permute-start.1 = (bf16[1,4,240,128]{3,2,1,0:T(8,128)(2,1)}, bf16[1,4,240,128]{3,2,1,0:T(8,128)(2,1)S(1)}, u32[]{:S(2)}, u32[]{:S(2)}) collective-permute-start(bf16[1,4,240,128]{3,2,1,0:T(8,128)(2,1)} %get-tuple-element.26), channel_id=1, source_target_pairs={{1,0},{2,1},{3,2},{5,4},{6,5},{7,6},{9,8},{10,9},{11,10},{13,12},{... | collective-permute-start | bytes 737288 | tf_op jit(solution)/shard_map/ppermute | solution.py:14
  15.9 16.9 %collective-permute-start.3 = (bf16[4,2,240,128]{3,2,1,0:T(8,128)(2,1)}, bf16[4,2,240,128]{3,2,1,0:T(8,128)(2,1)S(1)}, u32[]{:S(2)}, u32[]{:S(2)}) collective-permute-start(bf16[4,2,240,128]{3,2,1,0:T(8,128)(2,1)} %slice.123), channel_id=1, source_target_pairs={{4,0},{8,4},{12,8},{16,12},{20,16},{24,20},{28,24},{32,28},{36,32}... | collective-permute-start | bytes 1474568 | tf_op jit(solution)/shard_map/ppermute | solution.py:24
  28.8 1.1 %copy-start.10 = (bf16[1,3,128,128]{3,2,1,0:T(8,128)(2,1)S(1)}, bf16[1,3,128,128]{3,2,1,0:T(8,128)(2,1)}, u32[]{:S(2)}) copy-start(bf16[1,3,128,128]{3,2,1,0:T(8,128)(2,1)} %get-tuple-element.32) | copy-start | bytes 294916
  29.8 1.0 copy-start.7
  30.8 1.0 copy-start.6
  37.2 22.7 %collective-permute-start.2 = (bf16[4,2,240,128]{3,2,1,0:T(8,128)(2,1)S(1)}, bf16[4,2,240,128]{3,2,1,0:T(8,128)(2,1)S(1)}, u32[]{:S(2)}, u32[]{:S(2)}) collective-permute-start(bf16[4,2,240,128]{3,2,1,0:T(8,128)(2,1)S(1)} %slice.120), channel_id=1, source_target_pairs={{0,4},{4,8},{8,12},{12,16},{16,20},{20,24},{24,28},{28,32},{32,36}... | collective-permute-start | bytes 1474568 | tf_op jit(solution)/shard_map/ppermute | solution.py:24
  40.5 5.5 %collective-permute-start.4 = (bf16[1,4,240,128]{3,2,1,0:T(8,128)(2,1)S(1)}, bf16[1,4,240,128]{3,2,1,0:T(8,128)(2,1)S(1)}, u32[]{:S(2)}, u32[]{:S(2)}) collective-permute-start(bf16[1,4,240,128]{3,2,1,0:T(8,128)(2,1)S(1)} %get-tuple-element.23), channel_id=1, source_target_pairs={{0,1},{1,2},{2,3},{4,5},{5,6},{6,7},{8,9},{9,10},{10,11},{12,13},{... | collective-permute-start | bytes 737288 | tf_op jit(solution)/shard_map/ppermute | solution.py:13
  42.8 13.6 %collective-permute-start.5 = (bf16[1,4,240,128]{3,2,1,0:T(8,128)(2,1)S(1)}, bf16[1,4,240,128]{3,2,1,0:T(8,128)(2,1)S(1)}, u32[]{:S(2)}, u32[]{:S(2)}) collective-permute-start(bf16[1,4,240,128]{3,2,1,0:T(8,128)(2,1)S(1)} %get-tuple-element.24), channel_id=1, source_target_pairs={{1,0},{2,1},{3,2},{5,4},{6,5},{7,6},{9,8},{10,9},{11,10},{13,12},{... | collective-permute-start | bytes 737288 | tf_op jit(solution)/shard_map/ppermute | solution.py:14
  60.0 1.2 %copy-start.5 = (bf16[1,4,4,240,128]{4,3,2,1,0:T(8,128)(2,1)S(1)}, bf16[1,4,4,240,128]{4,3,2,1,0:T(8,128)(2,1)}, u32[]{:S(2)}) copy-start(bf16[1,4,4,240,128]{4,3,2,1,0:T(8,128)(2,1)} %param.5) | copy-start | bytes 2949124
  61.3 1.9 %copy-start = (bf16[4,4,240,384]{3,2,1,0:T(8,128)(2,1)}, bf16[4,4,240,384]{3,2,1,0:T(8,128)(2,1)S(1)}, u32[]{:S(2)}) copy-start(bf16[4,4,240,384]{3,2,1,0:T(8,128)(2,1)S(1)} %fusion.10) | copy-start | bytes 8847364
  63.2 26.3 %all-to-all-start = ((f32[64,24,128]{2,1,0:T(8,128)}), f32[64,24,128]{2,1,0:T(8,128)}, u32[]{:S(2)}, u32[]{:S(2)}) async-start(f32[64,24,128]{2,1,0:T(8,128)} %bitcast.41), calls=%async_computation | async-start | bytes 1572864 | tf_op jit(solution)/shard_map/all_to_all | solution.py:28
  79.3 1.0 copy-start.8
  80.3 10.5 %copy-start.1 = (bf16[4,4,240,384]{3,2,1,0:T(8,128)(2,1)S(1)}, bf16[4,4,240,384]{3,2,1,0:T(8,128)(2,1)}, u32[]{:S(2)}) copy-start(bf16[4,4,240,384]{3,2,1,0:T(8,128)(2,1)} %copy-done) | copy-start | bytes 8847364
  80.3 10.5 %copy-start.9 = (bf16[3,128,128]{2,1,0:T(8,128)(2,1)S(1)}, bf16[3,128,128]{2,1,0:T(8,128)(2,1)}, u32[]{:S(2)}) copy-start(bf16[3,128,128]{2,1,0:T(8,128)(2,1)} %param.7) | copy-start | bytes 294916
  90.7 1.3 %collective-permute-start.6 = (f32[2,6,128]{2,1,0:T(8,128)S(1)}, f32[2,6,128]{2,1,0:T(8,128)S(1)}, u32[]{:S(2)}, u32[]{:S(2)}) collective-permute-start(f32[2,6,128]{2,1,0:T(8,128)S(1)} %dynamic-slice_bitcast_fusion), channel_id=1, source_target_pairs={{0,1},{1,0},{2,3},{3,2},{4,5},{5,4},{6,7},{7,6},{8,9},{9,8},{10,11... | collective-permute-start | bytes 18440 | tf_op jit(solution)/shard_map/ppermute | solution.py:41
  90.8 1.8 %copy-start.2 = (bf16[1,4,4,240,128]{4,3,2,1,0:T(8,128)(2,1)S(1)}, bf16[1,4,4,240,128]{4,3,2,1,0:T(8,128)(2,1)}, u32[]{:S(2)}) copy-start(bf16[1,4,4,240,128]{4,3,2,1,0:T(8,128)(2,1)} %param.4) | copy-start | bytes 2949124
  92.0 6.4 %collective-permute-start.7 = (f32[1,6,128]{2,1,0:T(8,128)S(1)}, f32[1,6,128]{2,1,0:T(8,128)S(1)}, u32[]{:S(2)}, u32[]{:S(2)}) collective-permute-start(f32[1,6,128]{2,1,0:T(8,128)S(1)} %constant_dynamic-slice_fusion), channel_id=1, source_target_pairs={{0,2},{1,3},{2,0},{3,1},{4,6},{5,7},{6,4},{7,5},{8,10},{9,11},{10,... | collective-permute-start | bytes 9224 | tf_op jit(solution)/shard_map/ppermute | solution.py:41

commit v12 on v11

--- a/solution.py
+++ b/solution.py
@@ -50,7 +50,7 @@
     chans = terms.shape[-1]
     blocks = terms.reshape(n_dp * n_frame, n_row * rows, chans)
     blocks = a2a_sum(blocks, ("dp", "frame"))
-    return halving_sum(blocks.reshape(n_row, rows, chans), "row")
+    return a2a_sum(blocks.reshape(n_row, rows, chans), "row")
 
 
 def width_taps(a, reverse):

time: 99.4 us -> 101 us (1.016)
  starting transfers between devices: 33 us -> 35.3 us
  other arithmetic: 9.25 us -> 8.11 us
    ppermute x2 -> x0, waiting for transfers between devices: 4.61 us -> none  [halving_sum(): got = lax.ppermute(send, axis, [(i, i ^ bit) for i in range(n)])]
    all_to_all x1 -> x2, waiting for transfers between devices: 7.19 us -> 11.1 us  [a2a_sum(): got = lax.all_to_all(blocks, axis, split_axis=0, concat_axis=0, tiled=True)]
    all_to_all x1 -> x2, starting transfers between devices: 11.1 us -> 14.2 us  [a2a_sum(): got = lax.all_to_all(blocks, axis, split_axis=0, concat_axis=0, tiled=True)]
    reduce_sum x1 -> x2, other arithmetic: 1.22 us -> 0.09 us  [a2a_sum(): return jnp.sum(got, axis=0)]
    unnamed x27 -> x31, local copies, waits for them, and re-layouts: 4.47 us -> 4.49 us
  transfers between devices with their start and end apart: 9 -> 8, of which waited for: 5 -> 4; matrix products, arithmetic and copies ran while one was open for 25% -> 24% of each run, Pallas kernels for 0% -> 0%
where the time goes in v12:
time: 101 us; the launch traced here: 100 us
  starting transfers between devices  35.3 us (35%)
  waiting for transfers between devices  28.1 us (28%)
  local copies, waits for them, and re-layouts  16 us (16%)
  matrix products  11.4 us (11%)
  other arithmetic  8.11 us (8%)
  between operations  1.09 us (1%)
    ppermute x2, waiting for transfers between devices, row_halo(): after = lax.ppermute(shard[:1], 'row', down)  16.9 us
    all_to_all x2, starting transfers between devices, a2a_sum(): got = lax.all_to_all(blocks, axis, split_axis=0, concat_axis=0, tiled=True)  14.2 us
    ppermute x2, starting transfers between devices, row_halo(): before = lax.ppermute(shard[-1:], 'row', up)  12.6 us
    all_to_all x2, waiting for transfers between devices, a2a_sum(): got = lax.all_to_all(blocks, axis, split_axis=0, concat_axis=0, tiled=True)  11.1 us
    ppermute x2, starting transfers between devices, frame_shift(): return lax.ppermute(piece, 'frame', pairs)  4.5 us
    unnamed x31, local copies, waits for them, and re-layouts  4.49 us
    slice x1, local copies, waits for them, and re-layouts, on_device(): piece = pg3[2 - i:2 - i + rows].reshape(-1, 3 * chans)  4.1 us
    ppermute x2, starting transfers between devices, row_halo(): after = lax.ppermute(shard[:1], 'row', down)  4.03 us
  transfers between devices with their start and end apart: 8, of which 4 were waited for; matrix products, arithmetic and copies ran while one was open for 24% of the time, Pallas kernels for 0%

profile of v12, /device:TPU:1, one launch (start us, length us, event | category | flops | bytes accessed | tf_op | source)
XLA Modules:
  0.0 100.1 jit_solution(15529697629507565191)
XLA Ops:
  0.7 1.4 %copy.33 = bf16[1,4,4,240,128]{4,3,1,2,0:T(8,128)(2,1)S(1)} copy(bf16[1,4,4,240,128]{4,3,2,1,0:T(8,128)(2,1)} %param.4) | data formatting | bytes 1966080 | tf_op args[0]
  2.8 10.2 %collective-permute-start = (bf16[1,4,240,128]{3,2,1,0:T(8,128)(2,1)}, bf16[1,4,240,128]{3,2,1,0:T(8,128)(2,1)S(1)}, u32[]{:S(2)}, u32[]{:S(2)}) collective-permute-start(bf16[1,4,240,128]{3,2,1,0:T(8,128)(2,1)} %get-tuple-element.25), channel_id=1, source_target_pairs={{0,1},{1,2},{2,3},{4,5},{5,6},{6,7},{8,9},{9,10},{10,11},{12,13},{... | collective-permute-start | bytes 737288 | tf_op jit(solution)/shard_map/ppermute | solution.py:13
  13.0 1.9 %collective-permute-start.1 = (bf16[1,4,240,128]{3,2,1,0:T(8,128)(2,1)}, bf16[1,4,240,128]{3,2,1,0:T(8,128)(2,1)S(1)}, u32[]{:S(2)}, u32[]{:S(2)}) collective-permute-start(bf16[1,4,240,128]{3,2,1,0:T(8,128)(2,1)} %get-tuple-element.26), channel_id=1, source_target_pairs={{1,0},{2,1},{3,2},{5,4},{6,5},{7,6},{9,8},{10,9},{11,10},{13,12},{... | collective-permute-start | bytes 737288 | tf_op jit(solution)/shard_map/ppermute | solution.py:14
  15.9 1.3 %collective-permute-start.3 = (bf16[4,2,240,128]{3,2,1,0:T(8,128)(2,1)}, bf16[4,2,240,128]{3,2,1,0:T(8,128)(2,1)S(1)}, u32[]{:S(2)}, u32[]{:S(2)}) collective-permute-start(bf16[4,2,240,128]{3,2,1,0:T(8,128)(2,1)} %slice.123), channel_id=1, source_target_pairs={{4,0},{8,4},{12,8},{16,12},{20,16},{24,20},{28,24},{32,28},{36,32}... | collective-permute-start | bytes 1474568 | tf_op jit(solution)/shard_map/ppermute | solution.py:24
  18.1 1.0 %copy.14 = bf16[3,128,128]{1,2,0:T(8,128)(2,1)S(1)} copy(bf16[3,128,128]{2,1,0:T(8,128)(2,1)} %param.7) | data formatting | bytes 196608 | tf_op args[3]
  19.9 6.5 %collective-permute-done.1 = bf16[1,4,240,128]{3,2,1,0:T(8,128)(2,1)S(1)} collective-permute-done((bf16[1,4,240,128]{3,2,1,0:T(8,128)(2,1)}, bf16[1,4,240,128]{3,2,1,0:T(8,128)(2,1)S(1)}, u32[]{:S(2)}, u32[]{:S(2)}) %collective-permute-start.1) | collective-permute-done | bytes 245792 | tf_op jit(solution)/shard_map/ppermute | solution.py:14
  27.4 1.4 %fusion.6 = bf16[6,4,240,384]{3,2,1,0:T(8,128)(2,1)S(1)} fusion(bf16[6,4,239,128]{3,2,1,0:T(8,128)(2,1)S(1)} %get-tuple-element.20, bf16[6,4,239,128]{3,2,1,0:T(8,128)(2,1)S(1)} %get-tuple-element.19, bf16[1,4,240,128]{3,2,1,0:T(8,128)(2,1)S(1)} %collective-permute-done.1, bf16[4,4,240,128]{3,2,1,0:T(8,128)(2,1)S(1)} %bitcast.105, ...), kind=kLoop, calls=%fused_computation.15 | loop fusion | flops 30965760 | bytes 8835072 | tf_op jit(solution)/shard_map/concatenate | solution.py:61
  28.8 1.1 %fusion.20 = (bf16[4,4,240,384]{3,2,1,0:T(8,128)(2,1)S(1)}, bf16[4,4,240,384]{3,2,1,0:T(8,128)(2,1)S(1)}, bf16[4,4,240,384]{3,2,1,0:T(8,128)(2,1)S(1)}) fusion(bf16[6,4,240,384]{3,2,1,0:T(8,128)(2,1)S(1)} %fusion.6), kind=kLoop, calls=%fused_computation.50 | loop fusion | bytes 17694720 | tf_op jit(solution)/shard_map/slice | solution.py:89
  29.8 0.9 fusion.28
  30.8 0.9 convolution_add_fusion.4
  31.8 1.0 convolution_add_fusion.3
  33.3 0.9 convolution_convert_fusion
  35.2 1.0 convolution_bitcast_fusion
  36.2 1.0 convolution_bitcast_fusion.1
  37.2 3.2 %collective-permute-start.2 = (bf16[4,2,240,128]{3,2,1,0:T(8,128)(2,1)S(1)}, bf16[4,2,240,128]{3,2,1,0:T(8,128)(2,1)S(1)}, u32[]{:S(2)}, u32[]{:S(2)}) collective-permute-start(bf16[4,2,240,128]{3,2,1,0:T(8,128)(2,1)S(1)} %slice.120), channel_id=1, source_target_pairs={{0,4},{4,8},{8,12},{12,16},{16,20},{20,24},{24,28},{28,32},{32,36}... | collective-permute-start | bytes 1474568 | tf_op jit(solution)/shard_map/ppermute | solution.py:24
  40.4 2.4 %collective-permute-start.4 = (bf16[1,4,240,128]{3,2,1,0:T(8,128)(2,1)S(1)}, bf16[1,4,240,128]{3,2,1,0:T(8,128)(2,1)S(1)}, u32[]{:S(2)}, u32[]{:S(2)}) collective-permute-start(bf16[1,4,240,128]{3,2,1,0:T(8,128)(2,1)S(1)} %get-tuple-element.23), channel_id=1, source_target_pairs={{0,1},{1,2},{2,3},{4,5},{5,6},{6,7},{8,9},{9,10},{10,11},{12,13},{... | collective-permute-start | bytes 737288 | tf_op jit(solution)/shard_map/ppermute | solution.py:13
  42.9 2.1 %collective-permute-start.5 = (bf16[1,4,240,128]{3,2,1,0:T(8,128)(2,1)S(1)}, bf16[1,4,240,128]{3,2,1,0:T(8,128)(2,1)S(1)}, u32[]{:S(2)}, u32[]{:S(2)}) collective-permute-start(bf16[1,4,240,128]{3,2,1,0:T(8,128)(2,1)S(1)} %get-tuple-element.24), channel_id=1, source_target_pairs={{1,0},{2,1},{3,2},{5,4},{6,5},{7,6},{9,8},{10,9},{11,10},{13,12},{... | collective-permute-start | bytes 737288 | tf_op jit(solution)/shard_map/ppermute | solution.py:14
  45.0 1.0 convolution_bitcast_fusion.2
  46.0 10.5 %collective-permute-done.5 = bf16[1,4,240,128]{3,2,1,0:T(8,128)(2,1)S(1)} collective-permute-done((bf16[1,4,240,128]{3,2,1,0:T(8,128)(2,1)S(1)}, bf16[1,4,240,128]{3,2,1,0:T(8,128)(2,1)S(1)}, u32[]{:S(2)}, u32[]{:S(2)}) %collective-permute-start.5) | collective-permute-done | bytes 245792 | tf_op jit(solution)/shard_map/ppermute | solution.py:14
  57.4 2.5 %fusion.8 = bf16[6,4,240,384]{3,2,1,0:T(8,128)(2,1)} fusion(bf16[6,4,239,128]{3,2,1,0:T(8,128)(2,1)S(1)} %get-tuple-element.18, bf16[6,4,239,128]{3,2,1,0:T(8,128)(2,1)S(1)} %get-tuple-element.17, bf16[1,4,240,128]{3,2,1,0:T(8,128)(2,1)S(1)} %collective-permute-done.5, bf16[4,4,240,128]{3,2,1,0:T(8,128)(2,1)S(1)} %get-tuple-element.15, ...), kind=kLoop, calls=%fused_computation.17 | loop fusion | flops 30965760 | bytes 8835072 | tf_op jit(solution)/shard_map/concatenate | solution.py:61
  61.2 1.0 convolution_bitcast_fusion.3
  62.2 0.9 pad_maximum_fusion.4
  63.1 11.0 %all-to-all-start = ((f32[64,24,128]{2,1,0:T(8,128)}), f32[64,24,128]{2,1,0:T(8,128)S(1)}, u32[]{:S(2)}, u32[]{:S(2)}) async-start(f32[64,24,128]{2,1,0:T(8,128)} %bitcast.41), calls=%async_computation | async-start | bytes 1572864 | tf_op jit(solution)/shard_map/all_to_all | solution.py:28
  74.1 4.1 %fusion.19 = (bf16[4,4,240,384]{3,2,1,0:T(8,128)(2,1)S(1)}, bf16[4,4,240,384]{3,2,1,0:T(8,128)(2,1)S(1)}, bf16[4,4,240,384]{3,2,1,0:T(8,128)(2,1)S(1)}) fusion(bf16[6,4,240,384]{3,2,1,0:T(8,128)(2,1)} %fusion.8), kind=kLoop, calls=%fused_computation.49 | loop fusion | bytes 17694720 | tf_op jit(solution)/shard_map/slice | solution.py:123
  78.3 1.0 convolution_add_fusion.2
  80.2 0.9 fusion.4
  81.2 1.0 %copy.32 = bf16[4,4,240,128]{3,2,0,1:T(8,128)(2,1)} copy(bf16[4,4,240,128]{3,2,1,0:T(8,128)(2,1)S(1)} %bitcast.106) | data formatting | bytes 1966080 | tf_op jit(solution)/shard_map/reshape | solution.py:125
  82.2 0.9 convolution_convert_fusion.1
  83.1 6.3 %all-to-all-done = f32[64,24,128]{2,1,0:T(8,128)S(1)} async-done(((f32[64,24,128]{2,1,0:T(8,128)}), f32[64,24,128]{2,1,0:T(8,128)S(1)}, u32[]{:S(2)}, u32[]{:S(2)}) %all-to-all-start) | async-done | bytes 786464 | tf_op jit(solution)/shard_map/all_to_all | solution.py:28
  90.1 3.2 %all-to-all-start.1 = ((f32[4,6,128]{2,1,0:T(8,128)}), f32[4,6,128]{2,1,0:T(8,128)S(1)}, u32[]{:S(2)}, u32[]{:S(2)}) async-start(f32[4,6,128]{2,1,0:T(8,128)} %reshape.94), calls=%async_computation.1 | async-start | bytes 32768 | tf_op jit(solution)/shard_map/all_to_all | solution.py:28
  93.6 1.0 %copy.17 = bf16[1,4,4,240,128]{4,3,2,1,0:T(8,128)(2,1)} copy(bf16[1,4,4,240,128]{4,3,1,2,0:T(8,128)(2,1)S(1)} %fusion.16) | data formatting | bytes 1966080
  94.6 4.8 %all-to-all-done.1 = f32[4,6,128]{2,1,0:T(8,128)S(1)} async-done(((f32[4,6,128]{2,1,0:T(8,128)}), f32[4,6,128]{2,1,0:T(8,128)S(1)}, u32[]{:S(2)}, u32[]{:S(2)}) %all-to-all-start.1) | async-done | bytes 12320 | tf_op jit(solution)/shard_map/all_to_all | solution.py:28
  (53 shorter events, 10.7 us)
Async XLA Ops:
  0.6 14.3 %copy-start.4 = (bf16[1,4,4,240,128]{4,3,2,1,0:T(8,128)(2,1)S(1)}, bf16[1,4,4,240,128]{4,3,2,1,0:T(8,128)(2,1)}, u32[]{:S(2)}) copy-start(bf16[1,4,4,240,128]{4,3,2,1,0:T(8,128)(2,1)} %param.5) | copy-start | bytes 2949124
  0.6 16.5 %copy-start.3 = (bf16[3,3,128,128]{3,2,1,0:T(8,128)(2,1)S(1)}, bf16[3,3,128,128]{3,2,1,0:T(8,128)(2,1)}, u32[]{:S(2)}) copy-start(bf16[3,3,128,128]{3,2,1,0:T(8,128)(2,1)} %param.6) | copy-start | bytes 884740
  2.8 17.0 %collective-permute-start = (bf16[1,4,240,128]{3,2,1,0:T(8,128)(2,1)}, bf16[1,4,240,128]{3,2,1,0:T(8,128)(2,1)S(1)}, u32[]{:S(2)}, u32[]{:S(2)}) collective-permute-start(bf16[1,4,240,128]{3,2,1,0:T(8,128)(2,1)} %get-tuple-element.25), channel_id=1, source_target_pairs={{0,1},{1,2},{2,3},{4,5},{5,6},{6,7},{8,9},{9,10},{10,11},{12,13},{... | collective-permute-start | bytes 737288 | tf_op jit(solution)/shard_map/ppermute | solution.py:13
  13.0 13.3 %collective-permute-start.1 = (bf16[1,4,240,128]{3,2,1,0:T(8,128)(2,1)}, bf16[1,4,240,128]{3,2,1,0:T(8,128)(2,1)S(1)}, u32[]{:S(2)}, u32[]{:S(2)}) collective-permute-start(bf16[1,4,240,128]{3,2,1,0:T(8,128)(2,1)} %get-tuple-element.26), channel_id=1, source_target_pairs={{1,0},{2,1},{3,2},{5,4},{6,5},{7,6},{9,8},{10,9},{11,10},{13,12},{... | collective-permute-start | bytes 737288 | tf_op jit(solution)/shard_map/ppermute | solution.py:14
  15.9 16.9 %collective-permute-start.3 = (bf16[4,2,240,128]{3,2,1,0:T(8,128)(2,1)}, bf16[4,2,240,128]{3,2,1,0:T(8,128)(2,1)S(1)}, u32[]{:S(2)}, u32[]{:S(2)}) collective-permute-start(bf16[4,2,240,128]{3,2,1,0:T(8,128)(2,1)} %slice.123), channel_id=1, source_target_pairs={{4,0},{8,4},{12,8},{16,12},{20,16},{24,20},{28,24},{32,28},{36,32}... | collective-permute-start | bytes 1474568 | tf_op jit(solution)/shard_map/ppermute | solution.py:24
  28.8 1.1 %copy-start.12 = (bf16[1,3,128,128]{3,2,1,0:T(8,128)(2,1)S(1)}, bf16[1,3,128,128]{3,2,1,0:T(8,128)(2,1)}, u32[]{:S(2)}) copy-start(bf16[1,3,128,128]{3,2,1,0:T(8,128)(2,1)} %get-tuple-element.32) | copy-start | bytes 294916
  29.8 1.0 copy-start.10
  30.8 1.0 copy-start.9
  37.2 22.7 %collective-permute-start.2 = (bf16[4,2,240,128]{3,2,1,0:T(8,128)(2,1)S(1)}, bf16[4,2,240,128]{3,2,1,0:T(8,128)(2,1)S(1)}, u32[]{:S(2)}, u32[]{:S(2)}) collective-permute-start(bf16[4,2,240,128]{3,2,1,0:T(8,128)(2,1)S(1)} %slice.120), channel_id=1, source_target_pairs={{0,4},{4,8},{8,12},{12,16},{16,20},{20,24},{24,28},{28,32},{32,36}... | collective-permute-start | bytes 1474568 | tf_op jit(solution)/shard_map/ppermute | solution.py:24
  40.4 5.5 %collective-permute-start.4 = (bf16[1,4,240,128]{3,2,1,0:T(8,128)(2,1)S(1)}, bf16[1,4,240,128]{3,2,1,0:T(8,128)(2,1)S(1)}, u32[]{:S(2)}, u32[]{:S(2)}) collective-permute-start(bf16[1,4,240,128]{3,2,1,0:T(8,128)(2,1)S(1)} %get-tuple-element.23), channel_id=1, source_target_pairs={{0,1},{1,2},{2,3},{4,5},{5,6},{6,7},{8,9},{9,10},{10,11},{12,13},{... | collective-permute-start | bytes 737288 | tf_op jit(solution)/shard_map/ppermute | solution.py:13
  42.9 13.6 %collective-permute-start.5 = (bf16[1,4,240,128]{3,2,1,0:T(8,128)(2,1)S(1)}, bf16[1,4,240,128]{3,2,1,0:T(8,128)(2,1)S(1)}, u32[]{:S(2)}, u32[]{:S(2)}) collective-permute-start(bf16[1,4,240,128]{3,2,1,0:T(8,128)(2,1)S(1)} %get-tuple-element.24), channel_id=1, source_target_pairs={{1,0},{2,1},{3,2},{5,4},{6,5},{7,6},{9,8},{10,9},{11,10},{13,12},{... | collective-permute-start | bytes 737288 | tf_op jit(solution)/shard_map/ppermute | solution.py:14
  60.0 1.2 %copy-start.5 = (bf16[1,4,4,240,128]{4,3,2,1,0:T(8,128)(2,1)S(1)}, bf16[1,4,4,240,128]{4,3,2,1,0:T(8,128)(2,1)}, u32[]{:S(2)}) copy-start(bf16[1,4,4,240,128]{4,3,2,1,0:T(8,128)(2,1)} %param.5) | copy-start | bytes 2949124
  61.2 1.9 %copy-start = (bf16[4,4,240,384]{3,2,1,0:T(8,128)(2,1)}, bf16[4,4,240,384]{3,2,1,0:T(8,128)(2,1)S(1)}, u32[]{:S(2)}) copy-start(bf16[4,4,240,384]{3,2,1,0:T(8,128)(2,1)S(1)} %fusion.10) | copy-start | bytes 8847364
  63.1 26.3 %all-to-all-start = ((f32[64,24,128]{2,1,0:T(8,128)}), f32[64,24,128]{2,1,0:T(8,128)S(1)}, u32[]{:S(2)}, u32[]{:S(2)}) async-start(f32[64,24,128]{2,1,0:T(8,128)} %bitcast.41), calls=%async_computation | async-start | bytes 1572864 | tf_op jit(solution)/shard_map/all_to_all | solution.py:28
  74.1 4.1 %copy-start.8 = (bf16[1,3,128,128]{3,2,1,0:T(8,128)(2,1)S(1)}, bf16[1,3,128,128]{3,2,1,0:T(8,128)(2,1)}, u32[]{:S(2)}) copy-start(bf16[1,3,128,128]{3,2,1,0:T(8,128)(2,1)} %get-tuple-element.29) | copy-start | bytes 294916
  78.3 1.0 copy-start.7
  79.2 0.9 copy-start.6
  80.2 2.0 %copy-start.1 = (bf16[4,4,240,384]{3,2,1,0:T(8,128)(2,1)S(1)}, bf16[4,4,240,384]{3,2,1,0:T(8,128)(2,1)}, u32[]{:S(2)}) copy-start(bf16[4,4,240,384]{3,2,1,0:T(8,128)(2,1)} %copy-done) | copy-start | bytes 8847364
  80.2 2.0 %copy-start.11 = (bf16[3,128,128]{2,1,0:T(8,128)(2,1)S(1)}, bf16[3,128,128]{2,1,0:T(8,128)(2,1)}, u32[]{:S(2)}) copy-start(bf16[3,128,128]{2,1,0:T(8,128)(2,1)} %param.7) | copy-start | bytes 294916
  82.2 11.2 %copy-start.2 = (bf16[1,4,4,240,128]{4,3,2,1,0:T(8,128)(2,1)S(1)}, bf16[1,4,4,240,128]{4,3,2,1,0:T(8,128)(2,1)}, u32[]{:S(2)}) copy-start(bf16[1,4,4,240,128]{4,3,2,1,0:T(8,128)(2,1)} %param.4) | copy-start | bytes 2949124
  90.1 9.4 %all-to-all-start.1 = ((f32[4,6,128]{2,1,0:T(8,128)}), f32[4,6,128]{2,1,0:T(8,128)S(1)}, u32[]{:S(2)}, u32[]{:S(2)}) async-start(f32[4,6,128]{2,1,0:T(8,128)} %reshape.94), calls=%async_computation.1 | async-start | bytes 32768 | tf_op jit(solution)/shard_map/all_to_all | solution.py:28

commit v13 on v11

--- a/solution.py
+++ b/solution.py
@@ -84,10 +84,8 @@
     g_next = frame_shift(g[:, :2], forward=False)
     x3 = width_taps(x_ext, reverse=False)
     fwd_weight = spatial_weight.reshape(3, 3 * chans, chans)
-    pre = jnp.zeros((rows * frames * cols, chans), f32)
-    for i in range(3):
-        piece = x3[i : i + rows].reshape(-1, 3 * chans)
-        pre = pre + jnp.dot(piece, fwd_weight[i], preferred_element_type=f32)
+    x9 = jnp.concatenate([x3[i : i + rows] for i in range(3)], axis=-1).reshape(-1, 9 * chans)
+    pre = jnp.dot(x9, fwd_weight.reshape(9 * chans, chans), preferred_element_type=f32)
     pre = pre.reshape(x.shape)
     act = jax.nn.silu(pre).astype(bf16)
     act_prev = frame_shift(act[:, frames - 2 :], forward=True)
@@ -110,21 +108,16 @@
     pre_grad = (act_grad.astype(f32) * sigma * (1.0 + pre * (1.0 - sigma))).astype(bf16)
     pg_flat = pre_grad.reshape(-1, chans)
 
-    spatial_list = []
-    for i in range(3):
-        piece = x3[i : i + rows].reshape(-1, 3 * chans)
-        spatial_list.append(
-            lax.dot_general(piece, pg_flat, (((0,), (0,)), ((), ())), preferred_element_type=f32)
-        )
+    spatial_grad = lax.dot_general(x9, pg_flat, (((0,), (0,)), ((), ())), preferred_element_type=f32)
     pg3 = width_taps(row_halo(pre_grad), reverse=True)
     back_weight = jnp.transpose(spatial_weight, (0, 1, 3, 2)).reshape(3, 3 * chans, chans)
-    back = g.astype(f32).reshape(-1, chans)
-    for i in range(3):
-        piece = pg3[2 - i : 2 - i + rows].reshape(-1, 3 * chans)
-        back = back + jnp.dot(piece, back_weight[i], preferred_element_type=f32)
+    pg9 = jnp.concatenate([pg3[2 - i : 2 - i + rows] for i in range(3)], axis=-1).reshape(-1, 9 * chans)
+    back = g.astype(f32).reshape(-1, chans) + jnp.dot(
+        pg9, back_weight.reshape(9 * chans, chans), preferred_element_type=f32
+    )
     input_grad = back.astype(bf16).reshape(x.shape)
 
-    partial_terms = jnp.concatenate(spatial_list + [temporal_grad], axis=0)
+    partial_terms = jnp.concatenate([spatial_grad, temporal_grad], axis=0)
     summed = staged_scatter(partial_terms)
     block_output = jnp.transpose(block_output, (1, 0, 2, 3))
     input_grad = jnp.transpose(input_grad, (1, 0, 2, 3))

time: 99.4 us -> 105 us (1.056)
  waiting for transfers between devices: 28.8 us -> 32.4 us
  other arithmetic: 9.25 us -> 12.6 us
    all_to_all x1, waiting for transfers between devices: 7.19 us -> 14.3 us  [a2a_sum(): got = lax.all_to_all(blocks, axis, split_axis=0, concat_axis=0, tiled=True)]
    concatenate x1 -> x2, other arithmetic: 0.93 us -> 5.37 us  [the longest x1 4.43 us: on_device(): jnp.concatenate([pg3[2 - i:2 - i + rows] for i in range(3)], axis=-1)]
    ppermute x2, waiting for transfers between devices: 17 us -> 13.1 us  [row_halo(): after = lax.ppermute(shard[:1], 'row', down)]
    unnamed x27 -> x23, local copies, waits for them, and re-layouts: 4.47 us -> 6.27 us
    slice x4 -> x2, local copies, waits for them, and re-layouts: 6.52 us -> 4.73 us  [the longest x1 3.71 us: on_device(): pg3[2 - i:2 - i + rows]]
    ppermute x2, starting transfers between devices: 0.76 us -> 2.24 us  [halving_sum(): got = lax.ppermute(send, axis, [(i, i ^ bit) for i in range(n)])]
    all_to_all x1, starting transfers between devices: 11.1 us -> 9.75 us  [a2a_sum(): got = lax.all_to_all(blocks, axis, split_axis=0, concat_axis=0, tiled=True)]
    concatenate x2, other arithmetic: 3.89 us -> 2.7 us  [width_taps(): return jnp.concatenate(parts, axis=-1)]
  transfers between devices with their start and end apart: 9 -> 9, of which waited for: 5 -> 4; matrix products, arithmetic and copies ran while one was open for 25% -> 27% of each run, Pallas kernels for 0% -> 0%
where the time goes in v13:
time: 105 us
  starting transfers between devices  33 us (31%)
  waiting for transfers between devices  32.4 us (31%)
  local copies, waits for them, and re-layouts  14.6 us (14%)
  other arithmetic  12.6 us (12%)
  matrix products  11.2 us (11%)
  between operations  1.09 us (1%)
    all_to_all x1, waiting for transfers between devices, a2a_sum(): got = lax.all_to_all(blocks, axis, split_axis=0, concat_axis=0, tiled=True)  14.3 us
    ppermute x2, waiting for transfers between devices, row_halo(): after = lax.ppermute(shard[:1], 'row', down)  13.1 us
    ppermute x2, starting transfers between devices, row_halo(): before = lax.ppermute(shard[-1:], 'row', up)  12.1 us
    all_to_all x1, starting transfers between devices, a2a_sum(): got = lax.all_to_all(blocks, axis, split_axis=0, concat_axis=0, tiled=True)  9.75 us
    unnamed x23, local copies, waits for them, and re-layouts  6.27 us
    ppermute x2, waiting for transfers between devices, halving_sum(): got = lax.ppermute(send, axis, [(i, i ^ bit) for i in range(n)])  4.96 us
    ppermute x2, starting transfers between devices, frame_shift(): return lax.ppermute(piece, 'frame', pairs)  4.52 us
    concatenate x1, other arithmetic, on_device(): jnp.concatenate([pg3[2 - i:2 - i + rows] for i in range(3)], axis=-1)  4.43 us
  transfers between devices with their start and end apart: 9, of which 4 were waited for; matrix products, arithmetic and copies ran while one was open for 27% of the time, Pallas kernels for 0%

profile of v13, /device:TPU:1, one launch (start us, length us, event | category | flops | bytes accessed | tf_op | source)
XLA Modules:
  0.0 104.8 jit_solution(11836440921233826211)
XLA Ops:
  0.7 1.4 %copy.32 = bf16[1,4,4,240,128]{4,3,1,2,0:T(8,128)(2,1)S(1)} copy(bf16[1,4,4,240,128]{4,3,2,1,0:T(8,128)(2,1)} %param.4) | data formatting | bytes 1966080 | tf_op args[0]
  2.0 0.8 fusion.30
  2.8 10.2 %collective-permute-start = (bf16[1,4,240,128]{3,2,1,0:T(8,128)(2,1)}, bf16[1,4,240,128]{3,2,1,0:T(8,128)(2,1)S(1)}, u32[]{:S(2)}, u32[]{:S(2)}) collective-permute-start(bf16[1,4,240,128]{3,2,1,0:T(8,128)(2,1)} %get-tuple-element.25), channel_id=1, source_target_pairs={{0,1},{1,2},{2,3},{4,5},{5,6},{6,7},{8,9},{9,10},{10,11},{12,13},{... | collective-permute-start | bytes 737288 | tf_op jit(solution)/shard_map/ppermute | solution.py:13
  13.0 1.9 %collective-permute-start.1 = (bf16[1,4,240,128]{3,2,1,0:T(8,128)(2,1)}, bf16[1,4,240,128]{3,2,1,0:T(8,128)(2,1)S(1)}, u32[]{:S(2)}, u32[]{:S(2)}) collective-permute-start(bf16[1,4,240,128]{3,2,1,0:T(8,128)(2,1)} %get-tuple-element.26), channel_id=1, source_target_pairs={{1,0},{2,1},{3,2},{5,4},{6,5},{7,6},{9,8},{10,9},{11,10},{13,12},{... | collective-permute-start | bytes 737288 | tf_op jit(solution)/shard_map/ppermute | solution.py:14
  15.1 1.3 %collective-permute-start.3 = (bf16[4,2,240,128]{3,2,1,0:T(8,128)(2,1)S(1)}, bf16[4,2,240,128]{3,2,1,0:T(8,128)(2,1)S(1)}, u32[]{:S(2)}, u32[]{:S(2)}) collective-permute-start(bf16[4,2,240,128]{3,2,1,0:T(8,128)(2,1)S(1)} %slice.90), channel_id=1, source_target_pairs={{4,0},{8,4},{12,8},{16,12},{20,16},{24,20},{28,24},{32,28},{36,32}... | collective-permute-start | bytes 1474568 | tf_op jit(solution)/shard_map/ppermute | solution.py:24
  17.2 1.8 %copy.15 = bf16[3,3,128,128]{2,3,1,0:T(8,128)(2,1)} copy(bf16[3,3,128,128]{3,2,1,0:T(8,128)(2,1)} %param.6) | data formatting | bytes 589824 | tf_op args[2]
  19.0 7.3 %collective-permute-done.1 = bf16[1,4,240,128]{3,2,1,0:T(8,128)(2,1)S(1)} collective-permute-done((bf16[1,4,240,128]{3,2,1,0:T(8,128)(2,1)}, bf16[1,4,240,128]{3,2,1,0:T(8,128)(2,1)S(1)}, u32[]{:S(2)}, u32[]{:S(2)}) %collective-permute-start.1) | collective-permute-done | bytes 245792 | tf_op jit(solution)/shard_map/ppermute | solution.py:14
  26.5 0.8 fusion.27
  27.4 1.4 %fusion.6 = bf16[6,4,240,384]{3,2,1,0:T(8,128)(2,1)S(1)} fusion(bf16[6,4,239,128]{3,2,1,0:T(8,128)(2,1)S(1)} %get-tuple-element.20, bf16[6,4,239,128]{3,2,1,0:T(8,128)(2,1)S(1)} %get-tuple-element.19, bf16[1,4,240,128]{3,2,1,0:T(8,128)(2,1)S(1)} %collective-permute-done.1, bf16[4,4,240,128]{3,2,1,0:T(8,128)(2,1)S(1)} %bitcast.77, ...), kind=kLoop, calls=%fused_computation.13 | loop fusion | flops 30965760 | bytes 8835072 | tf_op jit(solution)/shard_map/concatenate | solution.py:61
  28.8 1.0 fusion.25
  29.8 3.4 %fusion.10 = f32[4,4,240,128]{3,2,1,0:T(8,128)S(1)} fusion(bf16[1152,128,1,1]{1,0,3,2:T(8,128)(2,1)S(1)} %bitcast.86, bf16[4,4,240,384]{3,2,1,0:T(8,128)(2,1)S(1)} %get-tuple-element.13, bf16[4,4,240,384]{3,2,1,0:T(8,128)(2,1)S(1)} %get-tuple-element.14, bf16[4,4,240,384]{3,2,1,0:T(8,128)(2,1)S(1)} %get-tuple-element.12), kind=kOutput, calls=%fused_computation.17 | convolution fusion | flops 1159004160 | bytes 11108352 | tf_op jit(solution)/shard_map/dot_general | solution.py:88
  34.2 0.9 convolution_convert_fusion
  35.2 0.9 fusion.15
  36.1 1.9 %collective-permute-start.4 = (bf16[1,4,240,128]{3,2,1,0:T(8,128)(2,1)S(1)}, bf16[1,4,240,128]{3,2,1,0:T(8,128)(2,1)S(1)}, u32[]{:S(2)}, u32[]{:S(2)}) collective-permute-start(bf16[1,4,240,128]{3,2,1,0:T(8,128)(2,1)S(1)} %get-tuple-element.23), channel_id=1, source_target_pairs={{0,1},{1,2},{2,3},{4,5},{5,6},{6,7},{8,9},{9,10},{10,11},{12,13},{... | collective-permute-start | bytes 737288 | tf_op jit(solution)/shard_map/ppermute | solution.py:13
  38.1 2.4 %collective-permute-start.5 = (bf16[1,4,240,128]{3,2,1,0:T(8,128)(2,1)S(1)}, bf16[1,4,240,128]{3,2,1,0:T(8,128)(2,1)S(1)}, u32[]{:S(2)}, u32[]{:S(2)}) collective-permute-start(bf16[1,4,240,128]{3,2,1,0:T(8,128)(2,1)S(1)} %get-tuple-element.24), channel_id=1, source_target_pairs={{1,0},{2,1},{3,2},{5,4},{6,5},{7,6},{9,8},{10,9},{11,10},{13,12},{... | collective-permute-start | bytes 737288 | tf_op jit(solution)/shard_map/ppermute | solution.py:14
  40.5 2.5 %fusion.13 = f32[1152,128]{1,0:T(8,128)S(1)} fusion(bf16[4,4,240,128]{3,2,1,0:T(8,128)(2,1)S(1)} %get-tuple-element.15, bf16[4,4,240,384]{3,2,1,0:T(8,128)(2,1)S(1)} %get-tuple-element.13, bf16[4,4,240,384]{3,2,1,0:T(8,128)(2,1)S(1)} %get-tuple-element.14, bf16[4,4,240,384]{3,2,1,0:T(8,128)(2,1)S(1)} %get-tuple-element.12), kind=kOutput, calls=%fused_computation.22 | convolution fusion | flops 1159004160 | bytes 10420224 | tf_op jit(solution)/shard_map/dot_general | solution.py:111
  43.0 3.2 %collective-permute-start.2 = (bf16[4,2,240,128]{3,2,1,0:T(8,128)(2,1)S(1)}, bf16[4,2,240,128]{3,2,1,0:T(8,128)(2,1)S(1)}, u32[]{:S(2)}, u32[]{:S(2)}) collective-permute-start(bf16[4,2,240,128]{3,2,1,0:T(8,128)(2,1)S(1)} %slice.87), channel_id=1, source_target_pairs={{0,4},{4,8},{8,12},{12,16},{16,20},{20,24},{24,28},{28,32},{32,36}... | collective-permute-start | bytes 1474568 | tf_op jit(solution)/shard_map/ppermute | solution.py:24
  46.3 5.8 %collective-permute-done.5 = bf16[1,4,240,128]{3,2,1,0:T(8,128)(2,1)S(1)} collective-permute-done((bf16[1,4,240,128]{3,2,1,0:T(8,128)(2,1)S(1)}, bf16[1,4,240,128]{3,2,1,0:T(8,128)(2,1)S(1)}, u32[]{:S(2)}, u32[]{:S(2)}) %collective-permute-start.5) | collective-permute-done | bytes 245792 | tf_op jit(solution)/shard_map/ppermute | solution.py:14
  53.1 1.3 %fusion.8 = bf16[6,4,240,384]{3,2,1,0:T(8,128)(2,1)S(1)} fusion(bf16[6,4,239,128]{3,2,1,0:T(8,128)(2,1)S(1)} %get-tuple-element.18, bf16[6,4,239,128]{3,2,1,0:T(8,128)(2,1)S(1)} %get-tuple-element.17, bf16[1,4,240,128]{3,2,1,0:T(8,128)(2,1)S(1)} %collective-permute-done.5, bf16[4,4,240,128]{3,2,1,0:T(8,128)(2,1)S(1)} %get-tuple-element.15, ...), kind=kLoop, calls=%fused_computation.15 | loop fusion | flops 30965760 | bytes 8835072 | tf_op jit(solution)/shard_map/concatenate | solution.py:61
  54.4 3.7 %fusion.24 = (bf16[4,4,240,384]{3,2,1,0:T(8,128)(2,1)}, bf16[4,4,240,384]{3,2,1,0:T(8,128)(2,1)}, bf16[4,4,240,384]{3,2,1,0:T(8,128)(2,1)}) fusion(bf16[6,4,240,384]{3,2,1,0:T(8,128)(2,1)S(1)} %fusion.8), kind=kLoop, calls=%fused_computation.52 | loop fusion | bytes 17694720 | tf_op jit(solution)/shard_map/slice | solution.py:114
  59.4 1.0 convolution_bitcast_fusion
  60.4 0.9 pad_maximum_fusion.10
  61.3 9.8 %all-to-all-start = ((f32[64,24,128]{2,1,0:T(8,128)}), f32[64,24,128]{2,1,0:T(8,128)}, u32[]{:S(2)}, u32[]{:S(2)}) async-start(f32[64,24,128]{2,1,0:T(8,128)} %bitcast.81), calls=%async_computation | async-start | bytes 1572864 | tf_op jit(solution)/shard_map/all_to_all | solution.py:28
  71.1 4.4 %pad_maximum_fusion.1 = bf16[4,4,240,1152]{3,2,1,0:T(8,128)(2,1)S(1)} fusion(bf16[4,4,240,384]{3,2,1,0:T(8,128)(2,1)} %get-tuple-element.10, bf16[4,4,240,384]{3,2,1,0:T(8,128)(2,1)} %get-tuple-element.11, bf16[4,4,240,384]{3,2,1,0:T(8,128)(2,1)} %get-tuple-element.9), kind=kLoop, calls=%fused_computation.7 | loop fusion | flops 26542080 | bytes 17694720 | tf_op jit(solution)/shard_map/concatenate | solution.py:114
  75.6 2.5 %fusion.4 = bf16[3840,128]{1,0:T(8,128)(2,1)S(1)} fusion(bf16[3840,1152]{1,0:T(8,128)(2,1)S(1)} %bitcast.78, bf16[1152,128]{1,0:T(8,128)(2,1)S(1)} %bitcast.87, bf16[3840,128]{1,0:T(8,128)(2,1)S(1)} %bitcast.74), kind=kOutput, calls=%fused_computation.9 | convolution fusion | flops 1133936640 | bytes 11108352 | tf_op jit(solution)/shard_map/dot_general | solution.py:115
  78.1 1.0 copy.31
  79.1 14.3 %all-to-all-done = f32[64,24,128]{2,1,0:T(8,128)} async-done(((f32[64,24,128]{2,1,0:T(8,128)}), f32[64,24,128]{2,1,0:T(8,128)}, u32[]{:S(2)}, u32[]{:S(2)}) %all-to-all-start) | async-done | bytes 786464 | tf_op jit(solution)/shard_map/all_to_all | solution.py:28
  93.3 1.2 %reduce_sum.9 = f32[24,128]{1,0:T(8,128)S(1)} reduce(f32[64,24,128]{2,1,0:T(8,128)} %all-to-all-done, f32[]{:T(128)} %constant.58.clone.1), dimensions={0}, to_apply=%region_0.1 | reduce | flops 193536 | bytes 798724 | tf_op jit(solution)/shard_map/reduce_sum | solution.py:29
  94.6 2.1 %collective-permute-start.6 = (f32[2,6,128]{2,1,0:T(8,128)S(1)}, f32[2,6,128]{2,1,0:T(8,128)S(1)}, u32[]{:S(2)}, u32[]{:S(2)}) collective-permute-start(f32[2,6,128]{2,1,0:T(8,128)S(1)} %dynamic-slice_bitcast_fusion), channel_id=1, source_target_pairs={{0,1},{1,0},{2,3},{3,2},{4,5},{5,4},{6,7},{7,6},{8,9},{9,8},{10,11... | collective-permute-start | bytes 18440 | tf_op jit(solution)/shard_map/ppermute | solution.py:41
  96.7 0.9 convolution_convert_fusion.1
  98.2 1.0 copy.17
  99.2 5.0 %collective-permute-done.7 = f32[1,6,128]{2,1,0:T(8,128)S(1)} collective-permute-done((f32[1,6,128]{2,1,0:T(8,128)S(1)}, f32[1,6,128]{2,1,0:T(8,128)S(1)}, u32[]{:S(2)}, u32[]{:S(2)}) %collective-permute-start.7) | collective-permute-done | bytes 3104 | tf_op jit(solution)/shard_map/ppermute | solution.py:41
  (42 shorter events, 5.4 us)
Async XLA Ops:
  0.6 14.3 %copy-start.3 = (bf16[1,4,4,240,128]{4,3,2,1,0:T(8,128)(2,1)S(1)}, bf16[1,4,4,240,128]{4,3,2,1,0:T(8,128)(2,1)}, u32[]{:S(2)}) copy-start(bf16[1,4,4,240,128]{4,3,2,1,0:T(8,128)(2,1)} %param.5) | copy-start | bytes 2949124
  0.6 15.8 %copy-start.5 = (bf16[3,128,128]{2,1,0:T(8,128)(2,1)S(1)}, bf16[3,128,128]{2,1,0:T(8,128)(2,1)}, u32[]{:S(2)}) copy-start(bf16[3,128,128]{2,1,0:T(8,128)(2,1)} %param.7) | copy-start | bytes 294916
  2.8 16.2 %collective-permute-start = (bf16[1,4,240,128]{3,2,1,0:T(8,128)(2,1)}, bf16[1,4,240,128]{3,2,1,0:T(8,128)(2,1)S(1)}, u32[]{:S(2)}, u32[]{:S(2)}) collective-permute-start(bf16[1,4,240,128]{3,2,1,0:T(8,128)(2,1)} %get-tuple-element.25), channel_id=1, source_target_pairs={{0,1},{1,2},{2,3},{4,5},{5,6},{6,7},{8,9},{9,10},{10,11},{12,13},{... | collective-permute-start | bytes 737288 | tf_op jit(solution)/shard_map/ppermute | solution.py:13
  13.0 13.3 %collective-permute-start.1 = (bf16[1,4,240,128]{3,2,1,0:T(8,128)(2,1)}, bf16[1,4,240,128]{3,2,1,0:T(8,128)(2,1)S(1)}, u32[]{:S(2)}, u32[]{:S(2)}) collective-permute-start(bf16[1,4,240,128]{3,2,1,0:T(8,128)(2,1)} %get-tuple-element.26), channel_id=1, source_target_pairs={{1,0},{2,1},{3,2},{5,4},{6,5},{7,6},{9,8},{10,9},{11,10},{13,12},{... | collective-permute-start | bytes 737288 | tf_op jit(solution)/shard_map/ppermute | solution.py:14
  15.0 18.3 %copy-start = (bf16[1,4,4,240,128]{4,3,1,2,0:T(8,128)(2,1)}, bf16[1,4,4,240,128]{4,3,1,2,0:T(8,128)(2,1)S(1)}, u32[]{:S(2)}) copy-start(bf16[1,4,4,240,128]{4,3,1,2,0:T(8,128)(2,1)S(1)} %copy.33) | copy-start | bytes 2949124
  15.1 18.1 %collective-permute-start.3 = (bf16[4,2,240,128]{3,2,1,0:T(8,128)(2,1)S(1)}, bf16[4,2,240,128]{3,2,1,0:T(8,128)(2,1)S(1)}, u32[]{:S(2)}, u32[]{:S(2)}) collective-permute-start(bf16[4,2,240,128]{3,2,1,0:T(8,128)(2,1)S(1)} %slice.90), channel_id=1, source_target_pairs={{4,0},{8,4},{12,8},{16,12},{20,16},{24,20},{28,24},{32,28},{36,32}... | collective-permute-start | bytes 1474568 | tf_op jit(solution)/shard_map/ppermute | solution.py:24
  28.7 1.0 copy-start.7
  33.3 0.9 copy-start.6
  36.1 10.1 %collective-permute-start.4 = (bf16[1,4,240,128]{3,2,1,0:T(8,128)(2,1)S(1)}, bf16[1,4,240,128]{3,2,1,0:T(8,128)(2,1)S(1)}, u32[]{:S(2)}, u32[]{:S(2)}) collective-permute-start(bf16[1,4,240,128]{3,2,1,0:T(8,128)(2,1)S(1)} %get-tuple-element.23), channel_id=1, source_target_pairs={{0,1},{1,2},{2,3},{4,5},{5,6},{6,7},{8,9},{9,10},{10,11},{12,13},{... | collective-permute-start | bytes 737288 | tf_op jit(solution)/shard_map/ppermute | solution.py:13
  38.1 14.0 %collective-permute-start.5 = (bf16[1,4,240,128]{3,2,1,0:T(8,128)(2,1)S(1)}, bf16[1,4,240,128]{3,2,1,0:T(8,128)(2,1)S(1)}, u32[]{:S(2)}, u32[]{:S(2)}) collective-permute-start(bf16[1,4,240,128]{3,2,1,0:T(8,128)(2,1)S(1)} %get-tuple-element.24), channel_id=1, source_target_pairs={{1,0},{2,1},{3,2},{5,4},{6,5},{7,6},{9,8},{10,9},{11,10},{13,12},{... | collective-permute-start | bytes 737288 | tf_op jit(solution)/shard_map/ppermute | solution.py:14
  43.0 15.1 %collective-permute-start.2 = (bf16[4,2,240,128]{3,2,1,0:T(8,128)(2,1)S(1)}, bf16[4,2,240,128]{3,2,1,0:T(8,128)(2,1)S(1)}, u32[]{:S(2)}, u32[]{:S(2)}) collective-permute-start(bf16[4,2,240,128]{3,2,1,0:T(8,128)(2,1)S(1)} %slice.87), channel_id=1, source_target_pairs={{0,4},{4,8},{8,12},{12,16},{16,20},{20,24},{24,28},{28,32},{32,36}... | collective-permute-start | bytes 1474568 | tf_op jit(solution)/shard_map/ppermute | solution.py:24
  58.2 1.2 %copy-start.4 = (bf16[1,4,4,240,128]{4,3,2,1,0:T(8,128)(2,1)S(1)}, bf16[1,4,4,240,128]{4,3,2,1,0:T(8,128)(2,1)}, u32[]{:S(2)}) copy-start(bf16[1,4,4,240,128]{4,3,2,1,0:T(8,128)(2,1)} %param.5) | copy-start | bytes 2949124
  61.3 32.0 %all-to-all-start = ((f32[64,24,128]{2,1,0:T(8,128)}), f32[64,24,128]{2,1,0:T(8,128)}, u32[]{:S(2)}, u32[]{:S(2)}) async-start(f32[64,24,128]{2,1,0:T(8,128)} %bitcast.81), calls=%async_computation | async-start | bytes 1572864 | tf_op jit(solution)/shard_map/all_to_all | solution.py:28
  71.1 4.5 %copy-start.1 = (bf16[1,4,4,240,128]{4,3,1,2,0:T(8,128)(2,1)S(1)}, bf16[1,4,4,240,128]{4,3,1,2,0:T(8,128)(2,1)}, u32[]{:S(2)}) copy-start(bf16[1,4,4,240,128]{4,3,1,2,0:T(8,128)(2,1)} %copy-done) | copy-start | bytes 2949124
  71.1 4.5 %copy-start.8 = (bf16[3,3,128,128]{2,3,1,0:T(8,128)(2,1)S(1)}, bf16[3,3,128,128]{2,3,1,0:T(8,128)(2,1)}, u32[]{:S(2)}) copy-start(bf16[3,3,128,128]{2,3,1,0:T(8,128)(2,1)} %copy.15) | copy-start | bytes 884740
  94.6 3.1 %collective-permute-start.6 = (f32[2,6,128]{2,1,0:T(8,128)S(1)}, f32[2,6,128]{2,1,0:T(8,128)S(1)}, u32[]{:S(2)}, u32[]{:S(2)}) collective-permute-start(f32[2,6,128]{2,1,0:T(8,128)S(1)} %dynamic-slice_bitcast_fusion), channel_id=1, source_target_pairs={{0,1},{1,0},{2,3},{3,2},{4,5},{5,4},{6,7},{7,6},{8,9},{9,8},{10,11... | collective-permute-start | bytes 18440 | tf_op jit(solution)/shard_map/ppermute | solution.py:41
  96.7 1.2 %copy-start.2 = (bf16[1,4,4,240,128]{4,3,2,1,0:T(8,128)(2,1)S(1)}, bf16[1,4,4,240,128]{4,3,2,1,0:T(8,128)(2,1)}, u32[]{:S(2)}) copy-start(bf16[1,4,4,240,128]{4,3,2,1,0:T(8,128)(2,1)} %param.4) | copy-start | bytes 2949124
  97.7 6.5 %collective-permute-start.7 = (f32[1,6,128]{2,1,0:T(8,128)S(1)}, f32[1,6,128]{2,1,0:T(8,128)S(1)}, u32[]{:S(2)}, u32[]{:S(2)}) collective-permute-start(f32[1,6,128]{2,1,0:T(8,128)S(1)} %constant_dynamic-slice_fusion), channel_id=1, source_target_pairs={{0,2},{1,3},{2,0},{3,1},{4,6},{5,7},{6,4},{7,5},{8,10},{9,11},{10,... | collective-permute-start | bytes 9224 | tf_op jit(solution)/shard_map/ppermute | solution.py:41

commit v14 on v11

--- a/solution.py
+++ b/solution.py
@@ -32,15 +32,15 @@
 def halving_sum(blocks, axis):
     n = blocks.shape[0]
     me = lax.axis_index(axis)
-    bit = 1
-    while bit < n:
+    bit = n // 2
+    while bit >= 1:
         mine = (me // bit) % 2
-        halves = blocks.reshape((-1, 2) + blocks.shape[1:])
-        keep = lax.dynamic_index_in_dim(halves, mine, axis=1, keepdims=False)
-        send = lax.dynamic_index_in_dim(halves, 1 - mine, axis=1, keepdims=False)
+        halves = blocks.reshape((2, -1) + blocks.shape[1:])
+        keep = lax.dynamic_index_in_dim(halves, mine, axis=0, keepdims=False)
+        send = lax.dynamic_index_in_dim(halves, 1 - mine, axis=0, keepdims=False)
         got = lax.ppermute(send, axis, [(i, i ^ bit) for i in range(n)])
         blocks = keep + got
-        bit *= 2
+        bit //= 2
     return blocks[0]
 
 

time: 99.4 us -> 99.6 us (level)
  transfers between devices with their start and end apart: 9 -> 9, of which waited for: 5 -> 4; matrix products, arithmetic and copies ran while one was open for 25% -> 25% of each run, Pallas kernels for 0% -> 0%
where the time goes in v14:
time: 99.6 us; the launch traced here: 99.1 us
  starting transfers between devices  32.3 us (32%)
  waiting for transfers between devices  29.6 us (30%)
  local copies, waits for them, and re-layouts  15.3 us (15%)
  matrix products  11.4 us (11%)
  other arithmetic  9.25 us (9%)
  between operations  1.12 us (1%)
    ppermute x2, waiting for transfers between devices, row_halo(): after = lax.ppermute(shard[:1], 'row', down)  17 us
    ppermute x2, starting transfers between devices, row_halo(): before = lax.ppermute(shard[-1:], 'row', up)  12.5 us
    all_to_all x1, starting transfers between devices, a2a_sum(): got = lax.all_to_all(blocks, axis, split_axis=0, concat_axis=0, tiled=True)  11.1 us
    all_to_all x1, waiting for transfers between devices, a2a_sum(): got = lax.all_to_all(blocks, axis, split_axis=0, concat_axis=0, tiled=True)  7.19 us
    ppermute x2, waiting for transfers between devices, halving_sum(): got = lax.ppermute(send, axis, [(i, i ^ bit) for i in range(n)])  5.43 us
    ppermute x2, starting transfers between devices, frame_shift(): return lax.ppermute(piece, 'frame', pairs)  4.52 us
    unnamed x27, local copies, waits for them, and re-layouts  4.47 us
    ppermute x2, starting transfers between devices, row_halo(): after = lax.ppermute(shard[:1], 'row', down)  4.11 us
  transfers between devices with their start and end apart: 9, of which 4 were waited for; matrix products, arithmetic and copies ran while one was open for 25% of the time, Pallas kernels for 0%

profile of v14, /device:TPU:1, one launch (start us, length us, event | category | flops | bytes accessed | tf_op | source)
XLA Modules:
  0.0 99.1 jit_solution(17612282524152446053)
XLA Ops:
  0.7 1.4 %copy.33 = bf16[1,4,4,240,128]{4,3,1,2,0:T(8,128)(2,1)S(1)} copy(bf16[1,4,4,240,128]{4,3,2,1,0:T(8,128)(2,1)} %param.4) | data formatting | bytes 1966080 | tf_op args[0]
  2.8 10.2 %collective-permute-start = (bf16[1,4,240,128]{3,2,1,0:T(8,128)(2,1)}, bf16[1,4,240,128]{3,2,1,0:T(8,128)(2,1)S(1)}, u32[]{:S(2)}, u32[]{:S(2)}) collective-permute-start(bf16[1,4,240,128]{3,2,1,0:T(8,128)(2,1)} %get-tuple-element.25), channel_id=1, source_target_pairs={{0,1},{1,2},{2,3},{4,5},{5,6},{6,7},{8,9},{9,10},{10,11},{12,13},{... | collective-permute-start | bytes 737288 | tf_op jit(solution)/shard_map/ppermute | solution.py:13
  13.0 1.9 %collective-permute-start.1 = (bf16[1,4,240,128]{3,2,1,0:T(8,128)(2,1)}, bf16[1,4,240,128]{3,2,1,0:T(8,128)(2,1)S(1)}, u32[]{:S(2)}, u32[]{:S(2)}) collective-permute-start(bf16[1,4,240,128]{3,2,1,0:T(8,128)(2,1)} %get-tuple-element.26), channel_id=1, source_target_pairs={{1,0},{2,1},{3,2},{5,4},{6,5},{7,6},{9,8},{10,9},{11,10},{13,12},{... | collective-permute-start | bytes 737288 | tf_op jit(solution)/shard_map/ppermute | solution.py:14
  15.9 1.3 %collective-permute-start.3 = (bf16[4,2,240,128]{3,2,1,0:T(8,128)(2,1)}, bf16[4,2,240,128]{3,2,1,0:T(8,128)(2,1)S(1)}, u32[]{:S(2)}, u32[]{:S(2)}) collective-permute-start(bf16[4,2,240,128]{3,2,1,0:T(8,128)(2,1)} %slice.123), channel_id=1, source_target_pairs={{4,0},{8,4},{12,8},{16,12},{20,16},{24,20},{28,24},{32,28},{36,32}... | collective-permute-start | bytes 1474568 | tf_op jit(solution)/shard_map/ppermute | solution.py:24
  18.1 1.0 %copy.14 = bf16[3,128,128]{1,2,0:T(8,128)(2,1)S(1)} copy(bf16[3,128,128]{2,1,0:T(8,128)(2,1)} %param.7) | data formatting | bytes 196608 | tf_op args[3]
  19.8 6.6 %collective-permute-done.1 = bf16[1,4,240,128]{3,2,1,0:T(8,128)(2,1)S(1)} collective-permute-done((bf16[1,4,240,128]{3,2,1,0:T(8,128)(2,1)}, bf16[1,4,240,128]{3,2,1,0:T(8,128)(2,1)S(1)}, u32[]{:S(2)}, u32[]{:S(2)}) %collective-permute-start.1) | collective-permute-done | bytes 245792 | tf_op jit(solution)/shard_map/ppermute | solution.py:14
  27.4 1.4 %fusion.6 = bf16[6,4,240,384]{3,2,1,0:T(8,128)(2,1)S(1)} fusion(bf16[6,4,239,128]{3,2,1,0:T(8,128)(2,1)S(1)} %get-tuple-element.20, bf16[6,4,239,128]{3,2,1,0:T(8,128)(2,1)S(1)} %get-tuple-element.19, bf16[1,4,240,128]{3,2,1,0:T(8,128)(2,1)S(1)} %collective-permute-done.1, bf16[4,4,240,128]{3,2,1,0:T(8,128)(2,1)S(1)} %bitcast.111, ...), kind=kLoop, calls=%fused_computation.15 | loop fusion | flops 30965760 | bytes 8835072 | tf_op jit(solution)/shard_map/concatenate | solution.py:61
  28.8 1.1 %fusion.20 = (bf16[4,4,240,384]{3,2,1,0:T(8,128)(2,1)S(1)}, bf16[4,4,240,384]{3,2,1,0:T(8,128)(2,1)S(1)}, bf16[4,4,240,384]{3,2,1,0:T(8,128)(2,1)S(1)}) fusion(bf16[6,4,240,384]{3,2,1,0:T(8,128)(2,1)S(1)} %fusion.6), kind=kLoop, calls=%fused_computation.53 | loop fusion | bytes 17694720 | tf_op jit(solution)/shard_map/slice | solution.py:89
  29.8 0.9 fusion.28
  30.8 0.9 convolution_add_fusion.4
  31.8 1.0 convolution_add_fusion.3
  33.3 0.9 convolution_convert_fusion
  35.2 1.0 convolution_bitcast_fusion
  36.2 1.0 convolution_bitcast_fusion.1
  37.2 3.2 %collective-permute-start.2 = (bf16[4,2,240,128]{3,2,1,0:T(8,128)(2,1)S(1)}, bf16[4,2,240,128]{3,2,1,0:T(8,128)(2,1)S(1)}, u32[]{:S(2)}, u32[]{:S(2)}) collective-permute-start(bf16[4,2,240,128]{3,2,1,0:T(8,128)(2,1)S(1)} %slice.120), channel_id=1, source_target_pairs={{0,4},{4,8},{8,12},{12,16},{16,20},{20,24},{24,28},{28,32},{32,36}... | collective-permute-start | bytes 1474568 | tf_op jit(solution)/shard_map/ppermute | solution.py:24
  40.5 2.3 %collective-permute-start.4 = (bf16[1,4,240,128]{3,2,1,0:T(8,128)(2,1)S(1)}, bf16[1,4,240,128]{3,2,1,0:T(8,128)(2,1)S(1)}, u32[]{:S(2)}, u32[]{:S(2)}) collective-permute-start(bf16[1,4,240,128]{3,2,1,0:T(8,128)(2,1)S(1)} %get-tuple-element.23), channel_id=1, source_target_pairs={{0,1},{1,2},{2,3},{4,5},{5,6},{6,7},{8,9},{9,10},{10,11},{12,13},{... | collective-permute-start | bytes 737288 | tf_op jit(solution)/shard_map/ppermute | solution.py:13
  42.8 2.2 %collective-permute-start.5 = (bf16[1,4,240,128]{3,2,1,0:T(8,128)(2,1)S(1)}, bf16[1,4,240,128]{3,2,1,0:T(8,128)(2,1)S(1)}, u32[]{:S(2)}, u32[]{:S(2)}) collective-permute-start(bf16[1,4,240,128]{3,2,1,0:T(8,128)(2,1)S(1)} %get-tuple-element.24), channel_id=1, source_target_pairs={{1,0},{2,1},{3,2},{5,4},{6,5},{7,6},{9,8},{10,9},{11,10},{13,12},{... | collective-permute-start | bytes 737288 | tf_op jit(solution)/shard_map/ppermute | solution.py:14
  45.0 1.0 convolution_bitcast_fusion.2
  46.0 10.5 %collective-permute-done.5 = bf16[1,4,240,128]{3,2,1,0:T(8,128)(2,1)S(1)} collective-permute-done((bf16[1,4,240,128]{3,2,1,0:T(8,128)(2,1)S(1)}, bf16[1,4,240,128]{3,2,1,0:T(8,128)(2,1)S(1)}, u32[]{:S(2)}, u32[]{:S(2)}) %collective-permute-start.5) | collective-permute-done | bytes 245792 | tf_op jit(solution)/shard_map/ppermute | solution.py:14
  57.4 2.5 %fusion.8 = bf16[6,4,240,384]{3,2,1,0:T(8,128)(2,1)} fusion(bf16[6,4,239,128]{3,2,1,0:T(8,128)(2,1)S(1)} %get-tuple-element.18, bf16[6,4,239,128]{3,2,1,0:T(8,128)(2,1)S(1)} %get-tuple-element.17, bf16[1,4,240,128]{3,2,1,0:T(8,128)(2,1)S(1)} %collective-permute-done.5, bf16[4,4,240,128]{3,2,1,0:T(8,128)(2,1)S(1)} %get-tuple-element.15, ...), kind=kLoop, calls=%fused_computation.17 | loop fusion | flops 30965760 | bytes 8835072 | tf_op jit(solution)/shard_map/concatenate | solution.py:61
  61.3 1.0 convolution_bitcast_fusion.3
  62.2 0.9 pad_maximum_fusion.4
  63.2 11.1 %all-to-all-start = ((f32[64,24,128]{2,1,0:T(8,128)}), f32[64,24,128]{2,1,0:T(8,128)}, u32[]{:S(2)}, u32[]{:S(2)}) async-start(f32[64,24,128]{2,1,0:T(8,128)} %bitcast.41), calls=%async_computation | async-start | bytes 1572864 | tf_op jit(solution)/shard_map/all_to_all | solution.py:28
  74.3 4.1 %fusion.19 = (bf16[4,4,240,384]{3,2,1,0:T(8,128)(2,1)S(1)}, bf16[4,4,240,384]{3,2,1,0:T(8,128)(2,1)S(1)}, bf16[4,4,240,384]{3,2,1,0:T(8,128)(2,1)S(1)}) fusion(bf16[6,4,240,384]{3,2,1,0:T(8,128)(2,1)} %fusion.8), kind=kLoop, calls=%fused_computation.52 | loop fusion | bytes 17694720 | tf_op jit(solution)/shard_map/slice | solution.py:123
  78.4 0.9 convolution_add_fusion.2
  79.3 0.9 convolution_add_fusion.1
  80.3 0.9 fusion.4
  81.3 1.0 %copy.32 = bf16[4,4,240,128]{3,2,0,1:T(8,128)(2,1)} copy(bf16[4,4,240,128]{3,2,1,0:T(8,128)(2,1)S(1)} %bitcast.112) | data formatting | bytes 1966080 | tf_op jit(solution)/shard_map/reshape | solution.py:125
  82.3 7.2 %all-to-all-done = f32[64,24,128]{2,1,0:T(8,128)} async-done(((f32[64,24,128]{2,1,0:T(8,128)}), f32[64,24,128]{2,1,0:T(8,128)}, u32[]{:S(2)}, u32[]{:S(2)}) %all-to-all-start) | async-done | bytes 786464 | tf_op jit(solution)/shard_map/all_to_all | solution.py:28
  89.5 1.2 %reduce_sum.9 = f32[24,128]{1,0:T(8,128)S(1)} reduce(f32[64,24,128]{2,1,0:T(8,128)} %all-to-all-done, f32[]{:T(128)} %constant.58.clone.1), dimensions={0}, to_apply=%region_0.1 | reduce | flops 193536 | bytes 798724 | tf_op jit(solution)/shard_map/reduce_sum | solution.py:29
  91.8 5.4 %collective-permute-done.6 = f32[2,6,128]{2,1,0:T(8,128)S(1)} collective-permute-done((f32[2,6,128]{2,1,0:T(8,128)S(1)}, f32[2,6,128]{2,1,0:T(8,128)S(1)}, u32[]{:S(2)}, u32[]{:S(2)}) %collective-permute-start.6) | collective-permute-done | bytes 6176 | tf_op jit(solution)/shard_map/ppermute | solution.py:41
  97.5 1.0 %copy.17 = bf16[1,4,4,240,128]{4,3,2,1,0:T(8,128)(2,1)} copy(bf16[1,4,4,240,128]{4,3,1,2,0:T(8,128)(2,1)S(1)} %fusion.16) | data formatting | bytes 1966080
  (53 shorter events, 10.0 us)
Async XLA Ops:
  0.6 14.3 %copy-start.4 = (bf16[1,4,4,240,128]{4,3,2,1,0:T(8,128)(2,1)S(1)}, bf16[1,4,4,240,128]{4,3,2,1,0:T(8,128)(2,1)}, u32[]{:S(2)}) copy-start(bf16[1,4,4,240,128]{4,3,2,1,0:T(8,128)(2,1)} %param.5) | copy-start | bytes 2949124
  0.6 16.5 %copy-start.3 = (bf16[3,3,128,128]{3,2,1,0:T(8,128)(2,1)S(1)}, bf16[3,3,128,128]{3,2,1,0:T(8,128)(2,1)}, u32[]{:S(2)}) copy-start(bf16[3,3,128,128]{3,2,1,0:T(8,128)(2,1)} %param.6) | copy-start | bytes 884740
  2.8 17.0 %collective-permute-start = (bf16[1,4,240,128]{3,2,1,0:T(8,128)(2,1)}, bf16[1,4,240,128]{3,2,1,0:T(8,128)(2,1)S(1)}, u32[]{:S(2)}, u32[]{:S(2)}) collective-permute-start(bf16[1,4,240,128]{3,2,1,0:T(8,128)(2,1)} %get-tuple-element.25), channel_id=1, source_target_pairs={{0,1},{1,2},{2,3},{4,5},{5,6},{6,7},{8,9},{9,10},{10,11},{12,13},{... | collective-permute-start | bytes 737288 | tf_op jit(solution)/shard_map/ppermute | solution.py:13
  13.0 13.3 %collective-permute-start.1 = (bf16[1,4,240,128]{3,2,1,0:T(8,128)(2,1)}, bf16[1,4,240,128]{3,2,1,0:T(8,128)(2,1)S(1)}, u32[]{:S(2)}, u32[]{:S(2)}) collective-permute-start(bf16[1,4,240,128]{3,2,1,0:T(8,128)(2,1)} %get-tuple-element.26), channel_id=1, source_target_pairs={{1,0},{2,1},{3,2},{5,4},{6,5},{7,6},{9,8},{10,9},{11,10},{13,12},{... | collective-permute-start | bytes 737288 | tf_op jit(solution)/shard_map/ppermute | solution.py:14
  15.9 16.9 %collective-permute-start.3 = (bf16[4,2,240,128]{3,2,1,0:T(8,128)(2,1)}, bf16[4,2,240,128]{3,2,1,0:T(8,128)(2,1)S(1)}, u32[]{:S(2)}, u32[]{:S(2)}) collective-permute-start(bf16[4,2,240,128]{3,2,1,0:T(8,128)(2,1)} %slice.123), channel_id=1, source_target_pairs={{4,0},{8,4},{12,8},{16,12},{20,16},{24,20},{28,24},{32,28},{36,32}... | collective-permute-start | bytes 1474568 | tf_op jit(solution)/shard_map/ppermute | solution.py:24
  28.8 1.1 %copy-start.10 = (bf16[1,3,128,128]{3,2,1,0:T(8,128)(2,1)S(1)}, bf16[1,3,128,128]{3,2,1,0:T(8,128)(2,1)}, u32[]{:S(2)}) copy-start(bf16[1,3,128,128]{3,2,1,0:T(8,128)(2,1)} %get-tuple-element.32) | copy-start | bytes 294916
  29.8 1.0 copy-start.7
  30.8 1.0 copy-start.6
  37.2 22.7 %collective-permute-start.2 = (bf16[4,2,240,128]{3,2,1,0:T(8,128)(2,1)S(1)}, bf16[4,2,240,128]{3,2,1,0:T(8,128)(2,1)S(1)}, u32[]{:S(2)}, u32[]{:S(2)}) collective-permute-start(bf16[4,2,240,128]{3,2,1,0:T(8,128)(2,1)S(1)} %slice.120), channel_id=1, source_target_pairs={{0,4},{4,8},{8,12},{12,16},{16,20},{20,24},{24,28},{28,32},{32,36}... | collective-permute-start | bytes 1474568 | tf_op jit(solution)/shard_map/ppermute | solution.py:24
  40.5 5.5 %collective-permute-start.4 = (bf16[1,4,240,128]{3,2,1,0:T(8,128)(2,1)S(1)}, bf16[1,4,240,128]{3,2,1,0:T(8,128)(2,1)S(1)}, u32[]{:S(2)}, u32[]{:S(2)}) collective-permute-start(bf16[1,4,240,128]{3,2,1,0:T(8,128)(2,1)S(1)} %get-tuple-element.23), channel_id=1, source_target_pairs={{0,1},{1,2},{2,3},{4,5},{5,6},{6,7},{8,9},{9,10},{10,11},{12,13},{... | collective-permute-start | bytes 737288 | tf_op jit(solution)/shard_map/ppermute | solution.py:13
  42.8 13.6 %collective-permute-start.5 = (bf16[1,4,240,128]{3,2,1,0:T(8,128)(2,1)S(1)}, bf16[1,4,240,128]{3,2,1,0:T(8,128)(2,1)S(1)}, u32[]{:S(2)}, u32[]{:S(2)}) collective-permute-start(bf16[1,4,240,128]{3,2,1,0:T(8,128)(2,1)S(1)} %get-tuple-element.24), channel_id=1, source_target_pairs={{1,0},{2,1},{3,2},{5,4},{6,5},{7,6},{9,8},{10,9},{11,10},{13,12},{... | collective-permute-start | bytes 737288 | tf_op jit(solution)/shard_map/ppermute | solution.py:14
  60.0 1.2 %copy-start.5 = (bf16[1,4,4,240,128]{4,3,2,1,0:T(8,128)(2,1)S(1)}, bf16[1,4,4,240,128]{4,3,2,1,0:T(8,128)(2,1)}, u32[]{:S(2)}) copy-start(bf16[1,4,4,240,128]{4,3,2,1,0:T(8,128)(2,1)} %param.5) | copy-start | bytes 2949124
  61.3 1.9 %copy-start = (bf16[4,4,240,384]{3,2,1,0:T(8,128)(2,1)}, bf16[4,4,240,384]{3,2,1,0:T(8,128)(2,1)S(1)}, u32[]{:S(2)}) copy-start(bf16[4,4,240,384]{3,2,1,0:T(8,128)(2,1)S(1)} %fusion.10) | copy-start | bytes 8847364
  63.2 26.3 %all-to-all-start = ((f32[64,24,128]{2,1,0:T(8,128)}), f32[64,24,128]{2,1,0:T(8,128)}, u32[]{:S(2)}, u32[]{:S(2)}) async-start(f32[64,24,128]{2,1,0:T(8,128)} %bitcast.41), calls=%async_computation | async-start | bytes 1572864 | tf_op jit(solution)/shard_map/all_to_all | solution.py:28
  79.3 1.0 copy-start.8
  80.3 10.5 %copy-start.1 = (bf16[4,4,240,384]{3,2,1,0:T(8,128)(2,1)S(1)}, bf16[4,4,240,384]{3,2,1,0:T(8,128)(2,1)}, u32[]{:S(2)}) copy-start(bf16[4,4,240,384]{3,2,1,0:T(8,128)(2,1)} %copy-done) | copy-start | bytes 8847364
  80.3 10.5 %copy-start.9 = (bf16[3,128,128]{2,1,0:T(8,128)(2,1)S(1)}, bf16[3,128,128]{2,1,0:T(8,128)(2,1)}, u32[]{:S(2)}) copy-start(bf16[3,128,128]{2,1,0:T(8,128)(2,1)} %param.7) | copy-start | bytes 294916
  90.7 6.5 %collective-permute-start.6 = (f32[2,6,128]{2,1,0:T(8,128)S(1)}, f32[2,6,128]{2,1,0:T(8,128)S(1)}, u32[]{:S(2)}, u32[]{:S(2)}) collective-permute-start(f32[2,6,128]{2,1,0:T(8,128)S(1)} %dynamic-slice_bitcast_fusion), channel_id=1, source_target_pairs={{0,2},{1,3},{2,0},{3,1},{4,6},{5,7},{6,4},{7,5},{8,10},{9,11},{10,... | collective-permute-start | bytes 18440 | tf_op jit(solution)/shard_map/ppermute | solution.py:41
  90.8 6.4 %copy-start.2 = (bf16[1,4,4,240,128]{4,3,2,1,0:T(8,128)(2,1)S(1)}, bf16[1,4,4,240,128]{4,3,2,1,0:T(8,128)(2,1)}, u32[]{:S(2)}) copy-start(bf16[1,4,4,240,128]{4,3,2,1,0:T(8,128)(2,1)} %param.4) | copy-start | bytes 2949124
  97.2 1.3 %collective-permute-start.7 = (f32[1,6,128]{2,1,0:T(8,128)S(1)}, f32[1,6,128]{2,1,0:T(8,128)S(1)}, u32[]{:S(2)}, u32[]{:S(2)}) collective-permute-start(f32[1,6,128]{2,1,0:T(8,128)S(1)} %constant_dynamic-slice_fusion), channel_id=1, source_target_pairs={{0,1},{1,0},{2,3},{3,2},{4,5},{5,4},{6,7},{7,6},{8,9},{9,8},{10,11... | collective-permute-start | bytes 9224 | tf_op jit(solution)/shard_map/ppermute | solution.py:41
